TPU v7x, 32 devices: a whole 2x2x4 slice. The times are simulated.
32 devices in a mesh: row: 8 (over z, x), col: 4 (over y, core).
Axes of the slice: x: 2, y: 2, z: 4, core: 2. Of those that a mesh axis runs over, the one named last changes fastest.
Arguments:
- displacement: bfloat16 [3, 8, 512, 1024], P(None, 'row', 'col'), may hold values from -8 to 8
- magnetic: bfloat16 [3, 8, 512, 1024], P(None, 'row', 'col'), may hold values from -6 to 6
- region: int32 [8, 512, 1024], P('row', 'col'), may hold values from 0 to 7
- permittivity: float32 [8], replicated, may hold values from 1 to 12
Outputs:
- magnetic_new: bfloat16 [3, 8, 512, 1024], P(None, 'row', 'col')
All inputs are finite; a program needn't handle non-finite values.
Results may differ from a plain program's by a relative error of at most 0.0065.
Values may be sent and summed in bfloat16 or wider, within the bound.
No kernel may reach another device: no remote copies, remote signals or barrier semaphores. Data moves between devices by JAX's collectives and lax.ppermute only.
A program may use at most 64 MiB of HBM per device.

v0:
```python
import math

import numpy as np
import jax
import jax.numpy as jnp
from jax import lax
from jax.sharding import PartitionSpec as P

TIME_STEP = 0.5
F32 = jnp.float32
BF16 = jnp.bfloat16


def wavenumber(wave_index, length):
    signed = jnp.where(2 * wave_index < length, wave_index, wave_index - length)
    return jnp.where(
        2 * wave_index == length, 0.0, signed.astype(F32) * (2.0 * math.pi / length)
    )


def rounded(values):
    return lax.reduce_precision(values, exponent_bits=8, mantissa_bits=7)


def split_parts(values):
    high = rounded(values)
    low = values - high
    return high.astype(BF16), low.astype(BF16)


def direct_phase(rows, cols, length, step):
    product = (lax.iota(jnp.int32, rows)[:, None] * step) * lax.iota(jnp.int32, cols)[None, :]
    angle = (product % length).astype(F32) * (2.0 * math.pi / length)
    return jnp.cos(angle), jnp.sin(angle)


def phase_table(rows, cols, length):
    block = 32
    if rows % block or rows <= block:
        return direct_phase(rows, cols, length, 1)
    outer_cos, outer_sin = direct_phase(rows // block, cols, length, block)
    inner_cos, inner_sin = direct_phase(block, cols, length, 1)
    outer_cos, outer_sin = outer_cos[:, None], outer_sin[:, None]
    inner_cos, inner_sin = inner_cos[None], inner_sin[None]
    cosine = outer_cos * inner_cos - outer_sin * inner_sin
    sine = outer_sin * inner_cos + outer_cos * inner_sin
    return cosine.reshape(rows, cols), sine.reshape(rows, cols)


def x_kernel(span_x):
    index = np.arange(span_x)
    signed = np.where(2 * index < span_x, index, index - span_x)
    qx = np.where(2 * index == span_x, 0.0, signed * (2.0 * math.pi / span_x))
    shift = np.arange(span_x)
    phases = np.exp(2j * math.pi * np.outer(shift, index) / span_x)
    taps = (phases * (-0.5j * qx)[None, :]).sum(axis=1) / span_x
    taps = taps.real
    matrix = taps[(shift[:, None] - shift[None, :]) % span_x]
    return matrix.astype(np.float32)


def mat(table_parts, operand, spec):
    total = None
    for part in table_parts:
        term = jnp.einsum(spec, part, operand, preferred_element_type=F32)
        total = term if total is None else total + term
    return total


def curl_update(y_real, y_imag, wave_y, wave_z, kernel):
    half = TIME_STEP

    def along_x(values):
        return jnp.einsum("ab,jbk->jak", kernel, values, precision=lax.Precision.HIGHEST)

    xr, yr, zr = y_real[0], y_real[1], y_real[2]
    xi, yi, zi = y_imag[0], y_imag[1], y_imag[2]
    qy = half * wave_y
    qz = half * wave_z[:, None, None]
    gyr, gyi = along_x(yr), along_x(yi)
    gzr, gzi = along_x(zr), along_x(zi)
    b_real = jnp.stack([qy * zi - qz * yi, qz * xi - gzr, gyr - qy * xi])
    b_imag = jnp.stack([qz * yr - qy * zr, -qz * xr - gzi, gyi + qy * xr])
    return b_real, b_imag


def on_device(displacement, magnetic, region, permittivity):
    row_count = lax.axis_size("row")
    col_count = lax.axis_size("col")
    devices = row_count * col_count
    members, local_x, local_y, depth = displacement.shape
    width_y = local_y * col_count
    span_x = local_x * row_count
    hermitian = (depth // 2) % devices == 0
    columns = depth // 2 if hermitian else depth
    per_device = columns // devices
    me = lax.axis_index("row") * col_count + lax.axis_index("col")

    reciprocal = 1.0 / permittivity
    cell_scale = jnp.zeros(region.shape, F32)
    for region_id in range(permittivity.shape[0]):
        cell_scale = jnp.where(region == region_id, reciprocal[region_id], cell_scale)
    electric = displacement.astype(F32) * cell_scale[None]

    cos_z, sin_z = phase_table(depth, columns, depth)
    if hermitian:
        parity = (1 - 2 * (lax.iota(jnp.int32, depth) % 2)).astype(F32)
        sin_part = jnp.concatenate([parity[:, None], -sin_z[:, 1:]], axis=1)
    else:
        sin_part = -sin_z
    table_z = jnp.concatenate([cos_z, sin_part], axis=1)
    z_high, z_low = split_parts(table_z)

    e_high, e_low = split_parts(electric)
    spec_z = "zk,clyz->clky"
    spectrum = (
        jnp.einsum(spec_z, z_high, e_high, preferred_element_type=F32)
        + jnp.einsum(spec_z, z_high, e_low, preferred_element_type=F32)
        + jnp.einsum(spec_z, z_low, e_high, preferred_element_type=F32)
    )
    spectrum = spectrum.astype(BF16).reshape(
        members, local_x, 2, devices, per_device, local_y
    )
    gathered = lax.all_to_all(
        spectrum, ("row", "col"), split_axis=3, concat_axis=5, tiled=True
    )
    gathered = gathered.reshape(members, local_x, 2, per_device, row_count, width_y)
    gathered = jnp.moveaxis(gathered, 1, 4).reshape(
        members, 2, per_device, span_x, width_y
    )

    cos_y, sin_y = phase_table(width_y, width_y, width_y)
    cos_y_parts = split_parts(cos_y)
    sin_y_parts = split_parts(sin_y)
    spec_y = "yk,cpjxy->cpjxk"
    by_cos = mat(cos_y_parts, gathered, spec_y)
    by_sin = mat(sin_y_parts, gathered, spec_y)
    y_real = by_cos[:, 0] + by_sin[:, 1]
    y_imag = by_cos[:, 1] - by_sin[:, 0]

    kernel = jnp.asarray(x_kernel(span_x))
    wave_y = wavenumber(lax.iota(jnp.int32, width_y), width_y)
    wave_z = wavenumber(me * per_device + lax.iota(jnp.int32, per_device), depth)

    def inverse_y(b_real, b_imag):
        stacked = jnp.stack([b_real, b_imag], axis=1).astype(BF16)
        by_cos = mat(cos_y_parts, stacked, spec_y)
        by_sin = mat(sin_y_parts, stacked, spec_y)
        scale = 1.0 / width_y
        out_real = (by_cos[:, 0] - by_sin[:, 1]) * scale
        out_imag = (by_cos[:, 1] + by_sin[:, 0]) * scale
        return rounded(out_real), rounded(out_imag)

    b_real, b_imag = curl_update(rounded(y_real), rounded(y_imag), wave_y, wave_z, kernel)
    back_real, back_imag = inverse_y(rounded(b_real), rounded(b_imag))

    if hermitian:
        first_real = y_real[:, 0]
        first_imag = y_imag[:, 0]

        def mirrored(values):
            return jnp.roll(jnp.flip(values, axis=-1), 1, axis=-1)

        mirror_real = mirrored(first_real)
        mirror_imag = mirrored(first_imag)
        plane_real = jnp.stack(
            [0.5 * (first_real + mirror_real), 0.5 * (first_imag + mirror_imag)], axis=1
        )
        plane_imag = jnp.stack(
            [0.5 * (first_imag - mirror_imag), -0.5 * (first_real - mirror_real)], axis=1
        )
        pb_real, pb_imag = curl_update(
            rounded(plane_real), rounded(plane_imag), wave_y, jnp.zeros((2,), F32), kernel
        )
        pback_real, _ = inverse_y(rounded(pb_real), rounded(pb_imag))
        is_first = me == 0
        fixed_real = jnp.where(is_first, pback_real[:, 0], back_real[:, 0])
        fixed_imag = jnp.where(is_first, pback_real[:, 1], back_imag[:, 0])
        back_real = jnp.concatenate([fixed_real[:, None], back_real[:, 1:]], axis=1)
        back_imag = jnp.concatenate([fixed_imag[:, None], back_imag[:, 1:]], axis=1)

    outgoing = jnp.stack([back_real, back_imag], axis=1).astype(BF16)
    outgoing = outgoing.reshape(
        members, 2, per_device, row_count, local_x, col_count, local_y
    )
    outgoing = jnp.moveaxis(outgoing, 4, 1).reshape(
        members, local_x, 2, per_device, devices, local_y
    )
    returned = lax.all_to_all(
        outgoing, ("row", "col"), split_axis=4, concat_axis=3, tiled=True
    )
    returned = returned.reshape(members, local_x, 2 * columns, local_y)

    weight = np.full((2 * columns,), 1.0 / depth, np.float32)
    if hermitian:
        weight[:] = 2.0 / depth
        weight[0] = 1.0 / depth
        weight[columns] = 1.0 / depth
    weight = jnp.asarray(weight)[:, None]
    weighted = (returned.astype(F32) * weight).astype(BF16)
    spec_back = "clky,zk->clyz"
    field = jnp.einsum(spec_back, weighted, z_high, preferred_element_type=F32) + jnp.einsum(
        spec_back, weighted, z_low, preferred_element_type=F32
    )
    return (magnetic.astype(F32) + field).astype(BF16)


def solution(mesh):
    in_specs = (
        P(None, "row", "col", None),
        P(None, "row", "col", None),
        P("row", "col", None),
        P(),
    )
    out_specs = P(None, "row", "col", None)
    return jax.shard_map(
        on_device, mesh=mesh, in_specs=in_specs, out_specs=out_specs, check_vma=False
    )
```

profile of v0, /device:TPU:0, one launch (start us, length us, event | category | flops | bytes accessed | tf_op | source)
XLA Modules:
  0.0 97.9 jit_solution(12638625969823282704)
XLA Ops:
  3.7 0.9 copy-done.15
  4.6 5.4 %select_bitcast_fusion = f32[128,1024]{1,0:T(8,128)S(1)} fusion(s32[1,128,1024]{2,1,0:T(8,128)S(1)} %copy-done.15, f32[]{:T(128)} %bitcast.8, f32[]{:T(128)} %bitcast.7, f32[]{:T(128)} %bitcast.6, f32[]{:T(128)} %bitcast.5, f32[]{:T(128)} %bitcast.4, f32[]{:T(128)} %bitcast.3, f32[]{:T(128)} %bitcast.2, f32[]{:T(128)} %bitcast.1), kind=kLoop, calls=%fused_computation.112 | loop fusion | flops 2097152 | bytes 1048608 | tf_op jit(solution)/shard_map/mul | solution.py:103
  10.0 1.0 %fusion.28 = f32[3,128,1024]{2,1,0:T(8,128)S(1)} fusion(bf16[1024,1024,1]{1,0,2:T(8,128)(2,1)S(1)} %fusion.2, bf16[3,1,128,1024]{3,2,1,0:T(8,128)(2,1)S(1)} %copy-done.18, f32[128,1024]{1,0:T(8,128)S(1)} %select_bitcast_fusion), kind=kOutput, calls=%fused_computation.62 | convolution fusion | flops 807272448 | bytes 4980736 | tf_op jit(solution)/shard_map/zk,clyz->clky/dot_general | solution.py:118
  11.0 1.0 %fusion.71 = f32[3,128,1024]{2,1,0:T(8,128)S(1)} fusion(bf16[1024,1024,1]{1,0,2:T(8,128)(2,1)S(1)} %fusion.2, bf16[3,1,128,1024]{3,2,1,0:T(8,128)(2,1)S(1)} %copy-done.18, f32[128,1024]{1,0:T(8,128)S(1)} %select_bitcast_fusion), kind=kOutput, calls=%fused_computation.120 | convolution fusion | flops 806879232 | bytes 4980736 | tf_op jit(solution)/shard_map/zk,clyz->clky/dot_general | solution.py:117
  12.1 2.1 %fusion.5 = bf16[3,1,1024,128]{2,3,0,1:T(8,128)(2,1)} fusion(f32[3,128,1024]{2,1,0:T(8,128)S(1)} %fusion.71, f32[3,128,1024]{2,1,0:T(8,128)S(1)} %fusion.28, bf16[3,1,128,1024]{3,2,1,0:T(8,128)(2,1)S(1)} %copy-done.18, f32[128,1024]{1,0:T(8,128)S(1)} %select_bitcast_fusion, f32[1024,511]{1,0:T(8,128)S(1)} %slice_negate_fusion, f32[1024,1]{1,0:T(8,128)S(1)} %fusion.48, ...), kind=kOutput, calls=%fused_computation.29 | convolution fusion | flops 813301760 | bytes 9437184 | tf_op jit(solution)/shard_map/zk,clyz->clky/dot_general | solution.py:119
  14.2 1.5 %copy.42 = bf16[3,1,1024,128]{3,2,0,1:T(8,128)(2,1)S(1)} copy(bf16[3,1,1024,128]{2,3,0,1:T(8,128)(2,1)} %fusion.5) | data formatting | bytes 1572864 | tf_op jit(solution)/shard_map/convert_element_type | solution.py:121
  15.7 1.0 %copy.43 = bf16[3,1,2,32,16,128]{5,4,2,0,1,3:T(8,128)(2,1)} copy(bf16[3,1,2,32,16,128]{5,4,3,2,0,1:T(8,128)(2,1)S(1)} %bitcast.304) | data formatting | bytes 1572864 | tf_op jit(solution)/shard_map/reshape | solution.py:121
  16.8 7.5 %all-to-all-start = ((bf16[3,1,2,32,16,128]{5,4,2,0,1,3:T(8,128)(2,1)}), bf16[3,1,2,32,16,128]{5,4,2,0,1,3:T(8,128)(2,1)S(1)}, u32[]{:S(2)}, u32[]{:S(2)}) async-start(bf16[3,1,2,32,16,128]{5,4,2,0,1,3:T(8,128)(2,1)} %copy.43), calls=%async_computation | async-start | bytes 1572864 | tf_op jit(solution)/shard_map/all_to_all | solution.py:124
  25.0 1.9 %multiply_subtract_fusion.1 = (f32[16,32,512]{2,1,0:T(8,128)S(1)}, f32[16,32,512]{2,1,0:T(8,128)S(1)}, bf16[16,32,512]{2,1,0:T(8,128)(2,1)}, bf16[16,32,512]{2,1...) fusion(f32[32,512]{1,0:T(8,128)S(1)} %fusion.115, f32[16,512]{1,0:T(8,128)S(1)} %get-tuple-element.44, ...), kind=kLoop, calls=%fused_computation.60 | loop fusion | flops 3670016 | bytes 4390912 | tf_op jit(solution)/shard_map/sub | solution.py:45
  26.9 1.4 %fusion.25 = (bf16[512,512]{1,0:T(8,128)(2,1)}, bf16[512,512]{1,0:T(8,128)(2,1)}, bf16[512,512]{1,0:T(8,128)(2,1)}, bf16[512,512]{1,0:T(8,128)(2,1)S(1)}) fusion(f32[16,32,512]{2,1,0:T(8,128)S(1)} %get-tuple-element.23, f32[16,32,512]{2,1,0:T(8,128)S(1)} %get-tuple-element.24), kind=kLoop, calls=%fused_computation.57 | loop fusion | flops 2097152 | bytes 4194304 | tf_op jit(solution)/shard_map/convert_element_type | solution.py:28
  28.3 16.3 %all-to-all-done = bf16[3,1,2,32,16,128]{5,4,2,0,1,3:T(8,128)(2,1)S(1)} async-done(((bf16[3,1,2,32,16,128]{5,4,2,0,1,3:T(8,128)(2,1)}), bf16[3,1,2,32,16,128]{5,4,2,0,1,3:T(8,128)(2,1)S(1)}, u32[]{:S(2)}, u32[]{:S(2)}) %all-to-all-start) | async-done | bytes 786464 | tf_op jit(solution)/shard_map/all_to_all | solution.py:124
  44.7 1.2 %copy.44 = bf16[3,1,2,1,16,32,128]{6,5,4,2,0,3,1:T(8,128)(2,1)} copy(bf16[3,1,2,1,16,32,128]{6,4,2,0,5,3,1:T(8,128)(2,1)S(1)} %bitcast.303) | data formatting | bytes 1572864 | tf_op jit(solution)/shard_map/all_to_all | solution.py:124
  45.9 1.6 %reshape_transpose_reshape.4 = bf16[3,2,16,8,512]{4,3,2,1,0:T(8,128)(2,1)S(1)} reshape(bf16[3,1,2,1,16,32,128]{6,5,4,2,0,3,1:T(8,128)(2,1)} %copy.44) | data formatting | bytes 1572864 | tf_op jit(solution)/shard_map/reshape;transpose;reshape | solution.py:128
  47.4 1.7 %fusion.145 = f32[3,2,16,8,512]{4,3,2,1,0:T(8,128)S(1)} fusion(bf16[3,2,16,8,512]{4,3,2,1,0:T(8,128)(2,1)S(1)} %reshape_transpose_reshape.4, bf16[512,512,1,1,1]{1,0,4,3,2:T(8,128)(2,1)} %bitcast.308), kind=kOutput, calls=%fused_computation.239 | convolution fusion | flops 402653184 | bytes 2883584 | tf_op jit(solution)/shard_map/yk,cpjxy->cpjxk/dot_general | solution.py:65
  51.8 1.3 %fusion.140 = (f32[3,16,8,512]{3,2,1,0:T(8,128)S(1)}, f32[3,16,8,512]{3,2,1,0:T(8,128)S(1)}, f32[3,16,8,512]{3,2,1,0:T(8,128)}, f32[3,16,8,512]{3,2,1,0:T(8,128)S(1)}) fusion(f32[3,2,16,8,512]{4,3,2,0,1:T(8,128)S(1)} %convolution_add_fusion.2, f32[3,2,16,8,512]{4,3,2,1,0:T(8,128)S(1)} %convolution_add_fusion.3), kind=kLoop, calls=%fused_computation.234 | loop fusion | flops 786432 | bytes 6291456 | tf_op jit(solution)/shard_map/reduce_precision | solution.py:22
  53.2 0.8 copy-done.13
  54.3 1.5 %reverse.5 = f32[3,8,512]{2,1,0:T(8,128)} reverse(f32[3,8,512]{2,1,0:T(8,128)S(1)} %bitcast.309), dimensions={2} | reverse | bytes 98304
  55.8 1.5 %slice_bitcast_fusion.10 = f32[3,1,8,511]{3,2,1,0:T(8,128)} fusion(f32[3,8,512]{2,1,0:T(8,128)} %reverse.5), kind=kLoop, calls=%fused_computation.237 | loop fusion | bytes 98112 | tf_op jit(solution)/shard_map/jit(_roll_static)/concatenate | solution.py:162
  57.7 1.0 subtract_multiply_fusion
  58.6 0.9 subtract_multiply_fusion.1
  67.6 24.0 %all_to_all.24 = bf16[3,1,2,16,32,128]{5,3,2,0,1,4:T(8,128)(2,1)S(1)} all-to-all(bf16[3,1,2,16,32,128]{5,3,2,0,1,4:T(8,128)(2,1)S(1)} %pad_maximum_fusion.2), channel_id=1, replica_groups=mesh['row'=8,'col'=4] {'row','col'}, dimensions={4} | all-to-all | bytes 1572864 | tf_op jit(solution)/shard_map/all_to_all | solution.py:189
  91.7 1.4 %copy-done.3 = bf16[1024,1024,1]{1,0,2:T(8,128)(2,1)S(1)} copy-done((bf16[1024,1024,1]{1,0,2:T(8,128)(2,1)S(1)}, bf16[1024,1024,1]{1,0,2:T(8,128)(2,1)}, u32[]{:S(2)}) %copy-start.3) | copy-done | bytes 2097176
  93.2 1.3 %fusion.137 = f32[3,128,1024]{2,1,0:T(8,128)S(1)} fusion(bf16[1024,1024,1]{1,0,2:T(8,128)(2,1)S(1)} %copy-done.3, f32[3,1024,128]{2,1,0:T(8,128)S(1)} %bitcast.301, f32[1024]{0:T(1024)S(1)} %copy-done.17), kind=kOutput, calls=%fused_computation.233 | convolution fusion | flops 806092800 | bytes 5246976 | tf_op jit(solution)/shard_map/clky,zk->clyz/dot_general | solution.py:202
  95.1 2.8 %fusion.6 = bf16[3,1,128,1024]{3,2,1,0:T(8,128)(2,1)} fusion(f32[3,128,1024]{2,1,0:T(8,128)S(1)} %fusion.137, bf16[3,1,128,1024]{3,2,1,0:T(8,128)(2,1)S(1)} %copy-done.19, f32[3,1024,128]{2,1,0:T(8,128)S(1)} %bitcast.302, f32[1024]{0:T(1024)S(1)} %copy-done.17, f32[1024,511]{1,0:T(8,128)S(1)} %copy-done.1, f32[1024,1]{1,0:T(8,128)S(1)} %copy-done.12, ...), kind=kOutput, calls=%fused_computation.30 | convolution fusion | flops 812908544 | bytes 8916992 | tf_op jit(solution)/shard_map/clky,zk->clyz/dot_general | solution.py:202
  (100 shorter events, 16.3 us)
Async XLA Ops:
  0.4 11.7 %copy-start.11 = (f32[1024,1]{1,0:T(8,128)}, f32[1024,1]{1,0:T(8,128)S(1)}, u32[]{:S(2)}) copy-start(f32[1024,1]{1,0:T(8,128)S(1)} %fusion.48) | copy-start | bytes 12292
  3.2 8.9 %copy-start = (f32[1024,511]{1,0:T(8,128)}, f32[1024,511]{1,0:T(8,128)S(1)}, u32[]{:S(2)}) copy-start(f32[1024,511]{1,0:T(8,128)S(1)} %slice_negate_fusion) | copy-start | bytes 6279172
  3.2 1.4 %copy-start.15 = (s32[1,128,1024]{2,1,0:T(8,128)S(1)}, s32[1,128,1024]{2,1,0:T(8,128)}, u32[]{:S(2)}) copy-start(s32[1,128,1024]{2,1,0:T(8,128)} %param.8) | copy-start | bytes 1572868
  3.2 6.8 %copy-start.18 = (bf16[3,1,128,1024]{3,2,1,0:T(8,128)(2,1)S(1)}, bf16[3,1,128,1024]{3,2,1,0:T(8,128)(2,1)}, u32[]{:S(2)}) copy-start(bf16[3,1,128,1024]{3,2,1,0:T(8,128)(2,1)} %param.6) | copy-start | bytes 2359300
  3.7 7.3 %copy-start.2 = (bf16[1024,1024,1]{1,0,2:T(8,128)(2,1)}, bf16[1024,1024,1]{1,0,2:T(8,128)(2,1)S(1)}, u32[]{:S(2)}) copy-start(bf16[1024,1024,1]{1,0,2:T(8,128)(2,1)S(1)} %fusion.2) | copy-start | bytes 6291460
  16.8 27.9 %all-to-all-start = ((bf16[3,1,2,32,16,128]{5,4,2,0,1,3:T(8,128)(2,1)}), bf16[3,1,2,32,16,128]{5,4,2,0,1,3:T(8,128)(2,1)S(1)}, u32[]{:S(2)}, u32[]{:S(2)}) async-start(bf16[3,1,2,32,16,128]{5,4,2,0,1,3:T(8,128)(2,1)} %copy.43), calls=%async_computation | async-start | bytes 1572864 | tf_op jit(solution)/shard_map/all_to_all | solution.py:124
  47.4 1.7 %copy-start.10 = (bf16[16,32,512]{2,1,0:T(8,128)(2,1)S(1)}, bf16[16,32,512]{2,1,0:T(8,128)(2,1)}, u32[]{:S(2)}) copy-start(bf16[16,32,512]{2,1,0:T(8,128)(2,1)} %get-tuple-element.28) | copy-start | bytes 1572868
  49.1 1.0 %copy-start.9 = (bf16[16,32,512]{2,1,0:T(8,128)(2,1)S(1)}, bf16[16,32,512]{2,1,0:T(8,128)(2,1)}, u32[]{:S(2)}) copy-start(bf16[16,32,512]{2,1,0:T(8,128)(2,1)} %get-tuple-element.25) | copy-start | bytes 1572868
  50.2 1.0 %copy-start.8 = (bf16[16,32,512]{2,1,0:T(8,128)(2,1)S(1)}, bf16[16,32,512]{2,1,0:T(8,128)(2,1)}, u32[]{:S(2)}) copy-start(bf16[16,32,512]{2,1,0:T(8,128)(2,1)} %get-tuple-element.27) | copy-start | bytes 1572868
  53.1 0.9 copy-start.13
  53.1 1.2 %copy-start.14 = (f32[3,16,8,512]{3,2,1,0:T(8,128)}, f32[3,16,8,512]{3,2,1,0:T(8,128)S(1)}, u32[]{:S(2)}) copy-start(f32[3,16,8,512]{3,2,1,0:T(8,128)S(1)} %get-tuple-element.12) | copy-start | bytes 2359300
  53.1 6.5 %copy-start.16 = (f32[8,8,1]{1,0,2:T(8,128)S(1)}, f32[8,8,1]{1,0,2:T(8,128)}, u32[]{:S(2)}) copy-start(f32[8,8,1]{1,0,2:T(8,128)} %constant.126) | copy-start | bytes 772
  57.6 2.7 %copy-start.4 = (f32[3,16,8,512]{3,2,1,0:T(8,128)S(1)}, f32[3,16,8,512]{3,2,1,0:T(8,128)}, u32[]{:S(2)}) copy-start(f32[3,16,8,512]{3,2,1,0:T(8,128)} %get-tuple-element.11) | copy-start | bytes 2359300
  60.6 1.0 %copy-start.7 = (bf16[512,512]{1,0:T(8,128)(2,1)S(1)}, bf16[512,512]{1,0:T(8,128)(2,1)}, u32[]{:S(2)}) copy-start(bf16[512,512]{1,0:T(8,128)(2,1)} %get-tuple-element.14) | copy-start | bytes 1572868
  61.0 1.1 %copy-start.6 = (bf16[512,512]{1,0:T(8,128)(2,1)S(1)}, bf16[512,512]{1,0:T(8,128)(2,1)}, u32[]{:S(2)}) copy-start(bf16[512,512]{1,0:T(8,128)(2,1)} %get-tuple-element.49) | copy-start | bytes 1572868
  63.4 1.0 %copy-start.5 = (bf16[512,512]{1,0:T(8,128)(2,1)S(1)}, bf16[512,512]{1,0:T(8,128)(2,1)}, u32[]{:S(2)}) copy-start(bf16[512,512]{1,0:T(8,128)(2,1)} %get-tuple-element.13) | copy-start | bytes 1572868
  91.6 1.6 %copy-start.3 = (bf16[1024,1024,1]{1,0,2:T(8,128)(2,1)S(1)}, bf16[1024,1024,1]{1,0,2:T(8,128)(2,1)}, u32[]{:S(2)}) copy-start(bf16[1024,1024,1]{1,0,2:T(8,128)(2,1)} %copy-done.2) | copy-start | bytes 6291460
  91.6 1.6 %copy-start.17 = (f32[1024]{0:T(1024)S(1)}, f32[1024]{0:T(1024)}, u32[]{:S(2)}) copy-start(f32[1024]{0:T(1024)} %constant.122.clone) | copy-start | bytes 12292
  93.2 1.6 %copy-start.1 = (f32[1024,511]{1,0:T(8,128)S(1)}, f32[1024,511]{1,0:T(8,128)}, u32[]{:S(2)}) copy-start(f32[1024,511]{1,0:T(8,128)} %copy-done) | copy-start | bytes 6279172
  93.2 1.7 %copy-start.12 = (f32[1024,1]{1,0:T(8,128)S(1)}, f32[1024,1]{1,0:T(8,128)}, u32[]{:S(2)}) copy-start(f32[1024,1]{1,0:T(8,128)} %copy-done.11) | copy-start | bytes 12292
  93.2 1.9 %copy-start.19 = (bf16[3,1,128,1024]{3,2,1,0:T(8,128)(2,1)S(1)}, bf16[3,1,128,1024]{3,2,1,0:T(8,128)(2,1)}, u32[]{:S(2)}) copy-start(bf16[3,1,128,1024]{3,2,1,0:T(8,128)(2,1)} %param.7) | copy-start | bytes 2359300
where the time goes:
time: 98.6 us; the launch traced here: 97.9 us
  blocking collectives  24 us (24%)
  matrix products  16.8 us (17%)
  other arithmetic  16.6 us (17%)
  waiting for transfers between devices  16.3 us (17%)
  local copies, waits for them, and re-layouts  16 us (16%)
  starting transfers between devices  7.48 us (8%)
    all_to_all x1, blocking collectives, on_device(): lax.all_to_all(outgoing, ('row', 'col'), split_axis=4, concat_axis=3, til...  24 us
    all_to_all x1, waiting for transfers between devices, on_device(): lax.all_to_all(spectrum, ('row', 'col'), split_axis=3, concat_axis=5, til...  16.3 us
    unnamed x42, local copies, waits for them, and re-layouts  7.5 us
    all_to_all x1, starting transfers between devices, on_device(): lax.all_to_all(spectrum, ('row', 'col'), split_axis=3, concat_axis=5, til...  7.48 us
    dot_general x12, matrix products, mat(): term = jnp.einsum(spec, part, operand, preferred_element_type=F32)  6.54 us
    mul x1, other arithmetic, on_device(): electric = displacement.astype(F32) * cell_scale[None]  5.4 us
    dot_general x1, matrix products, on_device(): jnp.einsum(spec_back, weighted, z_low, preferred_element_type=F32)  2.76 us
    sub x2, other arithmetic, phase_table(): cosine = outer_cos * inner_cos - outer_sin * inner_sin  2.31 us
  transfers between devices with their start and end apart: 1, of which 1 were waited for; matrix products, arithmetic and copies ran while one was open for 4% of the time, Pallas kernels for 0%

commit v1 on v0

--- a/solution.py
+++ b/solution.py
@@ -109,38 +109,26 @@
     else:
         sin_part = -sin_z
     table_z = jnp.concatenate([cos_z, sin_part], axis=1)
-    z_high, z_low = split_parts(table_z)
+    weight = np.full((2 * columns,), 2.0 / depth if hermitian else 1.0 / depth, np.float32)
+    if hermitian:
+        weight[0] = 1.0 / depth
+        weight[columns] = 1.0 / depth
+    chunks = 2 if per_device % 2 == 0 else 1
+    chunk = per_device // chunks
+
+    def chunk_columns(values, index):
+        values = values.reshape(values.shape[:-1] + (2, devices, per_device))
+        values = values[..., index * chunk : (index + 1) * chunk]
+        return values.reshape(values.shape[:-3] + (2 * devices * chunk,))
 
     e_high, e_low = split_parts(electric)
-    spec_z = "zk,clyz->clky"
-    spectrum = (
-        jnp.einsum(spec_z, z_high, e_high, preferred_element_type=F32)
-        + jnp.einsum(spec_z, z_high, e_low, preferred_element_type=F32)
-        + jnp.einsum(spec_z, z_low, e_high, preferred_element_type=F32)
-    )
-    spectrum = spectrum.astype(BF16).reshape(
-        members, local_x, 2, devices, per_device, local_y
-    )
-    gathered = lax.all_to_all(
-        spectrum, ("row", "col"), split_axis=3, concat_axis=5, tiled=True
-    )
-    gathered = gathered.reshape(members, local_x, 2, per_device, row_count, width_y)
-    gathered = jnp.moveaxis(gathered, 1, 4).reshape(
-        members, 2, per_device, span_x, width_y
-    )
-
     cos_y, sin_y = phase_table(width_y, width_y, width_y)
     cos_y_parts = split_parts(cos_y)
     sin_y_parts = split_parts(sin_y)
     spec_y = "yk,cpjxy->cpjxk"
-    by_cos = mat(cos_y_parts, gathered, spec_y)
-    by_sin = mat(sin_y_parts, gathered, spec_y)
-    y_real = by_cos[:, 0] + by_sin[:, 1]
-    y_imag = by_cos[:, 1] - by_sin[:, 0]
-
     kernel = jnp.asarray(x_kernel(span_x))
     wave_y = wavenumber(lax.iota(jnp.int32, width_y), width_y)
-    wave_z = wavenumber(me * per_device + lax.iota(jnp.int32, per_device), depth)
+    is_first = me == 0
 
     def inverse_y(b_real, b_imag):
         stacked = jnp.stack([b_real, b_imag], axis=1).astype(BF16)
@@ -151,57 +139,80 @@
         out_imag = (by_cos[:, 1] + by_sin[:, 0]) * scale
         return rounded(out_real), rounded(out_imag)
 
-    b_real, b_imag = curl_update(rounded(y_real), rounded(y_imag), wave_y, wave_z, kernel)
-    back_real, back_imag = inverse_y(rounded(b_real), rounded(b_imag))
-
-    if hermitian:
-        first_real = y_real[:, 0]
-        first_imag = y_imag[:, 0]
-
-        def mirrored(values):
-            return jnp.roll(jnp.flip(values, axis=-1), 1, axis=-1)
-
-        mirror_real = mirrored(first_real)
-        mirror_imag = mirrored(first_imag)
-        plane_real = jnp.stack(
-            [0.5 * (first_real + mirror_real), 0.5 * (first_imag + mirror_imag)], axis=1
-        )
-        plane_imag = jnp.stack(
-            [0.5 * (first_imag - mirror_imag), -0.5 * (first_real - mirror_real)], axis=1
-        )
-        pb_real, pb_imag = curl_update(
-            rounded(plane_real), rounded(plane_imag), wave_y, jnp.zeros((2,), F32), kernel
-        )
-        pback_real, _ = inverse_y(rounded(pb_real), rounded(pb_imag))
-        is_first = me == 0
-        fixed_real = jnp.where(is_first, pback_real[:, 0], back_real[:, 0])
-        fixed_imag = jnp.where(is_first, pback_real[:, 1], back_imag[:, 0])
-        back_real = jnp.concatenate([fixed_real[:, None], back_real[:, 1:]], axis=1)
-        back_imag = jnp.concatenate([fixed_imag[:, None], back_imag[:, 1:]], axis=1)
-
-    outgoing = jnp.stack([back_real, back_imag], axis=1).astype(BF16)
-    outgoing = outgoing.reshape(
-        members, 2, per_device, row_count, local_x, col_count, local_y
-    )
-    outgoing = jnp.moveaxis(outgoing, 4, 1).reshape(
-        members, local_x, 2, per_device, devices, local_y
-    )
-    returned = lax.all_to_all(
-        outgoing, ("row", "col"), split_axis=4, concat_axis=3, tiled=True
-    )
-    returned = returned.reshape(members, local_x, 2 * columns, local_y)
-
-    weight = np.full((2 * columns,), 1.0 / depth, np.float32)
-    if hermitian:
-        weight[:] = 2.0 / depth
-        weight[0] = 1.0 / depth
-        weight[columns] = 1.0 / depth
-    weight = jnp.asarray(weight)[:, None]
-    weighted = (returned.astype(F32) * weight).astype(BF16)
-    spec_back = "clky,zk->clyz"
-    field = jnp.einsum(spec_back, weighted, z_high, preferred_element_type=F32) + jnp.einsum(
-        spec_back, weighted, z_low, preferred_element_type=F32
-    )
+    def forward_z(index):
+        z_high, z_low = split_parts(chunk_columns(table_z, index))
+        spec_z = "zk,clyz->clky"
+        spectrum = (
+            jnp.einsum(spec_z, z_high, e_high, preferred_element_type=F32)
+            + jnp.einsum(spec_z, z_high, e_low, preferred_element_type=F32)
+            + jnp.einsum(spec_z, z_low, e_high, preferred_element_type=F32)
+        )
+        spectrum = spectrum.astype(BF16).reshape(
+            members, local_x, 2, devices, chunk, local_y
+        )
+        return lax.all_to_all(
+            spectrum, ("row", "col"), split_axis=3, concat_axis=5, tiled=True
+        )
+
+    def middle(gathered, index):
+        gathered = gathered.reshape(members, local_x, 2, chunk, row_count, width_y)
+        gathered = jnp.moveaxis(gathered, 1, 4).reshape(members, 2, chunk, span_x, width_y)
+        by_cos = mat(cos_y_parts, gathered, spec_y)
+        by_sin = mat(sin_y_parts, gathered, spec_y)
+        y_real = by_cos[:, 0] + by_sin[:, 1]
+        y_imag = by_cos[:, 1] - by_sin[:, 0]
+        first_m = me * per_device + index * chunk
+        wave_z = wavenumber(first_m + lax.iota(jnp.int32, chunk), depth)
+        b_real, b_imag = curl_update(rounded(y_real), rounded(y_imag), wave_y, wave_z, kernel)
+        back_real, back_imag = inverse_y(rounded(b_real), rounded(b_imag))
+
+        if hermitian and index == 0:
+            first_real = y_real[:, 0]
+            first_imag = y_imag[:, 0]
+
+            def mirrored(values):
+                return jnp.roll(jnp.flip(values, axis=-1), 1, axis=-1)
+
+            mirror_real = mirrored(first_real)
+            mirror_imag = mirrored(first_imag)
+            plane_real = jnp.stack(
+                [0.5 * (first_real + mirror_real), 0.5 * (first_imag + mirror_imag)], axis=1
+            )
+            plane_imag = jnp.stack(
+                [0.5 * (first_imag - mirror_imag), -0.5 * (first_real - mirror_real)], axis=1
+            )
+            pb_real, pb_imag = curl_update(
+                rounded(plane_real), rounded(plane_imag), wave_y, jnp.zeros((2,), F32), kernel
+            )
+            pback_real, _ = inverse_y(rounded(pb_real), rounded(pb_imag))
+            fixed_real = jnp.where(is_first, pback_real[:, 0], back_real[:, 0])
+            fixed_imag = jnp.where(is_first, pback_real[:, 1], back_imag[:, 0])
+            back_real = jnp.concatenate([fixed_real[:, None], back_real[:, 1:]], axis=1)
+            back_imag = jnp.concatenate([fixed_imag[:, None], back_imag[:, 1:]], axis=1)
+
+        outgoing = jnp.stack([back_real, back_imag], axis=1).astype(BF16)
+        outgoing = outgoing.reshape(members, 2, chunk, row_count, local_x, col_count, local_y)
+        outgoing = jnp.moveaxis(outgoing, 4, 1).reshape(
+            members, local_x, 2, chunk, devices, local_y
+        )
+        return lax.all_to_all(
+            outgoing, ("row", "col"), split_axis=4, concat_axis=3, tiled=True
+        )
+
+    def inverse_z(returned, index):
+        returned = returned.reshape(members, local_x, 2 * devices * chunk, local_y)
+        scale = chunk_columns(jnp.asarray(weight), index)[:, None]
+        weighted = (returned.astype(F32) * scale).astype(BF16)
+        z_high, z_low = split_parts(chunk_columns(table_z, index))
+        spec_back = "clky,zk->clyz"
+        return jnp.einsum(spec_back, weighted, z_high, preferred_element_type=F32) + jnp.einsum(
+            spec_back, weighted, z_low, preferred_element_type=F32
+        )
+
+    field = None
+    for index in range(chunks):
+        part = inverse_z(middle(forward_z(index), index), index)
+        field = part if field is None else field + part
     return (magnetic.astype(F32) + field).astype(BF16)
 
 

time: 98.6 us -> 139 us (1.41); the launches traced: 97.9 us -> 137 us
  blocking collectives: 24 us -> 0 us
  local copies, waits for them, and re-layouts: 16 us -> 35.4 us
  other arithmetic: 16.6 us -> 32.1 us
  matrix products: 16.8 us -> 27.5 us
  starting transfers between devices: 7.48 us -> 18.1 us
  waiting for transfers between devices: 16.3 us -> 22.8 us
    all_to_all x1 -> x0, blocking collectives: 24 us -> none  [on_device(): lax.all_to_all(outgoing, ('row', 'col'), split_axis=4, concat_axis=3, til...]
    all_to_all x1 -> x4, starting transfers between devices: 7.48 us -> 18.1 us  [the longest x2 11.5 us: forward_z(): lax.all_to_all(spectrum, ('row', 'col'), split_axis=3, concat_axis=5, til...]
    all_to_all x1 -> x4, waiting for transfers between devices: 16.3 us -> 22.8 us  [the longest x2 14.4 us: middle(): lax.all_to_all(outgoing, ('row', 'col'), split_axis=4, concat_axis=3, til...]
    concatenate x0 -> x1, local copies, waits for them, and re-layouts: none -> 5.34 us  [on_device(): table_z = jnp.concatenate([cos_z, sin_part], axis=1)]
    dot_general x12 -> x20, matrix products: 6.54 us -> 10.9 us  [mat(): term = jnp.einsum(spec, part, operand, preferred_element_type=F32)]
    another operation x6 -> x10, other arithmetic: 0.2 us -> 4.5 us  [the longest x2 3.51 us: middle(): outgoing = jnp.stack([back_real, back_imag], axis=1).astype(BF16)]
    dot_general x5 -> x10, matrix products: 8.22 us -> 12.4 us  [the longest x2 4.82 us: inverse_z(): jnp.einsum(spec_back, weighted, z_low, preferred_element_type=F32)]
    convert_element_type x2, other arithmetic: 1.97 us -> 5.72 us  [split_parts(): return (high.astype(BF16), low.astype(BF16))]
  transfers between devices with their start and end apart: 1 -> 4, of which waited for: 1 -> 4; matrix products, arithmetic and copies ran while one was open for 4% -> 20% of each run, Pallas kernels for 0% -> 0%
where the time goes in v1:
time: 139 us; the launch traced here: 137 us
  local copies, waits for them, and re-layouts  35.4 us (25%)
  other arithmetic  32.1 us (23%)
  matrix products  27.5 us (20%)
  waiting for transfers between devices  22.8 us (16%)
  starting transfers between devices  18.1 us (13%)
    all_to_all x2, waiting for transfers between devices, middle(): lax.all_to_all(outgoing, ('row', 'col'), split_axis=4, concat_axis=3, til...  14.4 us
    all_to_all x2, starting transfers between devices, forward_z(): lax.all_to_all(spectrum, ('row', 'col'), split_axis=3, concat_axis=5, til...  11.5 us
    dot_general x20, matrix products, mat(): term = jnp.einsum(spec, part, operand, preferred_element_type=F32)  10.9 us
    unnamed x66, local copies, waits for them, and re-layouts  10.2 us
    all_to_all x2, waiting for transfers between devices, forward_z(): lax.all_to_all(spectrum, ('row', 'col'), split_axis=3, concat_axis=5, til...  8.42 us
    all_to_all x2, starting transfers between devices, middle(): lax.all_to_all(outgoing, ('row', 'col'), split_axis=4, concat_axis=3, til...  6.61 us
    convert_element_type x2, other arithmetic, split_parts(): return (high.astype(BF16), low.astype(BF16))  5.72 us
    mul x1, other arithmetic, on_device(): electric = displacement.astype(F32) * cell_scale[None]  5.51 us
  transfers between devices with their start and end apart: 4, of which 4 were waited for; matrix products, arithmetic and copies ran while one was open for 20% of the time, Pallas kernels for 0%

profile of v1, /device:TPU:0, one launch (start us, length us, event | category | flops | bytes accessed | tf_op | source)
XLA Modules:
  0.0 136.8 jit_solution(5190706117714321359)
XLA Ops:
  3.3 2.7 %pad_maximum_fusion = f32[1024,1024]{1,0:T(8,128)} fusion(f32[1024,511]{1,0:T(8,128)S(1)} %slice_negate_fusion, f32[1024,1]{1,0:T(8,128)S(1)} %fusion.43, f32[1024,512]{1,0:T(8,128)S(1)} %bitcast.468), kind=kLoop, calls=%fused_computation | loop fusion | flops 2097152 | bytes 8388608 | tf_op jit(solution)/shard_map/concatenate | solution.py:111
  6.0 5.3 %copy.110 = f32[1024,1024]{0,1:T(8,128)} copy(f32[1024,1024]{1,0:T(8,128)} %pad_maximum_fusion) | data formatting | bytes 8388608 | tf_op jit(solution)/shard_map/concatenate | solution.py:111
  11.4 4.2 %fusion = (bf16[1024,2,32,8]{0,3,2,1:T(8,128)(2,1)}, bf16[1024,2,32,8]{0,3,2,1:T(8,128)(2,1)S(1)}, bf16[1024,2,32,8]{0,3,2,1:T(8,128)(2,1)S(1)}, bf16[1024,2,32,8]{0,3,2,1:T(8,128)(2,1)S(1)}) fusion(f32[1024,2,32,16]{0,3,2,1:T(8,128)} %bitcast.457), kind=kLoop, calls=%fused_computation.7 | loop fusion | flops 4194304 | bytes 8388608 | tf_op jit(solution)/shard_map/convert_element_type | solution.py:28
  15.6 5.5 %select_bitcast_fusion = f32[128,1024]{1,0:T(8,128)S(1)} fusion(s32[1,128,1024]{2,1,0:T(8,128)S(1)} %copy-done.25, f32[]{:T(128)} %bitcast.8, f32[]{:T(128)} %bitcast.7, f32[]{:T(128)} %bitcast.6, f32[]{:T(128)} %bitcast.5, f32[]{:T(128)} %bitcast.4, f32[]{:T(128)} %bitcast.3, f32[]{:T(128)} %bitcast.2, f32[]{:T(128)} %bitcast.1), kind=kLoop, calls=%fused_computation.116 | loop fusion | flops 2097152 | bytes 1048608 | tf_op jit(solution)/shard_map/mul | solution.py:103
  23.8 1.9 %copy.138 = bf16[3,1,512,128]{3,2,0,1:T(8,128)(2,1)} copy(bf16[3,1,512,128]{2,3,0,1:T(8,128)(2,1)} %fusion.7) | data formatting | bytes 786432 | tf_op jit(solution)/shard_map/convert_element_type | solution.py:150
  25.7 1.8 %copy.139 = bf16[3,1,2,32,8,128]{5,4,2,0,1,3:T(8,128)(2,1)} copy(bf16[3,1,2,32,8,128]{5,4,3,2,0,1:T(8,128)(2,1)} %bitcast.482) | data formatting | bytes 786432 | tf_op jit(solution)/shard_map/reshape | solution.py:150
  27.5 7.4 %all-to-all-start.2 = ((bf16[3,1,2,32,8,128]{5,4,2,0,1,3:T(8,128)(2,1)}), bf16[3,1,2,32,8,128]{5,4,2,0,1,3:T(8,128)(2,1)}, u32[]{:S(2)}, u32[]{:S(2)}) async-start(bf16[3,1,2,32,8,128]{5,4,2,0,1,3:T(8,128)(2,1)} %copy.139), calls=%async_computation.2 | async-start | bytes 786432 | tf_op jit(solution)/shard_map/all_to_all | solution.py:153
  42.8 1.8 %multiply_subtract_fusion.1 = (f32[16,32,512]{2,1,0:T(8,128)S(1)}, f32[16,32,512]{2,1,0:T(8,128)S(1)}, bf16[16,32,512]{2,1,0:T(8,128)(2,1)}, bf16[16,32,512]{2,1...) fusion(f32[32,512]{1,0:T(8,128)S(1)} %fusion.155, f32[16,512]{1,0:T(8,128)S(1)} %copy-done.28, ...), kind=kLoop, calls=%fused_computation.82 | loop fusion | flops 3670016 | bytes 4390912 | tf_op jit(solution)/shard_map/sub | solution.py:45
  46.1 2.0 %all-to-all-done.2 = bf16[3,1,2,32,8,128]{5,4,2,0,1,3:T(8,128)(2,1)} async-done(((bf16[3,1,2,32,8,128]{5,4,2,0,1,3:T(8,128)(2,1)}), bf16[3,1,2,32,8,128]{5,4,2,0,1,3:T(8,128)(2,1)}, u32[]{:S(2)}, u32[]{:S(2)}) %all-to-all-start.2) | async-done | bytes 393248 | tf_op jit(solution)/shard_map/all_to_all | solution.py:153
  48.1 4.1 %all-to-all-start = ((bf16[3,1,2,32,8,128]{5,4,2,0,1,3:T(8,128)(2,1)}), bf16[3,1,2,32,8,128]{5,4,2,0,1,3:T(8,128)(2,1)}, u32[]{:S(2)}, u32[]{:S(2)}) async-start(bf16[3,1,2,32,8,128]{5,4,2,0,1,3:T(8,128)(2,1)} %copy.115), calls=%async_computation | async-start | bytes 786432 | tf_op jit(solution)/shard_map/all_to_all | solution.py:153
  58.7 6.4 %all-to-all-done = bf16[3,1,2,32,8,128]{5,4,2,0,1,3:T(8,128)(2,1)} async-done(((bf16[3,1,2,32,8,128]{5,4,2,0,1,3:T(8,128)(2,1)}), bf16[3,1,2,32,8,128]{5,4,2,0,1,3:T(8,128)(2,1)}, u32[]{:S(2)}, u32[]{:S(2)}) %all-to-all-start) | async-done | bytes 393248 | tf_op jit(solution)/shard_map/all_to_all | solution.py:153
  65.2 1.9 %copy.116 = bf16[3,1,2,1,8,32,128]{6,5,4,2,0,3,1:T(8,128)(2,1)} copy(bf16[3,1,2,1,8,32,128]{6,4,2,0,5,3,1:T(8,128)(2,1)} %bitcast.24) | data formatting | bytes 786432 | tf_op jit(solution)/shard_map/all_to_all | solution.py:153
  75.3 2.8 %reverse.4 = f32[3,8,512]{2,1,0:T(8,128)} reverse(f32[3,8,512]{2,1,0:T(8,128)} %bitcast.484), dimensions={2} | reverse | bytes 98304
  78.1 1.5 %slice_bitcast_fusion.13 = f32[3,1,8,511]{3,2,1,0:T(8,128)} fusion(f32[3,8,512]{2,1,0:T(8,128)} %reverse.4), kind=kLoop, calls=%fused_computation.313 | loop fusion | bytes 98112 | tf_op jit(solution)/shard_map/jit(_roll_static)/concatenate | solution.py:174
  79.6 2.8 %reverse.5 = f32[3,8,512]{2,1,0:T(8,128)} reverse(f32[3,8,512]{2,1,0:T(8,128)} %bitcast.485), dimensions={2} | reverse | bytes 98304
  96.1 1.8 %pad_maximum_fusion.2 = bf16[3,1,2,8,32,128]{5,3,2,0,1,4:T(8,128)(2,1)} fusion(bf16[3,1,1,8,32,128]{5,3,2,0,1,4:T(8,128)(2,1)S(1)} %copy.129, bf16[3,1,1,8,32,128]{5,3,2,0,1,4:T(8,128)(2,1)} %copy.128), kind=kLoop, calls=%fused_computation.149 | loop fusion | flops 196608 | bytes 786432 | tf_op jit(solution)/shard_map/stack | solution.py:193
  97.8 3.3 %all-to-all-start.1 = ((bf16[3,1,2,8,32,128]{5,3,2,0,1,4:T(8,128)(2,1)}), bf16[3,1,2,8,32,128]{5,3,2,0,1,4:T(8,128)(2,1)}, u32[]{:S(2)}, u32[]{:S(2)}) async-start(bf16[3,1,2,8,32,128]{5,3,2,0,1,4:T(8,128)(2,1)} %pad_maximum_fusion.2), calls=%async_computation.1 | async-start | bytes 786432 | tf_op jit(solution)/shard_map/all_to_all | solution.py:198
  106.7 1.8 %pad_maximum_fusion.4 = bf16[3,1,2,8,32,128]{5,3,2,0,1,4:T(8,128)(2,1)} fusion(bf16[3,1,1,8,32,128]{5,3,2,0,1,4:T(8,128)(2,1)S(1)} %copy.146, bf16[3,1,1,8,32,128]{5,3,2,0,1,4:T(8,128)(2,1)} %copy.145), kind=kLoop, calls=%fused_computation.155 | loop fusion | flops 196608 | bytes 786432 | tf_op jit(solution)/shard_map/stack | solution.py:193
  108.4 5.9 %all-to-all-done.1 = bf16[3,1,2,8,32,128]{5,3,2,0,1,4:T(8,128)(2,1)} async-done(((bf16[3,1,2,8,32,128]{5,3,2,0,1,4:T(8,128)(2,1)}), bf16[3,1,2,8,32,128]{5,3,2,0,1,4:T(8,128)(2,1)}, u32[]{:S(2)}, u32[]{:S(2)}) %all-to-all-start.1) | async-done | bytes 393248 | tf_op jit(solution)/shard_map/all_to_all | solution.py:198
  114.3 3.3 %all-to-all-start.3 = ((bf16[3,1,2,8,32,128]{5,3,2,0,1,4:T(8,128)(2,1)}), bf16[3,1,2,8,32,128]{5,3,2,0,1,4:T(8,128)(2,1)}, u32[]{:S(2)}, u32[]{:S(2)}) async-start(bf16[3,1,2,8,32,128]{5,3,2,0,1,4:T(8,128)(2,1)} %pad_maximum_fusion.4), calls=%async_computation.3 | async-start | bytes 786432 | tf_op jit(solution)/shard_map/all_to_all | solution.py:198
  118.8 1.7 %fusion.193 = f32[3,128,1024]{2,1,0:T(8,128)} fusion(bf16[3,512,128]{2,1,0:T(8,128)(2,1)S(1)} %bitcast.478, bf16[1024,512,1]{0,1,2:T(8,128)(2,1)S(1)} %bitcast.465), kind=kOutput, calls=%fused_computation.316 | convolution fusion | flops 402653184 | bytes 3014656 | tf_op jit(solution)/shard_map/clky,zk->clyz/dot_general | solution.py:208
  120.5 1.8 %fusion.192 = f32[3,128,1024]{2,1,0:T(8,128)} fusion(bf16[3,512,128]{2,1,0:T(8,128)(2,1)S(1)} %bitcast.479, bf16[1024,512,1]{0,1,2:T(8,128)(2,1)S(1)} %bitcast.463), kind=kOutput, calls=%fused_computation.315 | convolution fusion | flops 402653184 | bytes 3014656 | tf_op jit(solution)/shard_map/clky,zk->clyz/dot_general | solution.py:208
  122.3 8.5 %all-to-all-done.3 = bf16[3,1,2,8,32,128]{5,3,2,0,1,4:T(8,128)(2,1)} async-done(((bf16[3,1,2,8,32,128]{5,3,2,0,1,4:T(8,128)(2,1)}), bf16[3,1,2,8,32,128]{5,3,2,0,1,4:T(8,128)(2,1)}, u32[]{:S(2)}, u32[]{:S(2)}) %all-to-all-start.3) | async-done | bytes 393248 | tf_op jit(solution)/shard_map/all_to_all | solution.py:198
  133.7 3.1 %fusion.4 = bf16[3,1,128,1024]{3,2,1,0:T(8,128)(2,1)} fusion(f32[3,128,1024]{2,1,0:T(8,128)S(1)} %fusion.196, bf16[3,512,128]{2,1,0:T(8,128)(2,1)S(1)} %bitcast.481, bf16[1024,512,1]{0,1,2:T(8,128)(2,1)S(1)} %bitcast.467, f32[3,128,1024]{2,1,0:T(8,128)} %fusion.192, f32[3,128,1024]{2,1,0:T(8,128)S(1)} %copy-done.8, bf16[3,1,128,1024]{3,2,1,0:T(8,128)(2,1)S(1)} %copy-done.21), kind=kOutput, calls=%fused_computation.36 | convolution fusion | flops 405012480 | bytes 7733248 | tf_op jit(solution)/shard_map/clky,zk->clyz/dot_general | solution.py:208
  (163 shorter events, 52.6 us)
Async XLA Ops:
  11.4 4.2 %copy-start.25 = (s32[1,128,1024]{2,1,0:T(8,128)S(1)}, s32[1,128,1024]{2,1,0:T(8,128)}, u32[]{:S(2)}) copy-start(s32[1,128,1024]{2,1,0:T(8,128)} %param.8) | copy-start | bytes 1572868
  11.4 9.8 %copy-start = (bf16[3,1,128,1024]{3,2,1,0:T(8,128)(2,1)S(1)}, bf16[3,1,128,1024]{3,2,1,0:T(8,128)(2,1)}, u32[]{:S(2)}) copy-start(bf16[3,1,128,1024]{3,2,1,0:T(8,128)(2,1)} %param.6) | copy-start | bytes 2359300
  15.6 6.8 %copy-start.3 = (bf16[1024,2,32,8]{0,3,2,1:T(8,128)(2,1)}, bf16[1024,2,32,8]{0,3,2,1:T(8,128)(2,1)S(1)}, u32[]{:S(2)}) copy-start(bf16[1024,2,32,8]{0,3,2,1:T(8,128)(2,1)S(1)} %get-tuple-element.10) | copy-start | bytes 3145732
  27.5 20.6 %all-to-all-start.2 = ((bf16[3,1,2,32,8,128]{5,4,2,0,1,3:T(8,128)(2,1)}), bf16[3,1,2,32,8,128]{5,4,2,0,1,3:T(8,128)(2,1)}, u32[]{:S(2)}, u32[]{:S(2)}) async-start(bf16[3,1,2,32,8,128]{5,4,2,0,1,3:T(8,128)(2,1)} %copy.139), calls=%async_computation.2 | async-start | bytes 786432 | tf_op jit(solution)/shard_map/all_to_all | solution.py:153
  40.2 2.6 %copy-start.27 = (f32[16,512]{1,0:T(8,128)S(1)}, f32[16,512]{1,0:T(8,128)}, u32[]{:S(2)}) copy-start(f32[16,512]{1,0:T(8,128)} %get-tuple-element.57) | copy-start | bytes 98308
  40.2 2.7 %copy-start.28 = (f32[16,512]{1,0:T(8,128)S(1)}, f32[16,512]{1,0:T(8,128)}, u32[]{:S(2)}) copy-start(f32[16,512]{1,0:T(8,128)} %get-tuple-element.58) | copy-start | bytes 98308
  48.1 17.1 %all-to-all-start = ((bf16[3,1,2,32,8,128]{5,4,2,0,1,3:T(8,128)(2,1)}), bf16[3,1,2,32,8,128]{5,4,2,0,1,3:T(8,128)(2,1)}, u32[]{:S(2)}, u32[]{:S(2)}) async-start(bf16[3,1,2,32,8,128]{5,4,2,0,1,3:T(8,128)(2,1)} %copy.115), calls=%async_computation | async-start | bytes 786432 | tf_op jit(solution)/shard_map/all_to_all | solution.py:153
  53.5 1.5 %copy-start.13 = (bf16[16,32,512]{2,1,0:T(8,128)(2,1)S(1)}, bf16[16,32,512]{2,1,0:T(8,128)(2,1)}, u32[]{:S(2)}) copy-start(bf16[16,32,512]{2,1,0:T(8,128)(2,1)} %get-tuple-element.36) | copy-start | bytes 1572868
  57.1 29.0 %copy-start.15 = (f32[3,1,8,8,512]{4,3,2,1,0:T(8,128)}, f32[3,1,8,8,512]{4,3,2,1,0:T(8,128)S(1)}, u32[]{:S(2)}) copy-start(f32[3,1,8,8,512]{4,3,2,1,0:T(8,128)S(1)} %get-tuple-element.19) | copy-start | bytes 1179652
  68.3 1.5 %copy-start.12 = (bf16[16,32,512]{2,1,0:T(8,128)(2,1)S(1)}, bf16[16,32,512]{2,1,0:T(8,128)(2,1)}, u32[]{:S(2)}) copy-start(bf16[16,32,512]{2,1,0:T(8,128)(2,1)} %get-tuple-element.33) | copy-start | bytes 1572868
  69.8 1.4 %copy-start.10 = (bf16[16,32,512]{2,1,0:T(8,128)(2,1)S(1)}, bf16[16,32,512]{2,1,0:T(8,128)(2,1)}, u32[]{:S(2)}) copy-start(bf16[16,32,512]{2,1,0:T(8,128)(2,1)} %get-tuple-element.35) | copy-start | bytes 1572868
  72.7 1.3 copy-start.22
  72.7 1.3 copy-start.23
  72.7 13.1 %copy-start.17 = (f32[3,1,8,8,512]{4,3,2,1,0:T(8,128)S(1)}, f32[3,1,8,8,512]{4,3,2,1,0:T(8,128)}, u32[]{:S(2)}) copy-start(f32[3,1,8,8,512]{4,3,2,1,0:T(8,128)} %copy-done.16) | copy-start | bytes 1179652
  82.3 3.8 %copy-start.18 = (f32[3,8,8,512]{3,2,1,0:T(8,128)S(1)}, f32[3,8,8,512]{3,2,1,0:T(8,128)}, u32[]{:S(2)}) copy-start(f32[3,8,8,512]{3,2,1,0:T(8,128)} %get-tuple-element.5) | copy-start | bytes 1179652
  82.3 3.8 %copy-start.19 = (f32[3,8,8,512]{3,2,1,0:T(8,128)S(1)}, f32[3,8,8,512]{3,2,1,0:T(8,128)}, u32[]{:S(2)}) copy-start(f32[3,8,8,512]{3,2,1,0:T(8,128)} %get-tuple-element.15) | copy-start | bytes 1179652
  86.3 1.3 copy-start.6
  88.3 1.8 %copy-start.5 = (bf16[512,512]{1,0:T(8,128)(2,1)S(1)}, bf16[512,512]{1,0:T(8,128)(2,1)}, u32[]{:S(2)}) copy-start(bf16[512,512]{1,0:T(8,128)(2,1)} %get-tuple-element.60) | copy-start | bytes 1572868
  97.8 16.5 %all-to-all-start.1 = ((bf16[3,1,2,8,32,128]{5,3,2,0,1,4:T(8,128)(2,1)}), bf16[3,1,2,8,32,128]{5,3,2,0,1,4:T(8,128)(2,1)}, u32[]{:S(2)}, u32[]{:S(2)}) async-start(bf16[3,1,2,8,32,128]{5,3,2,0,1,4:T(8,128)(2,1)} %pad_maximum_fusion.2), calls=%async_computation.1 | async-start | bytes 786432 | tf_op jit(solution)/shard_map/all_to_all | solution.py:198
  104.5 13.1 %copy-start.29 = (f32[2,32,8]{2,1,0:T(8,128)S(1)}, f32[2,32,8]{2,1,0:T(8,128)}, u32[]{:S(2)}) copy-start(f32[2,32,8]{2,1,0:T(8,128)} %constant.130) | copy-start | bytes 6148
  105.4 13.3 %copy-start.2 = (bf16[1024,2,32,8]{0,3,2,1:T(8,128)(2,1)S(1)}, bf16[1024,2,32,8]{0,3,2,1:T(8,128)(2,1)}, u32[]{:S(2)}) copy-start(bf16[1024,2,32,8]{0,3,2,1:T(8,128)(2,1)} %get-tuple-element.9) | copy-start | bytes 3145732
  114.3 16.5 %all-to-all-start.3 = ((bf16[3,1,2,8,32,128]{5,3,2,0,1,4:T(8,128)(2,1)}), bf16[3,1,2,8,32,128]{5,3,2,0,1,4:T(8,128)(2,1)}, u32[]{:S(2)}, u32[]{:S(2)}) async-start(bf16[3,1,2,8,32,128]{5,3,2,0,1,4:T(8,128)(2,1)} %pad_maximum_fusion.4), calls=%async_computation.3 | async-start | bytes 786432 | tf_op jit(solution)/shard_map/all_to_all | solution.py:198
  130.8 1.8 %copy-start.21 = (bf16[3,1,128,1024]{3,2,1,0:T(8,128)(2,1)S(1)}, bf16[3,1,128,1024]{3,2,1,0:T(8,128)(2,1)}, u32[]{:S(2)}) copy-start(bf16[3,1,128,1024]{3,2,1,0:T(8,128)(2,1)} %param.7) | copy-start | bytes 2359300
  131.9 1.7 %copy-start.8 = (f32[3,128,1024]{2,1,0:T(8,128)S(1)}, f32[3,128,1024]{2,1,0:T(8,128)}, u32[]{:S(2)}) copy-start(f32[3,128,1024]{2,1,0:T(8,128)} %fusion.193) | copy-start | bytes 4718596
  (12 other events, 12.4 us)

commit v2 on v0

--- a/solution.py
+++ b/solution.py
@@ -97,9 +97,20 @@
     me = lax.axis_index("row") * col_count + lax.axis_index("col")
 
     reciprocal = 1.0 / permittivity
-    cell_scale = jnp.zeros(region.shape, F32)
-    for region_id in range(permittivity.shape[0]):
-        cell_scale = jnp.where(region == region_id, reciprocal[region_id], cell_scale)
+    regions = permittivity.shape[0]
+    if regions == 8:
+        level = [reciprocal[region_id] for region_id in range(regions)]
+        for bit in (1, 2, 4):
+            chosen = (region & bit) != 0
+            level = [
+                jnp.where(chosen, level[pair + 1], level[pair])
+                for pair in range(0, len(level), 2)
+            ]
+        cell_scale = level[0]
+    else:
+        cell_scale = jnp.zeros(region.shape, F32)
+        for region_id in range(regions):
+            cell_scale = jnp.where(region == region_id, reciprocal[region_id], cell_scale)
     electric = displacement.astype(F32) * cell_scale[None]
 
     cos_z, sin_z = phase_table(depth, columns, depth)
@@ -155,20 +166,8 @@
     back_real, back_imag = inverse_y(rounded(b_real), rounded(b_imag))
 
     if hermitian:
-        first_real = y_real[:, 0]
-        first_imag = y_imag[:, 0]
-
-        def mirrored(values):
-            return jnp.roll(jnp.flip(values, axis=-1), 1, axis=-1)
-
-        mirror_real = mirrored(first_real)
-        mirror_imag = mirrored(first_imag)
-        plane_real = jnp.stack(
-            [0.5 * (first_real + mirror_real), 0.5 * (first_imag + mirror_imag)], axis=1
-        )
-        plane_imag = jnp.stack(
-            [0.5 * (first_imag - mirror_imag), -0.5 * (first_real - mirror_real)], axis=1
-        )
+        plane_real = by_cos[:, :, 0]
+        plane_imag = -by_sin[:, :, 0]
         pb_real, pb_imag = curl_update(
             rounded(plane_real), rounded(plane_imag), wave_y, jnp.zeros((2,), F32), kernel
         )

time: 98.6 us -> 90.6 us (0.919)
  local copies, waits for them, and re-layouts: 16 us -> 11 us
  other arithmetic: 16.6 us -> 13.8 us
    unnamed x42 -> x34, local copies, waits for them, and re-layouts: 7.5 us -> 4.22 us
    mul x2 -> x0, other arithmetic: 1.85 us -> none  [the longest x1 0.97 us: on_device(): -0.5 * (first_real - mirror_real)]
    concatenate x4 -> x0, local copies, waits for them, and re-layouts: 1.57 us -> none  [mirrored(): return jnp.roll(jnp.flip(values, axis=-1), 1, axis=-1)]
  transfers between devices with their start and end apart: 1 -> 1, of which waited for: 1 -> 1; matrix products, arithmetic and copies ran while one was open for 4% -> 5% of each run, Pallas kernels for 0% -> 0%
where the time goes in v2:
time: 90.6 us; the launch traced here: 90 us
  blocking collectives  24.1 us (27%)
  matrix products  16.8 us (19%)
  waiting for transfers between devices  16.3 us (18%)
  other arithmetic  13.8 us (15%)
  local copies, waits for them, and re-layouts  11 us (12%)
  starting transfers between devices  7.48 us (8%)
    all_to_all x1, blocking collectives, on_device(): lax.all_to_all(outgoing, ('row', 'col'), split_axis=4, concat_axis=3, til...  24.1 us
    all_to_all x1, waiting for transfers between devices, on_device(): lax.all_to_all(spectrum, ('row', 'col'), split_axis=3, concat_axis=5, til...  16.3 us
    all_to_all x1, starting transfers between devices, on_device(): lax.all_to_all(spectrum, ('row', 'col'), split_axis=3, concat_axis=5, til...  7.48 us
    dot_general x12, matrix products, mat(): term = jnp.einsum(spec, part, operand, preferred_element_type=F32)  6.53 us
    mul x1, other arithmetic, on_device(): electric = displacement.astype(F32) * cell_scale[None]  5.25 us
    unnamed x34, local copies, waits for them, and re-layouts  4.22 us
    dot_general x1, matrix products, on_device(): jnp.einsum(spec_back, weighted, z_low, preferred_element_type=F32)  2.77 us
    sub x2, other arithmetic, phase_table(): cosine = outer_cos * inner_cos - outer_sin * inner_sin  2.34 us
  transfers between devices with their start and end apart: 1, of which 1 were waited for; matrix products, arithmetic and copies ran while one was open for 5% of the time, Pallas kernels for 0%

profile of v2, /device:TPU:0, one launch (start us, length us, event | category | flops | bytes accessed | tf_op | source)
XLA Modules:
  0.0 90.0 jit_solution(9168752551996266752)
XLA Ops:
  0.4 0.7 broadcast_divide_fusion
  1.1 0.7 fusion.146
  2.6 0.6 slice_negate_fusion
  3.7 0.9 copy-done.12
  4.6 5.2 %select_bitcast_fusion = f32[128,1024]{1,0:T(8,128)S(1)} fusion(s32[1,128,1024]{2,1,0:T(8,128)S(1)} %copy-done.12, f32[]{:T(128)} %bitcast.8, f32[]{:T(128)} %bitcast.7, f32[]{:T(128)} %bitcast.6, f32[]{:T(128)} %bitcast.5, f32[]{:T(128)} %bitcast.4, f32[]{:T(128)} %bitcast.3, f32[]{:T(128)} %bitcast.2, f32[]{:T(128)} %bitcast.1), kind=kLoop, calls=%fused_computation.107 | loop fusion | flops 1703936 | bytes 1048608 | tf_op jit(solution)/shard_map/mul | solution.py:114
  9.9 1.0 %fusion.28 = f32[3,128,1024]{2,1,0:T(8,128)S(1)} fusion(bf16[1024,1024,1]{1,0,2:T(8,128)(2,1)S(1)} %fusion.2, bf16[3,1,128,1024]{3,2,1,0:T(8,128)(2,1)S(1)} %copy-done.15, f32[128,1024]{1,0:T(8,128)S(1)} %select_bitcast_fusion), kind=kOutput, calls=%fused_computation.62 | convolution fusion | flops 807272448 | bytes 4980736 | tf_op jit(solution)/shard_map/zk,clyz->clky/dot_general | solution.py:129
  10.9 1.0 %fusion.67 = f32[3,128,1024]{2,1,0:T(8,128)S(1)} fusion(bf16[1024,1024,1]{1,0,2:T(8,128)(2,1)S(1)} %fusion.2, bf16[3,1,128,1024]{3,2,1,0:T(8,128)(2,1)S(1)} %copy-done.15, f32[128,1024]{1,0:T(8,128)S(1)} %select_bitcast_fusion), kind=kOutput, calls=%fused_computation.118 | convolution fusion | flops 806879232 | bytes 4980736 | tf_op jit(solution)/shard_map/zk,clyz->clky/dot_general | solution.py:128
  11.9 2.1 %fusion.5 = bf16[3,1,1024,128]{2,3,0,1:T(8,128)(2,1)} fusion(f32[3,128,1024]{2,1,0:T(8,128)S(1)} %fusion.67, f32[3,128,1024]{2,1,0:T(8,128)S(1)} %fusion.28, bf16[3,1,128,1024]{3,2,1,0:T(8,128)(2,1)S(1)} %copy-done.15, f32[128,1024]{1,0:T(8,128)S(1)} %select_bitcast_fusion, f32[1024,511]{1,0:T(8,128)S(1)} %slice_negate_fusion, f32[1024,1]{1,0:T(8,128)S(1)} %fusion.44, ...), kind=kOutput, calls=%fused_computation.29 | convolution fusion | flops 813301760 | bytes 9437184 | tf_op jit(solution)/shard_map/zk,clyz->clky/dot_general | solution.py:130
  14.1 1.5 %copy.34 = bf16[3,1,1024,128]{3,2,0,1:T(8,128)(2,1)S(1)} copy(bf16[3,1,1024,128]{2,3,0,1:T(8,128)(2,1)} %fusion.5) | data formatting | bytes 1572864 | tf_op jit(solution)/shard_map/convert_element_type | solution.py:132
  15.6 1.0 %copy.35 = bf16[3,1,2,32,16,128]{5,4,2,0,1,3:T(8,128)(2,1)} copy(bf16[3,1,2,32,16,128]{5,4,3,2,0,1:T(8,128)(2,1)S(1)} %bitcast.317) | data formatting | bytes 1572864 | tf_op jit(solution)/shard_map/reshape | solution.py:132
  16.6 7.5 %all-to-all-start = ((bf16[3,1,2,32,16,128]{5,4,2,0,1,3:T(8,128)(2,1)}), bf16[3,1,2,32,16,128]{5,4,2,0,1,3:T(8,128)(2,1)S(1)}, u32[]{:S(2)}, u32[]{:S(2)}) async-start(bf16[3,1,2,32,16,128]{5,4,2,0,1,3:T(8,128)(2,1)} %copy.35), calls=%async_computation | async-start | bytes 1572864 | tf_op jit(solution)/shard_map/all_to_all | solution.py:135
  24.9 1.9 %multiply_subtract_fusion.1 = (f32[16,32,512]{2,1,0:T(8,128)S(1)}, bf16[16,32,512]{2,1,0:T(8,128)(2,1)}, bf16[16,32,512]{2,1,0:T(8,128)(2,1)}, bf16[16,32,512]{2...) fusion(f32[32,512]{1,0:T(8,128)S(1)} %fusion.120, f32[16,512]{1,0:T(8,128)S(1)} %get-tuple-element.38, ...), kind=kLoop, calls=%fused_computation.59 | loop fusion | flops 3670016 | bytes 4390912 | tf_op jit(solution)/shard_map/sub | solution.py:45
  26.8 1.5 %fusion.25 = (bf16[512,512]{1,0:T(8,128)(2,1)S(1)}, bf16[512,512]{1,0:T(8,128)(2,1)}, bf16[512,512]{1,0:T(8,128)(2,1)}, bf16[512,512]{1,0:T(8,128)(2,1)}) fusion(f32[16,32,512]{2,1,0:T(8,128)S(1)} %get-tuple-element.17, f32[16,32,512]{2,1,0:T(8,128)S(1)} %get-tuple-element.22), kind=kLoop, calls=%fused_computation.57 | loop fusion | flops 2097152 | bytes 4194304 | tf_op jit(solution)/shard_map/convert_element_type | solution.py:28
  28.2 16.3 %all-to-all-done = bf16[3,1,2,32,16,128]{5,4,2,0,1,3:T(8,128)(2,1)S(1)} async-done(((bf16[3,1,2,32,16,128]{5,4,2,0,1,3:T(8,128)(2,1)}), bf16[3,1,2,32,16,128]{5,4,2,0,1,3:T(8,128)(2,1)S(1)}, u32[]{:S(2)}, u32[]{:S(2)}) %all-to-all-start) | async-done | bytes 786464 | tf_op jit(solution)/shard_map/all_to_all | solution.py:135
  44.5 1.2 %copy.36 = bf16[3,1,2,1,16,32,128]{6,5,4,2,0,3,1:T(8,128)(2,1)} copy(bf16[3,1,2,1,16,32,128]{6,4,2,0,5,3,1:T(8,128)(2,1)S(1)} %bitcast.316) | data formatting | bytes 1572864 | tf_op jit(solution)/shard_map/all_to_all | solution.py:135
  45.7 1.6 %reshape_transpose_reshape.4 = bf16[3,2,16,8,512]{4,3,2,1,0:T(8,128)(2,1)S(1)} reshape(bf16[3,1,2,1,16,32,128]{6,5,4,2,0,3,1:T(8,128)(2,1)} %copy.36) | data formatting | bytes 1572864 | tf_op jit(solution)/shard_map/reshape;transpose;reshape | solution.py:139
  47.3 1.7 %fusion.147 = f32[3,2,16,8,512]{4,3,2,1,0:T(8,128)S(1)} fusion(bf16[3,2,16,8,512]{4,3,2,1,0:T(8,128)(2,1)S(1)} %reshape_transpose_reshape.4, bf16[512,512,1,1,1]{1,0,4,3,2:T(8,128)(2,1)} %bitcast.321), kind=kOutput, calls=%fused_computation.236 | convolution fusion | flops 402653184 | bytes 2883584 | tf_op jit(solution)/shard_map/yk,cpjxy->cpjxk/dot_general | solution.py:65
  49.0 0.6 convolution_add_fusion.3
  57.0 0.6 convolution_add_fusion
  57.6 0.6 convolution_add_fusion.1
  59.7 24.1 %all_to_all.24 = bf16[3,1,2,16,32,128]{5,3,2,0,1,4:T(8,128)(2,1)S(1)} all-to-all(bf16[3,1,2,16,32,128]{5,3,2,0,1,4:T(8,128)(2,1)S(1)} %pad_maximum_fusion.2), channel_id=1, replica_groups=mesh['row'=8,'col'=4] {'row','col'}, dimensions={4} | all-to-all | bytes 1572864 | tf_op jit(solution)/shard_map/all_to_all | solution.py:188
  83.9 1.4 %copy-done.3 = bf16[1024,1024,1]{1,0,2:T(8,128)(2,1)S(1)} copy-done((bf16[1024,1024,1]{1,0,2:T(8,128)(2,1)S(1)}, bf16[1024,1024,1]{1,0,2:T(8,128)(2,1)}, u32[]{:S(2)}) %copy-start.3) | copy-done | bytes 2097176
  85.3 1.3 %fusion.143 = f32[3,128,1024]{2,1,0:T(8,128)S(1)} fusion(bf16[1024,1024,1]{1,0,2:T(8,128)(2,1)S(1)} %copy-done.3, f32[3,1024,128]{2,1,0:T(8,128)S(1)} %bitcast.314, f32[1024]{0:T(1024)S(1)} %copy-done.14), kind=kOutput, calls=%fused_computation.234 | convolution fusion | flops 806092800 | bytes 5246976 | tf_op jit(solution)/shard_map/clky,zk->clyz/dot_general | solution.py:201
  87.2 2.8 %fusion.6 = bf16[3,1,128,1024]{3,2,1,0:T(8,128)(2,1)} fusion(f32[3,128,1024]{2,1,0:T(8,128)S(1)} %fusion.143, bf16[3,1,128,1024]{3,2,1,0:T(8,128)(2,1)S(1)} %copy-done.16, f32[3,1024,128]{2,1,0:T(8,128)S(1)} %bitcast.315, f32[1024]{0:T(1024)S(1)} %copy-done.14, f32[1024,511]{1,0:T(8,128)S(1)} %copy-done.1, f32[1024,1]{1,0:T(8,128)S(1)} %copy-done.11, ...), kind=kOutput, calls=%fused_computation.30 | convolution fusion | flops 812908544 | bytes 8916992 | tf_op jit(solution)/shard_map/clky,zk->clyz/dot_general | solution.py:201
  (82 shorter events, 11.9 us)
Async XLA Ops:
  0.4 11.6 %copy-start.10 = (f32[1024,1]{1,0:T(8,128)}, f32[1024,1]{1,0:T(8,128)S(1)}, u32[]{:S(2)}) copy-start(f32[1024,1]{1,0:T(8,128)S(1)} %fusion.44) | copy-start | bytes 12292
  3.2 8.8 %copy-start = (f32[1024,511]{1,0:T(8,128)}, f32[1024,511]{1,0:T(8,128)S(1)}, u32[]{:S(2)}) copy-start(f32[1024,511]{1,0:T(8,128)S(1)} %slice_negate_fusion) | copy-start | bytes 6279172
  3.2 1.4 %copy-start.12 = (s32[1,128,1024]{2,1,0:T(8,128)S(1)}, s32[1,128,1024]{2,1,0:T(8,128)}, u32[]{:S(2)}) copy-start(s32[1,128,1024]{2,1,0:T(8,128)} %param.8) | copy-start | bytes 1572868
  3.2 6.7 %copy-start.15 = (bf16[3,1,128,1024]{3,2,1,0:T(8,128)(2,1)S(1)}, bf16[3,1,128,1024]{3,2,1,0:T(8,128)(2,1)}, u32[]{:S(2)}) copy-start(bf16[3,1,128,1024]{3,2,1,0:T(8,128)(2,1)} %param.6) | copy-start | bytes 2359300
  3.7 7.2 %copy-start.2 = (bf16[1024,1024,1]{1,0,2:T(8,128)(2,1)}, bf16[1024,1024,1]{1,0,2:T(8,128)(2,1)S(1)}, u32[]{:S(2)}) copy-start(bf16[1024,1024,1]{1,0,2:T(8,128)(2,1)S(1)} %fusion.2) | copy-start | bytes 6291460
  16.6 27.9 %all-to-all-start = ((bf16[3,1,2,32,16,128]{5,4,2,0,1,3:T(8,128)(2,1)}), bf16[3,1,2,32,16,128]{5,4,2,0,1,3:T(8,128)(2,1)S(1)}, u32[]{:S(2)}, u32[]{:S(2)}) async-start(bf16[3,1,2,32,16,128]{5,4,2,0,1,3:T(8,128)(2,1)} %copy.35), calls=%async_computation | async-start | bytes 1572864 | tf_op jit(solution)/shard_map/all_to_all | solution.py:135
  47.3 1.7 %copy-start.8 = (bf16[16,32,512]{2,1,0:T(8,128)(2,1)S(1)}, bf16[16,32,512]{2,1,0:T(8,128)(2,1)}, u32[]{:S(2)}) copy-start(bf16[16,32,512]{2,1,0:T(8,128)(2,1)} %get-tuple-element.18) | copy-start | bytes 1572868
  49.0 1.0 %copy-start.9 = (bf16[16,32,512]{2,1,0:T(8,128)(2,1)S(1)}, bf16[16,32,512]{2,1,0:T(8,128)(2,1)}, u32[]{:S(2)}) copy-start(bf16[16,32,512]{2,1,0:T(8,128)(2,1)} %get-tuple-element.21) | copy-start | bytes 1572868
  49.6 1.1 %copy-start.7 = (bf16[16,32,512]{2,1,0:T(8,128)(2,1)S(1)}, bf16[16,32,512]{2,1,0:T(8,128)(2,1)}, u32[]{:S(2)}) copy-start(bf16[16,32,512]{2,1,0:T(8,128)(2,1)} %get-tuple-element.20) | copy-start | bytes 1572868
  51.2 0.7 copy-start.13
  53.0 1.0 %copy-start.6 = (bf16[512,512]{1,0:T(8,128)(2,1)S(1)}, bf16[512,512]{1,0:T(8,128)(2,1)}, u32[]{:S(2)}) copy-start(bf16[512,512]{1,0:T(8,128)(2,1)} %get-tuple-element.43) | copy-start | bytes 1572868
  53.4 1.1 %copy-start.5 = (bf16[512,512]{1,0:T(8,128)(2,1)S(1)}, bf16[512,512]{1,0:T(8,128)(2,1)}, u32[]{:S(2)}) copy-start(bf16[512,512]{1,0:T(8,128)(2,1)} %get-tuple-element.12) | copy-start | bytes 1572868
  55.7 1.0 %copy-start.4 = (bf16[512,512]{1,0:T(8,128)(2,1)S(1)}, bf16[512,512]{1,0:T(8,128)(2,1)}, u32[]{:S(2)}) copy-start(bf16[512,512]{1,0:T(8,128)(2,1)} %get-tuple-element.44) | copy-start | bytes 1572868
  83.7 1.6 %copy-start.3 = (bf16[1024,1024,1]{1,0,2:T(8,128)(2,1)S(1)}, bf16[1024,1024,1]{1,0,2:T(8,128)(2,1)}, u32[]{:S(2)}) copy-start(bf16[1024,1024,1]{1,0,2:T(8,128)(2,1)} %copy-done.2) | copy-start | bytes 6291460
  83.7 1.6 %copy-start.14 = (f32[1024]{0:T(1024)S(1)}, f32[1024]{0:T(1024)}, u32[]{:S(2)}) copy-start(f32[1024]{0:T(1024)} %constant.110.clone) | copy-start | bytes 12292
  85.3 1.6 %copy-start.1 = (f32[1024,511]{1,0:T(8,128)S(1)}, f32[1024,511]{1,0:T(8,128)}, u32[]{:S(2)}) copy-start(f32[1024,511]{1,0:T(8,128)} %copy-done) | copy-start | bytes 6279172
  85.3 1.7 %copy-start.11 = (f32[1024,1]{1,0:T(8,128)S(1)}, f32[1024,1]{1,0:T(8,128)}, u32[]{:S(2)}) copy-start(f32[1024,1]{1,0:T(8,128)} %copy-done.10) | copy-start | bytes 12292
  85.3 1.9 %copy-start.16 = (bf16[3,1,128,1024]{3,2,1,0:T(8,128)(2,1)S(1)}, bf16[3,1,128,1024]{3,2,1,0:T(8,128)(2,1)}, u32[]{:S(2)}) copy-start(bf16[3,1,128,1024]{3,2,1,0:T(8,128)(2,1)} %param.7) | copy-start | bytes 2359300

commit v3 on v2

--- a/solution.py
+++ b/solution.py
@@ -98,19 +98,17 @@
 
     reciprocal = 1.0 / permittivity
     regions = permittivity.shape[0]
-    if regions == 8:
-        level = [reciprocal[region_id] for region_id in range(regions)]
-        for bit in (1, 2, 4):
-            chosen = (region & bit) != 0
-            level = [
-                jnp.where(chosen, level[pair + 1], level[pair])
-                for pair in range(0, len(level), 2)
-            ]
-        cell_scale = level[0]
-    else:
-        cell_scale = jnp.zeros(region.shape, F32)
-        for region_id in range(regions):
-            cell_scale = jnp.where(region == region_id, reciprocal[region_id], cell_scale)
+    one_hot = (region[..., None] == lax.iota(jnp.int32, regions)).astype(BF16)
+    first = rounded(reciprocal)
+    rest = reciprocal - first
+    second = rounded(rest)
+    parts = (first, second, rest - second)
+    cell_scale = None
+    for part in parts:
+        term = jnp.einsum(
+            "...k,k->...", one_hot, part.astype(BF16), preferred_element_type=F32
+        )
+        cell_scale = term if cell_scale is None else cell_scale + term
     electric = displacement.astype(F32) * cell_scale[None]
 
     cos_z, sin_z = phase_table(depth, columns, depth)

time: 90.6 us -> 88.1 us (0.972)
  other arithmetic: 13.8 us -> 8.19 us
  matrix products: 16.8 us -> 20.2 us
    mul x1 -> x0, other arithmetic: 5.25 us -> none  [on_device(): electric = displacement.astype(F32) * cell_scale[None]]
    dot_general x0 -> x3, matrix products: none -> 3.41 us  [on_device(): jnp.einsum('...k,k->...', one_hot, part.astype(BF16), preferred_element_t...]
    unnamed x34 -> x36, local copies, waits for them, and re-layouts: 4.22 us -> 4.69 us
where the time goes in v3:
time: 88.1 us; the launch traced here: 87.6 us
  blocking collectives  24 us (27%)
  matrix products  20.2 us (23%)
  waiting for transfers between devices  16.3 us (19%)
  local copies, waits for them, and re-layouts  10.8 us (12%)
  other arithmetic  8.19 us (9%)
  starting transfers between devices  7.49 us (9%)
    all_to_all x1, blocking collectives, on_device(): lax.all_to_all(outgoing, ('row', 'col'), split_axis=4, concat_axis=3, til...  24 us
    all_to_all x1, waiting for transfers between devices, on_device(): lax.all_to_all(spectrum, ('row', 'col'), split_axis=3, concat_axis=5, til...  16.3 us
    all_to_all x1, starting transfers between devices, on_device(): lax.all_to_all(spectrum, ('row', 'col'), split_axis=3, concat_axis=5, til...  7.49 us
    dot_general x12, matrix products, mat(): term = jnp.einsum(spec, part, operand, preferred_element_type=F32)  6.53 us
    unnamed x36, local copies, waits for them, and re-layouts  4.69 us
    dot_general x3, matrix products, on_device(): jnp.einsum('...k,k->...', one_hot, part.astype(BF16), preferred_element_t...  3.41 us
    dot_general x1, matrix products, on_device(): jnp.einsum(spec_back, weighted, z_low, preferred_element_type=F32)  2.77 us
    sub x2, other arithmetic, phase_table(): cosine = outer_cos * inner_cos - outer_sin * inner_sin  2.34 us
  transfers between devices with their start and end apart: 1, of which 1 were waited for; matrix products, arithmetic and copies ran while one was open for 5% of the time, Pallas kernels for 0%

profile of v3, /device:TPU:0, one launch (start us, length us, event | category | flops | bytes accessed | tf_op | source)
XLA Modules:
  0.0 87.6 jit_solution(6135148991190837202)
XLA Ops:
  0.4 2.0 %fusion.1 = f32[1,128,1024]{2,0,1:T(1,128)S(1)} fusion(s32[128,1024]{1,0:T(8,128)} %bitcast.330, f32[8]{0:T(128)} %param.9), kind=kOutput, calls=%fused_computation.5 | convolution fusion | flops 3145776 | bytes 1048608 | tf_op jit(solution)/shard_map/...k,k->.../dot_general | solution.py:108
  2.4 0.7 fusion.2
  3.1 0.7 fusion.3
  4.6 0.6 slice_negate_fusion
  6.1 1.0 %copy-done.14 = bf16[3,1,128,1024]{3,2,1,0:T(8,128)(2,1)S(1)} copy-done((bf16[3,1,128,1024]{3,2,1,0:T(8,128)(2,1)S(1)}, bf16[3,1,128,1024]{3,2,1,0:T(8,128)(2,1)}, u32[]{:S(2)}) %copy-start.14) | copy-done | bytes 786456
  7.1 1.0 %fusion.34 = f32[3,128,1024]{2,1,0:T(8,128)S(1)} fusion(bf16[1024,1024,1]{1,0,2:T(8,128)(2,1)S(1)} %fusion.5, bf16[3,1,128,1024]{3,2,1,0:T(8,128)(2,1)S(1)} %copy-done.14, f32[128,1024]{1,0:T(8,128)S(1)} %bitcast_add_fusion.1), kind=kOutput, calls=%fused_computation.69 | convolution fusion | flops 807272448 | bytes 4980736 | tf_op jit(solution)/shard_map/zk,clyz->clky/dot_general | solution.py:127
  8.5 1.0 %fusion.73 = f32[3,128,1024]{2,1,0:T(8,128)S(1)} fusion(bf16[1024,1024,1]{1,0,2:T(8,128)(2,1)S(1)} %fusion.5, bf16[3,1,128,1024]{3,2,1,0:T(8,128)(2,1)S(1)} %copy-done.14, f32[128,1024]{1,0:T(8,128)S(1)} %bitcast_add_fusion.1), kind=kOutput, calls=%fused_computation.123 | convolution fusion | flops 806879232 | bytes 4980736 | tf_op jit(solution)/shard_map/zk,clyz->clky/dot_general | solution.py:126
  9.5 2.2 %fusion.11 = bf16[3,1,1024,128]{2,3,0,1:T(8,128)(2,1)} fusion(f32[3,128,1024]{2,1,0:T(8,128)S(1)} %fusion.73, f32[3,128,1024]{2,1,0:T(8,128)S(1)} %fusion.34, bf16[3,1,128,1024]{3,2,1,0:T(8,128)(2,1)S(1)} %copy-done.14, f32[128,1024]{1,0:T(8,128)S(1)} %bitcast_add_fusion.1, f32[1024,511]{1,0:T(8,128)S(1)} %slice_negate_fusion, f32[1024,1]{1,0:T(8,128)S(1)} %fusion.50, ...), kind=kOutput, calls=%fused_computation.36 | convolution fusion | flops 813301760 | bytes 9437184 | tf_op jit(solution)/shard_map/zk,clyz->clky/dot_general | solution.py:128
  11.7 1.5 %copy.51 = bf16[3,1,1024,128]{3,2,0,1:T(8,128)(2,1)S(1)} copy(bf16[3,1,1024,128]{2,3,0,1:T(8,128)(2,1)} %fusion.11) | data formatting | bytes 1572864 | tf_op jit(solution)/shard_map/convert_element_type | solution.py:130
  13.2 1.0 %copy.52 = bf16[3,1,2,32,16,128]{5,4,2,0,1,3:T(8,128)(2,1)} copy(bf16[3,1,2,32,16,128]{5,4,3,2,0,1:T(8,128)(2,1)S(1)} %bitcast.325) | data formatting | bytes 1572864 | tf_op jit(solution)/shard_map/reshape | solution.py:130
  14.2 7.5 %all-to-all-start = ((bf16[3,1,2,32,16,128]{5,4,2,0,1,3:T(8,128)(2,1)}), bf16[3,1,2,32,16,128]{5,4,2,0,1,3:T(8,128)(2,1)S(1)}, u32[]{:S(2)}, u32[]{:S(2)}) async-start(bf16[3,1,2,32,16,128]{5,4,2,0,1,3:T(8,128)(2,1)} %copy.52), calls=%async_computation | async-start | bytes 1572864 | tf_op jit(solution)/shard_map/all_to_all | solution.py:133
  22.5 1.9 %multiply_subtract_fusion.1 = (f32[16,32,512]{2,1,0:T(8,128)S(1)}, bf16[16,32,512]{2,1,0:T(8,128)(2,1)}, bf16[16,32,512]{2,1,0:T(8,128)(2,1)}, bf16[16,32,512]{2...) fusion(f32[32,512]{1,0:T(8,128)S(1)} %fusion.126, f32[16,512]{1,0:T(8,128)S(1)} %get-tuple-element.30, ...), kind=kLoop, calls=%fused_computation.66 | loop fusion | flops 3670016 | bytes 4390912 | tf_op jit(solution)/shard_map/sub | solution.py:45
  24.4 1.5 %fusion.31 = (bf16[512,512]{1,0:T(8,128)(2,1)S(1)}, bf16[512,512]{1,0:T(8,128)(2,1)}, bf16[512,512]{1,0:T(8,128)(2,1)}, bf16[512,512]{1,0:T(8,128)(2,1)}) fusion(f32[16,32,512]{2,1,0:T(8,128)S(1)} %get-tuple-element.17, f32[16,32,512]{2,1,0:T(8,128)S(1)} %get-tuple-element.22), kind=kLoop, calls=%fused_computation.64 | loop fusion | flops 2097152 | bytes 4194304 | tf_op jit(solution)/shard_map/convert_element_type | solution.py:28
  25.8 16.3 %all-to-all-done = bf16[3,1,2,32,16,128]{5,4,2,0,1,3:T(8,128)(2,1)S(1)} async-done(((bf16[3,1,2,32,16,128]{5,4,2,0,1,3:T(8,128)(2,1)}), bf16[3,1,2,32,16,128]{5,4,2,0,1,3:T(8,128)(2,1)S(1)}, u32[]{:S(2)}, u32[]{:S(2)}) %all-to-all-start) | async-done | bytes 786464 | tf_op jit(solution)/shard_map/all_to_all | solution.py:133
  42.1 1.2 %copy.53 = bf16[3,1,2,1,16,32,128]{6,5,4,2,0,3,1:T(8,128)(2,1)} copy(bf16[3,1,2,1,16,32,128]{6,4,2,0,5,3,1:T(8,128)(2,1)S(1)} %bitcast.324) | data formatting | bytes 1572864 | tf_op jit(solution)/shard_map/all_to_all | solution.py:133
  43.3 1.6 %reshape_transpose_reshape.4 = bf16[3,2,16,8,512]{4,3,2,1,0:T(8,128)(2,1)S(1)} reshape(bf16[3,1,2,1,16,32,128]{6,5,4,2,0,3,1:T(8,128)(2,1)} %copy.53) | data formatting | bytes 1572864 | tf_op jit(solution)/shard_map/reshape;transpose;reshape | solution.py:137
  44.9 1.7 %fusion.159 = f32[3,2,16,8,512]{4,3,2,1,0:T(8,128)S(1)} fusion(bf16[3,2,16,8,512]{4,3,2,1,0:T(8,128)(2,1)S(1)} %reshape_transpose_reshape.4, bf16[512,512,1,1,1]{1,0,4,3,2:T(8,128)(2,1)} %bitcast.329), kind=kOutput, calls=%fused_computation.248 | convolution fusion | flops 402653184 | bytes 2883584 | tf_op jit(solution)/shard_map/yk,cpjxy->cpjxk/dot_general | solution.py:65
  46.6 0.6 convolution_add_fusion.3
  54.6 0.6 convolution_add_fusion
  55.2 0.6 convolution_add_fusion.1
  57.3 24.0 %all_to_all.24 = bf16[3,1,2,16,32,128]{5,3,2,0,1,4:T(8,128)(2,1)S(1)} all-to-all(bf16[3,1,2,16,32,128]{5,3,2,0,1,4:T(8,128)(2,1)S(1)} %pad_maximum_fusion.2), channel_id=1, replica_groups=mesh['row'=8,'col'=4] {'row','col'}, dimensions={4} | all-to-all | bytes 1572864 | tf_op jit(solution)/shard_map/all_to_all | solution.py:186
  81.5 1.4 %copy-done.3 = bf16[1024,1024,1]{1,0,2:T(8,128)(2,1)S(1)} copy-done((bf16[1024,1024,1]{1,0,2:T(8,128)(2,1)S(1)}, bf16[1024,1024,1]{1,0,2:T(8,128)(2,1)}, u32[]{:S(2)}) %copy-start.3) | copy-done | bytes 2097176
  82.9 1.3 %fusion.156 = f32[3,128,1024]{2,1,0:T(8,128)S(1)} fusion(bf16[1024,1024,1]{1,0,2:T(8,128)(2,1)S(1)} %copy-done.3, f32[3,1024,128]{2,1,0:T(8,128)S(1)} %bitcast.322, f32[1024]{0:T(1024)S(1)} %copy-done.13), kind=kOutput, calls=%fused_computation.247 | convolution fusion | flops 806092800 | bytes 5246976 | tf_op jit(solution)/shard_map/clky,zk->clyz/dot_general | solution.py:199
  84.8 2.8 %fusion.12 = bf16[3,1,128,1024]{3,2,1,0:T(8,128)(2,1)} fusion(f32[3,128,1024]{2,1,0:T(8,128)S(1)} %fusion.156, bf16[3,1,128,1024]{3,2,1,0:T(8,128)(2,1)S(1)} %copy-done.15, f32[3,1024,128]{2,1,0:T(8,128)S(1)} %bitcast.323, f32[1024]{0:T(1024)S(1)} %copy-done.13, f32[1024,511]{1,0:T(8,128)S(1)} %copy-done.1, f32[1024,1]{1,0:T(8,128)S(1)} %copy-done.11, ...), kind=kOutput, calls=%fused_computation.37 | convolution fusion | flops 812908544 | bytes 8916992 | tf_op jit(solution)/shard_map/clky,zk->clyz/dot_general | solution.py:199
  (85 shorter events, 12.5 us)
Async XLA Ops:
  0.0 2.4 %copy-start.17 = (f32[8]{0:T(128)S(1)}, f32[8]{0:T(128)}, u32[]{:S(2)}) copy-start(f32[8]{0:T(128)} %param.9) | copy-start | bytes 100
  0.0 2.4 %copy-start.16 = (s32[1,128,1024]{2,1,0:T(8,128)S(1)}, s32[1,128,1024]{2,1,0:T(8,128)}, u32[]{:S(2)}) copy-start(s32[1,128,1024]{2,1,0:T(8,128)} %param.8) | copy-start | bytes 1572868
  0.4 9.1 %copy-start.10 = (f32[1024,1]{1,0:T(8,128)}, f32[1024,1]{1,0:T(8,128)S(1)}, u32[]{:S(2)}) copy-start(f32[1024,1]{1,0:T(8,128)S(1)} %fusion.50) | copy-start | bytes 12292
  5.3 4.2 %copy-start = (f32[1024,511]{1,0:T(8,128)}, f32[1024,511]{1,0:T(8,128)S(1)}, u32[]{:S(2)}) copy-start(f32[1024,511]{1,0:T(8,128)S(1)} %slice_negate_fusion) | copy-start | bytes 6279172
  5.6 1.6 %copy-start.14 = (bf16[3,1,128,1024]{3,2,1,0:T(8,128)(2,1)S(1)}, bf16[3,1,128,1024]{3,2,1,0:T(8,128)(2,1)}, u32[]{:S(2)}) copy-start(bf16[3,1,128,1024]{3,2,1,0:T(8,128)(2,1)} %param.6) | copy-start | bytes 2359300
  7.1 1.3 %copy-start.2 = (bf16[1024,1024,1]{1,0,2:T(8,128)(2,1)}, bf16[1024,1024,1]{1,0,2:T(8,128)(2,1)S(1)}, u32[]{:S(2)}) copy-start(bf16[1024,1024,1]{1,0,2:T(8,128)(2,1)S(1)} %fusion.5) | copy-start | bytes 6291460
  14.2 27.9 %all-to-all-start = ((bf16[3,1,2,32,16,128]{5,4,2,0,1,3:T(8,128)(2,1)}), bf16[3,1,2,32,16,128]{5,4,2,0,1,3:T(8,128)(2,1)S(1)}, u32[]{:S(2)}, u32[]{:S(2)}) async-start(bf16[3,1,2,32,16,128]{5,4,2,0,1,3:T(8,128)(2,1)} %copy.52), calls=%async_computation | async-start | bytes 1572864 | tf_op jit(solution)/shard_map/all_to_all | solution.py:133
  44.9 1.7 %copy-start.8 = (bf16[16,32,512]{2,1,0:T(8,128)(2,1)S(1)}, bf16[16,32,512]{2,1,0:T(8,128)(2,1)}, u32[]{:S(2)}) copy-start(bf16[16,32,512]{2,1,0:T(8,128)(2,1)} %get-tuple-element.18) | copy-start | bytes 1572868
  46.6 1.0 %copy-start.9 = (bf16[16,32,512]{2,1,0:T(8,128)(2,1)S(1)}, bf16[16,32,512]{2,1,0:T(8,128)(2,1)}, u32[]{:S(2)}) copy-start(bf16[16,32,512]{2,1,0:T(8,128)(2,1)} %get-tuple-element.21) | copy-start | bytes 1572868
  47.2 1.1 %copy-start.7 = (bf16[16,32,512]{2,1,0:T(8,128)(2,1)S(1)}, bf16[16,32,512]{2,1,0:T(8,128)(2,1)}, u32[]{:S(2)}) copy-start(bf16[16,32,512]{2,1,0:T(8,128)(2,1)} %get-tuple-element.20) | copy-start | bytes 1572868
  48.8 0.7 copy-start.12
  50.6 1.0 %copy-start.6 = (bf16[512,512]{1,0:T(8,128)(2,1)S(1)}, bf16[512,512]{1,0:T(8,128)(2,1)}, u32[]{:S(2)}) copy-start(bf16[512,512]{1,0:T(8,128)(2,1)} %get-tuple-element.35) | copy-start | bytes 1572868
  51.0 1.1 %copy-start.5 = (bf16[512,512]{1,0:T(8,128)(2,1)S(1)}, bf16[512,512]{1,0:T(8,128)(2,1)}, u32[]{:S(2)}) copy-start(bf16[512,512]{1,0:T(8,128)(2,1)} %get-tuple-element.12) | copy-start | bytes 1572868
  53.3 1.0 %copy-start.4 = (bf16[512,512]{1,0:T(8,128)(2,1)S(1)}, bf16[512,512]{1,0:T(8,128)(2,1)}, u32[]{:S(2)}) copy-start(bf16[512,512]{1,0:T(8,128)(2,1)} %get-tuple-element.36) | copy-start | bytes 1572868
  81.3 1.6 %copy-start.3 = (bf16[1024,1024,1]{1,0,2:T(8,128)(2,1)S(1)}, bf16[1024,1024,1]{1,0,2:T(8,128)(2,1)}, u32[]{:S(2)}) copy-start(bf16[1024,1024,1]{1,0,2:T(8,128)(2,1)} %copy-done.2) | copy-start | bytes 6291460
  81.3 1.6 %copy-start.13 = (f32[1024]{0:T(1024)S(1)}, f32[1024]{0:T(1024)}, u32[]{:S(2)}) copy-start(f32[1024]{0:T(1024)} %constant.106.clone) | copy-start | bytes 12292
  82.9 1.6 %copy-start.1 = (f32[1024,511]{1,0:T(8,128)S(1)}, f32[1024,511]{1,0:T(8,128)}, u32[]{:S(2)}) copy-start(f32[1024,511]{1,0:T(8,128)} %copy-done) | copy-start | bytes 6279172
  82.9 1.7 %copy-start.11 = (f32[1024,1]{1,0:T(8,128)S(1)}, f32[1024,1]{1,0:T(8,128)}, u32[]{:S(2)}) copy-start(f32[1024,1]{1,0:T(8,128)} %copy-done.10) | copy-start | bytes 12292
  82.9 1.9 %copy-start.15 = (bf16[3,1,128,1024]{3,2,1,0:T(8,128)(2,1)S(1)}, bf16[3,1,128,1024]{3,2,1,0:T(8,128)(2,1)}, u32[]{:S(2)}) copy-start(bf16[3,1,128,1024]{3,2,1,0:T(8,128)(2,1)} %param.7) | copy-start | bytes 2359300

commit v4 on v3

--- a/solution.py
+++ b/solution.py
@@ -117,24 +117,30 @@
         sin_part = jnp.concatenate([parity[:, None], -sin_z[:, 1:]], axis=1)
     else:
         sin_part = -sin_z
-    table_z = jnp.concatenate([cos_z, sin_part], axis=1)
+    table_z = jnp.stack(
+        [cos_z.reshape(depth, devices, per_device), sin_part.reshape(depth, devices, per_device)],
+        axis=2,
+    ).reshape(depth, 2 * columns)
     z_high, z_low = split_parts(table_z)
-
-    e_high, e_low = split_parts(electric)
-    spec_z = "zk,clyz->clky"
+    rows = members * local_x * local_y
+
+    e_high, e_low = split_parts(electric.reshape(rows, depth))
+    spec_z = "zk,rz->kr"
     spectrum = (
         jnp.einsum(spec_z, z_high, e_high, preferred_element_type=F32)
         + jnp.einsum(spec_z, z_high, e_low, preferred_element_type=F32)
         + jnp.einsum(spec_z, z_low, e_high, preferred_element_type=F32)
     )
     spectrum = spectrum.astype(BF16).reshape(
-        members, local_x, 2, devices, per_device, local_y
+        devices, 2, per_device, members, local_x, local_y
     )
     gathered = lax.all_to_all(
-        spectrum, ("row", "col"), split_axis=3, concat_axis=5, tiled=True
-    )
-    gathered = gathered.reshape(members, local_x, 2, per_device, row_count, width_y)
-    gathered = jnp.moveaxis(gathered, 1, 4).reshape(
+        spectrum, ("row", "col"), split_axis=0, concat_axis=0, tiled=True
+    )
+    gathered = gathered.reshape(
+        row_count, col_count, 2, per_device, members, local_x, local_y
+    )
+    gathered = jnp.transpose(gathered, (4, 2, 3, 0, 5, 1, 6)).reshape(
         members, 2, per_device, span_x, width_y
     )
 
@@ -180,25 +186,25 @@
     outgoing = outgoing.reshape(
         members, 2, per_device, row_count, local_x, col_count, local_y
     )
-    outgoing = jnp.moveaxis(outgoing, 4, 1).reshape(
-        members, local_x, 2, per_device, devices, local_y
+    outgoing = jnp.transpose(outgoing, (3, 5, 1, 2, 0, 4, 6)).reshape(
+        devices, 2, per_device, members, local_x, local_y
     )
     returned = lax.all_to_all(
-        outgoing, ("row", "col"), split_axis=4, concat_axis=3, tiled=True
-    )
-    returned = returned.reshape(members, local_x, 2 * columns, local_y)
-
-    weight = np.full((2 * columns,), 1.0 / depth, np.float32)
+        outgoing, ("row", "col"), split_axis=0, concat_axis=0, tiled=True
+    )
+    returned = returned.reshape(2 * columns, rows)
+
+    weight = np.full((devices, 2, per_device), 1.0 / depth, np.float32)
     if hermitian:
         weight[:] = 2.0 / depth
-        weight[0] = 1.0 / depth
-        weight[columns] = 1.0 / depth
-    weight = jnp.asarray(weight)[:, None]
+        weight[0, :, 0] = 1.0 / depth
+    weight = jnp.asarray(weight.reshape(2 * columns, 1))
     weighted = (returned.astype(F32) * weight).astype(BF16)
-    spec_back = "clky,zk->clyz"
+    spec_back = "kr,zk->rz"
     field = jnp.einsum(spec_back, weighted, z_high, preferred_element_type=F32) + jnp.einsum(
         spec_back, weighted, z_low, preferred_element_type=F32
     )
+    field = field.reshape(members, local_x, local_y, depth)
     return (magnetic.astype(F32) + field).astype(BF16)
 
 

time: 88.1 us -> 111 us (1.26)
  local copies, waits for them, and re-layouts: 10.8 us -> 24.7 us
  other arithmetic: 8.19 us -> 16.8 us
    sub x0 -> x2, local copies, waits for them, and re-layouts: none -> 14.3 us  [phase_table(): cosine = outer_cos * inner_cos - outer_sin * inner_sin]
    concatenate x0 -> x1, local copies, waits for them, and re-layouts: none -> 2.89 us  [on_device(): sin_part = jnp.concatenate([parity[:, None], -sin_z[:, 1:]], axis=1)]
    reshape x1 -> x2, local copies, waits for them, and re-layouts: 1.02 us -> 3.44 us  [on_device(): spectrum.astype(BF16)]
    convert_element_type x2 -> x3, other arithmetic: 2.01 us -> 4.27 us  [split_parts(): return (high.astype(BF16), low.astype(BF16))]
    concatenate x2 -> x1, other arithmetic: 0.08 us -> 1.97 us  [on_device(): sin_part = jnp.concatenate([parity[:, None], -sin_z[:, 1:]], axis=1)]
    unnamed x36 -> x32, local copies, waits for them, and re-layouts: 4.69 us -> 2.84 us
    dot_general x1, matrix products: 2.77 us -> 1.01 us  [on_device(): jnp.einsum(spec_back, weighted, z_low, preferred_element_type=F32)]
    neg x1, other arithmetic: 0.61 us -> 2.2 us  [on_device(): sin_part = jnp.concatenate([parity[:, None], -sin_z[:, 1:]], axis=1)]
  transfers between devices with their start and end apart: 1 -> 1, of which waited for: 1 -> 1; matrix products, arithmetic and copies ran while one was open for 5% -> 4% of each run, Pallas kernels for 0% -> 0%
where the time goes in v4:
time: 111 us; the launch traced here: 110 us
  local copies, waits for them, and re-layouts  24.7 us (22%)
  blocking collectives  24.1 us (22%)
  matrix products  20.4 us (18%)
  other arithmetic  16.8 us (15%)
  waiting for transfers between devices  16.3 us (15%)
  starting transfers between devices  7.53 us (7%)
    all_to_all x1, blocking collectives, on_device(): lax.all_to_all(outgoing, ('row', 'col'), split_axis=0, concat_axis=0, til...  24.1 us
    all_to_all x1, waiting for transfers between devices, on_device(): lax.all_to_all(spectrum, ('row', 'col'), split_axis=0, concat_axis=0, til...  16.3 us
    sub x2, local copies, waits for them, and re-layouts, phase_table(): cosine = outer_cos * inner_cos - outer_sin * inner_sin  14.3 us
    all_to_all x1, starting transfers between devices, on_device(): lax.all_to_all(spectrum, ('row', 'col'), split_axis=0, concat_axis=0, til...  7.53 us
    dot_general x12, matrix products, mat(): term = jnp.einsum(spec, part, operand, preferred_element_type=F32)  6.75 us
    dot_general x3, matrix products, on_device(): jnp.einsum('...k,k->...', one_hot, part.astype(BF16), preferred_element_t...  4.83 us
    convert_element_type x3, other arithmetic, split_parts(): return (high.astype(BF16), low.astype(BF16))  4.27 us
    sub x2, other arithmetic, phase_table(): cosine = outer_cos * inner_cos - outer_sin * inner_sin  3.84 us
  transfers between devices with their start and end apart: 1, of which 1 were waited for; matrix products, arithmetic and copies ran while one was open for 4% of the time, Pallas kernels for 0%

profile of v4, /device:TPU:0, one launch (start us, length us, event | category | flops | bytes accessed | tf_op | source)
XLA Modules:
  0.0 110.4 jit_solution(17688476384396137378)
XLA Ops:
  0.4 1.8 %fusion.1 = f32[1,128,1024]{2,0,1:T(1,128)S(1)} fusion(s32[128,1024]{1,0:T(8,128)} %bitcast.332, f32[8]{0:T(128)} %param.9), kind=kOutput, calls=%fused_computation.5 | convolution fusion | flops 3145776 | bytes 1048608 | tf_op jit(solution)/shard_map/...k,k->.../dot_general | solution.py:108
  2.2 1.5 %fusion.2 = f32[1,128,1024]{2,0,1:T(1,128)} fusion(s32[128,1024]{1,0:T(8,128)S(1)} %bitcast.333, f32[8]{0:T(128)S(1)} %copy-done.15), kind=kOutput, calls=%fused_computation.6 | convolution fusion | flops 3145768 | bytes 1048608 | tf_op jit(solution)/shard_map/...k,k->.../dot_general | solution.py:108
  3.7 1.5 %fusion.3 = f32[1,128,1024]{2,0,1:T(1,128)} fusion(s32[128,1024]{1,0:T(8,128)S(1)} %bitcast.334, f32[8]{0:T(128)S(1)} %copy-done.15), kind=kOutput, calls=%fused_computation.7 | convolution fusion | flops 3145752 | bytes 1048608 | tf_op jit(solution)/shard_map/...k,k->.../dot_general | solution.py:108
  5.6 2.0 %multiply_subtract_fusion = (f32[32,32,512]{2,1,0:T(8,128)S(1)}, f32[32,32,512]{2,1,0:T(8,128)}) fusion(f32[32,512]{1,0:T(8,128)S(1)} %get-tuple-element.37, f32[32,512]{1,0:T(8,128)S(1)} %get-tuple-element.36, f32[32,512]{1,0:T(8,128)S(1)} %get-tuple-element.38, f32[32,512]{1,0:T(8,128)S(1)} %get-tuple-element.35), kind=kLoop, calls=%fused_computation.16 | loop fusion | flops 3145728 | bytes 4456448 | tf_op jit(solution)/shard_map/sub | solution.py:45
  7.6 7.7 %copy.65 = f32[32,32,512]{1,0,2:T(8,128)} copy(f32[32,32,512]{2,1,0:T(8,128)S(1)} %get-tuple-element.19) | data formatting | bytes 4194304 | tf_op jit(solution)/shard_map/sub | solution.py:45
  15.2 6.6 %sub.183 = f32[1024,32,1,16]{0,3,1,2:T(8,128)S(1)} reshape(f32[32,32,512]{1,0,2:T(8,128)} %copy.65) | data formatting | bytes 4194304 | tf_op jit(solution)/shard_map/sub | solution.py:45
  21.9 2.2 %slice_negate_fusion = f32[1024,511]{1,0:T(8,128)S(1)} fusion(f32[1024,512]{1,0:T(8,128)} %bitcast.319), kind=kLoop, calls=%fused_computation.10 | loop fusion | flops 523264 | bytes 4186112 | tf_op jit(solution)/shard_map/neg | solution.py:117
  24.1 2.0 %pad_maximum_fusion.1 = f32[1024,512]{1,0:T(8,128)} fusion(f32[1024,511]{1,0:T(8,128)S(1)} %slice_negate_fusion, f32[1024,1]{1,0:T(8,128)S(1)} %fusion.51), kind=kLoop, calls=%fused_computation.11 | loop fusion | flops 524288 | bytes 4194304 | tf_op jit(solution)/shard_map/concatenate | solution.py:117
  26.0 2.9 %copy.66 = f32[1024,512]{0,1:T(8,128)} copy(f32[1024,512]{1,0:T(8,128)} %pad_maximum_fusion.1) | data formatting | bytes 4194304 | tf_op jit(solution)/shard_map/concatenate | solution.py:117
  28.9 2.5 %fusion = (bf16[1024,32,2,16]{0,3,1,2:T(8,128)(2,1)S(1)}, bf16[1024,32,2,16]{0,3,1,2:T(8,128)(2,1)S(1)}) fusion(f32[1024,32,1,16]{0,3,1,2:T(8,128)} %bitcast.320, f32[1024,32,1,16]{0,3,1,2:T(8,128)S(1)} %sub.183), kind=kLoop, calls=%fused_computation.2 | loop fusion | flops 5242880 | bytes 8388608 | tf_op jit(solution)/shard_map/convert_element_type | solution.py:28
  33.3 1.3 %fusion.158 = f32[1024,384]{1,0:T(8,128)S(1)} fusion(bf16[1024,1024]{0,1:T(8,128)(2,1)S(1)} %bitcast.316, bf16[384,1024]{1,0:T(8,128)(2,1)S(1)} %bitcast.325), kind=kOutput, calls=%fused_computation.253 | convolution fusion | flops 805306368 | bytes 4456448 | tf_op jit(solution)/shard_map/zk,rz->kr/dot_general | solution.py:130
  34.6 1.3 %fusion.159 = f32[1024,384]{1,0:T(8,128)S(1)} fusion(bf16[1024,1024]{0,1:T(8,128)(2,1)S(1)} %bitcast.317, bf16[384,1024]{1,0:T(8,128)(2,1)S(1)} %bitcast.331), kind=kOutput, calls=%fused_computation.254 | convolution fusion | flops 805306368 | bytes 4456448 | tf_op jit(solution)/shard_map/zk,rz->kr/dot_general | solution.py:131
  36.0 2.2 %add_convert_fusion.1 = bf16[1024,384]{1,0:T(8,128)(2,1)} fusion(f32[1024,384]{1,0:T(8,128)S(1)} %fusion.158, f32[1024,384]{1,0:T(8,128)S(1)} %fusion.159, bf16[1024,1024]{0,1:T(8,128)(2,1)S(1)} %bitcast.314, bf16[384,1024]{1,0:T(8,128)(2,1)S(1)} %bitcast.326), kind=kOutput, calls=%fused_computation.20 | convolution fusion | flops 806486016 | bytes 6815744 | tf_op jit(solution)/shard_map/zk,rz->kr/dot_general | solution.py:132
  38.2 2.4 %reshape.697 = bf16[32,2,16,3,1,128]{5,3,2,1,0,4:T(4,128)(2,1)S(1)} reshape(bf16[1024,384]{1,0:T(8,128)(2,1)} %add_convert_fusion.1) | data formatting | bytes 1572864 | tf_op jit(solution)/shard_map/reshape | solution.py:134
  40.6 1.0 copy.69
  41.7 7.5 %all-to-all-start = ((bf16[32,2,16,3,1,128]{5,2,4,3,1,0:T(8,128)(2,1)}), bf16[32,2,16,3,1,128]{5,2,4,3,1,0:T(8,128)(2,1)S(1)}, u32[]{:S(2)}, u32[]{:S(2)}) async-start(bf16[32,2,16,3,1,128]{5,2,4,3,1,0:T(8,128)(2,1)} %copy.69), calls=%async_computation | async-start | bytes 1572864 | tf_op jit(solution)/shard_map/all_to_all | solution.py:137
  50.0 1.9 %multiply_subtract_fusion.1 = (f32[16,32,512]{2,1,0:T(8,128)S(1)}, bf16[16,32,512]{2,1,0:T(8,128)(2,1)}, bf16[16,32,512]{2,1,0:T(8,128)(2,1)}, bf16[16,32,512]{2...) fusion(f32[32,512]{1,0:T(8,128)S(1)} %fusion.128, f32[16,512]{1,0:T(8,128)S(1)} %get-tuple-element.34, ...), kind=kLoop, calls=%fused_computation.63 | loop fusion | flops 3670016 | bytes 4390912 | tf_op jit(solution)/shard_map/sub | solution.py:45
  51.9 1.4 %fusion.26 = (bf16[512,512]{1,0:T(8,128)(2,1)}, bf16[512,512]{1,0:T(8,128)(2,1)}, bf16[512,512]{1,0:T(8,128)(2,1)}, bf16[512,512]{1,0:T(8,128)(2,1)S(1)}) fusion(f32[16,32,512]{2,1,0:T(8,128)S(1)} %get-tuple-element.21, f32[16,32,512]{2,1,0:T(8,128)S(1)} %get-tuple-element.26), kind=kLoop, calls=%fused_computation.61 | loop fusion | flops 2097152 | bytes 4194304 | tf_op jit(solution)/shard_map/convert_element_type | solution.py:28
  53.3 16.3 %all-to-all-done = bf16[32,2,16,3,1,128]{5,2,4,3,1,0:T(8,128)(2,1)S(1)} async-done(((bf16[32,2,16,3,1,128]{5,2,4,3,1,0:T(8,128)(2,1)}), bf16[32,2,16,3,1,128]{5,2,4,3,1,0:T(8,128)(2,1)S(1)}, u32[]{:S(2)}, u32[]{:S(2)}) %all-to-all-start) | async-done | bytes 786464 | tf_op jit(solution)/shard_map/all_to_all | solution.py:137
  69.6 1.7 %fusion.45 = f32[3,2,16,8,512]{4,3,2,1,0:T(8,128)S(1)} fusion(bf16[512,512,1,1,1]{1,0,4,3,2:T(8,128)(2,1)} %bitcast.330, bf16[8,4,2,16,3,1,128]{6,3,4,2,1,0,5:T(8,128)(2,1)S(1)} %bitcast.310), kind=kOutput, calls=%fused_computation.90 | convolution fusion | flops 402653184 | bytes 2883584 | tf_op jit(solution)/shard_map/yk,cpjxy->cpjxk/dot_general | solution.py:65
  81.4 24.1 %all_to_all.10 = bf16[32,2,16,3,1,128]{5,2,4,3,1,0:T(8,128)(2,1)S(1)} all-to-all(bf16[32,2,16,3,1,128]{5,2,4,3,1,0:T(8,128)(2,1)S(1)} %bitcast.324), channel_id=1, replica_groups=mesh['row'=8,'col'=4] {'row','col'}, dimensions={0} | all-to-all | bytes 1572864 | tf_op jit(solution)/shard_map/all_to_all | solution.py:192
  107.1 1.0 fusion.29
  108.1 1.0 convolution_add_fusion.4
  109.2 1.1 %add_convert_fusion = bf16[3,1,128,1024]{3,2,1,0:T(8,128)(2,1)} fusion(f32[3,1,128,1024]{3,2,1,0:T(8,128)S(1)} %bitcast.323, bf16[3,1,128,1024]{3,2,1,0:T(8,128)(2,1)S(1)} %copy-done.9), kind=kLoop, calls=%fused_computation.18 | loop fusion | flops 1179648 | bytes 3145728 | tf_op jit(solution)/shard_map/convert_element_type | solution.py:208
  (86 shorter events, 14.9 us)
Async XLA Ops:
  0.0 2.2 %copy-start.14 = (s32[1,128,1024]{2,1,0:T(8,128)S(1)}, s32[1,128,1024]{2,1,0:T(8,128)}, u32[]{:S(2)}) copy-start(s32[1,128,1024]{2,1,0:T(8,128)} %param.8) | copy-start | bytes 1572868
  0.0 2.2 %copy-start.15 = (f32[8]{0:T(128)S(1)}, f32[8]{0:T(128)}, u32[]{:S(2)}) copy-start(f32[8]{0:T(128)} %param.9) | copy-start | bytes 100
  31.4 1.0 copy-start.10
  31.5 1.2 %copy-start.11 = (f32[1,128,1024]{2,0,1:T(1,128)S(1)}, f32[1,128,1024]{2,0,1:T(1,128)}, u32[]{:S(2)}) copy-start(f32[1,128,1024]{2,0,1:T(1,128)} %fusion.3) | copy-start | bytes 1572868
  31.5 1.5 %copy-start.8 = (bf16[3,1,128,1024]{3,2,1,0:T(8,128)(2,1)S(1)}, bf16[3,1,128,1024]{3,2,1,0:T(8,128)(2,1)}, u32[]{:S(2)}) copy-start(bf16[3,1,128,1024]{3,2,1,0:T(8,128)(2,1)} %param.6) | copy-start | bytes 2359300
  32.6 1.9 %copy-start = (bf16[1024,32,2,16]{0,3,2,1:T(8,128)(2,1)}, bf16[1024,32,2,16]{0,3,2,1:T(8,128)(2,1)S(1)}, u32[]{:S(2)}) copy-start(bf16[1024,32,2,16]{0,3,2,1:T(8,128)(2,1)S(1)} %copy.67) | copy-start | bytes 6291460
  41.7 27.9 %all-to-all-start = ((bf16[32,2,16,3,1,128]{5,2,4,3,1,0:T(8,128)(2,1)}), bf16[32,2,16,3,1,128]{5,2,4,3,1,0:T(8,128)(2,1)S(1)}, u32[]{:S(2)}, u32[]{:S(2)}) async-start(bf16[32,2,16,3,1,128]{5,2,4,3,1,0:T(8,128)(2,1)} %copy.69), calls=%async_computation | async-start | bytes 1572864 | tf_op jit(solution)/shard_map/all_to_all | solution.py:137
  69.6 1.7 %copy-start.6 = (bf16[16,32,512]{2,1,0:T(8,128)(2,1)S(1)}, bf16[16,32,512]{2,1,0:T(8,128)(2,1)}, u32[]{:S(2)}) copy-start(bf16[16,32,512]{2,1,0:T(8,128)(2,1)} %get-tuple-element.22) | copy-start | bytes 1572868
  71.4 1.0 copy-start.7
  72.0 1.1 copy-start.5
  73.1 0.7 copy-start.12
  74.9 1.3 %copy-start.4 = (bf16[512,512]{1,0:T(8,128)(2,1)S(1)}, bf16[512,512]{1,0:T(8,128)(2,1)}, u32[]{:S(2)}) copy-start(bf16[512,512]{1,0:T(8,128)(2,1)} %get-tuple-element.16) | copy-start | bytes 1572868
  75.3 1.1 %copy-start.3 = (bf16[512,512]{1,0:T(8,128)(2,1)S(1)}, bf16[512,512]{1,0:T(8,128)(2,1)}, u32[]{:S(2)}) copy-start(bf16[512,512]{1,0:T(8,128)(2,1)} %get-tuple-element.39) | copy-start | bytes 1572868
  77.7 1.0 copy-start.2
  81.1 24.3 %copy-start.13 = (f32[32,2,16]{2,1,0:T(2,128)S(1)}, f32[32,2,16]{2,1,0:T(2,128)}, u32[]{:S(2)}) copy-start(f32[32,2,16]{2,1,0:T(2,128)} %constant.110) | copy-start | bytes 12292
  105.5 1.6 %copy-start.1 = (bf16[1024,32,2,16]{0,3,2,1:T(8,128)(2,1)S(1)}, bf16[1024,32,2,16]{0,3,2,1:T(8,128)(2,1)}, u32[]{:S(2)}) copy-start(bf16[1024,32,2,16]{0,3,2,1:T(8,128)(2,1)} %copy-done) | copy-start | bytes 6291460
  108.1 1.1 %copy-start.9 = (bf16[3,1,128,1024]{3,2,1,0:T(8,128)(2,1)S(1)}, bf16[3,1,128,1024]{3,2,1,0:T(8,128)(2,1)}, u32[]{:S(2)}) copy-start(bf16[3,1,128,1024]{3,2,1,0:T(8,128)(2,1)} %param.7) | copy-start | bytes 2359300

commit v5 on v4

--- a/solution.py
+++ b/solution.py
@@ -111,21 +111,21 @@
         cell_scale = term if cell_scale is None else cell_scale + term
     electric = displacement.astype(F32) * cell_scale[None]
 
-    cos_z, sin_z = phase_table(depth, columns, depth)
+    cos_z, sin_z = phase_table(columns, depth, depth)
     if hermitian:
         parity = (1 - 2 * (lax.iota(jnp.int32, depth) % 2)).astype(F32)
-        sin_part = jnp.concatenate([parity[:, None], -sin_z[:, 1:]], axis=1)
+        sin_part = jnp.concatenate([parity[None, :], -sin_z[1:]], axis=0)
     else:
         sin_part = -sin_z
     table_z = jnp.stack(
-        [cos_z.reshape(depth, devices, per_device), sin_part.reshape(depth, devices, per_device)],
-        axis=2,
-    ).reshape(depth, 2 * columns)
+        [cos_z.reshape(devices, per_device, depth), sin_part.reshape(devices, per_device, depth)],
+        axis=1,
+    ).reshape(2 * columns, depth)
     z_high, z_low = split_parts(table_z)
     rows = members * local_x * local_y
 
     e_high, e_low = split_parts(electric.reshape(rows, depth))
-    spec_z = "zk,rz->kr"
+    spec_z = "kz,rz->kr"
     spectrum = (
         jnp.einsum(spec_z, z_high, e_high, preferred_element_type=F32)
         + jnp.einsum(spec_z, z_high, e_low, preferred_element_type=F32)
@@ -200,7 +200,7 @@
         weight[0, :, 0] = 1.0 / depth
     weight = jnp.asarray(weight.reshape(2 * columns, 1))
     weighted = (returned.astype(F32) * weight).astype(BF16)
-    spec_back = "kr,zk->rz"
+    spec_back = "kr,kz->rz"
     field = jnp.einsum(spec_back, weighted, z_high, preferred_element_type=F32) + jnp.einsum(
         spec_back, weighted, z_low, preferred_element_type=F32
     )

time: 111 us -> 88.7 us (0.80)
  local copies, waits for them, and re-layouts: 24.7 us -> 8.71 us
  other arithmetic: 16.8 us -> 10.5 us
    sub x2 -> x0, local copies, waits for them, and re-layouts: 14.3 us -> none  [phase_table(): cosine = outer_cos * inner_cos - outer_sin * inner_sin]
    concatenate x1 -> x0, local copies, waits for them, and re-layouts: 2.89 us -> none  [on_device(): sin_part = jnp.concatenate([parity[:, None], -sin_z[:, 1:]], axis=1)]
    neg x1, other arithmetic: 2.2 us -> 0.27 us  [on_device(): sin_part = jnp.concatenate([parity[None, :], -sin_z[1:]], axis=0)]
    concatenate x1, other arithmetic: 1.97 us -> 0.23 us  [on_device(): sin_part = jnp.concatenate([parity[None, :], -sin_z[1:]], axis=0)]
    convert_element_type x3, other arithmetic: 4.27 us -> 2.6 us  [split_parts(): return (high.astype(BF16), low.astype(BF16))]
    sub x2, other arithmetic: 3.84 us -> 2.44 us  [phase_table(): cosine = outer_cos * inner_cos - outer_sin * inner_sin]
  transfers between devices with their start and end apart: 1 -> 1, of which waited for: 1 -> 1; matrix products, arithmetic and copies ran while one was open for 4% -> 5% of each run, Pallas kernels for 0% -> 0%
where the time goes in v5:
time: 88.7 us; the launch traced here: 88.1 us
  blocking collectives  24 us (27%)
  matrix products  20.4 us (23%)
  waiting for transfers between devices  16.4 us (18%)
  other arithmetic  10.5 us (12%)
  local copies, waits for them, and re-layouts  8.71 us (10%)
  starting transfers between devices  7.49 us (8%)
    all_to_all x1, blocking collectives, on_device(): lax.all_to_all(outgoing, ('row', 'col'), split_axis=0, concat_axis=0, til...  24 us
    all_to_all x1, waiting for transfers between devices, on_device(): lax.all_to_all(spectrum, ('row', 'col'), split_axis=0, concat_axis=0, til...  16.4 us
    all_to_all x1, starting transfers between devices, on_device(): lax.all_to_all(spectrum, ('row', 'col'), split_axis=0, concat_axis=0, til...  7.49 us
    dot_general x12, matrix products, mat(): term = jnp.einsum(spec, part, operand, preferred_element_type=F32)  6.74 us
    dot_general x3, matrix products, on_device(): jnp.einsum('...k,k->...', one_hot, part.astype(BF16), preferred_element_t...  4.83 us
    unnamed x32, local copies, waits for them, and re-layouts  3.6 us
    reshape x2, local copies, waits for them, and re-layouts, on_device(): spectrum.astype(BF16)  3.44 us
    convert_element_type x3, other arithmetic, split_parts(): return (high.astype(BF16), low.astype(BF16))  2.6 us
  transfers between devices with their start and end apart: 1, of which 1 were waited for; matrix products, arithmetic and copies ran while one was open for 5% of the time, Pallas kernels for 0%

profile of v5, /device:TPU:0, one launch (start us, length us, event | category | flops | bytes accessed | tf_op | source)
XLA Modules:
  0.0 88.1 jit_solution(1102814797512103673)
XLA Ops:
  0.6 1.8 %fusion.1 = f32[1,128,1024]{2,0,1:T(1,128)S(1)} fusion(s32[128,1024]{1,0:T(8,128)} %bitcast.334, f32[8]{0:T(128)} %param.9), kind=kOutput, calls=%fused_computation.5 | convolution fusion | flops 3145776 | bytes 1048608 | tf_op jit(solution)/shard_map/...k,k->.../dot_general | solution.py:108
  2.4 1.5 %fusion.2 = f32[1,128,1024]{2,0,1:T(1,128)} fusion(s32[128,1024]{1,0:T(8,128)S(1)} %bitcast.335, f32[8]{0:T(128)S(1)} %copy-done.15), kind=kOutput, calls=%fused_computation.6 | convolution fusion | flops 3145768 | bytes 1048608 | tf_op jit(solution)/shard_map/...k,k->.../dot_general | solution.py:108
  3.9 1.5 %fusion.3 = f32[1,128,1024]{2,0,1:T(1,128)} fusion(s32[128,1024]{1,0:T(8,128)S(1)} %bitcast.336, f32[8]{0:T(128)S(1)} %copy-done.15), kind=kOutput, calls=%fused_computation.7 | convolution fusion | flops 3145752 | bytes 1048608 | tf_op jit(solution)/shard_map/...k,k->.../dot_general | solution.py:108
  6.7 0.7 copy-done.10
  7.9 0.8 copy-done.8
  10.4 0.8 fusion
  11.2 1.3 %fusion.157 = f32[1024,384]{1,0:T(8,128)S(1)} fusion(bf16[1024,1024]{1,0:T(8,128)(2,1)S(1)} %bitcast.320, bf16[384,1024]{1,0:T(8,128)(2,1)S(1)} %bitcast.333), kind=kOutput, calls=%fused_computation.250 | convolution fusion | flops 805306368 | bytes 4456448 | tf_op jit(solution)/shard_map/kz,rz->kr/dot_general | solution.py:131
  12.5 1.3 %fusion.156 = f32[1024,384]{1,0:T(8,128)S(1)} fusion(bf16[1024,1024]{1,0:T(8,128)(2,1)S(1)} %bitcast.321, bf16[384,1024]{1,0:T(8,128)(2,1)S(1)} %bitcast.327), kind=kOutput, calls=%fused_computation.249 | convolution fusion | flops 805306368 | bytes 4456448 | tf_op jit(solution)/shard_map/kz,rz->kr/dot_general | solution.py:130
  13.8 2.2 %add_convert_fusion.1 = bf16[1024,384]{1,0:T(8,128)(2,1)} fusion(f32[1024,384]{1,0:T(8,128)S(1)} %fusion.156, f32[1024,384]{1,0:T(8,128)S(1)} %fusion.157, bf16[1024,1024]{1,0:T(8,128)(2,1)S(1)} %bitcast.314, bf16[384,1024]{1,0:T(8,128)(2,1)S(1)} %bitcast.328), kind=kOutput, calls=%fused_computation.20 | convolution fusion | flops 806486016 | bytes 6815744 | tf_op jit(solution)/shard_map/kz,rz->kr/dot_general | solution.py:132
  16.0 2.4 %reshape.680 = bf16[32,2,16,3,1,128]{5,3,2,1,0,4:T(4,128)(2,1)S(1)} reshape(bf16[1024,384]{1,0:T(8,128)(2,1)} %add_convert_fusion.1) | data formatting | bytes 1572864 | tf_op jit(solution)/shard_map/reshape | solution.py:134
  18.4 1.0 %copy.41 = bf16[32,2,16,3,1,128]{5,2,4,3,1,0:T(8,128)(2,1)} copy(bf16[32,2,16,3,1,128]{5,3,2,1,0,4:T(4,128)(2,1)S(1)} %reshape.680) | data formatting | bytes 1572864 | tf_op jit(solution)/shard_map/reshape | solution.py:134
  19.5 7.5 %all-to-all-start = ((bf16[32,2,16,3,1,128]{5,2,4,3,1,0:T(8,128)(2,1)}), bf16[32,2,16,3,1,128]{5,2,4,3,1,0:T(8,128)(2,1)S(1)}, u32[]{:S(2)}, u32[]{:S(2)}) async-start(bf16[32,2,16,3,1,128]{5,2,4,3,1,0:T(8,128)(2,1)} %copy.41), calls=%async_computation | async-start | bytes 1572864 | tf_op jit(solution)/shard_map/all_to_all | solution.py:137
  27.8 1.9 %multiply_subtract_fusion.1 = (f32[16,32,512]{2,1,0:T(8,128)S(1)}, bf16[16,32,512]{2,1,0:T(8,128)(2,1)}, bf16[16,32,512]{2,1,0:T(8,128)(2,1)}, bf16[16,32,512]{2...) fusion(f32[32,512]{1,0:T(8,128)S(1)} %fusion.123, f32[16,512]{1,0:T(8,128)S(1)} %get-tuple-element.32, ...), kind=kLoop, calls=%fused_computation.63 | loop fusion | flops 3670016 | bytes 4390912 | tf_op jit(solution)/shard_map/sub | solution.py:45
  29.6 1.5 %fusion.26 = (bf16[512,512]{1,0:T(8,128)(2,1)S(1)}, bf16[512,512]{1,0:T(8,128)(2,1)}, bf16[512,512]{1,0:T(8,128)(2,1)}, bf16[512,512]{1,0:T(8,128)(2,1)}) fusion(f32[16,32,512]{2,1,0:T(8,128)S(1)} %get-tuple-element.19, f32[16,32,512]{2,1,0:T(8,128)S(1)} %get-tuple-element.24), kind=kLoop, calls=%fused_computation.61 | loop fusion | flops 2097152 | bytes 4194304 | tf_op jit(solution)/shard_map/convert_element_type | solution.py:28
  31.1 16.4 %all-to-all-done = bf16[32,2,16,3,1,128]{5,2,4,3,1,0:T(8,128)(2,1)S(1)} async-done(((bf16[32,2,16,3,1,128]{5,2,4,3,1,0:T(8,128)(2,1)}), bf16[32,2,16,3,1,128]{5,2,4,3,1,0:T(8,128)(2,1)S(1)}, u32[]{:S(2)}, u32[]{:S(2)}) %all-to-all-start) | async-done | bytes 786464 | tf_op jit(solution)/shard_map/all_to_all | solution.py:137
  47.4 1.7 %fusion.45 = f32[3,2,16,8,512]{4,3,2,1,0:T(8,128)S(1)} fusion(bf16[512,512,1,1,1]{1,0,4,3,2:T(8,128)(2,1)} %bitcast.332, bf16[8,4,2,16,3,1,128]{6,3,4,2,1,0,5:T(8,128)(2,1)S(1)} %bitcast.310), kind=kOutput, calls=%fused_computation.90 | convolution fusion | flops 402653184 | bytes 2883584 | tf_op jit(solution)/shard_map/yk,cpjxy->cpjxk/dot_general | solution.py:65
  49.2 0.6 convolution_add_fusion.3
  50.2 0.6 fusion.42
  50.9 0.6 convolution_add_fusion.2
  59.2 24.0 %all_to_all.10 = bf16[32,2,16,3,1,128]{5,2,4,3,1,0:T(8,128)(2,1)S(1)} all-to-all(bf16[32,2,16,3,1,128]{5,2,4,3,1,0:T(8,128)(2,1)S(1)} %bitcast.326), channel_id=1, replica_groups=mesh['row'=8,'col'=4] {'row','col'}, dimensions={0} | all-to-all | bytes 1572864 | tf_op jit(solution)/shard_map/all_to_all | solution.py:192
  84.0 0.8 copy-done.1
  84.8 1.0 %fusion.29 = f32[384,1024]{1,0:T(8,128)S(1)} fusion(bf16[1024,1024]{1,0:T(8,128)(2,1)S(1)} %bitcast.322, bf16[128,8,3,128]{3,2,1,0:T(4,128)(2,1)S(1)} %bitcast.323), kind=kOutput, calls=%fused_computation.66 | convolution fusion | flops 805306368 | bytes 4456448 | tf_op jit(solution)/shard_map/kr,kz->rz/dot_general | solution.py:204
  85.8 1.0 %convolution_add_fusion.4 = f32[384,1024]{1,0:T(8,128)S(1)} fusion(f32[384,1024]{1,0:T(8,128)S(1)} %fusion.29, bf16[1024,1024]{1,0:T(8,128)(2,1)S(1)} %bitcast.315, bf16[128,8,3,128]{3,2,1,0:T(4,128)(2,1)S(1)} %bitcast.324), kind=kOutput, calls=%fused_computation.34 | convolution fusion | flops 805699584 | bytes 6029312 | tf_op jit(solution)/shard_map/kr,kz->rz/dot_general | solution.py:204
  87.0 1.1 %add_convert_fusion = bf16[3,1,128,1024]{3,2,1,0:T(8,128)(2,1)} fusion(f32[3,1,128,1024]{3,2,1,0:T(8,128)S(1)} %bitcast.325, bf16[3,1,128,1024]{3,2,1,0:T(8,128)(2,1)S(1)} %copy-done.9), kind=kLoop, calls=%fused_computation.18 | loop fusion | flops 1179648 | bytes 3145728 | tf_op jit(solution)/shard_map/convert_element_type | solution.py:208
  (87 shorter events, 13.4 us)
Async XLA Ops:
  0.0 2.3 %copy-start.15 = (f32[8]{0:T(128)S(1)}, f32[8]{0:T(128)}, u32[]{:S(2)}) copy-start(f32[8]{0:T(128)} %param.9) | copy-start | bytes 100
  0.0 2.3 %copy-start.14 = (s32[1,128,1024]{2,1,0:T(8,128)S(1)}, s32[1,128,1024]{2,1,0:T(8,128)}, u32[]{:S(2)}) copy-start(s32[1,128,1024]{2,1,0:T(8,128)} %param.8) | copy-start | bytes 1572868
  6.4 1.0 %copy-start.10 = (f32[1,128,1024]{2,0,1:T(1,128)S(1)}, f32[1,128,1024]{2,0,1:T(1,128)}, u32[]{:S(2)}) copy-start(f32[1,128,1024]{2,0,1:T(1,128)} %fusion.2) | copy-start | bytes 1572868
  6.4 1.2 %copy-start.11 = (f32[1,128,1024]{2,0,1:T(1,128)S(1)}, f32[1,128,1024]{2,0,1:T(1,128)}, u32[]{:S(2)}) copy-start(f32[1,128,1024]{2,0,1:T(1,128)} %fusion.3) | copy-start | bytes 1572868
  7.6 1.1 %copy-start.8 = (bf16[3,1,128,1024]{3,2,1,0:T(8,128)(2,1)S(1)}, bf16[3,1,128,1024]{3,2,1,0:T(8,128)(2,1)}, u32[]{:S(2)}) copy-start(bf16[3,1,128,1024]{3,2,1,0:T(8,128)(2,1)} %param.6) | copy-start | bytes 2359300
  11.2 1.3 %copy-start = (bf16[32,2,16,1024]{3,2,1,0:T(8,128)(2,1)}, bf16[32,2,16,1024]{3,2,1,0:T(8,128)(2,1)S(1)}, u32[]{:S(2)}) copy-start(bf16[32,2,16,1024]{3,2,1,0:T(8,128)(2,1)S(1)} %get-tuple-element.6) | copy-start | bytes 6291460
  19.5 27.9 %all-to-all-start = ((bf16[32,2,16,3,1,128]{5,2,4,3,1,0:T(8,128)(2,1)}), bf16[32,2,16,3,1,128]{5,2,4,3,1,0:T(8,128)(2,1)S(1)}, u32[]{:S(2)}, u32[]{:S(2)}) async-start(bf16[32,2,16,3,1,128]{5,2,4,3,1,0:T(8,128)(2,1)} %copy.41), calls=%async_computation | async-start | bytes 1572864 | tf_op jit(solution)/shard_map/all_to_all | solution.py:137
  47.4 1.7 %copy-start.6 = (bf16[16,32,512]{2,1,0:T(8,128)(2,1)S(1)}, bf16[16,32,512]{2,1,0:T(8,128)(2,1)}, u32[]{:S(2)}) copy-start(bf16[16,32,512]{2,1,0:T(8,128)(2,1)} %get-tuple-element.20) | copy-start | bytes 1572868
  49.1 1.0 %copy-start.7 = (bf16[16,32,512]{2,1,0:T(8,128)(2,1)S(1)}, bf16[16,32,512]{2,1,0:T(8,128)(2,1)}, u32[]{:S(2)}) copy-start(bf16[16,32,512]{2,1,0:T(8,128)(2,1)} %get-tuple-element.23) | copy-start | bytes 1572868
  49.8 1.1 %copy-start.5 = (bf16[16,32,512]{2,1,0:T(8,128)(2,1)S(1)}, bf16[16,32,512]{2,1,0:T(8,128)(2,1)}, u32[]{:S(2)}) copy-start(bf16[16,32,512]{2,1,0:T(8,128)(2,1)} %get-tuple-element.22) | copy-start | bytes 1572868
  51.5 0.7 copy-start.12
  52.9 1.3 %copy-start.4 = (bf16[512,512]{1,0:T(8,128)(2,1)S(1)}, bf16[512,512]{1,0:T(8,128)(2,1)}, u32[]{:S(2)}) copy-start(bf16[512,512]{1,0:T(8,128)(2,1)} %get-tuple-element.37) | copy-start | bytes 1572868
  53.3 1.1 %copy-start.3 = (bf16[512,512]{1,0:T(8,128)(2,1)S(1)}, bf16[512,512]{1,0:T(8,128)(2,1)}, u32[]{:S(2)}) copy-start(bf16[512,512]{1,0:T(8,128)(2,1)} %get-tuple-element.16) | copy-start | bytes 1572868
  55.7 1.0 %copy-start.2 = (bf16[512,512]{1,0:T(8,128)(2,1)S(1)}, bf16[512,512]{1,0:T(8,128)(2,1)}, u32[]{:S(2)}) copy-start(bf16[512,512]{1,0:T(8,128)(2,1)} %get-tuple-element.38) | copy-start | bytes 1572868
  58.9 24.3 %copy-start.13 = (f32[32,2,16]{2,1,0:T(2,128)S(1)}, f32[32,2,16]{2,1,0:T(2,128)}, u32[]{:S(2)}) copy-start(f32[32,2,16]{2,1,0:T(2,128)} %constant.116) | copy-start | bytes 12292
  83.2 1.6 %copy-start.1 = (bf16[32,2,16,1024]{3,2,1,0:T(8,128)(2,1)S(1)}, bf16[32,2,16,1024]{3,2,1,0:T(8,128)(2,1)}, u32[]{:S(2)}) copy-start(bf16[32,2,16,1024]{3,2,1,0:T(8,128)(2,1)} %copy-done) | copy-start | bytes 6291460
  85.8 1.1 %copy-start.9 = (bf16[3,1,128,1024]{3,2,1,0:T(8,128)(2,1)S(1)}, bf16[3,1,128,1024]{3,2,1,0:T(8,128)(2,1)}, u32[]{:S(2)}) copy-start(bf16[3,1,128,1024]{3,2,1,0:T(8,128)(2,1)} %param.7) | copy-start | bytes 2359300

commit v6 on v5

--- a/solution.py
+++ b/solution.py
@@ -131,9 +131,7 @@
         + jnp.einsum(spec_z, z_high, e_low, preferred_element_type=F32)
         + jnp.einsum(spec_z, z_low, e_high, preferred_element_type=F32)
     )
-    spectrum = spectrum.astype(BF16).reshape(
-        devices, 2, per_device, members, local_x, local_y
-    )
+    spectrum = spectrum.astype(BF16).reshape(devices, 2 * per_device, rows)
     gathered = lax.all_to_all(
         spectrum, ("row", "col"), split_axis=0, concat_axis=0, tiled=True
     )
@@ -187,7 +185,7 @@
         members, 2, per_device, row_count, local_x, col_count, local_y
     )
     outgoing = jnp.transpose(outgoing, (3, 5, 1, 2, 0, 4, 6)).reshape(
-        devices, 2, per_device, members, local_x, local_y
+        devices, 2 * per_device, rows
     )
     returned = lax.all_to_all(
         outgoing, ("row", "col"), split_axis=0, concat_axis=0, tiled=True

time: 88.7 us -> 90.5 us (1.020)
  matrix products: 20.4 us -> 22 us
    dot_general x12, matrix products: 6.74 us -> 8.31 us  [mat(): term = jnp.einsum(spec, part, operand, preferred_element_type=F32)]
    unnamed x32 -> x34, local copies, waits for them, and re-layouts: 3.6 us -> 2.66 us
where the time goes in v6:
time: 90.5 us; the launch traced here: 90 us
  blocking collectives  24.2 us (27%)
  matrix products  22 us (24%)
  waiting for transfers between devices  16.3 us (18%)
  other arithmetic  11.2 us (12%)
  local copies, waits for them, and re-layouts  8.19 us (9%)
  starting transfers between devices  7.41 us (8%)
    all_to_all x1, blocking collectives, on_device(): lax.all_to_all(outgoing, ('row', 'col'), split_axis=0, concat_axis=0, til...  24.2 us
    all_to_all x1, waiting for transfers between devices, on_device(): lax.all_to_all(spectrum, ('row', 'col'), split_axis=0, concat_axis=0, til...  16.3 us
    dot_general x12, matrix products, mat(): term = jnp.einsum(spec, part, operand, preferred_element_type=F32)  8.31 us
    all_to_all x1, starting transfers between devices, on_device(): lax.all_to_all(spectrum, ('row', 'col'), split_axis=0, concat_axis=0, til...  7.41 us
    dot_general x3, matrix products, on_device(): jnp.einsum('...k,k->...', one_hot, part.astype(BF16), preferred_element_t...  4.83 us
    convert_element_type x3, other arithmetic, split_parts(): return (high.astype(BF16), low.astype(BF16))  2.78 us
    unnamed x34, local copies, waits for them, and re-layouts  2.66 us
    reshape x1, local copies, waits for them, and re-layouts, on_device(): gathered.reshape(row_count, col_count, 2, per_device, members, local_x, l...  2.58 us
  transfers between devices with their start and end apart: 1, of which 1 were waited for; matrix products, arithmetic and copies ran while one was open for 5% of the time, Pallas kernels for 0%

profile of v6, /device:TPU:0, one launch (start us, length us, event | category | flops | bytes accessed | tf_op | source)
XLA Modules:
  0.0 90.0 jit_solution(2411567872900626901)
XLA Ops:
  0.6 1.8 %fusion.1 = f32[1,128,1024]{2,0,1:T(1,128)S(1)} fusion(s32[128,1024]{1,0:T(8,128)} %bitcast.328, f32[8]{0:T(128)} %param.9), kind=kOutput, calls=%fused_computation.5 | convolution fusion | flops 3145776 | bytes 1048608 | tf_op jit(solution)/shard_map/...k,k->.../dot_general | solution.py:108
  2.4 1.5 %fusion.2 = f32[1,128,1024]{2,0,1:T(1,128)} fusion(s32[128,1024]{1,0:T(8,128)S(1)} %bitcast.329, f32[8]{0:T(128)S(1)} %copy-done.16), kind=kOutput, calls=%fused_computation.6 | convolution fusion | flops 3145768 | bytes 1048608 | tf_op jit(solution)/shard_map/...k,k->.../dot_general | solution.py:108
  3.9 1.5 %fusion.3 = f32[1,128,1024]{2,0,1:T(1,128)} fusion(s32[128,1024]{1,0:T(8,128)S(1)} %bitcast.330, f32[8]{0:T(128)S(1)} %copy-done.16), kind=kOutput, calls=%fused_computation.7 | convolution fusion | flops 3145752 | bytes 1048608 | tf_op jit(solution)/shard_map/...k,k->.../dot_general | solution.py:108
  6.7 0.7 copy-done.11
  7.9 0.8 copy-done.9
  10.4 0.8 fusion
  11.2 1.3 %fusion.152 = f32[1024,384]{1,0:T(8,128)S(1)} fusion(bf16[1024,1024]{1,0:T(8,128)(2,1)S(1)} %bitcast.315, bf16[384,1024]{1,0:T(8,128)(2,1)S(1)} %bitcast.327), kind=kOutput, calls=%fused_computation.245 | convolution fusion | flops 805306368 | bytes 4456448 | tf_op jit(solution)/shard_map/kz,rz->kr/dot_general | solution.py:131
  12.6 1.3 %fusion.151 = f32[1024,384]{1,0:T(8,128)S(1)} fusion(bf16[1024,1024]{1,0:T(8,128)(2,1)S(1)} %bitcast.316, bf16[384,1024]{1,0:T(8,128)(2,1)S(1)} %bitcast.321), kind=kOutput, calls=%fused_computation.244 | convolution fusion | flops 805306368 | bytes 4456448 | tf_op jit(solution)/shard_map/kz,rz->kr/dot_general | solution.py:130
  13.8 2.2 %add_convert_fusion.1 = bf16[1024,384]{1,0:T(8,128)(2,1)} fusion(f32[1024,384]{1,0:T(8,128)S(1)} %fusion.151, f32[1024,384]{1,0:T(8,128)S(1)} %fusion.152, bf16[1024,1024]{1,0:T(8,128)(2,1)S(1)} %bitcast.305, bf16[384,1024]{1,0:T(8,128)(2,1)S(1)} %bitcast.322), kind=kOutput, calls=%fused_computation.20 | convolution fusion | flops 806486016 | bytes 6815744 | tf_op jit(solution)/shard_map/kz,rz->kr/dot_general | solution.py:132
  16.0 7.4 %all-to-all-start = ((bf16[32,32,384]{2,1,0:T(8,128)(2,1)}), bf16[32,32,384]{2,1,0:T(8,128)(2,1)}, u32[]{:S(2)}, u32[]{:S(2)}) async-start(bf16[32,32,384]{2,1,0:T(8,128)(2,1)} %bitcast.15), calls=%async_computation | async-start | bytes 1572864 | tf_op jit(solution)/shard_map/all_to_all | solution.py:135
  24.2 1.9 %multiply_subtract_fusion.1 = (f32[16,32,512]{2,1,0:T(8,128)S(1)}, bf16[16,32,512]{2,1,0:T(8,128)(2,1)}, bf16[16,32,512]{2,1,0:T(8,128)(2,1)}, bf16[16,32,512]{2...) fusion(f32[32,512]{1,0:T(8,128)S(1)} %fusion.118, f32[16,512]{1,0:T(8,128)S(1)} %get-tuple-element.34, ...), kind=kLoop, calls=%fused_computation.64 | loop fusion | flops 3670016 | bytes 4390912 | tf_op jit(solution)/shard_map/sub | solution.py:45
  26.1 1.6 %fusion.26 = (bf16[512,512]{1,0:T(8,128)(2,1)}, bf16[512,512]{1,0:T(8,128)(2,1)}, bf16[512,512]{1,0:T(8,128)(2,1)}, bf16[512,512]{1,0:T(8,128)(2,1)}) fusion(f32[16,32,512]{2,1,0:T(8,128)S(1)} %get-tuple-element.19, f32[16,32,512]{2,1,0:T(8,128)S(1)} %get-tuple-element.24), kind=kLoop, calls=%fused_computation.61 | loop fusion | flops 2097152 | bytes 4194304 | tf_op jit(solution)/shard_map/convert_element_type | solution.py:28
  27.7 16.3 %all-to-all-done = bf16[32,32,384]{2,1,0:T(8,128)(2,1)} async-done(((bf16[32,32,384]{2,1,0:T(8,128)(2,1)}), bf16[32,32,384]{2,1,0:T(8,128)(2,1)}, u32[]{:S(2)}, u32[]{:S(2)}) %all-to-all-start) | async-done | bytes 786464 | tf_op jit(solution)/shard_map/all_to_all | solution.py:135
  44.1 2.6 %reshape.681 = bf16[8,4,2,16,3,1,128]{6,4,3,2,1,0,5:T(4,128)(2,1)S(1)} reshape(bf16[32,32,384]{2,1,0:T(8,128)(2,1)} %all-to-all-done) | data formatting | bytes 1572864 | tf_op jit(solution)/shard_map/reshape | solution.py:138
  46.7 2.1 %fusion.42 = f32[3,2,16,8,512]{4,3,2,1,0:T(8,128)S(1)} fusion(bf16[512,512,1,1,1]{1,0,4,3,2:T(8,128)(2,1)} %bitcast.326, bf16[3,2,16,8,1,4,128]{6,0,2,1,5,3,4:T(4,128)(2,1)S(1)} %bitcast.307), kind=kOutput, calls=%fused_computation.87 | convolution fusion | flops 402653184 | bytes 2883584 | tf_op jit(solution)/shard_map/yk,cpjxy->cpjxk/dot_general | solution.py:65
  48.8 1.0 %convolution_add_fusion.3 = f32[3,2,16,8,512]{4,3,2,1,0:T(8,128)S(1)} fusion(f32[3,2,16,8,512]{4,3,2,1,0:T(8,128)S(1)} %fusion.42, bf16[512,512,1,1,1]{1,0,4,3,2:T(8,128)(2,1)S(1)} %bitcast.324, bf16[3,2,16,8,1,4,128]{6,0,2,1,5,3,4:T(4,128)(2,1)S(1)} %bitcast.308), kind=kOutput, calls=%fused_computation.33 | convolution fusion | flops 403046400 | bytes 4456448 | tf_op jit(solution)/shard_map/yk,cpjxy->cpjxk/dot_general | solution.py:65
  49.8 1.0 %fusion.39 = f32[3,2,16,8,512]{4,3,2,1,0:T(8,128)S(1)} fusion(bf16[512,512,1,1,1]{1,0,4,3,2:T(8,128)(2,1)S(1)} %bitcast.325, bf16[3,2,16,8,1,4,128]{6,0,2,1,5,3,4:T(4,128)(2,1)S(1)} %bitcast.309), kind=kOutput, calls=%fused_computation.84 | convolution fusion | flops 402653184 | bytes 2883584 | tf_op jit(solution)/shard_map/yk,cpjxy->cpjxk/dot_general | solution.py:65
  50.9 1.0 %convolution_add_fusion.2 = f32[3,2,16,8,512]{4,3,2,1,0:T(8,128)S(1)} fusion(f32[3,2,16,8,512]{4,3,2,1,0:T(8,128)S(1)} %fusion.39, bf16[512,512,1,1,1]{1,0,4,3,2:T(8,128)(2,1)S(1)} %bitcast.323, bf16[3,2,16,8,1,4,128]{6,0,2,1,5,3,4:T(4,128)(2,1)S(1)} %bitcast.310), kind=kOutput, calls=%fused_computation.32 | convolution fusion | flops 403046400 | bytes 4456448 | tf_op jit(solution)/shard_map/yk,cpjxy->cpjxk/dot_general | solution.py:65
  60.1 0.7 maximum_bitcast_fusion
  60.8 1.4 %reshape.683 = bf16[32,32,384]{2,1,0:T(8,128)(2,1)} reshape(bf16[8,4,2,16,3,1,128]{6,4,3,2,1,0,5:T(4,128)(2,1)S(1)} %maximum_bitcast_fusion) | data formatting | bytes 1572864 | tf_op jit(solution)/shard_map/reshape | solution.py:187
  62.2 24.2 %all_to_all.10 = bf16[32,32,384]{2,1,0:T(8,128)(2,1)S(1)} all-to-all(bf16[32,32,384]{2,1,0:T(8,128)(2,1)} %reshape.683), channel_id=1, replica_groups=mesh['row'=8,'col'=4] {'row','col'}, dimensions={0} | all-to-all | bytes 1572864 | tf_op jit(solution)/shard_map/all_to_all | solution.py:190
  86.7 1.0 %fusion.153 = f32[384,1024]{1,0:T(8,128)S(1)} fusion(bf16[1024,384]{1,0:T(8,128)(2,1)S(1)} %bitcast.318, bf16[1024,1024]{1,0:T(8,128)(2,1)S(1)} %bitcast.317), kind=kOutput, calls=%fused_computation.246 | convolution fusion | flops 805306368 | bytes 4456448 | tf_op jit(solution)/shard_map/kr,kz->rz/dot_general | solution.py:202
  87.7 1.0 %convolution_add_fusion.4 = f32[384,1024]{1,0:T(8,128)S(1)} fusion(f32[384,1024]{1,0:T(8,128)S(1)} %fusion.153, bf16[1024,384]{1,0:T(8,128)(2,1)S(1)} %bitcast.319, bf16[1024,1024]{1,0:T(8,128)(2,1)S(1)} %bitcast.306), kind=kOutput, calls=%fused_computation.34 | convolution fusion | flops 805699584 | bytes 6029312 | tf_op jit(solution)/shard_map/kr,kz->rz/dot_general | solution.py:202
  88.8 1.1 %add_convert_fusion = bf16[3,1,128,1024]{3,2,1,0:T(8,128)(2,1)} fusion(f32[3,1,128,1024]{3,2,1,0:T(8,128)S(1)} %bitcast.320, bf16[3,1,128,1024]{3,2,1,0:T(8,128)(2,1)S(1)} %copy-done.10), kind=kLoop, calls=%fused_computation.18 | loop fusion | flops 1179648 | bytes 3145728 | tf_op jit(solution)/shard_map/convert_element_type | solution.py:206
  (88 shorter events, 12.9 us)
Async XLA Ops:
  0.0 2.3 %copy-start.16 = (f32[8]{0:T(128)S(1)}, f32[8]{0:T(128)}, u32[]{:S(2)}) copy-start(f32[8]{0:T(128)} %param.9) | copy-start | bytes 100
  0.0 2.3 %copy-start.15 = (s32[1,128,1024]{2,1,0:T(8,128)S(1)}, s32[1,128,1024]{2,1,0:T(8,128)}, u32[]{:S(2)}) copy-start(s32[1,128,1024]{2,1,0:T(8,128)} %param.8) | copy-start | bytes 1572868
  6.4 1.0 %copy-start.11 = (f32[1,128,1024]{2,0,1:T(1,128)S(1)}, f32[1,128,1024]{2,0,1:T(1,128)}, u32[]{:S(2)}) copy-start(f32[1,128,1024]{2,0,1:T(1,128)} %fusion.2) | copy-start | bytes 1572868
  6.4 1.2 %copy-start.12 = (f32[1,128,1024]{2,0,1:T(1,128)S(1)}, f32[1,128,1024]{2,0,1:T(1,128)}, u32[]{:S(2)}) copy-start(f32[1,128,1024]{2,0,1:T(1,128)} %fusion.3) | copy-start | bytes 1572868
  7.6 1.1 %copy-start.9 = (bf16[3,1,128,1024]{3,2,1,0:T(8,128)(2,1)S(1)}, bf16[3,1,128,1024]{3,2,1,0:T(8,128)(2,1)}, u32[]{:S(2)}) copy-start(bf16[3,1,128,1024]{3,2,1,0:T(8,128)(2,1)} %param.6) | copy-start | bytes 2359300
  11.2 1.4 %copy-start = (bf16[32,2,16,1024]{3,2,1,0:T(8,128)(2,1)}, bf16[32,2,16,1024]{3,2,1,0:T(8,128)(2,1)S(1)}, u32[]{:S(2)}) copy-start(bf16[32,2,16,1024]{3,2,1,0:T(8,128)(2,1)S(1)} %get-tuple-element.6) | copy-start | bytes 6291460
  16.0 28.0 %all-to-all-start = ((bf16[32,32,384]{2,1,0:T(8,128)(2,1)}), bf16[32,32,384]{2,1,0:T(8,128)(2,1)}, u32[]{:S(2)}, u32[]{:S(2)}) async-start(bf16[32,32,384]{2,1,0:T(8,128)(2,1)} %bitcast.15), calls=%async_computation | async-start | bytes 1572864 | tf_op jit(solution)/shard_map/all_to_all | solution.py:135
  46.7 2.1 %copy-start.7 = (bf16[16,32,512]{2,1,0:T(8,128)(2,1)S(1)}, bf16[16,32,512]{2,1,0:T(8,128)(2,1)}, u32[]{:S(2)}) copy-start(bf16[16,32,512]{2,1,0:T(8,128)(2,1)} %get-tuple-element.20) | copy-start | bytes 1572868
  48.8 1.1 %copy-start.8 = (bf16[16,32,512]{2,1,0:T(8,128)(2,1)S(1)}, bf16[16,32,512]{2,1,0:T(8,128)(2,1)}, u32[]{:S(2)}) copy-start(bf16[16,32,512]{2,1,0:T(8,128)(2,1)} %get-tuple-element.23) | copy-start | bytes 1572868
  49.8 1.0 %copy-start.6 = (bf16[16,32,512]{2,1,0:T(8,128)(2,1)S(1)}, bf16[16,32,512]{2,1,0:T(8,128)(2,1)}, u32[]{:S(2)}) copy-start(bf16[16,32,512]{2,1,0:T(8,128)(2,1)} %get-tuple-element.22) | copy-start | bytes 1572868
  51.9 0.7 copy-start.13
  53.3 1.3 %copy-start.5 = (bf16[512,512]{1,0:T(8,128)(2,1)S(1)}, bf16[512,512]{1,0:T(8,128)(2,1)}, u32[]{:S(2)}) copy-start(bf16[512,512]{1,0:T(8,128)(2,1)} %get-tuple-element.35) | copy-start | bytes 1572868
  53.7 1.1 %copy-start.4 = (bf16[512,512]{1,0:T(8,128)(2,1)S(1)}, bf16[512,512]{1,0:T(8,128)(2,1)}, u32[]{:S(2)}) copy-start(bf16[512,512]{1,0:T(8,128)(2,1)} %get-tuple-element.16) | copy-start | bytes 1572868
  56.1 1.0 %copy-start.2 = (bf16[512,512]{1,0:T(8,128)(2,1)S(1)}, bf16[512,512]{1,0:T(8,128)(2,1)}, u32[]{:S(2)}) copy-start(bf16[512,512]{1,0:T(8,128)(2,1)} %get-tuple-element.15) | copy-start | bytes 1572868
  56.1 1.3 %copy-start.3 = (bf16[512,512]{1,0:T(8,128)(2,1)S(1)}, bf16[512,512]{1,0:T(8,128)(2,1)}, u32[]{:S(2)}) copy-start(bf16[512,512]{1,0:T(8,128)(2,1)} %get-tuple-element.36) | copy-start | bytes 1572868
  60.7 25.7 %copy-start.14 = (f32[32,32]{1,0:T(8,128)S(1)}, f32[32,32]{1,0:T(8,128)}, u32[]{:S(2)}) copy-start(f32[32,32]{1,0:T(8,128)} %constant.116) | copy-start | bytes 12292
  62.2 24.5 %copy-start.1 = (bf16[32,2,16,1024]{3,2,1,0:T(8,128)(2,1)S(1)}, bf16[32,2,16,1024]{3,2,1,0:T(8,128)(2,1)}, u32[]{:S(2)}) copy-start(bf16[32,2,16,1024]{3,2,1,0:T(8,128)(2,1)} %copy-done) | copy-start | bytes 6291460
  87.7 1.1 %copy-start.10 = (bf16[3,1,128,1024]{3,2,1,0:T(8,128)(2,1)S(1)}, bf16[3,1,128,1024]{3,2,1,0:T(8,128)(2,1)}, u32[]{:S(2)}) copy-start(bf16[3,1,128,1024]{3,2,1,0:T(8,128)(2,1)} %param.7) | copy-start | bytes 2359300

commit v7 on v5

--- a/solution.py
+++ b/solution.py
@@ -4,6 +4,8 @@
 import jax
 import jax.numpy as jnp
 from jax import lax
+from jax.experimental import pallas as pl
+from jax.experimental.pallas import tpu as pltpu
 from jax.sharding import PartitionSpec as P
 
 TIME_STEP = 0.5
@@ -47,6 +49,41 @@
     return cosine.reshape(rows, cols), sine.reshape(rows, cols)
 
 
+def electric_kernel(reciprocal_ref, region_ref, displacement_ref, high_ref, low_ref):
+    region = region_ref[...]
+    scale = jnp.zeros(region.shape, F32)
+    for region_id in range(reciprocal_ref.shape[0]):
+        scale = jnp.where(region == region_id, reciprocal_ref[region_id], scale)
+    for member in range(displacement_ref.shape[0]):
+        field = displacement_ref[member].astype(F32) * scale
+        high = field.astype(BF16)
+        high_ref[member] = high
+        low_ref[member] = (field - high.astype(F32)).astype(BF16)
+
+
+def electric_parts(displacement, region, reciprocal):
+    members, local_x, local_y, depth = displacement.shape
+    lines = local_x * local_y
+    block = 32 if lines % 32 == 0 else lines
+    field_spec = pl.BlockSpec((members, block, depth), lambda index: (0, index, 0))
+    shape = jax.ShapeDtypeStruct((members, lines, depth), BF16)
+    elements = members * lines * depth
+    return pl.pallas_call(
+        electric_kernel,
+        grid=(lines // block,),
+        in_specs=[
+            pl.BlockSpec(memory_space=pltpu.SMEM),
+            pl.BlockSpec((block, depth), lambda index: (index, 0)),
+            field_spec,
+        ],
+        out_specs=[field_spec, field_spec],
+        out_shape=[shape, shape],
+        cost_estimate=pl.CostEstimate(
+            flops=20 * elements, transcendentals=0, bytes_accessed=6 * elements + 4 * lines * depth
+        ),
+    )(reciprocal, region.reshape(lines, depth), displacement.reshape(members, lines, depth))
+
+
 def x_kernel(span_x):
     index = np.arange(span_x)
     signed = np.where(2 * index < span_x, index, index - span_x)
@@ -97,19 +134,6 @@
     me = lax.axis_index("row") * col_count + lax.axis_index("col")
 
     reciprocal = 1.0 / permittivity
-    regions = permittivity.shape[0]
-    one_hot = (region[..., None] == lax.iota(jnp.int32, regions)).astype(BF16)
-    first = rounded(reciprocal)
-    rest = reciprocal - first
-    second = rounded(rest)
-    parts = (first, second, rest - second)
-    cell_scale = None
-    for part in parts:
-        term = jnp.einsum(
-            "...k,k->...", one_hot, part.astype(BF16), preferred_element_type=F32
-        )
-        cell_scale = term if cell_scale is None else cell_scale + term
-    electric = displacement.astype(F32) * cell_scale[None]
 
     cos_z, sin_z = phase_table(columns, depth, depth)
     if hermitian:
@@ -124,7 +148,9 @@
     z_high, z_low = split_parts(table_z)
     rows = members * local_x * local_y
 
-    e_high, e_low = split_parts(electric.reshape(rows, depth))
+    e_high, e_low = electric_parts(displacement, region, reciprocal)
+    e_high = e_high.reshape(rows, depth)
+    e_low = e_low.reshape(rows, depth)
     spec_z = "kz,rz->kr"
     spectrum = (
         jnp.einsum(spec_z, z_high, e_high, preferred_element_type=F32)

time: 88.7 us -> 89.8 us (1.012)
  Pallas kernels: 0 us -> 3.81 us
  matrix products: 20.4 us -> 17.5 us
  other arithmetic: 10.5 us -> 12.6 us
  local copies, waits for them, and re-layouts: 8.71 us -> 6.91 us
    dot_general x3 -> x0, matrix products: 4.83 us -> none  [on_device(): jnp.einsum('...k,k->...', one_hot, part.astype(BF16), preferred_element_t...]
    pallas_call x0 -> x1, Pallas kernels: none -> 3.81 us  [electric_parts(): pl.pallas_call(electric_kernel, grid=(lines // block,), in_specs=[pl.Bloc...]
    dot_general x1, matrix products: 1.27 us -> 3.18 us  [on_device(): jnp.einsum(spec_z, z_high, e_low, preferred_element_type=F32)]
    unnamed x32 -> x24, local copies, waits for them, and re-layouts: 3.6 us -> 1.8 us
    div x0 -> x1, other arithmetic: none -> 1.24 us  [on_device(): reciprocal = 1.0 / permittivity]
    convert_element_type x3 -> x2, other arithmetic: 2.6 us -> 3.72 us  [split_parts(): return (high.astype(BF16), low.astype(BF16))]
where the time goes in v7:
time: 89.8 us; the launch traced here: 89.2 us
  blocking collectives  24 us (27%)
  matrix products  17.5 us (19%)
  waiting for transfers between devices  16.4 us (18%)
  other arithmetic  12.6 us (14%)
  starting transfers between devices  7.48 us (8%)
  local copies, waits for them, and re-layouts  6.91 us (8%)
  Pallas kernels  3.81 us (4%)
    all_to_all x1, blocking collectives, on_device(): lax.all_to_all(outgoing, ('row', 'col'), split_axis=0, concat_axis=0, til...  24 us
    all_to_all x1, waiting for transfers between devices, on_device(): lax.all_to_all(spectrum, ('row', 'col'), split_axis=0, concat_axis=0, til...  16.4 us
    all_to_all x1, starting transfers between devices, on_device(): lax.all_to_all(spectrum, ('row', 'col'), split_axis=0, concat_axis=0, til...  7.48 us
    dot_general x12, matrix products, mat(): term = jnp.einsum(spec, part, operand, preferred_element_type=F32)  6.74 us
    pallas_call x1, Pallas kernels, electric_parts(): pl.pallas_call(electric_kernel, grid=(lines // block,), in_specs=[pl.Bloc...  3.81 us
    convert_element_type x2, other arithmetic, split_parts(): return (high.astype(BF16), low.astype(BF16))  3.72 us
    reshape x2, local copies, waits for them, and re-layouts, on_device(): spectrum.astype(BF16)  3.44 us
    dot_general x1, matrix products, on_device(): jnp.einsum(spec_z, z_high, e_low, preferred_element_type=F32)  3.18 us
  transfers between devices with their start and end apart: 1, of which 1 were waited for; matrix products, arithmetic and copies ran while one was open for 5% of the time, Pallas kernels for 0%

profile of v7, /device:TPU:0, one launch (start us, length us, event | category | flops | bytes accessed | tf_op | source)
XLA Modules:
  0.0 89.2 jit_solution(13491845439391288202)
XLA Ops:
  0.5 1.2 %broadcast_divide_fusion.reciprocal_ref = f32[8]{0:T(128)} fusion(f32[8]{0:T(128)} %param.9), kind=kLoop, calls=%fused_computation.225 | loop fusion | flops 8 | bytes 64 | tf_op jit(solution)/shard_map/div | solution.py:136
  3.8 0.6 multiply_subtract_fusion
  4.4 2.3 %fusion = (bf16[32,2,16,1024]{3,2,1,0:T(8,128)(2,1)S(1)}, bf16[32,2,16,1024]{3,2,1,0:T(8,128)(2,1)}) fusion(f32[32,1,16,1024]{3,2,1,0:T(8,128)S(1)} %bitcast.302, f32[32,1,16,1024]{3,2,1,0:T(8,128)S(1)} %multiply_subtract_fusion), kind=kLoop, calls=%fused_computation.2 | loop fusion | flops 5242880 | bytes 8388608 | tf_op jit(solution)/shard_map/convert_element_type | solution.py:30
  6.6 3.8 %shard_map.64 = (bf16[3,128,1024]{2,1,0:T(8,128)(2,1)}, bf16[3,128,1024]{2,1,0:T(8,128)(2,1)}) custom-call(f32[8]{0:T(128)} %broadcast_divide_fusion.reciprocal_ref, s32[128,1024]{1,0:T(8,128)} %bitcast.318, bf16[3,128,1024]{2,1,0:T(8,128)(2,1)} %bitcast.315), custom_call_target="tpu_custom_call" | custom-call | flops 7864320 | bytes 2883584 | tf_op jit(solution)/shard_map/pallas_call | solution.py:71
  10.5 3.2 %fusion.143 = f32[1024,384]{1,0:T(8,128)S(1)} fusion(bf16[1024,1024]{1,0:T(8,128)(2,1)} %bitcast.304, bf16[384,1024]{1,0:T(8,128)(2,1)} %bitcast.319), kind=kOutput, calls=%fused_computation.229 | convolution fusion | flops 805306368 | bytes 4456448 | tf_op jit(solution)/shard_map/kz,rz->kr/dot_general | solution.py:157
  13.7 1.3 %fusion.142 = f32[1024,384]{1,0:T(8,128)S(1)} fusion(bf16[1024,1024]{1,0:T(8,128)(2,1)S(1)} %bitcast.305, bf16[384,1024]{1,0:T(8,128)(2,1)S(1)} %bitcast.316), kind=kOutput, calls=%fused_computation.228 | convolution fusion | flops 805306368 | bytes 4456448 | tf_op jit(solution)/shard_map/kz,rz->kr/dot_general | solution.py:156
  15.0 2.2 %add_convert_fusion.1 = bf16[1024,384]{1,0:T(8,128)(2,1)} fusion(f32[1024,384]{1,0:T(8,128)S(1)} %fusion.142, f32[1024,384]{1,0:T(8,128)S(1)} %fusion.143, bf16[1024,1024]{1,0:T(8,128)(2,1)S(1)} %bitcast.298, bf16[384,1024]{1,0:T(8,128)(2,1)S(1)} %bitcast.317), kind=kOutput, calls=%fused_computation.10 | convolution fusion | flops 806486016 | bytes 6815744 | tf_op jit(solution)/shard_map/kz,rz->kr/dot_general | solution.py:158
  17.2 2.4 %reshape.675 = bf16[32,2,16,3,1,128]{5,3,2,1,0,4:T(4,128)(2,1)S(1)} reshape(bf16[1024,384]{1,0:T(8,128)(2,1)} %add_convert_fusion.1) | data formatting | bytes 1572864 | tf_op jit(solution)/shard_map/reshape | solution.py:160
  19.6 1.0 %copy.28 = bf16[32,2,16,3,1,128]{5,2,4,3,1,0:T(8,128)(2,1)} copy(bf16[32,2,16,3,1,128]{5,3,2,1,0,4:T(4,128)(2,1)S(1)} %reshape.675) | data formatting | bytes 1572864 | tf_op jit(solution)/shard_map/reshape | solution.py:160
  20.6 7.5 %all-to-all-start = ((bf16[32,2,16,3,1,128]{5,2,4,3,1,0:T(8,128)(2,1)}), bf16[32,2,16,3,1,128]{5,2,4,3,1,0:T(8,128)(2,1)S(1)}, u32[]{:S(2)}, u32[]{:S(2)}) async-start(bf16[32,2,16,3,1,128]{5,2,4,3,1,0:T(8,128)(2,1)} %copy.28), calls=%async_computation | async-start | bytes 1572864 | tf_op jit(solution)/shard_map/all_to_all | solution.py:163
  28.9 1.8 %multiply_subtract_fusion.1 = (f32[16,32,512]{2,1,0:T(8,128)S(1)}, bf16[16,32,512]{2,1,0:T(8,128)(2,1)}, bf16[16,32,512]{2,1,0:T(8,128)(2,1)}, bf16[16,32,512]{2...) fusion(f32[32,512]{1,0:T(8,128)S(1)} %fusion.116, f32[16,512]{1,0:T(8,128)S(1)} %get-tuple-element.34, ...), kind=kLoop, calls=%fused_computation.52 | loop fusion | flops 3670016 | bytes 4390912 | tf_op jit(solution)/shard_map/sub | solution.py:47
  30.7 1.4 %fusion.19 = (bf16[512,512]{1,0:T(8,128)(2,1)S(1)}, bf16[512,512]{1,0:T(8,128)(2,1)}, bf16[512,512]{1,0:T(8,128)(2,1)}, bf16[512,512]{1,0:T(8,128)(2,1)}) fusion(f32[16,32,512]{2,1,0:T(8,128)S(1)} %get-tuple-element.21, f32[16,32,512]{2,1,0:T(8,128)S(1)} %get-tuple-element.26), kind=kLoop, calls=%fused_computation.50 | loop fusion | flops 2097152 | bytes 4194304 | tf_op jit(solution)/shard_map/convert_element_type | solution.py:30
  32.2 16.4 %all-to-all-done = bf16[32,2,16,3,1,128]{5,2,4,3,1,0:T(8,128)(2,1)S(1)} async-done(((bf16[32,2,16,3,1,128]{5,2,4,3,1,0:T(8,128)(2,1)}), bf16[32,2,16,3,1,128]{5,2,4,3,1,0:T(8,128)(2,1)S(1)}, u32[]{:S(2)}, u32[]{:S(2)}) %all-to-all-start) | async-done | bytes 786464 | tf_op jit(solution)/shard_map/all_to_all | solution.py:163
  48.5 1.7 %fusion.38 = f32[3,2,16,8,512]{4,3,2,1,0:T(8,128)S(1)} fusion(bf16[512,512,1,1,1]{1,0,4,3,2:T(8,128)(2,1)} %bitcast.314, bf16[8,4,2,16,3,1,128]{6,3,4,2,1,0,5:T(8,128)(2,1)S(1)} %bitcast.294), kind=kOutput, calls=%fused_computation.79 | convolution fusion | flops 402653184 | bytes 2883584 | tf_op jit(solution)/shard_map/yk,cpjxy->cpjxk/dot_general | solution.py:102
  50.3 0.6 convolution_add_fusion.3
  51.3 0.6 fusion.35
  52.0 0.6 convolution_add_fusion.2
  58.1 0.6 convolution_add_fusion
  58.7 0.6 convolution_add_fusion.1
  60.3 24.0 %all_to_all.10 = bf16[32,2,16,3,1,128]{5,2,4,3,1,0:T(8,128)(2,1)S(1)} all-to-all(bf16[32,2,16,3,1,128]{5,2,4,3,1,0:T(8,128)(2,1)S(1)} %bitcast.310), channel_id=1, replica_groups=mesh['row'=8,'col'=4] {'row','col'}, dimensions={0} | all-to-all | bytes 1572864 | tf_op jit(solution)/shard_map/all_to_all | solution.py:218
  85.1 0.8 copy-done.1
  85.9 1.0 %fusion.22 = f32[384,1024]{1,0:T(8,128)S(1)} fusion(bf16[1024,1024]{1,0:T(8,128)(2,1)S(1)} %bitcast.306, bf16[128,8,3,128]{3,2,1,0:T(4,128)(2,1)S(1)} %bitcast.307), kind=kOutput, calls=%fused_computation.55 | convolution fusion | flops 805306368 | bytes 4456448 | tf_op jit(solution)/shard_map/kr,kz->rz/dot_general | solution.py:230
  87.0 1.0 %convolution_add_fusion.4 = f32[384,1024]{1,0:T(8,128)S(1)} fusion(f32[384,1024]{1,0:T(8,128)S(1)} %fusion.22, bf16[1024,1024]{1,0:T(8,128)(2,1)S(1)} %bitcast.299, bf16[128,8,3,128]{3,2,1,0:T(4,128)(2,1)S(1)} %bitcast.308), kind=kOutput, calls=%fused_computation.23 | convolution fusion | flops 805699584 | bytes 6029312 | tf_op jit(solution)/shard_map/kr,kz->rz/dot_general | solution.py:230
  88.1 1.1 %add_convert_fusion = bf16[3,1,128,1024]{3,2,1,0:T(8,128)(2,1)} fusion(f32[3,1,128,1024]{3,2,1,0:T(8,128)S(1)} %bitcast.309, bf16[3,1,128,1024]{3,2,1,0:T(8,128)(2,1)S(1)} %copy-done.8), kind=kLoop, calls=%fused_computation.8 | loop fusion | flops 1179648 | bytes 3145728 | tf_op jit(solution)/shard_map/convert_element_type | solution.py:234
  (76 shorter events, 10.8 us)
Async XLA Ops:
  10.5 3.2 %copy-start = (bf16[32,2,16,1024]{3,2,1,0:T(8,128)(2,1)S(1)}, bf16[32,2,16,1024]{3,2,1,0:T(8,128)(2,1)}, u32[]{:S(2)}) copy-start(bf16[32,2,16,1024]{3,2,1,0:T(8,128)(2,1)} %get-tuple-element.10) | copy-start | bytes 6291460
  10.5 3.2 %copy-start.9 = (bf16[3,128,1024]{2,1,0:T(8,128)(2,1)S(1)}, bf16[3,128,1024]{2,1,0:T(8,128)(2,1)}, u32[]{:S(2)}) copy-start(bf16[3,128,1024]{2,1,0:T(8,128)(2,1)} %get-tuple-element.7) | copy-start | bytes 2359300
  20.6 27.9 %all-to-all-start = ((bf16[32,2,16,3,1,128]{5,2,4,3,1,0:T(8,128)(2,1)}), bf16[32,2,16,3,1,128]{5,2,4,3,1,0:T(8,128)(2,1)S(1)}, u32[]{:S(2)}, u32[]{:S(2)}) async-start(bf16[32,2,16,3,1,128]{5,2,4,3,1,0:T(8,128)(2,1)} %copy.28), calls=%async_computation | async-start | bytes 1572864 | tf_op jit(solution)/shard_map/all_to_all | solution.py:163
  48.5 1.7 %copy-start.6 = (bf16[16,32,512]{2,1,0:T(8,128)(2,1)S(1)}, bf16[16,32,512]{2,1,0:T(8,128)(2,1)}, u32[]{:S(2)}) copy-start(bf16[16,32,512]{2,1,0:T(8,128)(2,1)} %get-tuple-element.22) | copy-start | bytes 1572868
  50.3 1.0 %copy-start.7 = (bf16[16,32,512]{2,1,0:T(8,128)(2,1)S(1)}, bf16[16,32,512]{2,1,0:T(8,128)(2,1)}, u32[]{:S(2)}) copy-start(bf16[16,32,512]{2,1,0:T(8,128)(2,1)} %get-tuple-element.25) | copy-start | bytes 1572868
  50.9 1.1 %copy-start.5 = (bf16[16,32,512]{2,1,0:T(8,128)(2,1)S(1)}, bf16[16,32,512]{2,1,0:T(8,128)(2,1)}, u32[]{:S(2)}) copy-start(bf16[16,32,512]{2,1,0:T(8,128)(2,1)} %get-tuple-element.24) | copy-start | bytes 1572868
  52.6 0.7 copy-start.10
  54.0 1.3 %copy-start.4 = (bf16[512,512]{1,0:T(8,128)(2,1)S(1)}, bf16[512,512]{1,0:T(8,128)(2,1)}, u32[]{:S(2)}) copy-start(bf16[512,512]{1,0:T(8,128)(2,1)} %get-tuple-element.39) | copy-start | bytes 1572868
  54.4 1.1 %copy-start.3 = (bf16[512,512]{1,0:T(8,128)(2,1)S(1)}, bf16[512,512]{1,0:T(8,128)(2,1)}, u32[]{:S(2)}) copy-start(bf16[512,512]{1,0:T(8,128)(2,1)} %get-tuple-element.18) | copy-start | bytes 1572868
  56.8 1.0 %copy-start.2 = (bf16[512,512]{1,0:T(8,128)(2,1)S(1)}, bf16[512,512]{1,0:T(8,128)(2,1)}, u32[]{:S(2)}) copy-start(bf16[512,512]{1,0:T(8,128)(2,1)} %get-tuple-element.40) | copy-start | bytes 1572868
  60.0 24.3 %copy-start.11 = (f32[32,2,16]{2,1,0:T(2,128)S(1)}, f32[32,2,16]{2,1,0:T(2,128)}, u32[]{:S(2)}) copy-start(f32[32,2,16]{2,1,0:T(2,128)} %constant.116) | copy-start | bytes 12292
  84.3 1.6 %copy-start.1 = (bf16[32,2,16,1024]{3,2,1,0:T(8,128)(2,1)S(1)}, bf16[32,2,16,1024]{3,2,1,0:T(8,128)(2,1)}, u32[]{:S(2)}) copy-start(bf16[32,2,16,1024]{3,2,1,0:T(8,128)(2,1)} %get-tuple-element.10) | copy-start | bytes 6291460
  86.9 1.1 %copy-start.8 = (bf16[3,1,128,1024]{3,2,1,0:T(8,128)(2,1)S(1)}, bf16[3,1,128,1024]{3,2,1,0:T(8,128)(2,1)}, u32[]{:S(2)}) copy-start(bf16[3,1,128,1024]{3,2,1,0:T(8,128)(2,1)} %param.7) | copy-start | bytes 2359300

commit v8 on v5

--- a/solution.py
+++ b/solution.py
@@ -124,12 +124,8 @@
     z_high, z_low = split_parts(table_z)
     rows = members * local_x * local_y
 
-    e_high, e_low = split_parts(electric.reshape(rows, depth))
-    spec_z = "kz,rz->kr"
-    spectrum = (
-        jnp.einsum(spec_z, z_high, e_high, preferred_element_type=F32)
-        + jnp.einsum(spec_z, z_high, e_low, preferred_element_type=F32)
-        + jnp.einsum(spec_z, z_low, e_high, preferred_element_type=F32)
+    spectrum = jnp.einsum(
+        "kz,rz->kr", table_z, electric.reshape(rows, depth), precision=lax.Precision.HIGH
     )
     spectrum = spectrum.astype(BF16).reshape(
         devices, 2, per_device, members, local_x, local_y

time: 88.7 us -> 89.3 us (level)
  other arithmetic: 10.5 us -> 12.4 us
  local copies, waits for them, and re-layouts: 8.71 us -> 7.78 us
    convert_element_type x3 -> x2, other arithmetic: 2.6 us -> 4.3 us  [split_parts(): return (high.astype(BF16), low.astype(BF16))]
    unnamed x32 -> x30, local copies, waits for them, and re-layouts: 3.6 us -> 2.67 us
    dot_general x3 -> x1, matrix products: 4.75 us -> 4.37 us  [on_device(): jnp.einsum('kz,rz->kr', table_z, electric.reshape(rows, depth), precision...]
where the time goes in v8:
time: 89.3 us; the launch traced here: 88.7 us
  blocking collectives  24.1 us (27%)
  matrix products  20.1 us (23%)
  waiting for transfers between devices  16.4 us (18%)
  other arithmetic  12.4 us (14%)
  local copies, waits for them, and re-layouts  7.78 us (9%)
  starting transfers between devices  7.48 us (8%)
    all_to_all x1, blocking collectives, on_device(): lax.all_to_all(outgoing, ('row', 'col'), split_axis=0, concat_axis=0, til...  24.1 us
    all_to_all x1, waiting for transfers between devices, on_device(): lax.all_to_all(spectrum, ('row', 'col'), split_axis=0, concat_axis=0, til...  16.4 us
    all_to_all x1, starting transfers between devices, on_device(): lax.all_to_all(spectrum, ('row', 'col'), split_axis=0, concat_axis=0, til...  7.48 us
    dot_general x12, matrix products, mat(): term = jnp.einsum(spec, part, operand, preferred_element_type=F32)  6.74 us
    dot_general x3, matrix products, on_device(): jnp.einsum('...k,k->...', one_hot, part.astype(BF16), preferred_element_t...  4.83 us
    dot_general x1, matrix products, on_device(): jnp.einsum('kz,rz->kr', table_z, electric.reshape(rows, depth), precision...  4.37 us
    convert_element_type x2, other arithmetic, split_parts(): return (high.astype(BF16), low.astype(BF16))  4.3 us
    reshape x2, local copies, waits for them, and re-layouts, on_device(): spectrum.astype(BF16)  3.44 us
  transfers between devices with their start and end apart: 1, of which 1 were waited for; matrix products, arithmetic and copies ran while one was open for 5% of the time, Pallas kernels for 0%

profile of v8, /device:TPU:0, one launch (start us, length us, event | category | flops | bytes accessed | tf_op | source)
XLA Modules:
  0.0 88.7 jit_solution(3836274058130425659)
XLA Ops:
  0.6 1.8 %fusion.1 = f32[1,128,1024]{2,0,1:T(1,128)S(1)} fusion(s32[128,1024]{1,0:T(8,128)} %bitcast.326, f32[8]{0:T(128)} %param.9), kind=kOutput, calls=%fused_computation.5 | convolution fusion | flops 3145776 | bytes 1048608 | tf_op jit(solution)/shard_map/...k,k->.../dot_general | solution.py:108
  2.4 1.5 %fusion.2 = f32[1,128,1024]{2,0,1:T(1,128)} fusion(s32[128,1024]{1,0:T(8,128)S(1)} %bitcast.327, f32[8]{0:T(128)S(1)} %copy-done.14), kind=kOutput, calls=%fused_computation.6 | convolution fusion | flops 3145768 | bytes 1048608 | tf_op jit(solution)/shard_map/...k,k->.../dot_general | solution.py:108
  3.9 1.5 %fusion.3 = f32[1,128,1024]{2,0,1:T(1,128)} fusion(s32[128,1024]{1,0:T(8,128)S(1)} %bitcast.328, f32[8]{0:T(128)S(1)} %copy-done.14), kind=kOutput, calls=%fused_computation.7 | convolution fusion | flops 3145752 | bytes 1048608 | tf_op jit(solution)/shard_map/...k,k->.../dot_general | solution.py:108
  7.4 0.6 multiply_subtract_fusion
  8.0 2.8 %fusion = (bf16[32,2,16,1024]{3,2,1,0:T(8,128)(2,1)S(1)}, bf16[32,2,16,1024]{3,2,1,0:T(8,128)(2,1)}, f32[32,2,16,1024]{3,2,1,0:T(8,128)S(1)}) fusion(f32[32,1,16,1024]{3,2,1,0:T(8,128)S(1)} %bitcast.314, f32[32,1,16,1024]{3,2,1,0:T(8,128)S(1)} %multiply_subtract_fusion), kind=kLoop, calls=%fused_computation.2 | loop fusion | flops 5242880 | bytes 12582912 | tf_op jit(solution)/shard_map/convert_element_type | solution.py:28
  11.2 0.8 copy-done.7
  12.2 4.4 %convolution_convert_fusion = bf16[1024,384]{1,0:T(8,128)(2,1)} fusion(f32[1024,1024]{1,0:T(8,128)S(1)} %bitcast.310, f32[384,1024]{1,0:T(8,128)S(1)} %bitcast.320), kind=kOutput, calls=%fused_computation.31 | convolution fusion | flops 2416312320 | bytes 6553600 | tf_op jit(solution)/shard_map/kz,rz->kr/dot_general | solution.py:127
  16.6 2.4 %reshape.671 = bf16[32,2,16,3,1,128]{5,3,2,1,0,4:T(4,128)(2,1)S(1)} reshape(bf16[1024,384]{1,0:T(8,128)(2,1)} %convolution_convert_fusion) | data formatting | bytes 1572864 | tf_op jit(solution)/shard_map/reshape | solution.py:130
  19.0 1.0 %copy.41 = bf16[32,2,16,3,1,128]{5,2,4,3,1,0:T(8,128)(2,1)} copy(bf16[32,2,16,3,1,128]{5,3,2,1,0,4:T(4,128)(2,1)S(1)} %reshape.671) | data formatting | bytes 1572864 | tf_op jit(solution)/shard_map/reshape | solution.py:130
  20.1 7.5 %all-to-all-start = ((bf16[32,2,16,3,1,128]{5,2,4,3,1,0:T(8,128)(2,1)}), bf16[32,2,16,3,1,128]{5,2,4,3,1,0:T(8,128)(2,1)S(1)}, u32[]{:S(2)}, u32[]{:S(2)}) async-start(bf16[32,2,16,3,1,128]{5,2,4,3,1,0:T(8,128)(2,1)} %copy.41), calls=%async_computation | async-start | bytes 1572864 | tf_op jit(solution)/shard_map/all_to_all | solution.py:133
  28.3 1.8 %multiply_subtract_fusion.1 = (f32[16,32,512]{2,1,0:T(8,128)S(1)}, bf16[16,32,512]{2,1,0:T(8,128)(2,1)}, bf16[16,32,512]{2,1,0:T(8,128)(2,1)}, bf16[16,32,512]{2...) fusion(f32[32,512]{1,0:T(8,128)S(1)} %fusion.122, f32[16,512]{1,0:T(8,128)S(1)} %get-tuple-element.31, ...), kind=kLoop, calls=%fused_computation.60 | loop fusion | flops 3670016 | bytes 4390912 | tf_op jit(solution)/shard_map/sub | solution.py:45
  30.2 1.5 %fusion.25 = (bf16[512,512]{1,0:T(8,128)(2,1)}, bf16[512,512]{1,0:T(8,128)(2,1)}, bf16[512,512]{1,0:T(8,128)(2,1)}, bf16[512,512]{1,0:T(8,128)(2,1)S(1)}) fusion(f32[16,32,512]{2,1,0:T(8,128)S(1)} %get-tuple-element.18, f32[16,32,512]{2,1,0:T(8,128)S(1)} %get-tuple-element.23), kind=kLoop, calls=%fused_computation.58 | loop fusion | flops 2097152 | bytes 4194304 | tf_op jit(solution)/shard_map/convert_element_type | solution.py:28
  31.6 16.4 %all-to-all-done = bf16[32,2,16,3,1,128]{5,2,4,3,1,0:T(8,128)(2,1)S(1)} async-done(((bf16[32,2,16,3,1,128]{5,2,4,3,1,0:T(8,128)(2,1)}), bf16[32,2,16,3,1,128]{5,2,4,3,1,0:T(8,128)(2,1)S(1)}, u32[]{:S(2)}, u32[]{:S(2)}) %all-to-all-start) | async-done | bytes 786464 | tf_op jit(solution)/shard_map/all_to_all | solution.py:133
  48.0 1.7 %fusion.44 = f32[3,2,16,8,512]{4,3,2,1,0:T(8,128)S(1)} fusion(bf16[512,512,1,1,1]{1,0,4,3,2:T(8,128)(2,1)} %bitcast.325, bf16[8,4,2,16,3,1,128]{6,3,4,2,1,0,5:T(8,128)(2,1)S(1)} %bitcast.306), kind=kOutput, calls=%fused_computation.87 | convolution fusion | flops 402653184 | bytes 2883584 | tf_op jit(solution)/shard_map/yk,cpjxy->cpjxk/dot_general | solution.py:65
  49.7 0.6 convolution_add_fusion.3
  50.7 0.6 fusion.41
  51.4 0.6 convolution_add_fusion.2
  57.5 0.6 convolution_add_fusion.1
  58.1 0.6 convolution_add_fusion
  59.7 24.1 %all_to_all.10 = bf16[32,2,16,3,1,128]{5,2,4,3,1,0:T(8,128)(2,1)S(1)} all-to-all(bf16[32,2,16,3,1,128]{5,2,4,3,1,0:T(8,128)(2,1)S(1)} %bitcast.321), channel_id=1, replica_groups=mesh['row'=8,'col'=4] {'row','col'}, dimensions={0} | all-to-all | bytes 1572864 | tf_op jit(solution)/shard_map/all_to_all | solution.py:188
  84.6 0.8 copy-done
  85.4 1.0 %fusion.28 = f32[384,1024]{1,0:T(8,128)S(1)} fusion(bf16[1024,1024]{1,0:T(8,128)(2,1)S(1)} %bitcast.316, bf16[128,8,3,128]{3,2,1,0:T(4,128)(2,1)S(1)} %bitcast.317), kind=kOutput, calls=%fused_computation.63 | convolution fusion | flops 805306368 | bytes 4456448 | tf_op jit(solution)/shard_map/kr,kz->rz/dot_general | solution.py:200
  86.4 1.0 %convolution_add_fusion.4 = f32[384,1024]{1,0:T(8,128)S(1)} fusion(f32[384,1024]{1,0:T(8,128)S(1)} %fusion.28, bf16[1024,1024]{1,0:T(8,128)(2,1)S(1)} %bitcast.313, bf16[128,8,3,128]{3,2,1,0:T(4,128)(2,1)S(1)} %bitcast.318), kind=kOutput, calls=%fused_computation.30 | convolution fusion | flops 805699584 | bytes 6029312 | tf_op jit(solution)/shard_map/kr,kz->rz/dot_general | solution.py:200
  87.6 1.1 %add_convert_fusion = bf16[3,1,128,1024]{3,2,1,0:T(8,128)(2,1)} fusion(f32[3,1,128,1024]{3,2,1,0:T(8,128)S(1)} %bitcast.319, bf16[3,1,128,1024]{3,2,1,0:T(8,128)(2,1)S(1)} %copy-done.8), kind=kLoop, calls=%fused_computation.15 | loop fusion | flops 1179648 | bytes 3145728 | tf_op jit(solution)/shard_map/convert_element_type | solution.py:204
  (83 shorter events, 11.3 us)
Async XLA Ops:
  0.0 2.3 %copy-start.13 = (s32[1,128,1024]{2,1,0:T(8,128)S(1)}, s32[1,128,1024]{2,1,0:T(8,128)}, u32[]{:S(2)}) copy-start(s32[1,128,1024]{2,1,0:T(8,128)} %param.8) | copy-start | bytes 1572868
  0.0 2.3 %copy-start.14 = (f32[8]{0:T(128)S(1)}, f32[8]{0:T(128)}, u32[]{:S(2)}) copy-start(f32[8]{0:T(128)} %param.9) | copy-start | bytes 100
  8.0 2.9 %copy-start.9 = (f32[1,128,1024]{2,0,1:T(1,128)S(1)}, f32[1,128,1024]{2,0,1:T(1,128)}, u32[]{:S(2)}) copy-start(f32[1,128,1024]{2,0,1:T(1,128)} %fusion.2) | copy-start | bytes 1572868
  8.0 2.9 %copy-start.10 = (f32[1,128,1024]{2,0,1:T(1,128)S(1)}, f32[1,128,1024]{2,0,1:T(1,128)}, u32[]{:S(2)}) copy-start(f32[1,128,1024]{2,0,1:T(1,128)} %fusion.3) | copy-start | bytes 1572868
  10.9 1.1 %copy-start.7 = (bf16[3,1,128,1024]{3,2,1,0:T(8,128)(2,1)S(1)}, bf16[3,1,128,1024]{3,2,1,0:T(8,128)(2,1)}, u32[]{:S(2)}) copy-start(bf16[3,1,128,1024]{3,2,1,0:T(8,128)(2,1)} %param.6) | copy-start | bytes 2359300
  20.1 27.9 %all-to-all-start = ((bf16[32,2,16,3,1,128]{5,2,4,3,1,0:T(8,128)(2,1)}), bf16[32,2,16,3,1,128]{5,2,4,3,1,0:T(8,128)(2,1)S(1)}, u32[]{:S(2)}, u32[]{:S(2)}) async-start(bf16[32,2,16,3,1,128]{5,2,4,3,1,0:T(8,128)(2,1)} %copy.41), calls=%async_computation | async-start | bytes 1572864 | tf_op jit(solution)/shard_map/all_to_all | solution.py:133
  48.0 1.7 %copy-start.5 = (bf16[16,32,512]{2,1,0:T(8,128)(2,1)S(1)}, bf16[16,32,512]{2,1,0:T(8,128)(2,1)}, u32[]{:S(2)}) copy-start(bf16[16,32,512]{2,1,0:T(8,128)(2,1)} %get-tuple-element.19) | copy-start | bytes 1572868
  49.7 1.0 %copy-start.6 = (bf16[16,32,512]{2,1,0:T(8,128)(2,1)S(1)}, bf16[16,32,512]{2,1,0:T(8,128)(2,1)}, u32[]{:S(2)}) copy-start(bf16[16,32,512]{2,1,0:T(8,128)(2,1)} %get-tuple-element.22) | copy-start | bytes 1572868
  50.3 1.1 %copy-start.4 = (bf16[16,32,512]{2,1,0:T(8,128)(2,1)S(1)}, bf16[16,32,512]{2,1,0:T(8,128)(2,1)}, u32[]{:S(2)}) copy-start(bf16[16,32,512]{2,1,0:T(8,128)(2,1)} %get-tuple-element.21) | copy-start | bytes 1572868
  51.4 0.7 copy-start.11
  53.3 1.3 %copy-start.3 = (bf16[512,512]{1,0:T(8,128)(2,1)S(1)}, bf16[512,512]{1,0:T(8,128)(2,1)}, u32[]{:S(2)}) copy-start(bf16[512,512]{1,0:T(8,128)(2,1)} %get-tuple-element.15) | copy-start | bytes 1572868
  53.6 1.1 %copy-start.2 = (bf16[512,512]{1,0:T(8,128)(2,1)S(1)}, bf16[512,512]{1,0:T(8,128)(2,1)}, u32[]{:S(2)}) copy-start(bf16[512,512]{1,0:T(8,128)(2,1)} %get-tuple-element.36) | copy-start | bytes 1572868
  56.1 1.0 %copy-start.1 = (bf16[512,512]{1,0:T(8,128)(2,1)S(1)}, bf16[512,512]{1,0:T(8,128)(2,1)}, u32[]{:S(2)}) copy-start(bf16[512,512]{1,0:T(8,128)(2,1)} %get-tuple-element.14) | copy-start | bytes 1572868
  59.5 24.3 %copy-start.12 = (f32[32,2,16]{2,1,0:T(2,128)S(1)}, f32[32,2,16]{2,1,0:T(2,128)}, u32[]{:S(2)}) copy-start(f32[32,2,16]{2,1,0:T(2,128)} %constant.116) | copy-start | bytes 12292
  83.8 1.6 %copy-start = (bf16[32,2,16,1024]{3,2,1,0:T(8,128)(2,1)S(1)}, bf16[32,2,16,1024]{3,2,1,0:T(8,128)(2,1)}, u32[]{:S(2)}) copy-start(bf16[32,2,16,1024]{3,2,1,0:T(8,128)(2,1)} %get-tuple-element.6) | copy-start | bytes 6291460
  86.4 1.1 %copy-start.8 = (bf16[3,1,128,1024]{3,2,1,0:T(8,128)(2,1)S(1)}, bf16[3,1,128,1024]{3,2,1,0:T(8,128)(2,1)}, u32[]{:S(2)}) copy-start(bf16[3,1,128,1024]{3,2,1,0:T(8,128)(2,1)} %param.7) | copy-start | bytes 2359300

commit v9 on v8

--- a/solution.py
+++ b/solution.py
@@ -124,19 +124,25 @@
     z_high, z_low = split_parts(table_z)
     rows = members * local_x * local_y
 
-    spectrum = jnp.einsum(
-        "kz,rz->kr", table_z, electric.reshape(rows, depth), precision=lax.Precision.HIGH
-    )
-    spectrum = spectrum.astype(BF16).reshape(
-        devices, 2, per_device, members, local_x, local_y
-    )
+    e_high, e_low = split_parts(electric.reshape(rows, depth))
+    spec_z = "dpjz,cyz->dpcjy"
+    blocks = (devices, 2, per_device, depth)
+    lines = (members * local_x, local_y, depth)
+    z_high4, z_low4 = z_high.reshape(blocks), z_low.reshape(blocks)
+    e_high, e_low = e_high.reshape(lines), e_low.reshape(lines)
+    spectrum = (
+        jnp.einsum(spec_z, z_high4, e_high, preferred_element_type=F32)
+        + jnp.einsum(spec_z, z_high4, e_low, preferred_element_type=F32)
+        + jnp.einsum(spec_z, z_low4, e_high, preferred_element_type=F32)
+    )
+    spectrum = spectrum.astype(BF16)
     gathered = lax.all_to_all(
         spectrum, ("row", "col"), split_axis=0, concat_axis=0, tiled=True
     )
     gathered = gathered.reshape(
-        row_count, col_count, 2, per_device, members, local_x, local_y
-    )
-    gathered = jnp.transpose(gathered, (4, 2, 3, 0, 5, 1, 6)).reshape(
+        row_count, col_count, 2, members, local_x, per_device, local_y
+    )
+    gathered = jnp.transpose(gathered, (3, 2, 5, 0, 4, 1, 6)).reshape(
         members, 2, per_device, span_x, width_y
     )
 

time: 89.3 us -> 88.6 us (level)
  blocking collectives: 24.1 us -> 0 us
  waiting for transfers between devices: 16.4 us -> 30.4 us
  local copies, waits for them, and re-layouts: 7.78 us -> 13.9 us
  starting transfers between devices: 7.48 us -> 11.1 us
  matrix products: 20.1 us -> 19 us
    all_to_all x1 -> x0, blocking collectives: 24.1 us -> none  [on_device(): lax.all_to_all(outgoing, ('row', 'col'), split_axis=0, concat_axis=0, til...]
    all_to_all x0 -> x1, waiting for transfers between devices: none -> 13.8 us  [on_device(): lax.all_to_all(outgoing, ('row', 'col'), split_axis=0, concat_axis=0, til...]
    convert_element_type x0 -> x3, local copies, waits for them, and re-layouts: none -> 7.76 us  [the longest x2 6.58 us: split_parts(): return (high.astype(BF16), low.astype(BF16))]
    all_to_all x0 -> x1, starting transfers between devices: none -> 3.84 us  [on_device(): lax.all_to_all(outgoing, ('row', 'col'), split_axis=0, concat_axis=0, til...]
    reshape x2 -> x0, local copies, waits for them, and re-layouts: 3.44 us -> none  [on_device(): spectrum.astype(BF16)]
    convert_element_type x2, other arithmetic: 4.3 us -> 2.21 us  [split_parts(): return (high.astype(BF16), low.astype(BF16))]
    sub x2, other arithmetic: 2.46 us -> 4.2 us  [phase_table(): cosine = outer_cos * inner_cos - outer_sin * inner_sin]
    another operation x0 -> x1, local copies, waits for them, and re-layouts: none -> 1.22 us  [on_device(): jnp.stack([cos_z.reshape(devices, per_device, depth), sin_part.reshape(de...]
  transfers between devices with their start and end apart: 1 -> 2, of which waited for: 1 -> 2; matrix products, arithmetic and copies ran while one was open for 5% -> 12% of each run, Pallas kernels for 0% -> 0%
where the time goes in v9:
time: 88.6 us; the launch traced here: 88 us
  waiting for transfers between devices  30.4 us (34%)
  matrix products  19 us (21%)
  local copies, waits for them, and re-layouts  13.9 us (16%)
  other arithmetic  13 us (15%)
  starting transfers between devices  11.1 us (13%)
    all_to_all x1, waiting for transfers between devices, on_device(): lax.all_to_all(spectrum, ('row', 'col'), split_axis=0, concat_axis=0, til...  16.6 us
    all_to_all x1, waiting for transfers between devices, on_device(): lax.all_to_all(outgoing, ('row', 'col'), split_axis=0, concat_axis=0, til...  13.8 us
    all_to_all x1, starting transfers between devices, on_device(): lax.all_to_all(spectrum, ('row', 'col'), split_axis=0, concat_axis=0, til...  7.3 us
    dot_general x12, matrix products, mat(): term = jnp.einsum(spec, part, operand, preferred_element_type=F32)  6.74 us
    convert_element_type x2, local copies, waits for them, and re-layouts, split_parts(): return (high.astype(BF16), low.astype(BF16))  6.58 us
    sub x2, other arithmetic, phase_table(): cosine = outer_cos * inner_cos - outer_sin * inner_sin  4.2 us
    dot_general x3, matrix products, on_device(): jnp.einsum('...k,k->...', one_hot, part.astype(BF16), preferred_element_t...  4.02 us
    all_to_all x1, starting transfers between devices, on_device(): lax.all_to_all(outgoing, ('row', 'col'), split_axis=0, concat_axis=0, til...  3.84 us
  transfers between devices with their start and end apart: 2, of which 2 were waited for; matrix products, arithmetic and copies ran while one was open for 12% of the time, Pallas kernels for 0%

profile of v9, /device:TPU:0, one launch (start us, length us, event | category | flops | bytes accessed | tf_op | source)
XLA Modules:
  0.0 88.0 jit_solution(16837014856075577632)
XLA Ops:
  0.6 1.8 %fusion.1 = f32[1,128,1024]{2,0,1:T(1,128)S(1)} fusion(s32[128,1024]{1,0:T(8,128)} %bitcast.355, f32[8]{0:T(128)} %param.9), kind=kOutput, calls=%fused_computation.5 | convolution fusion | flops 3145776 | bytes 1048608 | tf_op jit(solution)/shard_map/...k,k->.../dot_general | solution.py:108
  2.4 0.7 fusion.2
  3.1 1.5 %fusion.3 = f32[1,128,1024]{2,0,1:T(1,128)} fusion(s32[128,1024]{1,0:T(8,128)S(1)} %bitcast.357, f32[8]{0:T(128)S(1)} %copy-done.15), kind=kOutput, calls=%fused_computation.7 | convolution fusion | flops 3145752 | bytes 1048608 | tf_op jit(solution)/shard_map/...k,k->.../dot_general | solution.py:108
  6.4 1.2 %copy.51 = f32[32,1,16,1024]{3,0,2,1:T(8,128)S(1)} copy(f32[32,1,16,1024]{3,2,0,1:T(8,128)S(1)} %bitcast.344) | data formatting | bytes 4194304 | tf_op jit(solution)/shard_map/stack;reshape | solution.py:120
  8.1 2.4 %fusion.10 = f32[32,1,16,1024]{3,0,2,1:T(8,128)S(1)} fusion(f32[32,1,16,1024]{3,2,0,1:T(8,128)S(1)} %bitcast.343, f32[32,1,16,1024]{3,2,0,1:T(8,128)S(1)} %bitcast.342, f32[32,1024]{1,0:T(8,128)S(1)} %mul.978, f32[32,1024]{1,0:T(8,128)S(1)} %mul.967), kind=kLoop, calls=%fused_computation.19 | loop fusion | flops 1572864 | bytes 6553600 | tf_op jit(solution)/shard_map/sub | solution.py:45
  10.5 0.8 fusion
  11.8 1.4 %copy-done.3 = bf16[3,1,128,1024]{3,2,1,0:T(8,128)(2,1)S(1)} copy-done((bf16[3,1,128,1024]{3,2,1,0:T(8,128)(2,1)S(1)}, bf16[3,1,128,1024]{3,2,1,0:T(8,128)(2,1)}, u32[]{:S(2)}) %copy-start.3) | copy-done | bytes 786456
  13.2 1.3 %fusion.4 = f32[3,128,32,2,16]{1,2,4,3,0:T(8,128)S(1)} fusion(bf16[32,2,16,1024]{3,0,2,1:T(8,128)(2,1)S(1)} %get-tuple-element.5, bf16[3,1,128,1024]{3,2,1,0:T(8,128)(2,1)S(1)} %copy-done.3, f32[128,1024]{1,0:T(8,128)S(1)} %bitcast_add_fusion), kind=kOutput, calls=%fused_computation.12 | convolution fusion | flops 806879232 | bytes 4980736 | tf_op jit(solution)/shard_map/dpjz,cyz->dpcjy/dot_general | solution.py:136
  14.5 1.3 %fusion.6 = f32[3,128,32,2,16]{1,2,4,3,0:T(8,128)S(1)} fusion(bf16[32,2,16,1024]{3,0,2,1:T(8,128)(2,1)S(1)} %get-tuple-element.6, bf16[3,1,128,1024]{3,2,1,0:T(8,128)(2,1)S(1)} %copy-done.3, f32[128,1024]{1,0:T(8,128)S(1)} %bitcast_add_fusion), kind=kOutput, calls=%fused_computation.14 | convolution fusion | flops 807272448 | bytes 4980736 | tf_op jit(solution)/shard_map/dpjz,cyz->dpcjy/dot_general | solution.py:135
  15.8 1.5 %fusion.17 = bf16[32,2,3,16,128]{4,0,3,1,2:T(8,128)(2,1)S(1)} fusion(f32[3,128,32,2,16]{1,2,4,3,0:T(8,128)S(1)} %fusion.4, f32[3,128,32,2,16]{1,2,4,3,0:T(8,128)S(1)} %fusion.6, bf16[32,2,16,1024]{3,0,2,1:T(8,128)(2,1)S(1)} %get-tuple-element.6, bf16[3,1,128,1024]{3,2,1,0:T(8,128)(2,1)S(1)} %copy-done.3, f32[128,1024]{1,0:T(8,128)S(1)} %bitcast_add_fusion), kind=kOutput, calls=%fused_computation.43 | convolution fusion | flops 808058880 | bytes 7340032 | tf_op jit(solution)/shard_map/dpjz,cyz->dpcjy/dot_general | solution.py:134
  17.3 1.2 %copy.52 = bf16[32,2,3,16,128]{4,3,1,2,0:T(8,128)(2,1)} copy(bf16[32,2,3,16,128]{4,0,3,1,2:T(8,128)(2,1)S(1)} %fusion.17) | data formatting | bytes 1572864 | tf_op jit(solution)/shard_map/convert_element_type | solution.py:138
  18.5 7.3 %all-to-all-start = ((bf16[32,2,3,16,128]{4,3,1,2,0:T(8,128)(2,1)}), bf16[32,2,3,16,128]{4,3,1,2,0:T(8,128)(2,1)S(1)}, u32[]{:S(2)}, u32[]{:S(2)}) async-start(bf16[32,2,3,16,128]{4,3,1,2,0:T(8,128)(2,1)} %copy.52), calls=%async_computation | async-start | bytes 1572864 | tf_op jit(solution)/shard_map/all_to_all | solution.py:139
  26.6 1.8 %multiply_subtract_fusion = (f32[16,32,512]{2,1,0:T(8,128)S(1)}, bf16[16,32,512]{2,1,0:T(8,128)(2,1)}, bf16[16,32,512]{2,1,0:T(8,128)(2,1)}, bf16[16,32,512]{2,1...) fusion(f32[32,512]{1,0:T(8,128)S(1)} %fusion.141, f32[16,512]{1,0:T(8,128)S(1)} %get-tuple-element.30, ...), kind=kLoop, calls=%fused_computation.72 | loop fusion | flops 3670016 | bytes 4390912 | tf_op jit(solution)/shard_map/sub | solution.py:45
  28.4 1.4 %fusion.38 = (bf16[512,512]{1,0:T(8,128)(2,1)S(1)}, bf16[512,512]{1,0:T(8,128)(2,1)}, bf16[512,512]{1,0:T(8,128)(2,1)}, bf16[512,512]{1,0:T(8,128)(2,1)}) fusion(f32[16,32,512]{2,1,0:T(8,128)S(1)} %get-tuple-element.17, f32[16,32,512]{2,1,0:T(8,128)S(1)} %get-tuple-element.22), kind=kLoop, calls=%fused_computation.70 | loop fusion | flops 2097152 | bytes 4194304 | tf_op jit(solution)/shard_map/convert_element_type | solution.py:28
  29.9 16.6 %all-to-all-done = bf16[32,2,3,16,128]{4,3,1,2,0:T(8,128)(2,1)S(1)} async-done(((bf16[32,2,3,16,128]{4,3,1,2,0:T(8,128)(2,1)}), bf16[32,2,3,16,128]{4,3,1,2,0:T(8,128)(2,1)S(1)}, u32[]{:S(2)}, u32[]{:S(2)}) %all-to-all-start) | async-done | bytes 786464 | tf_op jit(solution)/shard_map/all_to_all | solution.py:139
  46.4 1.7 %fusion.60 = f32[3,2,16,8,512]{4,3,2,1,0:T(8,128)S(1)} fusion(bf16[512,512,1,1,1]{1,0,4,3,2:T(8,128)(2,1)} %bitcast.354, bf16[8,4,2,3,1,16,128]{6,5,2,3,1,0,4:T(8,128)(2,1)S(1)} %bitcast.337), kind=kOutput, calls=%fused_computation.101 | convolution fusion | flops 402653184 | bytes 2883584 | tf_op jit(solution)/shard_map/yk,cpjxy->cpjxk/dot_general | solution.py:65
  58.1 0.9 %pad_maximum_fusion.3 = bf16[3,2,16,8,1,4,128]{6,2,4,0,1,5,3:T(8,128)(2,1)} fusion(bf16[3,1,16,8,1,4,128]{6,2,4,0,1,5,3:T(8,128)(2,1)S(1)} %copy.62, bf16[3,1,16,8,1,4,128]{6,2,4,0,1,5,3:T(8,128)(2,1)S(1)} %copy.61), kind=kLoop, calls=%fused_computation.96 | loop fusion | flops 393216 | bytes 1572864 | tf_op jit(solution)/shard_map/stack | solution.py:187
  59.0 3.8 %all-to-all-start.1 = ((bf16[32,2,16,3,1,128]{5,2,4,3,1,0:T(8,128)(2,1)}), bf16[32,2,16,3,1,128]{5,2,4,3,1,0:T(8,128)(2,1)S(1)}, u32[]{:S(2)}, u32[]{:S(2)}) async-start(bf16[32,2,16,3,1,128]{5,2,4,3,1,0:T(8,128)(2,1)} %bitcast.350), calls=%async_computation.1 | async-start | bytes 1572864 | tf_op jit(solution)/shard_map/all_to_all | solution.py:194
  62.9 4.1 %copy.65 = bf16[32,2,16,1024]{3,2,1,0:T(8,128)(2,1)} copy(bf16[32,2,16,1024]{3,0,2,1:T(8,128)(2,1)} %copy-done) | data formatting | bytes 4194304 | tf_op jit(solution)/shard_map/convert_element_type | solution.py:28
  67.0 2.5 %copy.64 = bf16[32,2,16,1024]{3,2,1,0:T(8,128)(2,1)} copy(bf16[32,2,16,1024]{3,0,2,1:T(8,128)(2,1)S(1)} %get-tuple-element.6) | data formatting | bytes 4194304 | tf_op jit(solution)/shard_map/convert_element_type | solution.py:28
  69.5 13.8 %all-to-all-done.1 = bf16[32,2,16,3,1,128]{5,2,4,3,1,0:T(8,128)(2,1)S(1)} async-done(((bf16[32,2,16,3,1,128]{5,2,4,3,1,0:T(8,128)(2,1)}), bf16[32,2,16,3,1,128]{5,2,4,3,1,0:T(8,128)(2,1)S(1)}, u32[]{:S(2)}, u32[]{:S(2)}) %all-to-all-start.1) | async-done | bytes 786464 | tf_op jit(solution)/shard_map/all_to_all | solution.py:194
  84.1 1.0 %fusion.44 = f32[384,1024]{1,0:T(8,128)S(1)} fusion(bf16[1024,1024]{1,0:T(8,128)(2,1)S(1)} %bitcast.345, bf16[128,8,3,128]{3,2,1,0:T(4,128)(2,1)S(1)} %bitcast.347), kind=kOutput, calls=%fused_computation.77 | convolution fusion | flops 805306368 | bytes 4456448 | tf_op jit(solution)/shard_map/kr,kz->rz/dot_general | solution.py:206
  85.7 1.0 %convolution_add_fusion.4 = f32[384,1024]{1,0:T(8,128)S(1)} fusion(f32[384,1024]{1,0:T(8,128)S(1)} %fusion.44, bf16[1024,1024]{1,0:T(8,128)(2,1)S(1)} %bitcast.341, bf16[128,8,3,128]{3,2,1,0:T(4,128)(2,1)S(1)} %bitcast.348), kind=kOutput, calls=%fused_computation.42 | convolution fusion | flops 805699584 | bytes 6029312 | tf_op jit(solution)/shard_map/kr,kz->rz/dot_general | solution.py:206
  86.8 1.1 %add_convert_fusion = bf16[3,1,128,1024]{3,2,1,0:T(8,128)(2,1)} fusion(f32[3,1,128,1024]{3,2,1,0:T(8,128)S(1)} %bitcast.349, bf16[3,1,128,1024]{3,2,1,0:T(8,128)(2,1)S(1)} %copy-done.10), kind=kLoop, calls=%fused_computation.26 | loop fusion | flops 1179648 | bytes 3145728 | tf_op jit(solution)/shard_map/convert_element_type | solution.py:210
  (89 shorter events, 15.2 us)
Async XLA Ops:
  0.0 2.3 %copy-start.15 = (f32[8]{0:T(128)S(1)}, f32[8]{0:T(128)}, u32[]{:S(2)}) copy-start(f32[8]{0:T(128)} %param.9) | copy-start | bytes 100
  0.0 2.3 %copy-start.14 = (s32[1,128,1024]{2,1,0:T(8,128)S(1)}, s32[1,128,1024]{2,1,0:T(8,128)}, u32[]{:S(2)}) copy-start(s32[1,128,1024]{2,1,0:T(8,128)} %param.8) | copy-start | bytes 1572868
  10.5 1.0 %copy-start.11 = (f32[1,128,1024]{2,0,1:T(1,128)S(1)}, f32[1,128,1024]{2,0,1:T(1,128)}, u32[]{:S(2)}) copy-start(f32[1,128,1024]{2,0,1:T(1,128)} %fusion.3) | copy-start | bytes 1572868
  11.5 3.0 %copy-start = (bf16[32,2,16,1024]{3,0,2,1:T(8,128)(2,1)}, bf16[32,2,16,1024]{3,0,2,1:T(8,128)(2,1)S(1)}, u32[]{:S(2)}) copy-start(bf16[32,2,16,1024]{3,0,2,1:T(8,128)(2,1)S(1)} %get-tuple-element.5) | copy-start | bytes 6291460
  11.5 1.7 %copy-start.3 = (bf16[3,1,128,1024]{3,2,1,0:T(8,128)(2,1)S(1)}, bf16[3,1,128,1024]{3,2,1,0:T(8,128)(2,1)}, u32[]{:S(2)}) copy-start(bf16[3,1,128,1024]{3,2,1,0:T(8,128)(2,1)} %param.6) | copy-start | bytes 2359300
  18.5 27.9 %all-to-all-start = ((bf16[32,2,3,16,128]{4,3,1,2,0:T(8,128)(2,1)}), bf16[32,2,3,16,128]{4,3,1,2,0:T(8,128)(2,1)S(1)}, u32[]{:S(2)}, u32[]{:S(2)}) async-start(bf16[32,2,3,16,128]{4,3,1,2,0:T(8,128)(2,1)} %copy.52), calls=%async_computation | async-start | bytes 1572864 | tf_op jit(solution)/shard_map/all_to_all | solution.py:139
  46.4 1.7 %copy-start.8 = (bf16[16,32,512]{2,1,0:T(8,128)(2,1)S(1)}, bf16[16,32,512]{2,1,0:T(8,128)(2,1)}, u32[]{:S(2)}) copy-start(bf16[16,32,512]{2,1,0:T(8,128)(2,1)} %get-tuple-element.18) | copy-start | bytes 1572868
  48.2 1.0 %copy-start.9 = (bf16[16,32,512]{2,1,0:T(8,128)(2,1)S(1)}, bf16[16,32,512]{2,1,0:T(8,128)(2,1)}, u32[]{:S(2)}) copy-start(bf16[16,32,512]{2,1,0:T(8,128)(2,1)} %get-tuple-element.21) | copy-start | bytes 1572868
  48.8 1.1 %copy-start.7 = (bf16[16,32,512]{2,1,0:T(8,128)(2,1)S(1)}, bf16[16,32,512]{2,1,0:T(8,128)(2,1)}, u32[]{:S(2)}) copy-start(bf16[16,32,512]{2,1,0:T(8,128)(2,1)} %get-tuple-element.20) | copy-start | bytes 1572868
  50.5 0.7 copy-start.12
  51.9 1.3 %copy-start.6 = (bf16[512,512]{1,0:T(8,128)(2,1)S(1)}, bf16[512,512]{1,0:T(8,128)(2,1)}, u32[]{:S(2)}) copy-start(bf16[512,512]{1,0:T(8,128)(2,1)} %get-tuple-element.35) | copy-start | bytes 1572868
  52.3 1.1 %copy-start.5 = (bf16[512,512]{1,0:T(8,128)(2,1)S(1)}, bf16[512,512]{1,0:T(8,128)(2,1)}, u32[]{:S(2)}) copy-start(bf16[512,512]{1,0:T(8,128)(2,1)} %get-tuple-element.14) | copy-start | bytes 1572868
  54.7 1.0 %copy-start.4 = (bf16[512,512]{1,0:T(8,128)(2,1)S(1)}, bf16[512,512]{1,0:T(8,128)(2,1)}, u32[]{:S(2)}) copy-start(bf16[512,512]{1,0:T(8,128)(2,1)} %get-tuple-element.36) | copy-start | bytes 1572868
  59.0 24.2 %all-to-all-start.1 = ((bf16[32,2,16,3,1,128]{5,2,4,3,1,0:T(8,128)(2,1)}), bf16[32,2,16,3,1,128]{5,2,4,3,1,0:T(8,128)(2,1)S(1)}, u32[]{:S(2)}, u32[]{:S(2)}) async-start(bf16[32,2,16,3,1,128]{5,2,4,3,1,0:T(8,128)(2,1)} %bitcast.350), calls=%async_computation.1 | async-start | bytes 1572864 | tf_op jit(solution)/shard_map/all_to_all | solution.py:194
  67.0 16.3 %copy-start.13 = (f32[32,2,16]{2,1,0:T(2,128)S(1)}, f32[32,2,16]{2,1,0:T(2,128)}, u32[]{:S(2)}) copy-start(f32[32,2,16]{2,1,0:T(2,128)} %constant.116) | copy-start | bytes 12292
  69.5 14.6 %copy-start.2 = (bf16[32,2,16,1024]{3,2,1,0:T(8,128)(2,1)S(1)}, bf16[32,2,16,1024]{3,2,1,0:T(8,128)(2,1)}, u32[]{:S(2)}) copy-start(bf16[32,2,16,1024]{3,2,1,0:T(8,128)(2,1)} %copy.64) | copy-start | bytes 6291460
  84.1 1.6 %copy-start.1 = (bf16[32,2,16,1024]{3,2,1,0:T(8,128)(2,1)S(1)}, bf16[32,2,16,1024]{3,2,1,0:T(8,128)(2,1)}, u32[]{:S(2)}) copy-start(bf16[32,2,16,1024]{3,2,1,0:T(8,128)(2,1)} %copy.65) | copy-start | bytes 6291460
  85.7 1.1 %copy-start.10 = (bf16[3,1,128,1024]{3,2,1,0:T(8,128)(2,1)S(1)}, bf16[3,1,128,1024]{3,2,1,0:T(8,128)(2,1)}, u32[]{:S(2)}) copy-start(bf16[3,1,128,1024]{3,2,1,0:T(8,128)(2,1)} %param.7) | copy-start | bytes 2359300

commit v10 on v9

--- a/solution.py
+++ b/solution.py
@@ -98,17 +98,13 @@
 
     reciprocal = 1.0 / permittivity
     regions = permittivity.shape[0]
-    one_hot = (region[..., None] == lax.iota(jnp.int32, regions)).astype(BF16)
     first = rounded(reciprocal)
     rest = reciprocal - first
     second = rounded(rest)
-    parts = (first, second, rest - second)
-    cell_scale = None
-    for part in parts:
-        term = jnp.einsum(
-            "...k,k->...", one_hot, part.astype(BF16), preferred_element_type=F32
-        )
-        cell_scale = term if cell_scale is None else cell_scale + term
+    parts = jnp.concatenate([first, second, rest - second]).astype(BF16)
+    slots = lax.iota(jnp.int32, 3 * regions) % regions
+    one_hot = (region[..., None] == slots).astype(BF16)
+    cell_scale = jnp.einsum("...k,k->...", one_hot, parts, preferred_element_type=F32)
     electric = displacement.astype(F32) * cell_scale[None]
 
     cos_z, sin_z = phase_table(columns, depth, depth)
@@ -125,7 +121,7 @@
     rows = members * local_x * local_y
 
     e_high, e_low = split_parts(electric.reshape(rows, depth))
-    spec_z = "dpjz,cyz->dpcjy"
+    spec_z = "dpjz,cyz->dcpjy"
     blocks = (devices, 2, per_device, depth)
     lines = (members * local_x, local_y, depth)
     z_high4, z_low4 = z_high.reshape(blocks), z_low.reshape(blocks)
@@ -140,9 +136,9 @@
         spectrum, ("row", "col"), split_axis=0, concat_axis=0, tiled=True
     )
     gathered = gathered.reshape(
-        row_count, col_count, 2, members, local_x, per_device, local_y
-    )
-    gathered = jnp.transpose(gathered, (3, 2, 5, 0, 4, 1, 6)).reshape(
+        row_count, col_count, members, local_x, 2, per_device, local_y
+    )
+    gathered = jnp.transpose(gathered, (2, 4, 5, 0, 3, 1, 6)).reshape(
         members, 2, per_device, span_x, width_y
     )
 

time: 88.6 us -> 87.1 us (0.983)
  matrix products: 19 us -> 17.8 us
    dot_general x3 -> x1, matrix products: 4.02 us -> 2.98 us  [on_device(): jnp.einsum('...k,k->...', one_hot, parts, preferred_element_type=F32)]
    unnamed x32 -> x26, local copies, waits for them, and re-layouts: 3.21 us -> 2.24 us
where the time goes in v10:
time: 87.1 us; the launch traced here: 86.5 us
  waiting for transfers between devices  30.4 us (35%)
  matrix products  17.8 us (20%)
  other arithmetic  13.4 us (15%)
  local copies, waits for them, and re-layouts  13.1 us (15%)
  starting transfers between devices  11.1 us (13%)
    all_to_all x1, waiting for transfers between devices, on_device(): lax.all_to_all(spectrum, ('row', 'col'), split_axis=0, concat_axis=0, til...  16.5 us
    all_to_all x1, waiting for transfers between devices, on_device(): lax.all_to_all(outgoing, ('row', 'col'), split_axis=0, concat_axis=0, til...  13.8 us
    all_to_all x1, starting transfers between devices, on_device(): lax.all_to_all(spectrum, ('row', 'col'), split_axis=0, concat_axis=0, til...  7.3 us
    dot_general x12, matrix products, mat(): term = jnp.einsum(spec, part, operand, preferred_element_type=F32)  6.73 us
    convert_element_type x2, local copies, waits for them, and re-layouts, split_parts(): return (high.astype(BF16), low.astype(BF16))  6.55 us
    sub x2, other arithmetic, phase_table(): cosine = outer_cos * inner_cos - outer_sin * inner_sin  4.19 us
    all_to_all x1, starting transfers between devices, on_device(): lax.all_to_all(outgoing, ('row', 'col'), split_axis=0, concat_axis=0, til...  3.84 us
    dot_general x1, matrix products, on_device(): jnp.einsum('...k,k->...', one_hot, parts, preferred_element_type=F32)  2.98 us
  transfers between devices with their start and end apart: 2, of which 2 were waited for; matrix products, arithmetic and copies ran while one was open for 12% of the time, Pallas kernels for 0%

profile of v10, /device:TPU:0, one launch (start us, length us, event | category | flops | bytes accessed | tf_op | source)
XLA Modules:
  0.0 86.5 jit_solution(8350247073985342741)
XLA Ops:
  0.6 0.7 reduce-precision_convert_fusion.7
  1.9 3.0 %fusion = f32[1,128,1024]{2,0,1:T(1,128)S(1)} fusion(s32[128,1024]{1,0:T(8,128)} %bitcast.347, s32[24]{0:T(128)S(1)} %and_select_fusion.1, bf16[8]{0:T(256)(128)(2,1)S(1)} %get-tuple-element.32, bf16[8]{0:T(256)(128)(2,1)S(1)} %get-tuple-element.31, bf16[8]{0:T(256)(128)(2,1)S(1)} %get-tuple-element.5), kind=kOutput, calls=%fused_computation | convolution fusion | flops 9437328 | bytes 1048720 | tf_op jit(solution)/shard_map/...k,k->.../dot_general | solution.py:107
  6.1 1.2 %copy.51 = f32[32,1,16,1024]{3,0,2,1:T(8,128)S(1)} copy(f32[32,1,16,1024]{3,2,0,1:T(8,128)S(1)} %bitcast.336) | data formatting | bytes 4194304 | tf_op jit(solution)/shard_map/stack;reshape | solution.py:116
  7.8 2.4 %fusion.11 = f32[32,1,16,1024]{3,0,2,1:T(8,128)S(1)} fusion(f32[32,1,16,1024]{3,2,0,1:T(8,128)S(1)} %bitcast.335, f32[32,1,16,1024]{3,2,0,1:T(8,128)S(1)} %bitcast.334, f32[32,1024]{1,0:T(8,128)S(1)} %mul.978, f32[32,1024]{1,0:T(8,128)S(1)} %mul.967), kind=kLoop, calls=%fused_computation.19 | loop fusion | flops 1572864 | bytes 6553600 | tf_op jit(solution)/shard_map/sub | solution.py:45
  10.2 0.8 fusion.4
  11.3 1.3 %fusion.5 = f32[3,128,32,2,16]{1,2,4,3,0:T(8,128)S(1)} fusion(bf16[32,2,16,1024]{3,0,2,1:T(8,128)(2,1)S(1)} %get-tuple-element.7, bf16[3,1,128,1024]{3,2,1,0:T(8,128)(2,1)S(1)} %copy-done.3, f32[128,1024]{1,0:T(8,128)S(1)} %bitcast.326), kind=kOutput, calls=%fused_computation.12 | convolution fusion | flops 806879232 | bytes 4980736 | tf_op jit(solution)/shard_map/dpjz,cyz->dcpjy/dot_general | solution.py:132
  12.6 1.3 %fusion.7 = f32[3,128,32,2,16]{1,2,4,3,0:T(8,128)S(1)} fusion(bf16[32,2,16,1024]{3,0,2,1:T(8,128)(2,1)S(1)} %get-tuple-element.8, bf16[3,1,128,1024]{3,2,1,0:T(8,128)(2,1)S(1)} %copy-done.3, f32[128,1024]{1,0:T(8,128)S(1)} %bitcast.327), kind=kOutput, calls=%fused_computation.14 | convolution fusion | flops 807272448 | bytes 4980736 | tf_op jit(solution)/shard_map/dpjz,cyz->dcpjy/dot_general | solution.py:131
  13.9 1.4 %fusion.15 = bf16[32,3,2,16,128]{4,0,3,2,1:T(8,128)(2,1)S(1)} fusion(f32[3,128,32,2,16]{1,2,4,3,0:T(8,128)S(1)} %fusion.5, f32[3,128,32,2,16]{1,2,4,3,0:T(8,128)S(1)} %fusion.7, bf16[32,2,16,1024]{3,0,2,1:T(8,128)(2,1)S(1)} %get-tuple-element.8, bf16[3,1,128,1024]{3,2,1,0:T(8,128)(2,1)S(1)} %copy-done.3, f32[128,1024]{1,0:T(8,128)S(1)} %bitcast.328), kind=kOutput, calls=%fused_computation.40 | convolution fusion | flops 808058880 | bytes 7340032 | tf_op jit(solution)/shard_map/dpjz,cyz->dcpjy/dot_general | solution.py:130
  15.3 1.4 %copy.52 = bf16[32,3,2,16,128]{4,3,2,1,0:T(8,128)(2,1)} copy(bf16[32,3,2,16,128]{4,0,3,2,1:T(8,128)(2,1)S(1)} %fusion.15) | data formatting | bytes 1572864 | tf_op jit(solution)/shard_map/convert_element_type | solution.py:134
  16.7 7.3 %all-to-all-start = ((bf16[32,3,2,16,128]{4,3,2,1,0:T(8,128)(2,1)}), bf16[32,3,2,16,128]{4,3,2,1,0:T(8,128)(2,1)S(1)}, u32[]{:S(2)}, u32[]{:S(2)}) async-start(bf16[32,3,2,16,128]{4,3,2,1,0:T(8,128)(2,1)} %copy.52), calls=%async_computation | async-start | bytes 1572864 | tf_op jit(solution)/shard_map/all_to_all | solution.py:135
  24.8 1.8 %multiply_subtract_fusion = (f32[16,32,512]{2,1,0:T(8,128)S(1)}, bf16[16,32,512]{2,1,0:T(8,128)(2,1)}, bf16[16,32,512]{2,1,0:T(8,128)(2,1)}, bf16[16,32,512]{2,1...) fusion(f32[32,512]{1,0:T(8,128)S(1)} %fusion.139, f32[16,512]{1,0:T(8,128)S(1)} %get-tuple-element.34, ...), kind=kLoop, calls=%fused_computation.69 | loop fusion | flops 3670016 | bytes 4390912 | tf_op jit(solution)/shard_map/sub | solution.py:45
  26.6 1.5 %fusion.36 = (bf16[512,512]{1,0:T(8,128)(2,1)S(1)}, bf16[512,512]{1,0:T(8,128)(2,1)}, bf16[512,512]{1,0:T(8,128)(2,1)}, bf16[512,512]{1,0:T(8,128)(2,1)}) fusion(f32[16,32,512]{2,1,0:T(8,128)S(1)} %get-tuple-element.19, f32[16,32,512]{2,1,0:T(8,128)S(1)} %get-tuple-element.24), kind=kLoop, calls=%fused_computation.67 | loop fusion | flops 2097152 | bytes 4194304 | tf_op jit(solution)/shard_map/convert_element_type | solution.py:28
  28.1 16.5 %all-to-all-done = bf16[32,3,2,16,128]{4,3,2,1,0:T(8,128)(2,1)S(1)} async-done(((bf16[32,3,2,16,128]{4,3,2,1,0:T(8,128)(2,1)}), bf16[32,3,2,16,128]{4,3,2,1,0:T(8,128)(2,1)S(1)}, u32[]{:S(2)}, u32[]{:S(2)}) %all-to-all-start) | async-done | bytes 786464 | tf_op jit(solution)/shard_map/all_to_all | solution.py:135
  44.6 1.7 %fusion.58 = f32[3,2,16,8,512]{4,3,2,1,0:T(8,128)S(1)} fusion(bf16[512,512,1,1,1]{1,0,4,3,2:T(8,128)(2,1)} %bitcast.346, bf16[8,4,3,1,2,16,128]{6,5,4,2,1,0,3:T(8,128)(2,1)S(1)} %bitcast.329), kind=kOutput, calls=%fused_computation.98 | convolution fusion | flops 402653184 | bytes 2883584 | tf_op jit(solution)/shard_map/yk,cpjxy->cpjxk/dot_general | solution.py:65
  46.3 0.6 convolution_add_fusion.3
  48.1 0.6 convolution_add_fusion.2
  56.6 0.9 %pad_maximum_fusion.3 = bf16[3,2,16,8,1,4,128]{6,2,4,0,1,5,3:T(8,128)(2,1)} fusion(bf16[3,1,16,8,1,4,128]{6,2,4,0,1,5,3:T(8,128)(2,1)S(1)} %copy.62, bf16[3,1,16,8,1,4,128]{6,2,4,0,1,5,3:T(8,128)(2,1)S(1)} %copy.61), kind=kLoop, calls=%fused_computation.93 | loop fusion | flops 393216 | bytes 1572864 | tf_op jit(solution)/shard_map/stack | solution.py:183
  57.5 3.8 %all-to-all-start.1 = ((bf16[32,2,16,3,1,128]{5,2,4,3,1,0:T(8,128)(2,1)}), bf16[32,2,16,3,1,128]{5,2,4,3,1,0:T(8,128)(2,1)S(1)}, u32[]{:S(2)}, u32[]{:S(2)}) async-start(bf16[32,2,16,3,1,128]{5,2,4,3,1,0:T(8,128)(2,1)} %bitcast.342), calls=%async_computation.1 | async-start | bytes 1572864 | tf_op jit(solution)/shard_map/all_to_all | solution.py:190
  61.3 4.1 %copy.65 = bf16[32,2,16,1024]{3,2,1,0:T(8,128)(2,1)} copy(bf16[32,2,16,1024]{3,0,2,1:T(8,128)(2,1)} %copy-done) | data formatting | bytes 4194304 | tf_op jit(solution)/shard_map/convert_element_type | solution.py:28
  65.4 2.5 %copy.64 = bf16[32,2,16,1024]{3,2,1,0:T(8,128)(2,1)} copy(bf16[32,2,16,1024]{3,0,2,1:T(8,128)(2,1)S(1)} %get-tuple-element.8) | data formatting | bytes 4194304 | tf_op jit(solution)/shard_map/convert_element_type | solution.py:28
  67.9 13.8 %all-to-all-done.1 = bf16[32,2,16,3,1,128]{5,2,4,3,1,0:T(8,128)(2,1)S(1)} async-done(((bf16[32,2,16,3,1,128]{5,2,4,3,1,0:T(8,128)(2,1)}), bf16[32,2,16,3,1,128]{5,2,4,3,1,0:T(8,128)(2,1)S(1)}, u32[]{:S(2)}, u32[]{:S(2)}) %all-to-all-start.1) | async-done | bytes 786464 | tf_op jit(solution)/shard_map/all_to_all | solution.py:190
  82.6 1.0 %fusion.42 = f32[384,1024]{1,0:T(8,128)S(1)} fusion(bf16[1024,1024]{1,0:T(8,128)(2,1)S(1)} %bitcast.337, bf16[128,8,3,128]{3,2,1,0:T(4,128)(2,1)S(1)} %bitcast.339), kind=kOutput, calls=%fused_computation.74 | convolution fusion | flops 805306368 | bytes 4456448 | tf_op jit(solution)/shard_map/kr,kz->rz/dot_general | solution.py:202
  84.2 1.0 %convolution_add_fusion.4 = f32[384,1024]{1,0:T(8,128)S(1)} fusion(f32[384,1024]{1,0:T(8,128)S(1)} %fusion.42, bf16[1024,1024]{1,0:T(8,128)(2,1)S(1)} %bitcast.333, bf16[128,8,3,128]{3,2,1,0:T(4,128)(2,1)S(1)} %bitcast.340), kind=kOutput, calls=%fused_computation.39 | convolution fusion | flops 805699584 | bytes 6029312 | tf_op jit(solution)/shard_map/kr,kz->rz/dot_general | solution.py:202
  85.3 1.1 %add_convert_fusion = bf16[3,1,128,1024]{3,2,1,0:T(8,128)(2,1)} fusion(f32[3,1,128,1024]{3,2,1,0:T(8,128)S(1)} %bitcast.341, bf16[3,1,128,1024]{3,2,1,0:T(8,128)(2,1)S(1)} %copy-done.10), kind=kLoop, calls=%fused_computation.23 | loop fusion | flops 1179648 | bytes 3145728 | tf_op jit(solution)/shard_map/convert_element_type | solution.py:206
  (84 shorter events, 14.1 us)
Async XLA Ops:
  10.2 1.1 %copy-start.3 = (bf16[3,1,128,1024]{3,2,1,0:T(8,128)(2,1)S(1)}, bf16[3,1,128,1024]{3,2,1,0:T(8,128)(2,1)}, u32[]{:S(2)}) copy-start(bf16[3,1,128,1024]{3,2,1,0:T(8,128)(2,1)} %param.6) | copy-start | bytes 2359300
  11.0 1.6 %copy-start = (bf16[32,2,16,1024]{3,0,2,1:T(8,128)(2,1)}, bf16[32,2,16,1024]{3,0,2,1:T(8,128)(2,1)S(1)}, u32[]{:S(2)}) copy-start(bf16[32,2,16,1024]{3,0,2,1:T(8,128)(2,1)S(1)} %get-tuple-element.7) | copy-start | bytes 6291460
  16.7 27.9 %all-to-all-start = ((bf16[32,3,2,16,128]{4,3,2,1,0:T(8,128)(2,1)}), bf16[32,3,2,16,128]{4,3,2,1,0:T(8,128)(2,1)S(1)}, u32[]{:S(2)}, u32[]{:S(2)}) async-start(bf16[32,3,2,16,128]{4,3,2,1,0:T(8,128)(2,1)} %copy.52), calls=%async_computation | async-start | bytes 1572864 | tf_op jit(solution)/shard_map/all_to_all | solution.py:135
  44.6 1.7 %copy-start.8 = (bf16[16,32,512]{2,1,0:T(8,128)(2,1)S(1)}, bf16[16,32,512]{2,1,0:T(8,128)(2,1)}, u32[]{:S(2)}) copy-start(bf16[16,32,512]{2,1,0:T(8,128)(2,1)} %get-tuple-element.20) | copy-start | bytes 1572868
  46.3 1.0 %copy-start.9 = (bf16[16,32,512]{2,1,0:T(8,128)(2,1)S(1)}, bf16[16,32,512]{2,1,0:T(8,128)(2,1)}, u32[]{:S(2)}) copy-start(bf16[16,32,512]{2,1,0:T(8,128)(2,1)} %get-tuple-element.23) | copy-start | bytes 1572868
  47.0 1.1 %copy-start.7 = (bf16[16,32,512]{2,1,0:T(8,128)(2,1)S(1)}, bf16[16,32,512]{2,1,0:T(8,128)(2,1)}, u32[]{:S(2)}) copy-start(bf16[16,32,512]{2,1,0:T(8,128)(2,1)} %get-tuple-element.22) | copy-start | bytes 1572868
  48.7 0.7 copy-start.11
  50.4 1.0 %copy-start.6 = (bf16[512,512]{1,0:T(8,128)(2,1)S(1)}, bf16[512,512]{1,0:T(8,128)(2,1)}, u32[]{:S(2)}) copy-start(bf16[512,512]{1,0:T(8,128)(2,1)} %get-tuple-element.39) | copy-start | bytes 1572868
  50.8 1.1 %copy-start.5 = (bf16[512,512]{1,0:T(8,128)(2,1)S(1)}, bf16[512,512]{1,0:T(8,128)(2,1)}, u32[]{:S(2)}) copy-start(bf16[512,512]{1,0:T(8,128)(2,1)} %get-tuple-element.16) | copy-start | bytes 1572868
  53.2 1.0 %copy-start.4 = (bf16[512,512]{1,0:T(8,128)(2,1)S(1)}, bf16[512,512]{1,0:T(8,128)(2,1)}, u32[]{:S(2)}) copy-start(bf16[512,512]{1,0:T(8,128)(2,1)} %get-tuple-element.40) | copy-start | bytes 1572868
  57.5 24.2 %all-to-all-start.1 = ((bf16[32,2,16,3,1,128]{5,2,4,3,1,0:T(8,128)(2,1)}), bf16[32,2,16,3,1,128]{5,2,4,3,1,0:T(8,128)(2,1)S(1)}, u32[]{:S(2)}, u32[]{:S(2)}) async-start(bf16[32,2,16,3,1,128]{5,2,4,3,1,0:T(8,128)(2,1)} %bitcast.342), calls=%async_computation.1 | async-start | bytes 1572864 | tf_op jit(solution)/shard_map/all_to_all | solution.py:190
  65.4 16.3 %copy-start.12 = (f32[32,2,16]{2,1,0:T(2,128)S(1)}, f32[32,2,16]{2,1,0:T(2,128)}, u32[]{:S(2)}) copy-start(f32[32,2,16]{2,1,0:T(2,128)} %constant.131) | copy-start | bytes 12292
  67.9 14.7 %copy-start.2 = (bf16[32,2,16,1024]{3,2,1,0:T(8,128)(2,1)S(1)}, bf16[32,2,16,1024]{3,2,1,0:T(8,128)(2,1)}, u32[]{:S(2)}) copy-start(bf16[32,2,16,1024]{3,2,1,0:T(8,128)(2,1)} %copy.64) | copy-start | bytes 6291460
  82.6 1.6 %copy-start.1 = (bf16[32,2,16,1024]{3,2,1,0:T(8,128)(2,1)S(1)}, bf16[32,2,16,1024]{3,2,1,0:T(8,128)(2,1)}, u32[]{:S(2)}) copy-start(bf16[32,2,16,1024]{3,2,1,0:T(8,128)(2,1)} %copy.65) | copy-start | bytes 6291460
  84.2 1.1 %copy-start.10 = (bf16[3,1,128,1024]{3,2,1,0:T(8,128)(2,1)S(1)}, bf16[3,1,128,1024]{3,2,1,0:T(8,128)(2,1)}, u32[]{:S(2)}) copy-start(bf16[3,1,128,1024]{3,2,1,0:T(8,128)(2,1)} %param.7) | copy-start | bytes 2359300

commit v11 on v10

--- a/solution.py
+++ b/solution.py
@@ -110,7 +110,8 @@
     cos_z, sin_z = phase_table(columns, depth, depth)
     if hermitian:
         parity = (1 - 2 * (lax.iota(jnp.int32, depth) % 2)).astype(F32)
-        sin_part = jnp.concatenate([parity[None, :], -sin_z[1:]], axis=0)
+        first_row = (lax.iota(jnp.int32, columns) == 0)[:, None]
+        sin_part = jnp.where(first_row, parity[None, :], -sin_z)
     else:
         sin_part = -sin_z
     table_z = jnp.stack(
@@ -175,10 +176,9 @@
         )
         pback_real, _ = inverse_y(rounded(pb_real), rounded(pb_imag))
         is_first = me == 0
-        fixed_real = jnp.where(is_first, pback_real[:, 0], back_real[:, 0])
-        fixed_imag = jnp.where(is_first, pback_real[:, 1], back_imag[:, 0])
-        back_real = jnp.concatenate([fixed_real[:, None], back_real[:, 1:]], axis=1)
-        back_imag = jnp.concatenate([fixed_imag[:, None], back_imag[:, 1:]], axis=1)
+        packed = ((lax.iota(jnp.int32, per_device) == 0) & is_first)[None, :, None, None]
+        back_real = jnp.where(packed, pback_real[:, 0:1], back_real)
+        back_imag = jnp.where(packed, pback_real[:, 1:2], back_imag)
 
     outgoing = jnp.stack([back_real, back_imag], axis=1).astype(BF16)
     outgoing = outgoing.reshape(

time: 87.1 us -> 85.2 us (0.978)
  local copies, waits for them, and re-layouts: 13.1 us -> 11.7 us
    another operation x1 -> x0, local copies, waits for them, and re-layouts: 1.22 us -> none  [on_device(): jnp.stack([cos_z.reshape(devices, per_device, depth), sin_part.reshape(de...]
  transfers between devices with their start and end apart: 2 -> 2, of which waited for: 2 -> 2; matrix products, arithmetic and copies ran while one was open for 12% -> 13% of each run, Pallas kernels for 0% -> 0%
where the time goes in v11:
time: 85.2 us; the launch traced here: 84.6 us
  waiting for transfers between devices  30.2 us (35%)
  matrix products  17.8 us (21%)
  other arithmetic  13.1 us (15%)
  local copies, waits for them, and re-layouts  11.7 us (14%)
  starting transfers between devices  11.3 us (13%)
    all_to_all x1, waiting for transfers between devices, on_device(): lax.all_to_all(spectrum, ('row', 'col'), split_axis=0, concat_axis=0, til...  16.4 us
    all_to_all x1, waiting for transfers between devices, on_device(): lax.all_to_all(outgoing, ('row', 'col'), split_axis=0, concat_axis=0, til...  13.8 us
    all_to_all x1, starting transfers between devices, on_device(): lax.all_to_all(spectrum, ('row', 'col'), split_axis=0, concat_axis=0, til...  7.48 us
    dot_general x12, matrix products, mat(): term = jnp.einsum(spec, part, operand, preferred_element_type=F32)  6.77 us
    convert_element_type x2, local copies, waits for them, and re-layouts, split_parts(): return (high.astype(BF16), low.astype(BF16))  6.58 us
    sub x2, other arithmetic, phase_table(): cosine = outer_cos * inner_cos - outer_sin * inner_sin  4.46 us
    all_to_all x1, starting transfers between devices, on_device(): lax.all_to_all(outgoing, ('row', 'col'), split_axis=0, concat_axis=0, til...  3.84 us
    dot_general x1, matrix products, on_device(): jnp.einsum('...k,k->...', one_hot, parts, preferred_element_type=F32)  2.98 us
  transfers between devices with their start and end apart: 2, of which 2 were waited for; matrix products, arithmetic and copies ran while one was open for 13% of the time, Pallas kernels for 0%

profile of v11, /device:TPU:0, one launch (start us, length us, event | category | flops | bytes accessed | tf_op | source)
XLA Modules:
  0.0 84.6 jit_solution(7678722254501254975)
XLA Ops:
  1.0 0.7 reduce-precision_convert_fusion.7
  2.3 3.0 %fusion = f32[1,128,1024]{2,0,1:T(1,128)S(1)} fusion(s32[128,1024]{1,0:T(8,128)} %bitcast.335, s32[24]{0:T(128)S(1)} %and_select_fusion, bf16[8]{0:T(256)(128)(2,1)S(1)} %get-tuple-element.34, bf16[8]{0:T(256)(128)(2,1)S(1)} %get-tuple-element.33, bf16[8]{0:T(256)(128)(2,1)S(1)} %get-tuple-element.5), kind=kOutput, calls=%fused_computation | convolution fusion | flops 9437328 | bytes 1048720 | tf_op jit(solution)/shard_map/...k,k->.../dot_general | solution.py:107
  5.9 2.6 %multiply_subtract_fusion = (f32[32,1,16,1024]{3,0,2,1:T(8,128)S(1)}, f32[32,1,16,1024]{3,0,2,1:T(8,128)S(1)}) fusion(f32[32,1,16,1024]{3,2,0,1:T(8,128)S(1)} %bitcast.324, f32[32,1,16,1024]{3,2,0,1:T(8,128)S(1)} %bitcast.325, f32[32,1024]{1,0:T(8,128)S(1)} %mul.999, f32[32,1024]{1,0:T(8,128)S(1)} %mul.988, f32[1024]{0:T(1024)S(1)} %fusion.151, ...), kind=kLoop, calls=%fused_computation.17 | loop fusion | flops 4194304 | bytes 8655360 | tf_op jit(solution)/shard_map/sub | solution.py:45
  8.6 0.8 fusion.4
  9.7 1.3 %fusion.5 = f32[3,128,32,2,16]{1,2,4,3,0:T(8,128)S(1)} fusion(bf16[32,2,16,1024]{3,0,2,1:T(8,128)(2,1)S(1)} %get-tuple-element.9, bf16[3,1,128,1024]{3,2,1,0:T(8,128)(2,1)S(1)} %copy-done.3, f32[128,1024]{1,0:T(8,128)S(1)} %bitcast.316), kind=kOutput, calls=%fused_computation.10 | convolution fusion | flops 806879232 | bytes 4980736 | tf_op jit(solution)/shard_map/dpjz,cyz->dcpjy/dot_general | solution.py:133
  11.0 1.3 %fusion.7 = f32[3,128,32,2,16]{1,2,4,3,0:T(8,128)S(1)} fusion(bf16[32,2,16,1024]{3,0,2,1:T(8,128)(2,1)S(1)} %get-tuple-element.10, bf16[3,1,128,1024]{3,2,1,0:T(8,128)(2,1)S(1)} %copy-done.3, f32[128,1024]{1,0:T(8,128)S(1)} %bitcast.317), kind=kOutput, calls=%fused_computation.12 | convolution fusion | flops 807272448 | bytes 4980736 | tf_op jit(solution)/shard_map/dpjz,cyz->dcpjy/dot_general | solution.py:132
  12.3 1.4 %fusion.14 = bf16[32,3,2,16,128]{4,0,3,2,1:T(8,128)(2,1)S(1)} fusion(f32[3,128,32,2,16]{1,2,4,3,0:T(8,128)S(1)} %fusion.5, f32[3,128,32,2,16]{1,2,4,3,0:T(8,128)S(1)} %fusion.7, bf16[32,2,16,1024]{3,0,2,1:T(8,128)(2,1)S(1)} %get-tuple-element.10, bf16[3,1,128,1024]{3,2,1,0:T(8,128)(2,1)S(1)} %copy-done.3, f32[128,1024]{1,0:T(8,128)S(1)} %bitcast.318), kind=kOutput, calls=%fused_computation.36 | convolution fusion | flops 808058880 | bytes 7340032 | tf_op jit(solution)/shard_map/dpjz,cyz->dcpjy/dot_general | solution.py:131
  13.7 1.2 %copy.43 = bf16[32,3,2,16,128]{4,3,2,1,0:T(8,128)(2,1)} copy(bf16[32,3,2,16,128]{4,0,3,2,1:T(8,128)(2,1)S(1)} %fusion.14) | data formatting | bytes 1572864 | tf_op jit(solution)/shard_map/convert_element_type | solution.py:135
  14.8 7.5 %all-to-all-start = ((bf16[32,3,2,16,128]{4,3,2,1,0:T(8,128)(2,1)}), bf16[32,3,2,16,128]{4,3,2,1,0:T(8,128)(2,1)S(1)}, u32[]{:S(2)}, u32[]{:S(2)}) async-start(bf16[32,3,2,16,128]{4,3,2,1,0:T(8,128)(2,1)} %copy.43), calls=%async_computation | async-start | bytes 1572864 | tf_op jit(solution)/shard_map/all_to_all | solution.py:136
  23.1 1.8 %multiply_subtract_fusion.1 = (f32[16,32,512]{2,1,0:T(8,128)S(1)}, bf16[16,32,512]{2,1,0:T(8,128)(2,1)}, bf16[16,32,512]{2,1,0:T(8,128)(2,1)}, bf16[16,32,512]{2...) fusion(f32[32,512]{1,0:T(8,128)S(1)} %fusion.136, f32[16,512]{1,0:T(8,128)S(1)} %get-tuple-element.36, ...), kind=kLoop, calls=%fused_computation.65 | loop fusion | flops 3670016 | bytes 4390912 | tf_op jit(solution)/shard_map/sub | solution.py:45
  25.0 1.4 %fusion.35 = (bf16[512,512]{1,0:T(8,128)(2,1)S(1)}, bf16[512,512]{1,0:T(8,128)(2,1)}, bf16[512,512]{1,0:T(8,128)(2,1)}, bf16[512,512]{1,0:T(8,128)(2,1)}) fusion(f32[16,32,512]{2,1,0:T(8,128)S(1)} %get-tuple-element.21, f32[16,32,512]{2,1,0:T(8,128)S(1)} %get-tuple-element.26), kind=kLoop, calls=%fused_computation.63 | loop fusion | flops 2097152 | bytes 4194304 | tf_op jit(solution)/shard_map/convert_element_type | solution.py:28
  26.4 16.4 %all-to-all-done = bf16[32,3,2,16,128]{4,3,2,1,0:T(8,128)(2,1)S(1)} async-done(((bf16[32,3,2,16,128]{4,3,2,1,0:T(8,128)(2,1)}), bf16[32,3,2,16,128]{4,3,2,1,0:T(8,128)(2,1)S(1)}, u32[]{:S(2)}, u32[]{:S(2)}) %all-to-all-start) | async-done | bytes 786464 | tf_op jit(solution)/shard_map/all_to_all | solution.py:136
  42.8 1.7 %fusion.59 = f32[3,2,16,8,512]{4,3,2,1,0:T(8,128)S(1)} fusion(bf16[512,512,1,1,1]{1,0,4,3,2:T(8,128)(2,1)} %bitcast.334, bf16[8,4,3,1,2,16,128]{6,5,4,2,1,0,3:T(8,128)(2,1)S(1)} %bitcast.319), kind=kOutput, calls=%fused_computation.96 | convolution fusion | flops 402653184 | bytes 2883584 | tf_op jit(solution)/shard_map/yk,cpjxy->cpjxk/dot_general | solution.py:65
  44.5 0.6 convolution_add_fusion.3
  45.5 0.6 fusion.56
  46.2 0.6 convolution_add_fusion.2
  54.7 0.9 %pad_maximum_fusion.2 = bf16[3,2,16,8,1,4,128]{6,2,4,0,1,5,3:T(8,128)(2,1)} fusion(bf16[3,1,16,8,1,4,128]{6,2,4,0,1,5,3:T(8,128)(2,1)S(1)} %copy.49, bf16[3,1,16,8,1,4,128]{6,2,4,0,1,5,3:T(8,128)(2,1)S(1)} %copy.48), kind=kLoop, calls=%fused_computation.91 | loop fusion | flops 393216 | bytes 1572864 | tf_op jit(solution)/shard_map/stack | solution.py:183
  55.6 3.8 %all-to-all-start.1 = ((bf16[32,2,16,3,1,128]{5,2,4,3,1,0:T(8,128)(2,1)}), bf16[32,2,16,3,1,128]{5,2,4,3,1,0:T(8,128)(2,1)S(1)}, u32[]{:S(2)}, u32[]{:S(2)}) async-start(bf16[32,2,16,3,1,128]{5,2,4,3,1,0:T(8,128)(2,1)} %bitcast.330), calls=%async_computation.1 | async-start | bytes 1572864 | tf_op jit(solution)/shard_map/all_to_all | solution.py:190
  59.5 4.1 %copy.52 = bf16[32,2,16,1024]{3,2,1,0:T(8,128)(2,1)} copy(bf16[32,2,16,1024]{3,0,2,1:T(8,128)(2,1)} %copy-done) | data formatting | bytes 4194304 | tf_op jit(solution)/shard_map/convert_element_type | solution.py:28
  63.5 2.5 %copy.51 = bf16[32,2,16,1024]{3,2,1,0:T(8,128)(2,1)} copy(bf16[32,2,16,1024]{3,0,2,1:T(8,128)(2,1)S(1)} %get-tuple-element.10) | data formatting | bytes 4194304 | tf_op jit(solution)/shard_map/convert_element_type | solution.py:28
  66.1 13.8 %all-to-all-done.1 = bf16[32,2,16,3,1,128]{5,2,4,3,1,0:T(8,128)(2,1)S(1)} async-done(((bf16[32,2,16,3,1,128]{5,2,4,3,1,0:T(8,128)(2,1)}), bf16[32,2,16,3,1,128]{5,2,4,3,1,0:T(8,128)(2,1)S(1)}, u32[]{:S(2)}, u32[]{:S(2)}) %all-to-all-start.1) | async-done | bytes 786464 | tf_op jit(solution)/shard_map/all_to_all | solution.py:190
  80.7 1.0 %fusion.41 = f32[384,1024]{1,0:T(8,128)S(1)} fusion(bf16[1024,1024]{1,0:T(8,128)(2,1)S(1)} %bitcast.326, bf16[128,8,3,128]{3,2,1,0:T(4,128)(2,1)S(1)} %bitcast.327), kind=kOutput, calls=%fused_computation.70 | convolution fusion | flops 805306368 | bytes 4456448 | tf_op jit(solution)/shard_map/kr,kz->rz/dot_general | solution.py:202
  82.3 1.0 %convolution_add_fusion.4 = f32[384,1024]{1,0:T(8,128)S(1)} fusion(f32[384,1024]{1,0:T(8,128)S(1)} %fusion.41, bf16[1024,1024]{1,0:T(8,128)(2,1)S(1)} %bitcast.323, bf16[128,8,3,128]{3,2,1,0:T(4,128)(2,1)S(1)} %bitcast.328), kind=kOutput, calls=%fused_computation.35 | convolution fusion | flops 805699584 | bytes 6029312 | tf_op jit(solution)/shard_map/kr,kz->rz/dot_general | solution.py:202
  83.4 1.1 %add_convert_fusion = bf16[3,1,128,1024]{3,2,1,0:T(8,128)(2,1)} fusion(f32[3,1,128,1024]{3,2,1,0:T(8,128)S(1)} %bitcast.329, bf16[3,1,128,1024]{3,2,1,0:T(8,128)(2,1)S(1)} %copy-done.10), kind=kLoop, calls=%fused_computation.19 | loop fusion | flops 1179648 | bytes 3145728 | tf_op jit(solution)/shard_map/convert_element_type | solution.py:206
  (78 shorter events, 12.9 us)
Async XLA Ops:
  8.6 1.1 %copy-start.3 = (bf16[3,1,128,1024]{3,2,1,0:T(8,128)(2,1)S(1)}, bf16[3,1,128,1024]{3,2,1,0:T(8,128)(2,1)}, u32[]{:S(2)}) copy-start(bf16[3,1,128,1024]{3,2,1,0:T(8,128)(2,1)} %param.6) | copy-start | bytes 2359300
  9.4 1.6 %copy-start = (bf16[32,2,16,1024]{3,0,2,1:T(8,128)(2,1)}, bf16[32,2,16,1024]{3,0,2,1:T(8,128)(2,1)S(1)}, u32[]{:S(2)}) copy-start(bf16[32,2,16,1024]{3,0,2,1:T(8,128)(2,1)S(1)} %get-tuple-element.9) | copy-start | bytes 6291460
  14.8 27.9 %all-to-all-start = ((bf16[32,3,2,16,128]{4,3,2,1,0:T(8,128)(2,1)}), bf16[32,3,2,16,128]{4,3,2,1,0:T(8,128)(2,1)S(1)}, u32[]{:S(2)}, u32[]{:S(2)}) async-start(bf16[32,3,2,16,128]{4,3,2,1,0:T(8,128)(2,1)} %copy.43), calls=%async_computation | async-start | bytes 1572864 | tf_op jit(solution)/shard_map/all_to_all | solution.py:136
  42.8 1.7 %copy-start.8 = (bf16[16,32,512]{2,1,0:T(8,128)(2,1)S(1)}, bf16[16,32,512]{2,1,0:T(8,128)(2,1)}, u32[]{:S(2)}) copy-start(bf16[16,32,512]{2,1,0:T(8,128)(2,1)} %get-tuple-element.22) | copy-start | bytes 1572868
  44.5 1.0 %copy-start.9 = (bf16[16,32,512]{2,1,0:T(8,128)(2,1)S(1)}, bf16[16,32,512]{2,1,0:T(8,128)(2,1)}, u32[]{:S(2)}) copy-start(bf16[16,32,512]{2,1,0:T(8,128)(2,1)} %get-tuple-element.25) | copy-start | bytes 1572868
  45.1 1.1 %copy-start.7 = (bf16[16,32,512]{2,1,0:T(8,128)(2,1)S(1)}, bf16[16,32,512]{2,1,0:T(8,128)(2,1)}, u32[]{:S(2)}) copy-start(bf16[16,32,512]{2,1,0:T(8,128)(2,1)} %get-tuple-element.24) | copy-start | bytes 1572868
  46.9 0.7 copy-start.11
  48.6 1.0 %copy-start.6 = (bf16[512,512]{1,0:T(8,128)(2,1)S(1)}, bf16[512,512]{1,0:T(8,128)(2,1)}, u32[]{:S(2)}) copy-start(bf16[512,512]{1,0:T(8,128)(2,1)} %get-tuple-element.39) | copy-start | bytes 1572868
  49.0 1.1 %copy-start.5 = (bf16[512,512]{1,0:T(8,128)(2,1)S(1)}, bf16[512,512]{1,0:T(8,128)(2,1)}, u32[]{:S(2)}) copy-start(bf16[512,512]{1,0:T(8,128)(2,1)} %get-tuple-element.18) | copy-start | bytes 1572868
  51.4 1.0 %copy-start.4 = (bf16[512,512]{1,0:T(8,128)(2,1)S(1)}, bf16[512,512]{1,0:T(8,128)(2,1)}, u32[]{:S(2)}) copy-start(bf16[512,512]{1,0:T(8,128)(2,1)} %get-tuple-element.40) | copy-start | bytes 1572868
  55.6 24.2 %all-to-all-start.1 = ((bf16[32,2,16,3,1,128]{5,2,4,3,1,0:T(8,128)(2,1)}), bf16[32,2,16,3,1,128]{5,2,4,3,1,0:T(8,128)(2,1)S(1)}, u32[]{:S(2)}, u32[]{:S(2)}) async-start(bf16[32,2,16,3,1,128]{5,2,4,3,1,0:T(8,128)(2,1)} %bitcast.330), calls=%async_computation.1 | async-start | bytes 1572864 | tf_op jit(solution)/shard_map/all_to_all | solution.py:190
  63.5 16.3 %copy-start.12 = (f32[32,2,16]{2,1,0:T(2,128)S(1)}, f32[32,2,16]{2,1,0:T(2,128)}, u32[]{:S(2)}) copy-start(f32[32,2,16]{2,1,0:T(2,128)} %constant.134) | copy-start | bytes 12292
  66.1 14.6 %copy-start.2 = (bf16[32,2,16,1024]{3,2,1,0:T(8,128)(2,1)S(1)}, bf16[32,2,16,1024]{3,2,1,0:T(8,128)(2,1)}, u32[]{:S(2)}) copy-start(bf16[32,2,16,1024]{3,2,1,0:T(8,128)(2,1)} %copy.51) | copy-start | bytes 6291460
  80.7 1.6 %copy-start.1 = (bf16[32,2,16,1024]{3,2,1,0:T(8,128)(2,1)S(1)}, bf16[32,2,16,1024]{3,2,1,0:T(8,128)(2,1)}, u32[]{:S(2)}) copy-start(bf16[32,2,16,1024]{3,2,1,0:T(8,128)(2,1)} %copy.52) | copy-start | bytes 6291460
  82.3 1.1 %copy-start.10 = (bf16[3,1,128,1024]{3,2,1,0:T(8,128)(2,1)S(1)}, bf16[3,1,128,1024]{3,2,1,0:T(8,128)(2,1)}, u32[]{:S(2)}) copy-start(bf16[3,1,128,1024]{3,2,1,0:T(8,128)(2,1)} %param.7) | copy-start | bytes 2359300

commit v12 on v11

--- a/solution.py
+++ b/solution.py
@@ -103,8 +103,8 @@
     second = rounded(rest)
     parts = jnp.concatenate([first, second, rest - second]).astype(BF16)
     slots = lax.iota(jnp.int32, 3 * regions) % regions
-    one_hot = (region[..., None] == slots).astype(BF16)
-    cell_scale = jnp.einsum("...k,k->...", one_hot, parts, preferred_element_type=F32)
+    one_hot = (region[None] == slots.reshape((-1,) + (1,) * region.ndim)).astype(BF16)
+    cell_scale = jnp.einsum("k...,k->...", one_hot, parts, preferred_element_type=F32)
     electric = displacement.astype(F32) * cell_scale[None]
 
     cos_z, sin_z = phase_table(columns, depth, depth)

time: 85.2 us -> 88.7 us (1.041)
  waiting for transfers between devices: 30.2 us -> 33.3 us
  local copies, waits for them, and re-layouts: 11.7 us -> 9 us
  other arithmetic: 13.1 us -> 14.9 us
  matrix products: 17.8 us -> 19.3 us
    convert_element_type x2, local copies, waits for them, and re-layouts: 6.58 us -> 3.62 us  [split_parts(): return (high.astype(BF16), low.astype(BF16))]
    all_to_all x1, waiting for transfers between devices: 13.8 us -> 16.8 us  [on_device(): lax.all_to_all(outgoing, ('row', 'col'), split_axis=0, concat_axis=0, til...]
    eq x0 -> x1, other arithmetic: none -> 1.82 us  [on_device(): region[None] == slots.reshape((-1,) + (1,) * region.ndim)]
    dot_general x1, matrix products: 2.98 us -> 4.31 us  [on_device(): jnp.einsum('k...,k->...', one_hot, parts, preferred_element_type=F32)]
    unnamed x26 -> x28, local copies, waits for them, and re-layouts: 2.24 us -> 2.48 us
  transfers between devices with their start and end apart: 2 -> 2, of which waited for: 2 -> 2; matrix products, arithmetic and copies ran while one was open for 13% -> 9% of each run, Pallas kernels for 0% -> 0%
where the time goes in v12:
time: 88.7 us; the launch traced here: 88.2 us
  waiting for transfers between devices  33.3 us (38%)
  matrix products  19.3 us (22%)
  other arithmetic  14.9 us (17%)
  starting transfers between devices  11.1 us (13%)
  local copies, waits for them, and re-layouts  9 us (10%)
    all_to_all x1, waiting for transfers between devices, on_device(): lax.all_to_all(outgoing, ('row', 'col'), split_axis=0, concat_axis=0, til...  16.8 us
    all_to_all x1, waiting for transfers between devices, on_device(): lax.all_to_all(spectrum, ('row', 'col'), split_axis=0, concat_axis=0, til...  16.6 us
    all_to_all x1, starting transfers between devices, on_device(): lax.all_to_all(spectrum, ('row', 'col'), split_axis=0, concat_axis=0, til...  7.3 us
    dot_general x12, matrix products, mat(): term = jnp.einsum(spec, part, operand, preferred_element_type=F32)  6.78 us
    sub x2, other arithmetic, phase_table(): cosine = outer_cos * inner_cos - outer_sin * inner_sin  4.44 us
    dot_general x1, matrix products, on_device(): jnp.einsum('k...,k->...', one_hot, parts, preferred_element_type=F32)  4.31 us
    all_to_all x1, starting transfers between devices, on_device(): lax.all_to_all(outgoing, ('row', 'col'), split_axis=0, concat_axis=0, til...  3.84 us
    convert_element_type x2, local copies, waits for them, and re-layouts, split_parts(): return (high.astype(BF16), low.astype(BF16))  3.62 us
  transfers between devices with their start and end apart: 2, of which 2 were waited for; matrix products, arithmetic and copies ran while one was open for 9% of the time, Pallas kernels for 0%

profile of v12, /device:TPU:0, one launch (start us, length us, event | category | flops | bytes accessed | tf_op | source)
XLA Modules:
  0.0 88.2 jit_solution(13909116240457904646)
XLA Ops:
  1.7 0.7 reduce-precision_convert_fusion.7
  2.4 1.8 %broadcast_compare_fusion = pred[24,128,1024]{2,1,0:T(32,128)(4,1)S(1)} fusion(s32[128,1024]{1,0:T(8,128)S(1)} %bitcast.335, s32[24]{0:T(128)S(1)} %and_select_fusion), kind=kLoop, calls=%fused_computation.2 | loop fusion | flops 3145728 | bytes 3670112 | tf_op jit(solution)/shard_map/eq | solution.py:106
  4.2 4.3 %fusion = f32[1,128,1024]{2,0,1:T(1,128)S(1)} fusion(pred[24,128,1024]{2,1,0:T(32,128)(4,1)S(1)} %broadcast_compare_fusion, bf16[8]{0:T(256)(128)(2,1)S(1)} %get-tuple-element.34, bf16[8]{0:T(256)(128)(2,1)S(1)} %get-tuple-element.33, bf16[8]{0:T(256)(128)(2,1)S(1)} %get-tuple-element.5), kind=kOutput, calls=%fused_computation | convolution fusion | flops 6291600 | bytes 3670064 | tf_op jit(solution)/shard_map/k...,k->.../dot_general | solution.py:107
  9.1 2.6 %multiply_subtract_fusion = (f32[32,1,16,1024]{3,0,2,1:T(8,128)S(1)}, f32[32,1,16,1024]{3,0,2,1:T(8,128)S(1)}) fusion(f32[32,1,16,1024]{3,2,0,1:T(8,128)S(1)} %bitcast.325, f32[32,1,16,1024]{3,2,0,1:T(8,128)S(1)} %bitcast.324, f32[32,1024]{1,0:T(8,128)S(1)} %mul.999, f32[32,1024]{1,0:T(8,128)S(1)} %mul.988, f32[1024]{0:T(1024)S(1)} %fusion.149, ...), kind=kLoop, calls=%fused_computation.16 | loop fusion | flops 4194304 | bytes 8655360 | tf_op jit(solution)/shard_map/sub | solution.py:45
  11.7 0.8 fusion.2
  12.9 1.3 %fusion.5 = f32[3,128,32,2,16]{1,2,4,3,0:T(8,128)S(1)} fusion(bf16[32,2,16,1024]{3,0,2,1:T(8,128)(2,1)S(1)} %get-tuple-element.10, bf16[3,1,128,1024]{3,2,1,0:T(8,128)(2,1)S(1)} %copy-done.3, f32[128,1024]{1,0:T(8,128)S(1)} %bitcast.316), kind=kOutput, calls=%fused_computation.11 | convolution fusion | flops 807272448 | bytes 4980736 | tf_op jit(solution)/shard_map/dpjz,cyz->dcpjy/dot_general | solution.py:132
  14.2 1.5 %fusion.3 = f32[3,128,32,2,16]{1,2,4,3,0:T(8,128)S(1)} fusion(bf16[32,2,16,1024]{3,0,2,1:T(8,128)(2,1)S(1)} %get-tuple-element.9, bf16[3,1,128,1024]{3,2,1,0:T(8,128)(2,1)S(1)} %copy-done.3, f32[128,1024]{1,0:T(8,128)S(1)} %bitcast.317), kind=kOutput, calls=%fused_computation.9 | convolution fusion | flops 806879232 | bytes 4980736 | tf_op jit(solution)/shard_map/dpjz,cyz->dcpjy/dot_general | solution.py:133
  15.7 1.4 %fusion.12 = bf16[32,3,2,16,128]{4,0,3,2,1:T(8,128)(2,1)S(1)} fusion(f32[3,128,32,2,16]{1,2,4,3,0:T(8,128)S(1)} %fusion.3, f32[3,128,32,2,16]{1,2,4,3,0:T(8,128)S(1)} %fusion.5, bf16[32,2,16,1024]{3,0,2,1:T(8,128)(2,1)S(1)} %get-tuple-element.10, bf16[3,1,128,1024]{3,2,1,0:T(8,128)(2,1)S(1)} %copy-done.3, f32[128,1024]{1,0:T(8,128)S(1)} %bitcast.318), kind=kOutput, calls=%fused_computation.35 | convolution fusion | flops 808058880 | bytes 7340032 | tf_op jit(solution)/shard_map/dpjz,cyz->dcpjy/dot_general | solution.py:131
  17.0 1.2 %copy.28 = bf16[32,3,2,16,128]{4,3,2,1,0:T(8,128)(2,1)} copy(bf16[32,3,2,16,128]{4,0,3,2,1:T(8,128)(2,1)S(1)} %fusion.12) | data formatting | bytes 1572864 | tf_op jit(solution)/shard_map/convert_element_type | solution.py:135
  18.2 7.3 %all-to-all-start = ((bf16[32,3,2,16,128]{4,3,2,1,0:T(8,128)(2,1)}), bf16[32,3,2,16,128]{4,3,2,1,0:T(8,128)(2,1)S(1)}, u32[]{:S(2)}, u32[]{:S(2)}) async-start(bf16[32,3,2,16,128]{4,3,2,1,0:T(8,128)(2,1)} %copy.28), calls=%async_computation | async-start | bytes 1572864 | tf_op jit(solution)/shard_map/all_to_all | solution.py:136
  26.3 1.8 %multiply_subtract_fusion.1 = (f32[16,32,512]{2,1,0:T(8,128)S(1)}, bf16[16,32,512]{2,1,0:T(8,128)(2,1)}, bf16[16,32,512]{2,1,0:T(8,128)(2,1)}, bf16[16,32,512]{2...) fusion(f32[32,512]{1,0:T(8,128)S(1)} %fusion.134, f32[16,512]{1,0:T(8,128)S(1)} %get-tuple-element.36, ...), kind=kLoop, calls=%fused_computation.64 | loop fusion | flops 3670016 | bytes 4390912 | tf_op jit(solution)/shard_map/sub | solution.py:45
  28.1 1.4 %fusion.33 = (bf16[512,512]{1,0:T(8,128)(2,1)}, bf16[512,512]{1,0:T(8,128)(2,1)}, bf16[512,512]{1,0:T(8,128)(2,1)}, bf16[512,512]{1,0:T(8,128)(2,1)S(1)}) fusion(f32[16,32,512]{2,1,0:T(8,128)S(1)} %get-tuple-element.21, f32[16,32,512]{2,1,0:T(8,128)S(1)} %get-tuple-element.26), kind=kLoop, calls=%fused_computation.62 | loop fusion | flops 2097152 | bytes 4194304 | tf_op jit(solution)/shard_map/convert_element_type | solution.py:28
  29.6 16.6 %all-to-all-done = bf16[32,3,2,16,128]{4,3,2,1,0:T(8,128)(2,1)S(1)} async-done(((bf16[32,3,2,16,128]{4,3,2,1,0:T(8,128)(2,1)}), bf16[32,3,2,16,128]{4,3,2,1,0:T(8,128)(2,1)S(1)}, u32[]{:S(2)}, u32[]{:S(2)}) %all-to-all-start) | async-done | bytes 786464 | tf_op jit(solution)/shard_map/all_to_all | solution.py:136
  46.1 1.7 %fusion.57 = f32[3,2,16,8,512]{4,3,2,1,0:T(8,128)S(1)} fusion(bf16[512,512,1,1,1]{1,0,4,3,2:T(8,128)(2,1)} %bitcast.334, bf16[8,4,3,1,2,16,128]{6,5,4,2,1,0,3:T(8,128)(2,1)S(1)} %bitcast.319), kind=kOutput, calls=%fused_computation.95 | convolution fusion | flops 402653184 | bytes 2883584 | tf_op jit(solution)/shard_map/yk,cpjxy->cpjxk/dot_general | solution.py:65
  47.9 0.6 convolution_add_fusion.3
  58.1 0.9 %pad_maximum_fusion.2 = bf16[3,2,16,8,1,4,128]{6,2,4,0,1,5,3:T(8,128)(2,1)} fusion(bf16[3,1,16,8,1,4,128]{6,2,4,0,1,5,3:T(8,128)(2,1)S(1)} %copy.34, bf16[3,1,16,8,1,4,128]{6,2,4,0,1,5,3:T(8,128)(2,1)S(1)} %copy.33), kind=kLoop, calls=%fused_computation.90 | loop fusion | flops 393216 | bytes 1572864 | tf_op jit(solution)/shard_map/stack | solution.py:183
  59.0 3.8 %all-to-all-start.1 = ((bf16[32,2,16,3,1,128]{5,2,4,3,1,0:T(8,128)(2,1)}), bf16[32,2,16,3,1,128]{5,2,4,3,1,0:T(8,128)(2,1)S(1)}, u32[]{:S(2)}, u32[]{:S(2)}) async-start(bf16[32,2,16,3,1,128]{5,2,4,3,1,0:T(8,128)(2,1)} %bitcast.330), calls=%async_computation.1 | async-start | bytes 1572864 | tf_op jit(solution)/shard_map/all_to_all | solution.py:190
  62.9 2.5 %copy.36 = bf16[32,2,16,1024]{3,2,1,0:T(8,128)(2,1)} copy(bf16[32,2,16,1024]{3,0,2,1:T(8,128)(2,1)S(1)} %get-tuple-element.10) | data formatting | bytes 4194304 | tf_op jit(solution)/shard_map/convert_element_type | solution.py:28
  65.3 1.2 %copy.37 = bf16[32,2,16,1024]{3,2,1,0:T(8,128)(2,1)S(1)} copy(bf16[32,2,16,1024]{3,0,2,1:T(8,128)(2,1)S(1)} %copy-done.1) | data formatting | bytes 4194304 | tf_op jit(solution)/shard_map/convert_element_type | solution.py:28
  66.5 16.8 %all-to-all-done.1 = bf16[32,2,16,3,1,128]{5,2,4,3,1,0:T(8,128)(2,1)S(1)} async-done(((bf16[32,2,16,3,1,128]{5,2,4,3,1,0:T(8,128)(2,1)}), bf16[32,2,16,3,1,128]{5,2,4,3,1,0:T(8,128)(2,1)S(1)}, u32[]{:S(2)}, u32[]{:S(2)}) %all-to-all-start.1) | async-done | bytes 786464 | tf_op jit(solution)/shard_map/all_to_all | solution.py:190
  84.1 0.8 copy-done.2
  84.9 1.0 %fusion.39 = f32[384,1024]{1,0:T(8,128)S(1)} fusion(bf16[1024,1024]{1,0:T(8,128)(2,1)S(1)} %bitcast.326, bf16[128,8,3,128]{3,2,1,0:T(4,128)(2,1)S(1)} %bitcast.327), kind=kOutput, calls=%fused_computation.69 | convolution fusion | flops 805306368 | bytes 4456448 | tf_op jit(solution)/shard_map/kr,kz->rz/dot_general | solution.py:202
  85.9 1.0 %convolution_add_fusion.4 = f32[384,1024]{1,0:T(8,128)S(1)} fusion(f32[384,1024]{1,0:T(8,128)S(1)} %fusion.39, bf16[1024,1024]{1,0:T(8,128)(2,1)S(1)} %bitcast.323, bf16[128,8,3,128]{3,2,1,0:T(4,128)(2,1)S(1)} %bitcast.328), kind=kOutput, calls=%fused_computation.34 | convolution fusion | flops 805699584 | bytes 6029312 | tf_op jit(solution)/shard_map/kr,kz->rz/dot_general | solution.py:202
  87.0 1.1 %add_convert_fusion = bf16[3,1,128,1024]{3,2,1,0:T(8,128)(2,1)} fusion(f32[3,1,128,1024]{3,2,1,0:T(8,128)S(1)} %bitcast.329, bf16[3,1,128,1024]{3,2,1,0:T(8,128)(2,1)S(1)} %copy-done.10), kind=kLoop, calls=%fused_computation.18 | loop fusion | flops 1179648 | bytes 3145728 | tf_op jit(solution)/shard_map/convert_element_type | solution.py:206
  (81 shorter events, 13.6 us)
Async XLA Ops:
  0.0 2.4 %copy-start.11 = (s32[1,128,1024]{2,1,0:T(8,128)S(1)}, s32[1,128,1024]{2,1,0:T(8,128)}, u32[]{:S(2)}) copy-start(s32[1,128,1024]{2,1,0:T(8,128)} %param.8) | copy-start | bytes 1572868
  11.7 1.1 %copy-start.3 = (bf16[3,1,128,1024]{3,2,1,0:T(8,128)(2,1)S(1)}, bf16[3,1,128,1024]{3,2,1,0:T(8,128)(2,1)}, u32[]{:S(2)}) copy-start(bf16[3,1,128,1024]{3,2,1,0:T(8,128)(2,1)} %param.6) | copy-start | bytes 2359300
  12.5 1.6 %copy-start = (bf16[32,2,16,1024]{3,0,2,1:T(8,128)(2,1)}, bf16[32,2,16,1024]{3,0,2,1:T(8,128)(2,1)S(1)}, u32[]{:S(2)}) copy-start(bf16[32,2,16,1024]{3,0,2,1:T(8,128)(2,1)S(1)} %get-tuple-element.9) | copy-start | bytes 6291460
  18.2 27.9 %all-to-all-start = ((bf16[32,3,2,16,128]{4,3,2,1,0:T(8,128)(2,1)}), bf16[32,3,2,16,128]{4,3,2,1,0:T(8,128)(2,1)S(1)}, u32[]{:S(2)}, u32[]{:S(2)}) async-start(bf16[32,3,2,16,128]{4,3,2,1,0:T(8,128)(2,1)} %copy.28), calls=%async_computation | async-start | bytes 1572864 | tf_op jit(solution)/shard_map/all_to_all | solution.py:136
  46.1 1.7 %copy-start.8 = (bf16[16,32,512]{2,1,0:T(8,128)(2,1)S(1)}, bf16[16,32,512]{2,1,0:T(8,128)(2,1)}, u32[]{:S(2)}) copy-start(bf16[16,32,512]{2,1,0:T(8,128)(2,1)} %get-tuple-element.22) | copy-start | bytes 1572868
  47.8 1.0 %copy-start.9 = (bf16[16,32,512]{2,1,0:T(8,128)(2,1)S(1)}, bf16[16,32,512]{2,1,0:T(8,128)(2,1)}, u32[]{:S(2)}) copy-start(bf16[16,32,512]{2,1,0:T(8,128)(2,1)} %get-tuple-element.25) | copy-start | bytes 1572868
  48.5 1.1 %copy-start.7 = (bf16[16,32,512]{2,1,0:T(8,128)(2,1)S(1)}, bf16[16,32,512]{2,1,0:T(8,128)(2,1)}, u32[]{:S(2)}) copy-start(bf16[16,32,512]{2,1,0:T(8,128)(2,1)} %get-tuple-element.24) | copy-start | bytes 1572868
  49.6 0.7 copy-start.12
  51.8 1.0 %copy-start.6 = (bf16[512,512]{1,0:T(8,128)(2,1)S(1)}, bf16[512,512]{1,0:T(8,128)(2,1)}, u32[]{:S(2)}) copy-start(bf16[512,512]{1,0:T(8,128)(2,1)} %get-tuple-element.18) | copy-start | bytes 1572868
  52.1 1.1 %copy-start.5 = (bf16[512,512]{1,0:T(8,128)(2,1)S(1)}, bf16[512,512]{1,0:T(8,128)(2,1)}, u32[]{:S(2)}) copy-start(bf16[512,512]{1,0:T(8,128)(2,1)} %get-tuple-element.39) | copy-start | bytes 1572868
  54.5 1.0 %copy-start.4 = (bf16[512,512]{1,0:T(8,128)(2,1)S(1)}, bf16[512,512]{1,0:T(8,128)(2,1)}, u32[]{:S(2)}) copy-start(bf16[512,512]{1,0:T(8,128)(2,1)} %get-tuple-element.17) | copy-start | bytes 1572868
  59.0 24.2 %all-to-all-start.1 = ((bf16[32,2,16,3,1,128]{5,2,4,3,1,0:T(8,128)(2,1)}), bf16[32,2,16,3,1,128]{5,2,4,3,1,0:T(8,128)(2,1)S(1)}, u32[]{:S(2)}, u32[]{:S(2)}) async-start(bf16[32,2,16,3,1,128]{5,2,4,3,1,0:T(8,128)(2,1)} %bitcast.330), calls=%async_computation.1 | async-start | bytes 1572864 | tf_op jit(solution)/shard_map/all_to_all | solution.py:190
  62.9 2.5 %copy-start.1 = (bf16[32,2,16,1024]{3,0,2,1:T(8,128)(2,1)S(1)}, bf16[32,2,16,1024]{3,0,2,1:T(8,128)(2,1)}, u32[]{:S(2)}) copy-start(bf16[32,2,16,1024]{3,0,2,1:T(8,128)(2,1)} %copy-done) | copy-start | bytes 6291460
  65.3 17.9 %copy-start.13 = (f32[32,2,16]{2,1,0:T(2,128)S(1)}, f32[32,2,16]{2,1,0:T(2,128)}, u32[]{:S(2)}) copy-start(f32[32,2,16]{2,1,0:T(2,128)} %constant.134) | copy-start | bytes 12292
  83.3 1.6 %copy-start.2 = (bf16[32,2,16,1024]{3,2,1,0:T(8,128)(2,1)S(1)}, bf16[32,2,16,1024]{3,2,1,0:T(8,128)(2,1)}, u32[]{:S(2)}) copy-start(bf16[32,2,16,1024]{3,2,1,0:T(8,128)(2,1)} %copy.36) | copy-start | bytes 6291460
  85.9 1.1 %copy-start.10 = (bf16[3,1,128,1024]{3,2,1,0:T(8,128)(2,1)S(1)}, bf16[3,1,128,1024]{3,2,1,0:T(8,128)(2,1)}, u32[]{:S(2)}) copy-start(bf16[3,1,128,1024]{3,2,1,0:T(8,128)(2,1)} %param.7) | copy-start | bytes 2359300

commit v13 on v11

--- a/solution.py
+++ b/solution.py
@@ -197,10 +197,11 @@
         weight[:] = 2.0 / depth
         weight[0, :, 0] = 1.0 / depth
     weight = jnp.asarray(weight.reshape(2 * columns, 1))
-    weighted = (returned.astype(F32) * weight).astype(BF16)
+    back_high = (z_high.astype(F32) * weight).astype(BF16)
+    back_low = (z_low.astype(F32) * weight).astype(BF16)
     spec_back = "kr,kz->rz"
-    field = jnp.einsum(spec_back, weighted, z_high, preferred_element_type=F32) + jnp.einsum(
-        spec_back, weighted, z_low, preferred_element_type=F32
+    field = jnp.einsum(spec_back, returned, back_high, preferred_element_type=F32) + jnp.einsum(
+        spec_back, returned, back_low, preferred_element_type=F32
     )
     field = field.reshape(members, local_x, local_y, depth)
     return (magnetic.astype(F32) + field).astype(BF16)

time: 85.2 us -> 84.4 us (level)
  local copies, waits for them, and re-layouts: 11.7 us -> 7.59 us
  matrix products: 17.8 us -> 19.3 us
  other arithmetic: 13.1 us -> 14.4 us
    convert_element_type x3 -> x2, local copies, waits for them, and re-layouts: 7.12 us -> 3.66 us  [the longest x1 2.5 us: on_device(): back_high = (z_high.astype(F32) * weight).astype(BF16)]
    convert_element_type x1, other arithmetic: 0.27 us -> 2.42 us  [on_device(): back_low = (z_low.astype(F32) * weight).astype(BF16)]
    dot_general x2, matrix products: 2.03 us -> 3.62 us  [the longest x1 2.61 us: on_device(): jnp.einsum(spec_back, returned, back_high, preferred_element_type=F32)]
    unnamed x26 -> x22, local copies, waits for them, and re-layouts: 2.24 us -> 1.02 us
    convert_element_type x2 -> x1, other arithmetic: 2.21 us -> 1.46 us  [split_parts(): return (high.astype(BF16), low.astype(BF16))]
  transfers between devices with their start and end apart: 2 -> 2, of which waited for: 2 -> 2; matrix products, arithmetic and copies ran while one was open for 13% -> 12% of each run, Pallas kernels for 0% -> 0%
where the time goes in v13:
time: 84.4 us; the launch traced here: 83.8 us
  waiting for transfers between devices  30.7 us (36%)
  matrix products  19.3 us (23%)
  other arithmetic  14.4 us (17%)
  starting transfers between devices  11.3 us (13%)
  local copies, waits for them, and re-layouts  7.59 us (9%)
    all_to_all x1, waiting for transfers between devices, on_device(): lax.all_to_all(spectrum, ('row', 'col'), split_axis=0, concat_axis=0, til...  16.4 us
    all_to_all x1, waiting for transfers between devices, on_device(): lax.all_to_all(outgoing, ('row', 'col'), split_axis=0, concat_axis=0, til...  14.3 us
    all_to_all x1, starting transfers between devices, on_device(): lax.all_to_all(spectrum, ('row', 'col'), split_axis=0, concat_axis=0, til...  7.48 us
    dot_general x12, matrix products, mat(): term = jnp.einsum(spec, part, operand, preferred_element_type=F32)  6.78 us
    sub x2, other arithmetic, phase_table(): cosine = outer_cos * inner_cos - outer_sin * inner_sin  4.45 us
    all_to_all x1, starting transfers between devices, on_device(): lax.all_to_all(outgoing, ('row', 'col'), split_axis=0, concat_axis=0, til...  3.83 us
    dot_general x1, matrix products, on_device(): jnp.einsum('...k,k->...', one_hot, parts, preferred_element_type=F32)  2.98 us
    dot_general x1, matrix products, on_device(): jnp.einsum(spec_back, returned, back_high, preferred_element_type=F32)  2.61 us
  transfers between devices with their start and end apart: 2, of which 2 were waited for; matrix products, arithmetic and copies ran while one was open for 12% of the time, Pallas kernels for 0%

profile of v13, /device:TPU:0, one launch (start us, length us, event | category | flops | bytes accessed | tf_op | source)
XLA Modules:
  0.0 83.8 jit_solution(960263851809437453)
XLA Ops:
  1.0 0.7 reduce-precision_convert_fusion.7
  2.3 3.0 %fusion = f32[1,128,1024]{2,0,1:T(1,128)S(1)} fusion(s32[128,1024]{1,0:T(8,128)} %bitcast.335, s32[24]{0:T(128)S(1)} %and_select_fusion, bf16[8]{0:T(256)(128)(2,1)S(1)} %get-tuple-element.34, bf16[8]{0:T(256)(128)(2,1)S(1)} %get-tuple-element.33, bf16[8]{0:T(256)(128)(2,1)S(1)} %get-tuple-element.5), kind=kOutput, calls=%fused_computation | convolution fusion | flops 9437328 | bytes 1048720 | tf_op jit(solution)/shard_map/...k,k->.../dot_general | solution.py:107
  5.9 2.6 %multiply_subtract_fusion = (f32[32,1,16,1024]{3,0,2,1:T(8,128)S(1)}, f32[32,1,16,1024]{3,0,2,1:T(8,128)S(1)}) fusion(f32[32,1,16,1024]{3,2,0,1:T(8,128)S(1)} %bitcast.321, f32[32,1,16,1024]{3,2,0,1:T(8,128)S(1)} %bitcast.322, f32[32,1024]{1,0:T(8,128)S(1)} %mul.1017, f32[32,1024]{1,0:T(8,128)S(1)} %mul.1006, f32[1024]{0:T(1024)S(1)} %fusion.151, ...), kind=kLoop, calls=%fused_computation.19 | loop fusion | flops 4194304 | bytes 8655360 | tf_op jit(solution)/shard_map/sub | solution.py:45
  8.6 1.3 %fusion.7 = f32[3,128,32,2,16]{1,2,4,3,0:T(8,128)S(1)} fusion(bf16[3,1,128,1024]{3,2,1,0:T(8,128)(2,1)S(1)} %copy-done.10, f32[128,1024]{1,0:T(8,128)S(1)} %bitcast.332, f32[32,1,16,1024]{3,0,2,1:T(8,128)S(1)} %get-tuple-element.8, f32[32,1,16,1024]{3,0,2,1:T(8,128)S(1)} %get-tuple-element.7), kind=kOutput, calls=%fused_computation.14 | convolution fusion | flops 810418176 | bytes 7077888 | tf_op jit(solution)/shard_map/dpjz,cyz->dcpjy/dot_general | solution.py:132
  9.9 1.3 %fusion.5 = f32[3,128,32,2,16]{1,2,4,3,0:T(8,128)S(1)} fusion(bf16[3,1,128,1024]{3,2,1,0:T(8,128)(2,1)S(1)} %copy-done.10, f32[128,1024]{1,0:T(8,128)S(1)} %bitcast.333, f32[32,1,16,1024]{3,0,2,1:T(8,128)S(1)} %get-tuple-element.8, f32[32,1,16,1024]{3,0,2,1:T(8,128)S(1)} %get-tuple-element.7), kind=kOutput, calls=%fused_computation.12 | convolution fusion | flops 811073536 | bytes 7077888 | tf_op jit(solution)/shard_map/dpjz,cyz->dcpjy/dot_general | solution.py:133
  11.2 1.3 %fusion.14 = bf16[32,3,2,16,128]{4,0,3,2,1:T(8,128)(2,1)S(1)} fusion(f32[3,128,32,2,16]{1,2,4,3,0:T(8,128)S(1)} %fusion.5, f32[3,128,32,2,16]{1,2,4,3,0:T(8,128)S(1)} %fusion.7, bf16[3,1,128,1024]{3,2,1,0:T(8,128)(2,1)S(1)} %copy-done.10, f32[128,1024]{1,0:T(8,128)S(1)} %bitcast.334, f32[32,1,16,1024]{3,0,2,1:T(8,128)S(1)} %get-tuple-element.8, ...), kind=kOutput, calls=%fused_computation.37 | convolution fusion | flops 811204608 | bytes 9437184 | tf_op jit(solution)/shard_map/dpjz,cyz->dcpjy/dot_general | solution.py:131
  12.5 1.2 %copy.43 = bf16[32,3,2,16,128]{4,3,2,1,0:T(8,128)(2,1)} copy(bf16[32,3,2,16,128]{4,0,3,2,1:T(8,128)(2,1)S(1)} %fusion.14) | data formatting | bytes 1572864 | tf_op jit(solution)/shard_map/convert_element_type | solution.py:135
  13.6 7.5 %all-to-all-start = ((bf16[32,3,2,16,128]{4,3,2,1,0:T(8,128)(2,1)}), bf16[32,3,2,16,128]{4,3,2,1,0:T(8,128)(2,1)S(1)}, u32[]{:S(2)}, u32[]{:S(2)}) async-start(bf16[32,3,2,16,128]{4,3,2,1,0:T(8,128)(2,1)} %copy.43), calls=%async_computation | async-start | bytes 1572864 | tf_op jit(solution)/shard_map/all_to_all | solution.py:136
  21.9 1.8 %multiply_subtract_fusion.1 = (f32[16,32,512]{2,1,0:T(8,128)S(1)}, bf16[16,32,512]{2,1,0:T(8,128)(2,1)}, bf16[16,32,512]{2,1,0:T(8,128)(2,1)}, bf16[16,32,512]{2...) fusion(f32[32,512]{1,0:T(8,128)S(1)} %fusion.136, f32[16,512]{1,0:T(8,128)S(1)} %get-tuple-element.36, ...), kind=kLoop, calls=%fused_computation.66 | loop fusion | flops 3670016 | bytes 4390912 | tf_op jit(solution)/shard_map/sub | solution.py:45
  23.8 1.5 %fusion.35 = (bf16[512,512]{1,0:T(8,128)(2,1)S(1)}, bf16[512,512]{1,0:T(8,128)(2,1)}, bf16[512,512]{1,0:T(8,128)(2,1)}, bf16[512,512]{1,0:T(8,128)(2,1)}) fusion(f32[16,32,512]{2,1,0:T(8,128)S(1)} %get-tuple-element.21, f32[16,32,512]{2,1,0:T(8,128)S(1)} %get-tuple-element.26), kind=kLoop, calls=%fused_computation.64 | loop fusion | flops 2097152 | bytes 4194304 | tf_op jit(solution)/shard_map/convert_element_type | solution.py:28
  25.2 16.4 %all-to-all-done = bf16[32,3,2,16,128]{4,3,2,1,0:T(8,128)(2,1)S(1)} async-done(((bf16[32,3,2,16,128]{4,3,2,1,0:T(8,128)(2,1)}), bf16[32,3,2,16,128]{4,3,2,1,0:T(8,128)(2,1)S(1)}, u32[]{:S(2)}, u32[]{:S(2)}) %all-to-all-start) | async-done | bytes 786464 | tf_op jit(solution)/shard_map/all_to_all | solution.py:136
  41.6 1.7 %fusion.59 = f32[3,2,16,8,512]{4,3,2,1,0:T(8,128)S(1)} fusion(bf16[512,512,1,1,1]{1,0,4,3,2:T(8,128)(2,1)} %bitcast.331, bf16[8,4,3,1,2,16,128]{6,5,4,2,1,0,3:T(8,128)(2,1)S(1)} %bitcast.316), kind=kOutput, calls=%fused_computation.97 | convolution fusion | flops 402653184 | bytes 2883584 | tf_op jit(solution)/shard_map/yk,cpjxy->cpjxk/dot_general | solution.py:65
  43.3 0.6 convolution_add_fusion.3
  44.3 0.6 fusion.56
  45.0 0.6 convolution_add_fusion.2
  53.2 0.9 %pad_maximum_fusion.2 = bf16[3,2,16,8,1,4,128]{6,2,4,0,1,5,3:T(8,128)(2,1)} fusion(bf16[3,1,16,8,1,4,128]{6,2,4,0,1,5,3:T(8,128)(2,1)S(1)} %copy.49, bf16[3,1,16,8,1,4,128]{6,2,4,0,1,5,3:T(8,128)(2,1)S(1)} %copy.48), kind=kLoop, calls=%fused_computation.92 | loop fusion | flops 393216 | bytes 1572864 | tf_op jit(solution)/shard_map/stack | solution.py:183
  54.1 3.8 %all-to-all-start.1 = ((bf16[32,2,16,3,1,128]{5,2,4,3,1,0:T(8,128)(2,1)}), bf16[32,2,16,3,1,128]{5,2,4,3,1,0:T(8,128)(2,1)S(1)}, u32[]{:S(2)}, u32[]{:S(2)}) async-start(bf16[32,2,16,3,1,128]{5,2,4,3,1,0:T(8,128)(2,1)} %bitcast.327), calls=%async_computation.1 | async-start | bytes 1572864 | tf_op jit(solution)/shard_map/all_to_all | solution.py:190
  58.0 2.4 %multiply_convert_fusion = (bf16[32,2,16,1024]{3,0,2,1:T(8,128)(2,1)S(1)}, bf16[32,2,16,1024]{3,0,2,1:T(8,128)(2,1)S(1)}) fusion(f32[32,2,16]{0,2,1:T(8,128)S(1)} %copy-done.9, f32[32,1,16,1024]{3,0,2,1:T(8,128)} %copy-done, f32[32,1,16,1024]{3,0,2,1:T(8,128)S(1)} %get-tuple-element.7), kind=kLoop, calls=%fused_computation.8 | loop fusion | flops 11534336 | bytes 8392704 | tf_op jit(solution)/shard_map/convert_element_type | solution.py:201
  60.4 1.2 %copy.52 = bf16[32,2,16,1024]{3,2,1,0:T(8,128)(2,1)S(1)} copy(bf16[32,2,16,1024]{3,0,2,1:T(8,128)(2,1)S(1)} %get-tuple-element.9) | data formatting | bytes 4194304 | tf_op jit(solution)/shard_map/convert_element_type | solution.py:201
  61.6 2.5 %copy.51 = bf16[32,2,16,1024]{3,2,1,0:T(8,128)(2,1)} copy(bf16[32,2,16,1024]{3,0,2,1:T(8,128)(2,1)S(1)} %get-tuple-element.10) | data formatting | bytes 4194304 | tf_op jit(solution)/shard_map/convert_element_type | solution.py:200
  64.1 14.3 %all-to-all-done.1 = bf16[32,2,16,3,1,128]{5,2,4,3,1,0:T(8,128)(2,1)S(1)} async-done(((bf16[32,2,16,3,1,128]{5,2,4,3,1,0:T(8,128)(2,1)}), bf16[32,2,16,3,1,128]{5,2,4,3,1,0:T(8,128)(2,1)S(1)}, u32[]{:S(2)}, u32[]{:S(2)}) %all-to-all-start.1) | async-done | bytes 786464 | tf_op jit(solution)/shard_map/all_to_all | solution.py:190
  78.9 2.6 %fusion.41 = f32[384,1024]{1,0:T(8,128)S(1)} fusion(bf16[1024,1024]{1,0:T(8,128)(2,1)} %bitcast.323, bf16[128,8,3,128]{3,2,1,0:T(4,128)(2,1)S(1)} %bitcast.324), kind=kOutput, calls=%fused_computation.71 | convolution fusion | flops 805306368 | bytes 4456448 | tf_op jit(solution)/shard_map/kr,kz->rz/dot_general | solution.py:203
  81.5 1.0 %convolution_add_fusion.4 = f32[384,1024]{1,0:T(8,128)S(1)} fusion(f32[384,1024]{1,0:T(8,128)S(1)} %fusion.41, bf16[1024,1024]{1,0:T(8,128)(2,1)S(1)} %bitcast.320, bf16[128,8,3,128]{3,2,1,0:T(4,128)(2,1)S(1)} %bitcast.325), kind=kOutput, calls=%fused_computation.36 | convolution fusion | flops 805699584 | bytes 6029312 | tf_op jit(solution)/shard_map/kr,kz->rz/dot_general | solution.py:203
  82.7 1.1 %add_convert_fusion = bf16[3,1,128,1024]{3,2,1,0:T(8,128)(2,1)} fusion(f32[3,1,128,1024]{3,2,1,0:T(8,128)S(1)} %bitcast.326, bf16[3,1,128,1024]{3,2,1,0:T(8,128)(2,1)S(1)} %copy-done.7), kind=kLoop, calls=%fused_computation.21 | loop fusion | flops 1179648 | bytes 3145728 | tf_op jit(solution)/shard_map/convert_element_type | solution.py:207
  (73 shorter events, 11.4 us)
Async XLA Ops:
  5.9 2.6 %copy-start.10 = (bf16[3,1,128,1024]{3,2,1,0:T(8,128)(2,1)S(1)}, bf16[3,1,128,1024]{3,2,1,0:T(8,128)(2,1)}, u32[]{:S(2)}) copy-start(bf16[3,1,128,1024]{3,2,1,0:T(8,128)(2,1)} %param.6) | copy-start | bytes 2359300
  8.6 2.6 %copy-start = (f32[32,1,16,1024]{3,0,2,1:T(8,128)}, f32[32,1,16,1024]{3,0,2,1:T(8,128)S(1)}, u32[]{:S(2)}) copy-start(f32[32,1,16,1024]{3,0,2,1:T(8,128)S(1)} %get-tuple-element.8) | copy-start | bytes 6291460
  13.6 27.9 %all-to-all-start = ((bf16[32,3,2,16,128]{4,3,2,1,0:T(8,128)(2,1)}), bf16[32,3,2,16,128]{4,3,2,1,0:T(8,128)(2,1)S(1)}, u32[]{:S(2)}, u32[]{:S(2)}) async-start(bf16[32,3,2,16,128]{4,3,2,1,0:T(8,128)(2,1)} %copy.43), calls=%async_computation | async-start | bytes 1572864 | tf_op jit(solution)/shard_map/all_to_all | solution.py:136
  41.6 1.7 %copy-start.5 = (bf16[16,32,512]{2,1,0:T(8,128)(2,1)S(1)}, bf16[16,32,512]{2,1,0:T(8,128)(2,1)}, u32[]{:S(2)}) copy-start(bf16[16,32,512]{2,1,0:T(8,128)(2,1)} %get-tuple-element.22) | copy-start | bytes 1572868
  43.3 1.0 %copy-start.6 = (bf16[16,32,512]{2,1,0:T(8,128)(2,1)S(1)}, bf16[16,32,512]{2,1,0:T(8,128)(2,1)}, u32[]{:S(2)}) copy-start(bf16[16,32,512]{2,1,0:T(8,128)(2,1)} %get-tuple-element.25) | copy-start | bytes 1572868
  43.9 1.1 %copy-start.4 = (bf16[16,32,512]{2,1,0:T(8,128)(2,1)S(1)}, bf16[16,32,512]{2,1,0:T(8,128)(2,1)}, u32[]{:S(2)}) copy-start(bf16[16,32,512]{2,1,0:T(8,128)(2,1)} %get-tuple-element.24) | copy-start | bytes 1572868
  45.7 0.7 copy-start.8
  47.0 1.3 %copy-start.3 = (bf16[512,512]{1,0:T(8,128)(2,1)S(1)}, bf16[512,512]{1,0:T(8,128)(2,1)}, u32[]{:S(2)}) copy-start(bf16[512,512]{1,0:T(8,128)(2,1)} %get-tuple-element.39) | copy-start | bytes 1572868
  47.4 1.1 %copy-start.2 = (bf16[512,512]{1,0:T(8,128)(2,1)S(1)}, bf16[512,512]{1,0:T(8,128)(2,1)}, u32[]{:S(2)}) copy-start(bf16[512,512]{1,0:T(8,128)(2,1)} %get-tuple-element.18) | copy-start | bytes 1572868
  49.8 1.0 %copy-start.1 = (bf16[512,512]{1,0:T(8,128)(2,1)S(1)}, bf16[512,512]{1,0:T(8,128)(2,1)}, u32[]{:S(2)}) copy-start(bf16[512,512]{1,0:T(8,128)(2,1)} %get-tuple-element.40) | copy-start | bytes 1572868
  53.0 5.0 %copy-start.9 = (f32[32,2,16]{0,2,1:T(8,128)S(1)}, f32[32,2,16]{0,2,1:T(8,128)}, u32[]{:S(2)}) copy-start(f32[32,2,16]{0,2,1:T(8,128)} %constant.134) | copy-start | bytes 12292
  54.1 24.2 %all-to-all-start.1 = ((bf16[32,2,16,3,1,128]{5,2,4,3,1,0:T(8,128)(2,1)}), bf16[32,2,16,3,1,128]{5,2,4,3,1,0:T(8,128)(2,1)S(1)}, u32[]{:S(2)}, u32[]{:S(2)}) async-start(bf16[32,2,16,3,1,128]{5,2,4,3,1,0:T(8,128)(2,1)} %bitcast.327), calls=%async_computation.1 | async-start | bytes 1572864 | tf_op jit(solution)/shard_map/all_to_all | solution.py:190
  81.5 1.1 %copy-start.7 = (bf16[3,1,128,1024]{3,2,1,0:T(8,128)(2,1)S(1)}, bf16[3,1,128,1024]{3,2,1,0:T(8,128)(2,1)}, u32[]{:S(2)}) copy-start(bf16[3,1,128,1024]{3,2,1,0:T(8,128)(2,1)} %param.7) | copy-start | bytes 2359300

commit v14 on v13

--- a/solution.py
+++ b/solution.py
@@ -144,11 +144,10 @@
     )
 
     cos_y, sin_y = phase_table(width_y, width_y, width_y)
-    cos_y_parts = split_parts(cos_y)
-    sin_y_parts = split_parts(sin_y)
+    both_y_parts = split_parts(jnp.concatenate([cos_y, sin_y], axis=1))
     spec_y = "yk,cpjxy->cpjxk"
-    by_cos = mat(cos_y_parts, gathered, spec_y)
-    by_sin = mat(sin_y_parts, gathered, spec_y)
+    by_both = mat(both_y_parts, gathered, spec_y)
+    by_cos, by_sin = by_both[..., :width_y], by_both[..., width_y:]
     y_real = by_cos[:, 0] + by_sin[:, 1]
     y_imag = by_cos[:, 1] - by_sin[:, 0]
 
@@ -158,8 +157,8 @@
 
     def inverse_y(b_real, b_imag):
         stacked = jnp.stack([b_real, b_imag], axis=1).astype(BF16)
-        by_cos = mat(cos_y_parts, stacked, spec_y)
-        by_sin = mat(sin_y_parts, stacked, spec_y)
+        by_both = mat(both_y_parts, stacked, spec_y)
+        by_cos, by_sin = by_both[..., :width_y], by_both[..., width_y:]
         scale = 1.0 / width_y
         out_real = (by_cos[:, 0] - by_sin[:, 1]) * scale
         out_imag = (by_cos[:, 1] + by_sin[:, 0]) * scale

time: 84.4 us -> 81.3 us (0.963)
  other arithmetic: 14.4 us -> 11.1 us
  waiting for transfers between devices: 30.7 us -> 33.9 us
  matrix products: 19.3 us -> 17.4 us
  local copies, waits for them, and re-layouts: 7.59 us -> 6.69 us
    all_to_all x1, waiting for transfers between devices: 16.4 us -> 19.6 us  [on_device(): lax.all_to_all(spectrum, ('row', 'col'), split_axis=0, concat_axis=0, til...]
    dot_general x12 -> x6, matrix products: 6.78 us -> 4.92 us  [mat(): term = jnp.einsum(spec, part, operand, preferred_element_type=F32)]
    sub x2, other arithmetic: 4.45 us -> 2.91 us  [phase_table(): cosine = outer_cos * inner_cos - outer_sin * inner_sin]
    convert_element_type x1 -> x0, other arithmetic: 1.46 us -> none  [split_parts(): return (high.astype(BF16), low.astype(BF16))]
    unnamed x22 -> x14, local copies, waits for them, and re-layouts: 1.02 us -> 0.14 us
  transfers between devices with their start and end apart: 2 -> 2, of which waited for: 2 -> 2; matrix products, arithmetic and copies ran while one was open for 12% -> 8% of each run, Pallas kernels for 0% -> 0%
where the time goes in v14:
time: 81.3 us; the launch traced here: 80.9 us
  waiting for transfers between devices  33.9 us (42%)
  matrix products  17.4 us (21%)
  starting transfers between devices  11.3 us (14%)
  other arithmetic  11.1 us (14%)
  local copies, waits for them, and re-layouts  6.69 us (8%)
    all_to_all x1, waiting for transfers between devices, on_device(): lax.all_to_all(spectrum, ('row', 'col'), split_axis=0, concat_axis=0, til...  19.6 us
    all_to_all x1, waiting for transfers between devices, on_device(): lax.all_to_all(outgoing, ('row', 'col'), split_axis=0, concat_axis=0, til...  14.3 us
    all_to_all x1, starting transfers between devices, on_device(): lax.all_to_all(spectrum, ('row', 'col'), split_axis=0, concat_axis=0, til...  7.48 us
    dot_general x6, matrix products, mat(): term = jnp.einsum(spec, part, operand, preferred_element_type=F32)  4.92 us
    all_to_all x1, starting transfers between devices, on_device(): lax.all_to_all(outgoing, ('row', 'col'), split_axis=0, concat_axis=0, til...  3.83 us
    dot_general x1, matrix products, on_device(): jnp.einsum('...k,k->...', one_hot, parts, preferred_element_type=F32)  2.98 us
    sub x2, other arithmetic, phase_table(): cosine = outer_cos * inner_cos - outer_sin * inner_sin  2.91 us
    dot_general x1, matrix products, on_device(): jnp.einsum(spec_back, returned, back_high, preferred_element_type=F32)  2.61 us
  transfers between devices with their start and end apart: 2, of which 2 were waited for; matrix products, arithmetic and copies ran while one was open for 8% of the time, Pallas kernels for 0%

profile of v14, /device:TPU:0, one launch (start us, length us, event | category | flops | bytes accessed | tf_op | source)
XLA Modules:
  0.0 80.9 jit_solution(12251224956549050434)
XLA Ops:
  0.5 0.5 fusion.100
  1.7 0.7 reduce-precision_convert_fusion.4
  2.4 3.0 %fusion = f32[1,128,1024]{2,0,1:T(1,128)S(1)} fusion(s32[128,1024]{1,0:T(8,128)} %bitcast.295, s32[24]{0:T(128)S(1)} %and_select_fusion, bf16[8]{0:T(256)(128)(2,1)S(1)} %get-tuple-element.28, bf16[8]{0:T(256)(128)(2,1)S(1)} %get-tuple-element.27, bf16[8]{0:T(256)(128)(2,1)S(1)} %get-tuple-element.5), kind=kOutput, calls=%fused_computation | convolution fusion | flops 9437328 | bytes 1048720 | tf_op jit(solution)/shard_map/...k,k->.../dot_general | solution.py:107
  6.0 2.6 %multiply_subtract_fusion = (f32[32,1,16,1024]{3,0,2,1:T(8,128)S(1)}, f32[32,1,16,1024]{3,0,2,1:T(8,128)S(1)}) fusion(f32[32,1,16,1024]{3,2,0,1:T(8,128)S(1)} %bitcast.286, f32[32,1,16,1024]{3,2,0,1:T(8,128)S(1)} %bitcast.285, f32[32,1024]{1,0:T(8,128)S(1)} %mul.661, f32[32,1024]{1,0:T(8,128)S(1)} %mul.650, f32[1024]{0:T(1024)S(1)} %fusion.132, ...), kind=kLoop, calls=%fused_computation.23 | loop fusion | flops 4194304 | bytes 8655360 | tf_op jit(solution)/shard_map/sub | solution.py:45
  8.6 1.3 %fusion.8 = f32[3,128,32,2,16]{1,2,4,3,0:T(8,128)S(1)} fusion(bf16[3,1,128,1024]{3,2,1,0:T(8,128)(2,1)S(1)} %copy-done.6, f32[128,1024]{1,0:T(8,128)S(1)} %bitcast.292, f32[32,1,16,1024]{3,0,2,1:T(8,128)S(1)} %get-tuple-element.8, f32[32,1,16,1024]{3,0,2,1:T(8,128)S(1)} %get-tuple-element.7), kind=kOutput, calls=%fused_computation.18 | convolution fusion | flops 810418176 | bytes 7077888 | tf_op jit(solution)/shard_map/dpjz,cyz->dcpjy/dot_general | solution.py:132
  9.9 1.3 %fusion.6 = f32[3,128,32,2,16]{1,2,4,3,0:T(8,128)S(1)} fusion(bf16[3,1,128,1024]{3,2,1,0:T(8,128)(2,1)S(1)} %copy-done.6, f32[128,1024]{1,0:T(8,128)S(1)} %bitcast.293, f32[32,1,16,1024]{3,0,2,1:T(8,128)S(1)} %get-tuple-element.8, f32[32,1,16,1024]{3,0,2,1:T(8,128)S(1)} %get-tuple-element.7), kind=kOutput, calls=%fused_computation.16 | convolution fusion | flops 811073536 | bytes 7077888 | tf_op jit(solution)/shard_map/dpjz,cyz->dcpjy/dot_general | solution.py:133
  11.2 1.3 %fusion.15 = bf16[32,3,2,16,128]{4,0,3,2,1:T(8,128)(2,1)S(1)} fusion(f32[3,128,32,2,16]{1,2,4,3,0:T(8,128)S(1)} %fusion.6, f32[3,128,32,2,16]{1,2,4,3,0:T(8,128)S(1)} %fusion.8, bf16[3,1,128,1024]{3,2,1,0:T(8,128)(2,1)S(1)} %copy-done.6, f32[128,1024]{1,0:T(8,128)S(1)} %bitcast.294, f32[32,1,16,1024]{3,0,2,1:T(8,128)S(1)} %get-tuple-element.8, ...), kind=kOutput, calls=%fused_computation.31 | convolution fusion | flops 811204608 | bytes 9437184 | tf_op jit(solution)/shard_map/dpjz,cyz->dcpjy/dot_general | solution.py:131
  12.5 1.2 %copy.43 = bf16[32,3,2,16,128]{4,3,2,1,0:T(8,128)(2,1)} copy(bf16[32,3,2,16,128]{4,0,3,2,1:T(8,128)(2,1)S(1)} %fusion.15) | data formatting | bytes 1572864 | tf_op jit(solution)/shard_map/convert_element_type | solution.py:135
  13.7 7.5 %all-to-all-start = ((bf16[32,3,2,16,128]{4,3,2,1,0:T(8,128)(2,1)}), bf16[32,3,2,16,128]{4,3,2,1,0:T(8,128)(2,1)S(1)}, u32[]{:S(2)}, u32[]{:S(2)}) async-start(bf16[32,3,2,16,128]{4,3,2,1,0:T(8,128)(2,1)} %copy.43), calls=%async_computation | async-start | bytes 1572864 | tf_op jit(solution)/shard_map/all_to_all | solution.py:136
  22.0 19.6 %all-to-all-done = bf16[32,3,2,16,128]{4,3,2,1,0:T(8,128)(2,1)S(1)} async-done(((bf16[32,3,2,16,128]{4,3,2,1,0:T(8,128)(2,1)}), bf16[32,3,2,16,128]{4,3,2,1,0:T(8,128)(2,1)S(1)}, u32[]{:S(2)}, u32[]{:S(2)}) %all-to-all-start) | async-done | bytes 786464 | tf_op jit(solution)/shard_map/all_to_all | solution.py:136
  41.6 1.1 %fusion.55 = f32[3,2,16,8,1024]{4,3,2,1,0:T(8,128)S(1)} fusion(bf16[8,4,3,1,2,16,128]{6,5,4,2,1,0,3:T(8,128)(2,1)S(1)} %bitcast.282, f32[512,512]{1,0:T(8,128)S(1)} %bitcast.276, f32[512,512]{1,0:T(8,128)S(1)} %bitcast.270), kind=kOutput, calls=%fused_computation.87 | convolution fusion | flops 806879232 | bytes 6029312 | tf_op jit(solution)/shard_map/yk,cpjxy->cpjxk/dot_general | solution.py:65
  42.7 1.2 %convolution_add_fusion.1 = f32[3,2,16,8,1024]{4,3,2,1,0:T(8,128)S(1)} fusion(f32[3,2,16,8,1024]{4,3,2,1,0:T(8,128)S(1)} %fusion.55, bf16[8,4,3,1,2,16,128]{6,5,4,2,1,0,3:T(8,128)(2,1)S(1)} %bitcast.283, f32[512,512]{1,0:T(8,128)S(1)} %bitcast.277, f32[512,512]{1,0:T(8,128)S(1)} %bitcast.271), kind=kOutput, calls=%fused_computation.25 | convolution fusion | flops 808189952 | bytes 9175040 | tf_op jit(solution)/shard_map/yk,cpjxy->cpjxk/dot_general | solution.py:65
  47.4 1.0 %fusion.62 = f32[3,2,16,8,1024]{4,3,2,1,0:T(8,128)S(1)} fusion(bf16[3,1,16,8,512]{4,3,2,1,0:T(8,128)(2,1)S(1)} %fusion.53, bf16[3,1,16,8,512]{4,3,2,1,0:T(8,128)(2,1)S(1)} %fusion.52, f32[512,512]{1,0:T(8,128)S(1)} %bitcast.280, f32[512,512]{1,0:T(8,128)S(1)} %bitcast.274), kind=kOutput, calls=%fused_computation.95 | convolution fusion | flops 807272448 | bytes 6029312 | tf_op jit(solution)/shard_map/yk,cpjxy->cpjxk/dot_general | solution.py:65
  48.4 1.0 %convolution_add_fusion = f32[3,2,16,8,1024]{4,3,2,1,0:T(8,128)S(1)} fusion(f32[3,2,16,8,1024]{4,3,2,1,0:T(8,128)S(1)} %fusion.62, bf16[3,1,16,8,512]{4,3,2,1,0:T(8,128)(2,1)S(1)} %fusion.53, bf16[3,1,16,8,512]{4,3,2,1,0:T(8,128)(2,1)S(1)} %fusion.52, f32[512,512]{1,0:T(8,128)S(1)} %bitcast.281, f32[512,512]{1,0:T(8,128)S(1)} %bitcast.275), kind=kOutput, calls=%fused_computation.24 | convolution fusion | flops 808583168 | bytes 9175040 | tf_op jit(solution)/shard_map/yk,cpjxy->cpjxk/dot_general | solution.py:65
  50.3 0.9 %pad_maximum_fusion.3 = bf16[3,2,16,8,1,4,128]{6,2,4,0,1,5,3:T(8,128)(2,1)} fusion(bf16[3,1,16,8,1,4,128]{6,2,4,0,1,5,3:T(8,128)(2,1)S(1)} %copy.49, bf16[3,1,16,8,1,4,128]{6,2,4,0,1,5,3:T(8,128)(2,1)S(1)} %copy.48), kind=kLoop, calls=%fused_computation.85 | loop fusion | flops 393216 | bytes 1572864 | tf_op jit(solution)/shard_map/stack | solution.py:182
  51.2 3.8 %all-to-all-start.1 = ((bf16[32,2,16,3,1,128]{5,2,4,3,1,0:T(8,128)(2,1)}), bf16[32,2,16,3,1,128]{5,2,4,3,1,0:T(8,128)(2,1)S(1)}, u32[]{:S(2)}, u32[]{:S(2)}) async-start(bf16[32,2,16,3,1,128]{5,2,4,3,1,0:T(8,128)(2,1)} %bitcast.291), calls=%async_computation.1 | async-start | bytes 1572864 | tf_op jit(solution)/shard_map/all_to_all | solution.py:189
  55.1 2.4 %multiply_convert_fusion = (bf16[32,2,16,1024]{3,0,2,1:T(8,128)(2,1)S(1)}, bf16[32,2,16,1024]{3,0,2,1:T(8,128)(2,1)S(1)}) fusion(f32[32,2,16]{0,2,1:T(8,128)S(1)} %copy-done.5, f32[32,1,16,1024]{3,0,2,1:T(8,128)} %copy-done.2, f32[32,1,16,1024]{3,0,2,1:T(8,128)S(1)} %copy-done.1), kind=kLoop, calls=%fused_computation.8 | loop fusion | flops 11534336 | bytes 8392704 | tf_op jit(solution)/shard_map/convert_element_type | solution.py:200
  57.5 2.5 %copy.51 = bf16[32,2,16,1024]{3,2,1,0:T(8,128)(2,1)} copy(bf16[32,2,16,1024]{3,0,2,1:T(8,128)(2,1)S(1)} %get-tuple-element.10) | data formatting | bytes 4194304 | tf_op jit(solution)/shard_map/convert_element_type | solution.py:199
  60.0 1.2 %copy.52 = bf16[32,2,16,1024]{3,2,1,0:T(8,128)(2,1)S(1)} copy(bf16[32,2,16,1024]{3,0,2,1:T(8,128)(2,1)S(1)} %get-tuple-element.9) | data formatting | bytes 4194304 | tf_op jit(solution)/shard_map/convert_element_type | solution.py:200
  61.1 14.3 %all-to-all-done.1 = bf16[32,2,16,3,1,128]{5,2,4,3,1,0:T(8,128)(2,1)S(1)} async-done(((bf16[32,2,16,3,1,128]{5,2,4,3,1,0:T(8,128)(2,1)}), bf16[32,2,16,3,1,128]{5,2,4,3,1,0:T(8,128)(2,1)S(1)}, u32[]{:S(2)}, u32[]{:S(2)}) %all-to-all-start.1) | async-done | bytes 786464 | tf_op jit(solution)/shard_map/all_to_all | solution.py:189
  75.5 0.5 copy.50
  76.0 2.6 %fusion.40 = f32[384,1024]{1,0:T(8,128)S(1)} fusion(bf16[1024,1024]{1,0:T(8,128)(2,1)} %bitcast.287, bf16[128,8,3,128]{3,2,1,0:T(4,128)(2,1)S(1)} %bitcast.288), kind=kOutput, calls=%fused_computation.64 | convolution fusion | flops 805306368 | bytes 4456448 | tf_op jit(solution)/shard_map/kr,kz->rz/dot_general | solution.py:202
  78.6 1.0 %convolution_add_fusion.2 = f32[384,1024]{1,0:T(8,128)S(1)} fusion(f32[384,1024]{1,0:T(8,128)S(1)} %fusion.40, bf16[1024,1024]{1,0:T(8,128)(2,1)S(1)} %bitcast.284, bf16[128,8,3,128]{3,2,1,0:T(4,128)(2,1)S(1)} %bitcast.289), kind=kOutput, calls=%fused_computation.30 | convolution fusion | flops 805699584 | bytes 6029312 | tf_op jit(solution)/shard_map/kr,kz->rz/dot_general | solution.py:202
  79.8 1.1 %add_convert_fusion = bf16[3,1,128,1024]{3,2,1,0:T(8,128)(2,1)} fusion(f32[3,1,128,1024]{3,2,1,0:T(8,128)S(1)} %bitcast.290, bf16[3,1,128,1024]{3,2,1,0:T(8,128)(2,1)S(1)} %copy-done.3), kind=kLoop, calls=%fused_computation.27 | loop fusion | flops 1179648 | bytes 3145728 | tf_op jit(solution)/shard_map/convert_element_type | solution.py:206
  (58 shorter events, 6.8 us)
Async XLA Ops:
  5.9 2.7 %copy-start.6 = (bf16[3,1,128,1024]{3,2,1,0:T(8,128)(2,1)S(1)}, bf16[3,1,128,1024]{3,2,1,0:T(8,128)(2,1)}, u32[]{:S(2)}) copy-start(bf16[3,1,128,1024]{3,2,1,0:T(8,128)(2,1)} %param.6) | copy-start | bytes 2359300
  8.6 2.6 %copy-start = (f32[32,1,16,1024]{3,0,2,1:T(8,128)}, f32[32,1,16,1024]{3,0,2,1:T(8,128)S(1)}, u32[]{:S(2)}) copy-start(f32[32,1,16,1024]{3,0,2,1:T(8,128)S(1)} %get-tuple-element.7) | copy-start | bytes 6291460
  8.6 2.6 %copy-start.2 = (f32[32,1,16,1024]{3,0,2,1:T(8,128)}, f32[32,1,16,1024]{3,0,2,1:T(8,128)S(1)}, u32[]{:S(2)}) copy-start(f32[32,1,16,1024]{3,0,2,1:T(8,128)S(1)} %get-tuple-element.8) | copy-start | bytes 6291460
  13.7 27.9 %all-to-all-start = ((bf16[32,3,2,16,128]{4,3,2,1,0:T(8,128)(2,1)}), bf16[32,3,2,16,128]{4,3,2,1,0:T(8,128)(2,1)S(1)}, u32[]{:S(2)}, u32[]{:S(2)}) async-start(bf16[32,3,2,16,128]{4,3,2,1,0:T(8,128)(2,1)} %copy.43), calls=%async_computation | async-start | bytes 1572864 | tf_op jit(solution)/shard_map/all_to_all | solution.py:136
  42.7 1.2 %copy-start.4 = (f32[8,8,1]{1,0,2:T(8,128)S(1)}, f32[8,8,1]{1,0,2:T(8,128)}, u32[]{:S(2)}) copy-start(f32[8,8,1]{1,0,2:T(8,128)} %constant.135) | copy-start | bytes 772
  50.1 5.0 %copy-start.1 = (f32[32,1,16,1024]{3,0,2,1:T(8,128)S(1)}, f32[32,1,16,1024]{3,0,2,1:T(8,128)}, u32[]{:S(2)}) copy-start(f32[32,1,16,1024]{3,0,2,1:T(8,128)} %copy-done) | copy-start | bytes 6291460
  50.1 5.0 %copy-start.5 = (f32[32,2,16]{0,2,1:T(8,128)S(1)}, f32[32,2,16]{0,2,1:T(8,128)}, u32[]{:S(2)}) copy-start(f32[32,2,16]{0,2,1:T(8,128)} %constant.134) | copy-start | bytes 12292
  51.2 24.2 %all-to-all-start.1 = ((bf16[32,2,16,3,1,128]{5,2,4,3,1,0:T(8,128)(2,1)}), bf16[32,2,16,3,1,128]{5,2,4,3,1,0:T(8,128)(2,1)S(1)}, u32[]{:S(2)}, u32[]{:S(2)}) async-start(bf16[32,2,16,3,1,128]{5,2,4,3,1,0:T(8,128)(2,1)} %bitcast.291), calls=%async_computation.1 | async-start | bytes 1572864 | tf_op jit(solution)/shard_map/all_to_all | solution.py:189
  78.6 1.1 %copy-start.3 = (bf16[3,1,128,1024]{3,2,1,0:T(8,128)(2,1)S(1)}, bf16[3,1,128,1024]{3,2,1,0:T(8,128)(2,1)}, u32[]{:S(2)}) copy-start(bf16[3,1,128,1024]{3,2,1,0:T(8,128)(2,1)} %param.7) | copy-start | bytes 2359300

commit v15 on v14

--- a/solution.py
+++ b/solution.py
@@ -127,10 +127,12 @@
     lines = (members * local_x, local_y, depth)
     z_high4, z_low4 = z_high.reshape(blocks), z_low.reshape(blocks)
     e_high, e_low = e_high.reshape(lines), e_low.reshape(lines)
+    z_both = jnp.stack([z_high4, z_low4])
+    by_high = jnp.einsum("h" + spec_z.replace("->", "->h"), z_both, e_high, preferred_element_type=F32)
     spectrum = (
-        jnp.einsum(spec_z, z_high4, e_high, preferred_element_type=F32)
+        by_high[0]
+        + by_high[1]
         + jnp.einsum(spec_z, z_high4, e_low, preferred_element_type=F32)
-        + jnp.einsum(spec_z, z_low4, e_high, preferred_element_type=F32)
     )
     spectrum = spectrum.astype(BF16)
     gathered = lax.all_to_all(
@@ -198,10 +200,9 @@
     weight = jnp.asarray(weight.reshape(2 * columns, 1))
     back_high = (z_high.astype(F32) * weight).astype(BF16)
     back_low = (z_low.astype(F32) * weight).astype(BF16)
-    spec_back = "kr,kz->rz"
-    field = jnp.einsum(spec_back, returned, back_high, preferred_element_type=F32) + jnp.einsum(
-        spec_back, returned, back_low, preferred_element_type=F32
-    )
+    back_both = jnp.stack([back_high, back_low], axis=1)
+    field = jnp.einsum("kr,khz->rhz", returned, back_both, preferred_element_type=F32)
+    field = field[:, 0] + field[:, 1]
     field = field.reshape(members, local_x, local_y, depth)
     return (magnetic.astype(F32) + field).astype(BF16)
 

time: 81.3 us -> 83.9 us (1.032)
  other arithmetic: 11.1 us -> 14 us
    convert_element_type x2 -> x0, local copies, waits for them, and re-layouts: 3.64 us -> none  [the longest x1 2.49 us: on_device(): back_high = (z_high.astype(F32) * weight).astype(BF16)]
    another operation x0 -> x1, local copies, waits for them, and re-layouts: none -> 2.43 us  [on_device(): jnp.stack([cos_z.reshape(devices, per_device, depth), sin_part.reshape(de...]
    another operation x6 -> x7, other arithmetic: 0.79 us -> 2.82 us  [the longest x1 2.02 us: on_device(): jnp.stack([cos_z.reshape(devices, per_device, depth), sin_part.reshape(de...]
    unnamed x14, local copies, waits for them, and re-layouts: 0.14 us -> 1.65 us
    convert_element_type x1 -> x2, other arithmetic: 2.42 us -> 3.05 us  [the longest x1 2.1 us: on_device(): back_high = (z_high.astype(F32) * weight).astype(BF16)]
    dot_general x4 -> x2, matrix products: 6.18 us -> 5.91 us  [the longest x1 3.46 us: on_device(): jnp.einsum('kr,khz->rhz', returned, back_both, preferred_element_type=F32)]
  transfers between devices with their start and end apart: 2 -> 2, of which waited for: 2 -> 2; matrix products, arithmetic and copies ran while one was open for 8% -> 9% of each run, Pallas kernels for 0% -> 0%
where the time goes in v15:
time: 83.9 us; the launch traced here: 83.4 us
  waiting for transfers between devices  33.4 us (40%)
  matrix products  17.2 us (21%)
  other arithmetic  14 us (17%)
  starting transfers between devices  11.3 us (13%)
  local copies, waits for them, and re-layouts  6.98 us (8%)
    all_to_all x1, waiting for transfers between devices, on_device(): lax.all_to_all(spectrum, ('row', 'col'), split_axis=0, concat_axis=0, til...  19.6 us
    all_to_all x1, waiting for transfers between devices, on_device(): lax.all_to_all(outgoing, ('row', 'col'), split_axis=0, concat_axis=0, til...  13.8 us
    all_to_all x1, starting transfers between devices, on_device(): lax.all_to_all(spectrum, ('row', 'col'), split_axis=0, concat_axis=0, til...  7.48 us
    dot_general x6, matrix products, mat(): term = jnp.einsum(spec, part, operand, preferred_element_type=F32)  4.91 us
    all_to_all x1, starting transfers between devices, on_device(): lax.all_to_all(outgoing, ('row', 'col'), split_axis=0, concat_axis=0, til...  3.84 us
    dot_general x1, matrix products, on_device(): jnp.einsum('kr,khz->rhz', returned, back_both, preferred_element_type=F32)  3.46 us
    dot_general x1, matrix products, on_device(): jnp.einsum('...k,k->...', one_hot, parts, preferred_element_type=F32)  2.98 us
    sub x2, other arithmetic, phase_table(): cosine = outer_cos * inner_cos - outer_sin * inner_sin  2.91 us
  transfers between devices with their start and end apart: 2, of which 2 were waited for; matrix products, arithmetic and copies ran while one was open for 9% of the time, Pallas kernels for 0%

profile of v15, /device:TPU:0, one launch (start us, length us, event | category | flops | bytes accessed | tf_op | source)
XLA Modules:
  0.0 83.4 jit_solution(3762625173599829024)
XLA Ops:
  1.7 0.7 reduce-precision_convert_fusion.6
  2.4 3.0 %fusion = f32[1,128,1024]{2,0,1:T(1,128)S(1)} fusion(s32[128,1024]{1,0:T(8,128)} %bitcast.298, s32[24]{0:T(128)S(1)} %and_select_fusion, bf16[8]{0:T(256)(128)(2,1)S(1)} %get-tuple-element.30, bf16[8]{0:T(256)(128)(2,1)S(1)} %get-tuple-element.29, bf16[8]{0:T(256)(128)(2,1)S(1)} %get-tuple-element.5), kind=kOutput, calls=%fused_computation | convolution fusion | flops 9437328 | bytes 1048720 | tf_op jit(solution)/shard_map/...k,k->.../dot_general | solution.py:107
  5.9 2.6 %multiply_subtract_fusion = (f32[32,1,16,1024]{3,0,2,1:T(8,128)S(1)}, f32[32,1,16,1024]{3,0,2,1:T(8,128)S(1)}) fusion(f32[32,1,16,1024]{3,2,0,1:T(8,128)S(1)} %bitcast.292, f32[32,1,16,1024]{3,2,0,1:T(8,128)S(1)} %bitcast.291, f32[32,1024]{1,0:T(8,128)S(1)} %mul.769, f32[32,1024]{1,0:T(8,128)S(1)} %mul.758, f32[1024]{0:T(1024)S(1)} %fusion.134, ...), kind=kLoop, calls=%fused_computation.32 | loop fusion | flops 4194304 | bytes 8655360 | tf_op jit(solution)/shard_map/sub | solution.py:45
  8.6 1.0 %reduce-precision_convert_fusion.1 = (bf16[1,32,2,16,1024]{4,1,3,2,0:T(8,128)(2,1)S(1)}, bf16[1,32,2,16,1024]{4,1,3,2,0:T(8,128)(2,1)S(1)}) fusion(f32[1,32,1,16,1024]{4,1,3,2,0:T(8,128)S(1)} %bitcast.287, f32[1,32,1,16,1024]{4,1,3,2,0:T(8,128)S(1)} %bitcast.286), kind=kLoop, calls=%fused_computation.7 | loop fusion | flops 5242880 | bytes 8388608 | tf_op jit(solution)/shard_map/convert_element_type | solution.py:28
  9.6 0.8 copy-done.6
  10.3 2.5 %fusion.17 = f32[2,32,3,2,16,128]{5,1,4,3,0,2:T(8,128)S(1)} fusion(bf16[1,32,2,16,1024]{4,1,3,2,0:T(8,128)(2,1)S(1)} %get-tuple-element.12, bf16[1,32,2,16,1024]{4,1,3,2,0:T(8,128)(2,1)S(1)} %get-tuple-element.11, bf16[3,1,128,1024]{3,2,1,0:T(8,128)(2,1)S(1)} %copy-done.6, f32[128,1024]{1,0:T(8,128)S(1)} %bitcast.296), kind=kOutput, calls=%fused_computation.33 | convolution fusion | flops 1620574208 | bytes 8650752 | tf_op jit(solution)/shard_map/hdpjz,cyz->hdcpjy/dot_general | solution.py:131
  12.8 1.3 %fusion.21 = bf16[32,3,2,16,128]{4,0,3,2,1:T(8,128)(2,1)S(1)} fusion(f32[2,32,3,2,16,128]{5,1,4,3,0,2:T(8,128)S(1)} %fusion.17, bf16[3,1,128,1024]{3,2,1,0:T(8,128)(2,1)S(1)} %copy-done.6, f32[128,1024]{1,0:T(8,128)S(1)} %bitcast.297, f32[32,1,16,1024]{3,0,2,1:T(8,128)S(1)} %get-tuple-element.8, f32[32,1,16,1024]{3,0,2,1:T(8,128)S(1)} %get-tuple-element.7), kind=kOutput, calls=%fused_computation.41 | convolution fusion | flops 811597824 | bytes 9437184 | tf_op jit(solution)/shard_map/dpjz,cyz->dcpjy/dot_general | solution.py:135
  14.1 1.2 %copy.43 = bf16[32,3,2,16,128]{4,3,2,1,0:T(8,128)(2,1)} copy(bf16[32,3,2,16,128]{4,0,3,2,1:T(8,128)(2,1)S(1)} %fusion.21) | data formatting | bytes 1572864 | tf_op jit(solution)/shard_map/convert_element_type | solution.py:137
  15.3 7.5 %all-to-all-start = ((bf16[32,3,2,16,128]{4,3,2,1,0:T(8,128)(2,1)}), bf16[32,3,2,16,128]{4,3,2,1,0:T(8,128)(2,1)S(1)}, u32[]{:S(2)}, u32[]{:S(2)}) async-start(bf16[32,3,2,16,128]{4,3,2,1,0:T(8,128)(2,1)} %copy.43), calls=%async_computation | async-start | bytes 1572864 | tf_op jit(solution)/shard_map/all_to_all | solution.py:138
  23.6 19.6 %all-to-all-done = bf16[32,3,2,16,128]{4,3,2,1,0:T(8,128)(2,1)S(1)} async-done(((bf16[32,3,2,16,128]{4,3,2,1,0:T(8,128)(2,1)}), bf16[32,3,2,16,128]{4,3,2,1,0:T(8,128)(2,1)S(1)}, u32[]{:S(2)}, u32[]{:S(2)}) %all-to-all-start) | async-done | bytes 786464 | tf_op jit(solution)/shard_map/all_to_all | solution.py:138
  43.2 1.1 %fusion.60 = f32[3,2,16,8,1024]{4,3,2,1,0:T(8,128)S(1)} fusion(bf16[8,4,3,1,2,16,128]{6,5,4,2,1,0,3:T(8,128)(2,1)S(1)} %bitcast.289, f32[512,512]{1,0:T(8,128)S(1)} %bitcast.280, f32[512,512]{1,0:T(8,128)S(1)} %bitcast.274), kind=kOutput, calls=%fused_computation.98 | convolution fusion | flops 806879232 | bytes 6029312 | tf_op jit(solution)/shard_map/yk,cpjxy->cpjxk/dot_general | solution.py:65
  44.3 1.2 %convolution_add_fusion.1 = f32[3,2,16,8,1024]{4,3,2,1,0:T(8,128)S(1)} fusion(f32[3,2,16,8,1024]{4,3,2,1,0:T(8,128)S(1)} %fusion.60, bf16[8,4,3,1,2,16,128]{6,5,4,2,1,0,3:T(8,128)(2,1)S(1)} %bitcast.290, f32[512,512]{1,0:T(8,128)S(1)} %bitcast.281, f32[512,512]{1,0:T(8,128)S(1)} %bitcast.275), kind=kOutput, calls=%fused_computation.35 | convolution fusion | flops 808189952 | bytes 9175040 | tf_op jit(solution)/shard_map/yk,cpjxy->cpjxk/dot_general | solution.py:65
  49.0 1.0 %fusion.66 = f32[3,2,16,8,1024]{4,3,2,1,0:T(8,128)S(1)} fusion(bf16[3,1,16,8,512]{4,3,2,1,0:T(8,128)(2,1)S(1)} %fusion.58, bf16[3,1,16,8,512]{4,3,2,1,0:T(8,128)(2,1)S(1)} %fusion.57, f32[512,512]{1,0:T(8,128)S(1)} %bitcast.284, f32[512,512]{1,0:T(8,128)S(1)} %bitcast.278), kind=kOutput, calls=%fused_computation.105 | convolution fusion | flops 807272448 | bytes 6029312 | tf_op jit(solution)/shard_map/yk,cpjxy->cpjxk/dot_general | solution.py:65
  50.0 1.0 %convolution_add_fusion = f32[3,2,16,8,1024]{4,3,2,1,0:T(8,128)S(1)} fusion(f32[3,2,16,8,1024]{4,3,2,1,0:T(8,128)S(1)} %fusion.66, bf16[3,1,16,8,512]{4,3,2,1,0:T(8,128)(2,1)S(1)} %fusion.58, bf16[3,1,16,8,512]{4,3,2,1,0:T(8,128)(2,1)S(1)} %fusion.57, f32[512,512]{1,0:T(8,128)S(1)} %bitcast.285, f32[512,512]{1,0:T(8,128)S(1)} %bitcast.279), kind=kOutput, calls=%fused_computation.34 | convolution fusion | flops 808583168 | bytes 9175040 | tf_op jit(solution)/shard_map/yk,cpjxy->cpjxk/dot_general | solution.py:65
  51.9 0.9 %pad_maximum_fusion.4 = bf16[3,2,16,8,1,4,128]{6,2,4,0,1,5,3:T(8,128)(2,1)} fusion(bf16[3,1,16,8,1,4,128]{6,2,4,0,1,5,3:T(8,128)(2,1)S(1)} %copy.49, bf16[3,1,16,8,1,4,128]{6,2,4,0,1,5,3:T(8,128)(2,1)S(1)} %copy.48), kind=kLoop, calls=%fused_computation.96 | loop fusion | flops 393216 | bytes 1572864 | tf_op jit(solution)/shard_map/stack | solution.py:184
  52.8 3.8 %all-to-all-start.1 = ((bf16[32,2,16,3,1,128]{5,2,4,3,1,0:T(8,128)(2,1)}), bf16[32,2,16,3,1,128]{5,2,4,3,1,0:T(8,128)(2,1)S(1)}, u32[]{:S(2)}, u32[]{:S(2)}) async-start(bf16[32,2,16,3,1,128]{5,2,4,3,1,0:T(8,128)(2,1)} %bitcast.294), calls=%async_computation.1 | async-start | bytes 1572864 | tf_op jit(solution)/shard_map/all_to_all | solution.py:191
  56.7 2.0 %pad_maximum_fusion.1 = f32[32,2,16,1024]{3,0,2,1:T(8,128)S(1)} fusion(f32[32,1,16,1024]{3,0,2,1:T(8,128)} %copy-done.2, f32[32,1,16,1024]{3,0,2,1:T(8,128)S(1)} %copy-done.1), kind=kLoop, calls=%fused_computation.15 | loop fusion | flops 1048576 | bytes 8388608 | tf_op jit(solution)/shard_map/stack | solution.py:117
  58.7 2.4 %copy.51 = f32[32,2,16,1024]{3,2,1,0:T(8,128)S(1)} copy(f32[32,2,16,1024]{3,0,2,1:T(8,128)S(1)} %pad_maximum_fusion.1) | data formatting | bytes 8388608 | tf_op jit(solution)/shard_map/stack | solution.py:117
  61.2 2.1 %multiply_convert_fusion.1 = (bf16[1024,1,1024]{2,0,1:T(8,128)(2,1)S(1)}, bf16[1024,1,1024]{2,0,1:T(8,128)(2,1)}) fusion(f32[1024,1,1024]{2,0,1:T(8,128)S(1)} %bitcast.288, f32[1024]{0:T(1024)S(1)} %copy-done.5), kind=kLoop, calls=%fused_computation.21 | loop fusion | flops 10485760 | bytes 8392704 | tf_op jit(solution)/shard_map/convert_element_type | solution.py:201
  63.3 13.8 %all-to-all-done.1 = bf16[32,2,16,3,1,128]{5,2,4,3,1,0:T(8,128)(2,1)S(1)} async-done(((bf16[32,2,16,3,1,128]{5,2,4,3,1,0:T(8,128)(2,1)}), bf16[32,2,16,3,1,128]{5,2,4,3,1,0:T(8,128)(2,1)S(1)}, u32[]{:S(2)}, u32[]{:S(2)}) %all-to-all-start.1) | async-done | bytes 786464 | tf_op jit(solution)/shard_map/all_to_all | solution.py:191
  77.1 0.5 copy.50
  77.6 3.5 %fusion.9 = f32[384,2,1024]{2,0,1:T(8,128)S(1)} fusion(bf16[1024,1,1024]{2,0,1:T(8,128)(2,1)} %get-tuple-element.10, bf16[1024,1,1024]{2,0,1:T(8,128)(2,1)S(1)} %get-tuple-element.9, bf16[128,8,3,128]{3,2,1,0:T(4,128)(2,1)S(1)} %bitcast.295), kind=kOutput, calls=%fused_computation.16 | convolution fusion | flops 1619001344 | bytes 8126464 | tf_op jit(solution)/shard_map/kr,khz->rhz/dot_general | solution.py:204
  81.4 0.9 %copy-done.3 = bf16[3,1,128,1024]{3,2,1,0:T(8,128)(2,1)S(1)} copy-done((bf16[3,1,128,1024]{3,2,1,0:T(8,128)(2,1)S(1)}, bf16[3,1,128,1024]{3,2,1,0:T(8,128)(2,1)}, u32[]{:S(2)}) %copy-start.3) | copy-done | bytes 786456
  82.2 1.1 %add_convert_fusion = bf16[3,1,128,1024]{3,2,1,0:T(8,128)(2,1)} fusion(f32[3,1,128,1024]{3,2,1,0:T(8,128)S(1)} %bitcast.293, bf16[3,1,128,1024]{3,2,1,0:T(8,128)(2,1)S(1)} %copy-done.3), kind=kLoop, calls=%fused_computation.42 | loop fusion | flops 1179648 | bytes 3145728 | tf_op jit(solution)/shard_map/convert_element_type | solution.py:207
  (58 shorter events, 7.5 us)
Async XLA Ops:
  8.6 4.2 %copy-start = (f32[32,1,16,1024]{3,0,2,1:T(8,128)}, f32[32,1,16,1024]{3,0,2,1:T(8,128)S(1)}, u32[]{:S(2)}) copy-start(f32[32,1,16,1024]{3,0,2,1:T(8,128)S(1)} %get-tuple-element.7) | copy-start | bytes 6291460
  8.6 4.2 %copy-start.2 = (f32[32,1,16,1024]{3,0,2,1:T(8,128)}, f32[32,1,16,1024]{3,0,2,1:T(8,128)S(1)}, u32[]{:S(2)}) copy-start(f32[32,1,16,1024]{3,0,2,1:T(8,128)S(1)} %get-tuple-element.8) | copy-start | bytes 6291460
  8.6 1.7 %copy-start.6 = (bf16[3,1,128,1024]{3,2,1,0:T(8,128)(2,1)S(1)}, bf16[3,1,128,1024]{3,2,1,0:T(8,128)(2,1)}, u32[]{:S(2)}) copy-start(bf16[3,1,128,1024]{3,2,1,0:T(8,128)(2,1)} %param.6) | copy-start | bytes 2359300
  15.3 27.9 %all-to-all-start = ((bf16[32,3,2,16,128]{4,3,2,1,0:T(8,128)(2,1)}), bf16[32,3,2,16,128]{4,3,2,1,0:T(8,128)(2,1)S(1)}, u32[]{:S(2)}, u32[]{:S(2)}) async-start(bf16[32,3,2,16,128]{4,3,2,1,0:T(8,128)(2,1)} %copy.43), calls=%async_computation | async-start | bytes 1572864 | tf_op jit(solution)/shard_map/all_to_all | solution.py:138
  44.3 1.2 %copy-start.4 = (f32[8,8,1]{1,0,2:T(8,128)S(1)}, f32[8,8,1]{1,0,2:T(8,128)}, u32[]{:S(2)}) copy-start(f32[8,8,1]{1,0,2:T(8,128)} %constant.135) | copy-start | bytes 772
  51.7 5.0 %copy-start.1 = (f32[32,1,16,1024]{3,0,2,1:T(8,128)S(1)}, f32[32,1,16,1024]{3,0,2,1:T(8,128)}, u32[]{:S(2)}) copy-start(f32[32,1,16,1024]{3,0,2,1:T(8,128)} %copy-done) | copy-start | bytes 6291460
  52.8 24.2 %all-to-all-start.1 = ((bf16[32,2,16,3,1,128]{5,2,4,3,1,0:T(8,128)(2,1)}), bf16[32,2,16,3,1,128]{5,2,4,3,1,0:T(8,128)(2,1)S(1)}, u32[]{:S(2)}, u32[]{:S(2)}) async-start(bf16[32,2,16,3,1,128]{5,2,4,3,1,0:T(8,128)(2,1)} %bitcast.294), calls=%async_computation.1 | async-start | bytes 1572864 | tf_op jit(solution)/shard_map/all_to_all | solution.py:191
  58.7 2.5 %copy-start.5 = (f32[1024]{0:T(1024)S(1)}, f32[1024]{0:T(1024)}, u32[]{:S(2)}) copy-start(f32[1024]{0:T(1024)} %constant.134) | copy-start | bytes 12292
  81.1 1.1 %copy-start.3 = (bf16[3,1,128,1024]{3,2,1,0:T(8,128)(2,1)S(1)}, bf16[3,1,128,1024]{3,2,1,0:T(8,128)(2,1)}, u32[]{:S(2)}) copy-start(bf16[3,1,128,1024]{3,2,1,0:T(8,128)(2,1)} %param.7) | copy-start | bytes 2359300

commit v16 on v15

--- a/solution.py
+++ b/solution.py
@@ -127,12 +127,10 @@
     lines = (members * local_x, local_y, depth)
     z_high4, z_low4 = z_high.reshape(blocks), z_low.reshape(blocks)
     e_high, e_low = e_high.reshape(lines), e_low.reshape(lines)
-    z_both = jnp.stack([z_high4, z_low4])
-    by_high = jnp.einsum("h" + spec_z.replace("->", "->h"), z_both, e_high, preferred_element_type=F32)
     spectrum = (
-        by_high[0]
-        + by_high[1]
+        jnp.einsum(spec_z, z_high4, e_high, preferred_element_type=F32)
         + jnp.einsum(spec_z, z_high4, e_low, preferred_element_type=F32)
+        + jnp.einsum(spec_z, z_low4, e_high, preferred_element_type=F32)
     )
     spectrum = spectrum.astype(BF16)
     gathered = lax.all_to_all(

time: 83.9 us -> 82.2 us (0.980)
  other arithmetic: 14 us -> 13.1 us
    convert_element_type x1 -> x0, other arithmetic: 0.95 us -> none  [split_parts(): return (high.astype(BF16), low.astype(BF16))]
    dot_general x1 -> x2, matrix products: 2.45 us -> 2.55 us  [the longest x1 1.28 us: on_device(): jnp.einsum(spec_z, z_high4, e_high, preferred_element_type=F32)]
where the time goes in v16:
time: 82.2 us; the launch traced here: 81.8 us
  waiting for transfers between devices  33.4 us (41%)
  matrix products  17.3 us (21%)
  other arithmetic  13.1 us (16%)
  starting transfers between devices  11.3 us (14%)
  local copies, waits for them, and re-layouts  6.23 us (8%)
    all_to_all x1, waiting for transfers between devices, on_device(): lax.all_to_all(spectrum, ('row', 'col'), split_axis=0, concat_axis=0, til...  19.6 us
    all_to_all x1, waiting for transfers between devices, on_device(): lax.all_to_all(outgoing, ('row', 'col'), split_axis=0, concat_axis=0, til...  13.8 us
    all_to_all x1, starting transfers between devices, on_device(): lax.all_to_all(spectrum, ('row', 'col'), split_axis=0, concat_axis=0, til...  7.48 us
    dot_general x6, matrix products, mat(): term = jnp.einsum(spec, part, operand, preferred_element_type=F32)  4.91 us
    all_to_all x1, starting transfers between devices, on_device(): lax.all_to_all(outgoing, ('row', 'col'), split_axis=0, concat_axis=0, til...  3.83 us
    dot_general x1, matrix products, on_device(): jnp.einsum('kr,khz->rhz', returned, back_both, preferred_element_type=F32)  3.46 us
    dot_general x1, matrix products, on_device(): jnp.einsum('...k,k->...', one_hot, parts, preferred_element_type=F32)  2.98 us
    sub x2, other arithmetic, phase_table(): cosine = outer_cos * inner_cos - outer_sin * inner_sin  2.91 us
  transfers between devices with their start and end apart: 2, of which 2 were waited for; matrix products, arithmetic and copies ran while one was open for 9% of the time, Pallas kernels for 0%

profile of v16, /device:TPU:0, one launch (start us, length us, event | category | flops | bytes accessed | tf_op | source)
XLA Modules:
  0.0 81.8 jit_solution(1627587523576416771)
XLA Ops:
  0.5 0.5 fusion.98
  1.7 0.7 reduce-precision_convert_fusion.5
  2.4 3.0 %fusion = f32[1,128,1024]{2,0,1:T(1,128)S(1)} fusion(s32[128,1024]{1,0:T(8,128)} %bitcast.286, s32[24]{0:T(128)S(1)} %and_select_fusion, bf16[8]{0:T(256)(128)(2,1)S(1)} %get-tuple-element.28, bf16[8]{0:T(256)(128)(2,1)S(1)} %get-tuple-element.27, bf16[8]{0:T(256)(128)(2,1)S(1)} %get-tuple-element.5), kind=kOutput, calls=%fused_computation | convolution fusion | flops 9437328 | bytes 1048720 | tf_op jit(solution)/shard_map/...k,k->.../dot_general | solution.py:107
  6.0 2.6 %multiply_subtract_fusion = (f32[32,1,16,1024]{3,0,2,1:T(8,128)S(1)}, f32[32,1,16,1024]{3,0,2,1:T(8,128)S(1)}) fusion(f32[32,1,16,1024]{3,2,0,1:T(8,128)S(1)} %bitcast.279, f32[32,1,16,1024]{3,2,0,1:T(8,128)S(1)} %bitcast.278, f32[32,1024]{1,0:T(8,128)S(1)} %mul.659, f32[32,1024]{1,0:T(8,128)S(1)} %mul.648, f32[1024]{0:T(1024)S(1)} %fusion.130, ...), kind=kLoop, calls=%fused_computation.27 | loop fusion | flops 4194304 | bytes 8655360 | tf_op jit(solution)/shard_map/sub | solution.py:45
  8.6 1.3 %fusion.12 = f32[3,128,32,2,16]{1,2,4,3,0:T(8,128)S(1)} fusion(bf16[3,1,128,1024]{3,2,1,0:T(8,128)(2,1)S(1)} %copy-done.6, f32[128,1024]{1,0:T(8,128)S(1)} %bitcast.283, f32[32,1,16,1024]{3,0,2,1:T(8,128)S(1)} %get-tuple-element.8, f32[32,1,16,1024]{3,0,2,1:T(8,128)S(1)} %get-tuple-element.7), kind=kOutput, calls=%fused_computation.23 | convolution fusion | flops 811073536 | bytes 7077888 | tf_op jit(solution)/shard_map/dpjz,cyz->dcpjy/dot_general | solution.py:133
  9.9 1.3 %fusion.58 = f32[3,128,32,2,16]{1,2,4,3,0:T(8,128)S(1)} fusion(bf16[3,1,128,1024]{3,2,1,0:T(8,128)(2,1)S(1)} %copy-done.6, f32[128,1024]{1,0:T(8,128)S(1)} %bitcast.284, f32[32,1,16,1024]{3,0,2,1:T(8,128)S(1)} %get-tuple-element.8, f32[32,1,16,1024]{3,0,2,1:T(8,128)S(1)} %get-tuple-element.7), kind=kOutput, calls=%fused_computation.95 | convolution fusion | flops 810024960 | bytes 7077888 | tf_op jit(solution)/shard_map/dpjz,cyz->dcpjy/dot_general | solution.py:131
  11.2 1.3 %fusion.16 = bf16[32,3,2,16,128]{4,0,3,2,1:T(8,128)(2,1)S(1)} fusion(f32[3,128,32,2,16]{1,2,4,3,0:T(8,128)S(1)} %fusion.12, f32[3,128,32,2,16]{1,2,4,3,0:T(8,128)S(1)} %fusion.58, bf16[3,1,128,1024]{3,2,1,0:T(8,128)(2,1)S(1)} %copy-done.6, f32[128,1024]{1,0:T(8,128)S(1)} %bitcast.285, f32[32,1,16,1024]{3,0,2,1:T(8,128)S(1)} %get-tuple-element.8, ...), kind=kOutput, calls=%fused_computation.35 | convolution fusion | flops 811597824 | bytes 9437184 | tf_op jit(solution)/shard_map/dpjz,cyz->dcpjy/dot_general | solution.py:132
  12.5 1.2 %copy.43 = bf16[32,3,2,16,128]{4,3,2,1,0:T(8,128)(2,1)} copy(bf16[32,3,2,16,128]{4,0,3,2,1:T(8,128)(2,1)S(1)} %fusion.16) | data formatting | bytes 1572864 | tf_op jit(solution)/shard_map/convert_element_type | solution.py:135
  13.7 7.5 %all-to-all-start = ((bf16[32,3,2,16,128]{4,3,2,1,0:T(8,128)(2,1)}), bf16[32,3,2,16,128]{4,3,2,1,0:T(8,128)(2,1)S(1)}, u32[]{:S(2)}, u32[]{:S(2)}) async-start(bf16[32,3,2,16,128]{4,3,2,1,0:T(8,128)(2,1)} %copy.43), calls=%async_computation | async-start | bytes 1572864 | tf_op jit(solution)/shard_map/all_to_all | solution.py:136
  22.0 19.6 %all-to-all-done = bf16[32,3,2,16,128]{4,3,2,1,0:T(8,128)(2,1)S(1)} async-done(((bf16[32,3,2,16,128]{4,3,2,1,0:T(8,128)(2,1)}), bf16[32,3,2,16,128]{4,3,2,1,0:T(8,128)(2,1)S(1)}, u32[]{:S(2)}, u32[]{:S(2)}) %all-to-all-start) | async-done | bytes 786464 | tf_op jit(solution)/shard_map/all_to_all | solution.py:136
  41.6 1.1 %fusion.52 = f32[3,2,16,8,1024]{4,3,2,1,0:T(8,128)S(1)} fusion(bf16[8,4,3,1,2,16,128]{6,5,4,2,1,0,3:T(8,128)(2,1)S(1)} %bitcast.276, f32[512,512]{1,0:T(8,128)S(1)} %bitcast.269, f32[512,512]{1,0:T(8,128)S(1)} %bitcast.263), kind=kOutput, calls=%fused_computation.90 | convolution fusion | flops 806879232 | bytes 6029312 | tf_op jit(solution)/shard_map/yk,cpjxy->cpjxk/dot_general | solution.py:65
  42.7 1.2 %convolution_add_fusion.1 = f32[3,2,16,8,1024]{4,3,2,1,0:T(8,128)S(1)} fusion(f32[3,2,16,8,1024]{4,3,2,1,0:T(8,128)S(1)} %fusion.52, bf16[8,4,3,1,2,16,128]{6,5,4,2,1,0,3:T(8,128)(2,1)S(1)} %bitcast.277, f32[512,512]{1,0:T(8,128)S(1)} %bitcast.270, f32[512,512]{1,0:T(8,128)S(1)} %bitcast.264), kind=kOutput, calls=%fused_computation.29 | convolution fusion | flops 808189952 | bytes 9175040 | tf_op jit(solution)/shard_map/yk,cpjxy->cpjxk/dot_general | solution.py:65
  47.4 1.0 %fusion.60 = f32[3,2,16,8,1024]{4,3,2,1,0:T(8,128)S(1)} fusion(bf16[3,1,16,8,512]{4,3,2,1,0:T(8,128)(2,1)S(1)} %fusion.50, bf16[3,1,16,8,512]{4,3,2,1,0:T(8,128)(2,1)S(1)} %fusion.49, f32[512,512]{1,0:T(8,128)S(1)} %bitcast.273, f32[512,512]{1,0:T(8,128)S(1)} %bitcast.267), kind=kOutput, calls=%fused_computation.97 | convolution fusion | flops 807272448 | bytes 6029312 | tf_op jit(solution)/shard_map/yk,cpjxy->cpjxk/dot_general | solution.py:65
  48.4 1.0 %convolution_add_fusion = f32[3,2,16,8,1024]{4,3,2,1,0:T(8,128)S(1)} fusion(f32[3,2,16,8,1024]{4,3,2,1,0:T(8,128)S(1)} %fusion.60, bf16[3,1,16,8,512]{4,3,2,1,0:T(8,128)(2,1)S(1)} %fusion.50, bf16[3,1,16,8,512]{4,3,2,1,0:T(8,128)(2,1)S(1)} %fusion.49, f32[512,512]{1,0:T(8,128)S(1)} %bitcast.274, f32[512,512]{1,0:T(8,128)S(1)} %bitcast.268), kind=kOutput, calls=%fused_computation.28 | convolution fusion | flops 808583168 | bytes 9175040 | tf_op jit(solution)/shard_map/yk,cpjxy->cpjxk/dot_general | solution.py:65
  50.3 0.9 %pad_maximum_fusion.3 = bf16[3,2,16,8,1,4,128]{6,2,4,0,1,5,3:T(8,128)(2,1)} fusion(bf16[3,1,16,8,1,4,128]{6,2,4,0,1,5,3:T(8,128)(2,1)S(1)} %copy.49, bf16[3,1,16,8,1,4,128]{6,2,4,0,1,5,3:T(8,128)(2,1)S(1)} %copy.48), kind=kLoop, calls=%fused_computation.88 | loop fusion | flops 393216 | bytes 1572864 | tf_op jit(solution)/shard_map/stack | solution.py:182
  51.2 3.8 %all-to-all-start.1 = ((bf16[32,2,16,3,1,128]{5,2,4,3,1,0:T(8,128)(2,1)}), bf16[32,2,16,3,1,128]{5,2,4,3,1,0:T(8,128)(2,1)S(1)}, u32[]{:S(2)}, u32[]{:S(2)}) async-start(bf16[32,2,16,3,1,128]{5,2,4,3,1,0:T(8,128)(2,1)} %bitcast.281), calls=%async_computation.1 | async-start | bytes 1572864 | tf_op jit(solution)/shard_map/all_to_all | solution.py:189
  55.1 2.0 %pad_maximum_fusion = f32[32,2,16,1024]{3,0,2,1:T(8,128)S(1)} fusion(f32[32,1,16,1024]{3,0,2,1:T(8,128)} %copy-done.2, f32[32,1,16,1024]{3,0,2,1:T(8,128)S(1)} %copy-done.1), kind=kLoop, calls=%fused_computation.10 | loop fusion | flops 1048576 | bytes 8388608 | tf_op jit(solution)/shard_map/stack | solution.py:117
  57.1 2.4 %copy.51 = f32[32,2,16,1024]{3,2,1,0:T(8,128)S(1)} copy(f32[32,2,16,1024]{3,0,2,1:T(8,128)S(1)} %pad_maximum_fusion) | data formatting | bytes 8388608 | tf_op jit(solution)/shard_map/stack | solution.py:117
  59.6 2.1 %multiply_convert_fusion.1 = (bf16[1024,1,1024]{2,0,1:T(8,128)(2,1)S(1)}, bf16[1024,1,1024]{2,0,1:T(8,128)(2,1)}) fusion(f32[1024,1,1024]{2,0,1:T(8,128)S(1)} %bitcast.275, f32[1024]{0:T(1024)S(1)} %copy-done.5), kind=kLoop, calls=%fused_computation.16 | loop fusion | flops 10485760 | bytes 8392704 | tf_op jit(solution)/shard_map/convert_element_type | solution.py:199
  61.7 13.8 %all-to-all-done.1 = bf16[32,2,16,3,1,128]{5,2,4,3,1,0:T(8,128)(2,1)S(1)} async-done(((bf16[32,2,16,3,1,128]{5,2,4,3,1,0:T(8,128)(2,1)}), bf16[32,2,16,3,1,128]{5,2,4,3,1,0:T(8,128)(2,1)S(1)}, u32[]{:S(2)}, u32[]{:S(2)}) %all-to-all-start.1) | async-done | bytes 786464 | tf_op jit(solution)/shard_map/all_to_all | solution.py:189
  75.5 0.5 copy.50
  76.0 3.5 %fusion.6 = f32[384,2,1024]{2,0,1:T(8,128)S(1)} fusion(bf16[1024,1,1024]{2,0,1:T(8,128)(2,1)} %get-tuple-element.10, bf16[1024,1,1024]{2,0,1:T(8,128)(2,1)S(1)} %get-tuple-element.9, bf16[128,8,3,128]{3,2,1,0:T(4,128)(2,1)S(1)} %bitcast.282), kind=kOutput, calls=%fused_computation.11 | convolution fusion | flops 1619001344 | bytes 8126464 | tf_op jit(solution)/shard_map/kr,khz->rhz/dot_general | solution.py:202
  79.8 0.9 %copy-done.3 = bf16[3,1,128,1024]{3,2,1,0:T(8,128)(2,1)S(1)} copy-done((bf16[3,1,128,1024]{3,2,1,0:T(8,128)(2,1)S(1)}, bf16[3,1,128,1024]{3,2,1,0:T(8,128)(2,1)}, u32[]{:S(2)}) %copy-start.3) | copy-done | bytes 786456
  80.6 1.1 %add_convert_fusion = bf16[3,1,128,1024]{3,2,1,0:T(8,128)(2,1)} fusion(f32[3,1,128,1024]{3,2,1,0:T(8,128)S(1)} %bitcast.280, bf16[3,1,128,1024]{3,2,1,0:T(8,128)(2,1)S(1)} %copy-done.3), kind=kLoop, calls=%fused_computation.32 | loop fusion | flops 1179648 | bytes 3145728 | tf_op jit(solution)/shard_map/convert_element_type | solution.py:205
  (58 shorter events, 7.0 us)
Async XLA Ops:
  5.9 2.7 %copy-start.6 = (bf16[3,1,128,1024]{3,2,1,0:T(8,128)(2,1)S(1)}, bf16[3,1,128,1024]{3,2,1,0:T(8,128)(2,1)}, u32[]{:S(2)}) copy-start(bf16[3,1,128,1024]{3,2,1,0:T(8,128)(2,1)} %param.6) | copy-start | bytes 2359300
  8.6 2.6 %copy-start = (f32[32,1,16,1024]{3,0,2,1:T(8,128)}, f32[32,1,16,1024]{3,0,2,1:T(8,128)S(1)}, u32[]{:S(2)}) copy-start(f32[32,1,16,1024]{3,0,2,1:T(8,128)S(1)} %get-tuple-element.7) | copy-start | bytes 6291460
  8.6 2.6 %copy-start.2 = (f32[32,1,16,1024]{3,0,2,1:T(8,128)}, f32[32,1,16,1024]{3,0,2,1:T(8,128)S(1)}, u32[]{:S(2)}) copy-start(f32[32,1,16,1024]{3,0,2,1:T(8,128)S(1)} %get-tuple-element.8) | copy-start | bytes 6291460
  13.7 27.9 %all-to-all-start = ((bf16[32,3,2,16,128]{4,3,2,1,0:T(8,128)(2,1)}), bf16[32,3,2,16,128]{4,3,2,1,0:T(8,128)(2,1)S(1)}, u32[]{:S(2)}, u32[]{:S(2)}) async-start(bf16[32,3,2,16,128]{4,3,2,1,0:T(8,128)(2,1)} %copy.43), calls=%async_computation | async-start | bytes 1572864 | tf_op jit(solution)/shard_map/all_to_all | solution.py:136
  42.7 1.2 %copy-start.4 = (f32[8,8,1]{1,0,2:T(8,128)S(1)}, f32[8,8,1]{1,0,2:T(8,128)}, u32[]{:S(2)}) copy-start(f32[8,8,1]{1,0,2:T(8,128)} %constant.135) | copy-start | bytes 772
  50.1 5.0 %copy-start.1 = (f32[32,1,16,1024]{3,0,2,1:T(8,128)S(1)}, f32[32,1,16,1024]{3,0,2,1:T(8,128)}, u32[]{:S(2)}) copy-start(f32[32,1,16,1024]{3,0,2,1:T(8,128)} %copy-done) | copy-start | bytes 6291460
  51.2 24.2 %all-to-all-start.1 = ((bf16[32,2,16,3,1,128]{5,2,4,3,1,0:T(8,128)(2,1)}), bf16[32,2,16,3,1,128]{5,2,4,3,1,0:T(8,128)(2,1)S(1)}, u32[]{:S(2)}, u32[]{:S(2)}) async-start(bf16[32,2,16,3,1,128]{5,2,4,3,1,0:T(8,128)(2,1)} %bitcast.281), calls=%async_computation.1 | async-start | bytes 1572864 | tf_op jit(solution)/shard_map/all_to_all | solution.py:189
  57.1 2.5 %copy-start.5 = (f32[1024]{0:T(1024)S(1)}, f32[1024]{0:T(1024)}, u32[]{:S(2)}) copy-start(f32[1024]{0:T(1024)} %constant.134) | copy-start | bytes 12292
  79.5 1.1 %copy-start.3 = (bf16[3,1,128,1024]{3,2,1,0:T(8,128)(2,1)S(1)}, bf16[3,1,128,1024]{3,2,1,0:T(8,128)(2,1)}, u32[]{:S(2)}) copy-start(bf16[3,1,128,1024]{3,2,1,0:T(8,128)(2,1)} %param.7) | copy-start | bytes 2359300

commit v17 on v14

--- a/solution.py
+++ b/solution.py
@@ -70,15 +70,17 @@
 def curl_update(y_real, y_imag, wave_y, wave_z, kernel):
     half = TIME_STEP
 
-    def along_x(values):
-        return jnp.einsum("ab,jbk->jak", kernel, values, precision=lax.Precision.HIGHEST)
-
     xr, yr, zr = y_real[0], y_real[1], y_real[2]
     xi, yi, zi = y_imag[0], y_imag[1], y_imag[2]
     qy = half * wave_y
     qz = half * wave_z[:, None, None]
-    gyr, gyi = along_x(yr), along_x(yi)
-    gzr, gzi = along_x(zr), along_x(zi)
+    mixed = jnp.einsum(
+        "ab,qjbk->qjak",
+        kernel,
+        jnp.stack([yr, yi, zr, zi]),
+        precision=lax.Precision.HIGHEST,
+    )
+    gyr, gyi, gzr, gzi = mixed[0], mixed[1], mixed[2], mixed[3]
     b_real = jnp.stack([qy * zi - qz * yi, qz * xi - gzr, gyr - qy * xi])
     b_imag = jnp.stack([qz * yr - qy * zr, -qz * xr - gzi, gyi + qy * xr])
     return b_real, b_imag

time: 81.3 us -> 81 us (level)
    dot_general x8 -> x2, matrix products: 2.07 us -> 1.25 us  [curl_update(): jnp.einsum('ab,qjbk->qjak', kernel, jnp.stack([yr, yi, zr, zi]), precisio...]
  transfers between devices with their start and end apart: 2 -> 2, of which waited for: 2 -> 2; matrix products, arithmetic and copies ran while one was open for 8% -> 9% of each run, Pallas kernels for 0% -> 0%
where the time goes in v17:
time: 81 us; the launch traced here: 80.5 us
  waiting for transfers between devices  33.9 us (42%)
  matrix products  16.6 us (20%)
  starting transfers between devices  11.3 us (14%)
  other arithmetic  11.2 us (14%)
  local copies, waits for them, and re-layouts  7.06 us (9%)
    all_to_all x1, waiting for transfers between devices, on_device(): lax.all_to_all(spectrum, ('row', 'col'), split_axis=0, concat_axis=0, til...  19.6 us
    all_to_all x1, waiting for transfers between devices, on_device(): lax.all_to_all(outgoing, ('row', 'col'), split_axis=0, concat_axis=0, til...  14.3 us
    all_to_all x1, starting transfers between devices, on_device(): lax.all_to_all(spectrum, ('row', 'col'), split_axis=0, concat_axis=0, til...  7.48 us
    dot_general x6, matrix products, mat(): term = jnp.einsum(spec, part, operand, preferred_element_type=F32)  4.91 us
    all_to_all x1, starting transfers between devices, on_device(): lax.all_to_all(outgoing, ('row', 'col'), split_axis=0, concat_axis=0, til...  3.85 us
    dot_general x1, matrix products, on_device(): jnp.einsum('...k,k->...', one_hot, parts, preferred_element_type=F32)  2.98 us
    sub x2, other arithmetic, phase_table(): cosine = outer_cos * inner_cos - outer_sin * inner_sin  2.91 us
    dot_general x1, matrix products, on_device(): jnp.einsum(spec_back, returned, back_high, preferred_element_type=F32)  2.61 us
  transfers between devices with their start and end apart: 2, of which 2 were waited for; matrix products, arithmetic and copies ran while one was open for 9% of the time, Pallas kernels for 0%

profile of v17, /device:TPU:0, one launch (start us, length us, event | category | flops | bytes accessed | tf_op | source)
XLA Modules:
  0.0 80.5 jit_solution(8876782973392384166)
XLA Ops:
  1.7 0.7 reduce-precision_convert_fusion.4
  2.4 3.0 %fusion = f32[1,128,1024]{2,0,1:T(1,128)S(1)} fusion(s32[128,1024]{1,0:T(8,128)} %bitcast.219, s32[24]{0:T(128)S(1)} %and_select_fusion, bf16[8]{0:T(256)(128)(2,1)S(1)} %get-tuple-element.48, bf16[8]{0:T(256)(128)(2,1)S(1)} %get-tuple-element.47, bf16[8]{0:T(256)(128)(2,1)S(1)} %get-tuple-element.5), kind=kOutput, calls=%fused_computation | convolution fusion | flops 9437328 | bytes 1048720 | tf_op jit(solution)/shard_map/...k,k->.../dot_general | solution.py:109
  6.0 2.6 %multiply_subtract_fusion = (f32[32,1,16,1024]{3,0,2,1:T(8,128)S(1)}, f32[32,1,16,1024]{3,0,2,1:T(8,128)S(1)}) fusion(f32[32,1,16,1024]{3,2,0,1:T(8,128)S(1)} %bitcast.210, f32[32,1,16,1024]{3,2,0,1:T(8,128)S(1)} %bitcast.209, f32[32,1024]{1,0:T(8,128)S(1)} %mul.661, f32[32,1024]{1,0:T(8,128)S(1)} %mul.650, f32[1024]{0:T(1024)S(1)} %fusion.115, ...), kind=kLoop, calls=%fused_computation.23 | loop fusion | flops 4194304 | bytes 8655360 | tf_op jit(solution)/shard_map/sub | solution.py:45
  8.6 1.3 %fusion.8 = f32[3,128,32,2,16]{1,2,4,3,0:T(8,128)S(1)} fusion(bf16[3,1,128,1024]{3,2,1,0:T(8,128)(2,1)S(1)} %copy-done.6, f32[128,1024]{1,0:T(8,128)S(1)} %bitcast.216, f32[32,1,16,1024]{3,0,2,1:T(8,128)S(1)} %get-tuple-element.8, f32[32,1,16,1024]{3,0,2,1:T(8,128)S(1)} %get-tuple-element.7), kind=kOutput, calls=%fused_computation.18 | convolution fusion | flops 810418176 | bytes 7077888 | tf_op jit(solution)/shard_map/dpjz,cyz->dcpjy/dot_general | solution.py:134
  9.9 1.3 %fusion.6 = f32[3,128,32,2,16]{1,2,4,3,0:T(8,128)S(1)} fusion(bf16[3,1,128,1024]{3,2,1,0:T(8,128)(2,1)S(1)} %copy-done.6, f32[128,1024]{1,0:T(8,128)S(1)} %bitcast.217, f32[32,1,16,1024]{3,0,2,1:T(8,128)S(1)} %get-tuple-element.8, f32[32,1,16,1024]{3,0,2,1:T(8,128)S(1)} %get-tuple-element.7), kind=kOutput, calls=%fused_computation.16 | convolution fusion | flops 811073536 | bytes 7077888 | tf_op jit(solution)/shard_map/dpjz,cyz->dcpjy/dot_general | solution.py:135
  11.2 1.3 %fusion.15 = bf16[32,3,2,16,128]{4,0,3,2,1:T(8,128)(2,1)S(1)} fusion(f32[3,128,32,2,16]{1,2,4,3,0:T(8,128)S(1)} %fusion.6, f32[3,128,32,2,16]{1,2,4,3,0:T(8,128)S(1)} %fusion.8, bf16[3,1,128,1024]{3,2,1,0:T(8,128)(2,1)S(1)} %copy-done.6, f32[128,1024]{1,0:T(8,128)S(1)} %bitcast.218, f32[32,1,16,1024]{3,0,2,1:T(8,128)S(1)} %get-tuple-element.8, ...), kind=kOutput, calls=%fused_computation.32 | convolution fusion | flops 811204608 | bytes 9437184 | tf_op jit(solution)/shard_map/dpjz,cyz->dcpjy/dot_general | solution.py:133
  12.5 1.2 %copy.43 = bf16[32,3,2,16,128]{4,3,2,1,0:T(8,128)(2,1)} copy(bf16[32,3,2,16,128]{4,0,3,2,1:T(8,128)(2,1)S(1)} %fusion.15) | data formatting | bytes 1572864 | tf_op jit(solution)/shard_map/convert_element_type | solution.py:137
  13.7 7.5 %all-to-all-start = ((bf16[32,3,2,16,128]{4,3,2,1,0:T(8,128)(2,1)}), bf16[32,3,2,16,128]{4,3,2,1,0:T(8,128)(2,1)S(1)}, u32[]{:S(2)}, u32[]{:S(2)}) async-start(bf16[32,3,2,16,128]{4,3,2,1,0:T(8,128)(2,1)} %copy.43), calls=%async_computation | async-start | bytes 1572864 | tf_op jit(solution)/shard_map/all_to_all | solution.py:138
  22.0 19.6 %all-to-all-done = bf16[32,3,2,16,128]{4,3,2,1,0:T(8,128)(2,1)S(1)} async-done(((bf16[32,3,2,16,128]{4,3,2,1,0:T(8,128)(2,1)}), bf16[32,3,2,16,128]{4,3,2,1,0:T(8,128)(2,1)S(1)}, u32[]{:S(2)}, u32[]{:S(2)}) %all-to-all-start) | async-done | bytes 786464 | tf_op jit(solution)/shard_map/all_to_all | solution.py:138
  41.6 1.1 %fusion.46 = f32[3,2,16,8,1024]{4,3,2,1,0:T(8,128)S(1)} fusion(bf16[8,4,3,1,2,16,128]{6,5,4,2,1,0,3:T(8,128)(2,1)S(1)} %bitcast.206, f32[512,512]{1,0:T(8,128)S(1)} %bitcast.200, f32[512,512]{1,0:T(8,128)S(1)} %bitcast.194), kind=kOutput, calls=%fused_computation.72 | convolution fusion | flops 806879232 | bytes 6029312 | tf_op jit(solution)/shard_map/yk,cpjxy->cpjxk/dot_general | solution.py:65
  42.7 1.2 %convolution_add_fusion.1 = f32[3,2,16,8,1024]{4,3,2,1,0:T(8,128)S(1)} fusion(f32[3,2,16,8,1024]{4,3,2,1,0:T(8,128)S(1)} %fusion.46, bf16[8,4,3,1,2,16,128]{6,5,4,2,1,0,3:T(8,128)(2,1)S(1)} %bitcast.207, f32[512,512]{1,0:T(8,128)S(1)} %bitcast.201, f32[512,512]{1,0:T(8,128)S(1)} %bitcast.195), kind=kOutput, calls=%fused_computation.25 | convolution fusion | flops 808189952 | bytes 9175040 | tf_op jit(solution)/shard_map/yk,cpjxy->cpjxk/dot_general | solution.py:65
  45.7 1.0 %convolution_bitcast_fusion = f32[4,16,8,512]{3,2,1,0:T(8,128)S(1)} fusion(f32[8,8,1,1]{1,0,3,2:T(8,128)S(1)} %copy-done.5, f32[1,16,8,512]{3,2,1,0:T(8,128)S(1)} %get-tuple-element.28, f32[1,16,8,512]{3,2,1,0:T(8,128)S(1)} %get-tuple-element.26, f32[1,16,8,512]{3,2,1,0:T(8,128)S(1)} %get-tuple-element.27, f32[1,16,8,512]{3,2,1,0:T(8,128)S(1)} %get-tuple-element.25), kind=kOutput, calls=%fused_computation.31 | convolution fusion | flops 25952256 | bytes 2097408 | tf_op jit(solution)/shard_map/ab,qjbk->qjak/dot_general | solution.py:77
  47.0 1.0 %fusion.53 = f32[3,2,16,8,1024]{4,3,2,1,0:T(8,128)S(1)} fusion(bf16[3,1,16,8,512]{4,3,2,1,0:T(8,128)(2,1)S(1)} %fusion.44, bf16[3,1,16,8,512]{4,3,2,1,0:T(8,128)(2,1)S(1)} %fusion.43, f32[512,512]{1,0:T(8,128)S(1)} %bitcast.204, f32[512,512]{1,0:T(8,128)S(1)} %bitcast.198), kind=kOutput, calls=%fused_computation.80 | convolution fusion | flops 807272448 | bytes 6029312 | tf_op jit(solution)/shard_map/yk,cpjxy->cpjxk/dot_general | solution.py:65
  48.0 1.0 %convolution_add_fusion = f32[3,2,16,8,1024]{4,3,2,1,0:T(8,128)S(1)} fusion(f32[3,2,16,8,1024]{4,3,2,1,0:T(8,128)S(1)} %fusion.53, bf16[3,1,16,8,512]{4,3,2,1,0:T(8,128)(2,1)S(1)} %fusion.44, bf16[3,1,16,8,512]{4,3,2,1,0:T(8,128)(2,1)S(1)} %fusion.43, f32[512,512]{1,0:T(8,128)S(1)} %bitcast.205, f32[512,512]{1,0:T(8,128)S(1)} %bitcast.199), kind=kOutput, calls=%fused_computation.24 | convolution fusion | flops 808583168 | bytes 9175040 | tf_op jit(solution)/shard_map/yk,cpjxy->cpjxk/dot_general | solution.py:65
  49.9 0.9 %pad_maximum_fusion.3 = bf16[3,2,16,8,1,4,128]{6,2,4,0,1,5,3:T(8,128)(2,1)} fusion(bf16[3,1,16,8,1,4,128]{6,2,4,0,1,5,3:T(8,128)(2,1)S(1)} %copy.49, bf16[3,1,16,8,1,4,128]{6,2,4,0,1,5,3:T(8,128)(2,1)S(1)} %copy.48), kind=kLoop, calls=%fused_computation.70 | loop fusion | flops 393216 | bytes 1572864 | tf_op jit(solution)/shard_map/stack | solution.py:184
  50.8 3.8 %all-to-all-start.1 = ((bf16[32,2,16,3,1,128]{5,2,4,3,1,0:T(8,128)(2,1)}), bf16[32,2,16,3,1,128]{5,2,4,3,1,0:T(8,128)(2,1)S(1)}, u32[]{:S(2)}, u32[]{:S(2)}) async-start(bf16[32,2,16,3,1,128]{5,2,4,3,1,0:T(8,128)(2,1)} %bitcast.215), calls=%async_computation.1 | async-start | bytes 1572864 | tf_op jit(solution)/shard_map/all_to_all | solution.py:191
  54.7 2.4 %multiply_convert_fusion = (bf16[32,2,16,1024]{3,0,2,1:T(8,128)(2,1)S(1)}, bf16[32,2,16,1024]{3,0,2,1:T(8,128)(2,1)S(1)}) fusion(f32[32,2,16]{0,2,1:T(8,128)S(1)} %copy-done.4, f32[32,1,16,1024]{3,0,2,1:T(8,128)} %copy-done.2, f32[32,1,16,1024]{3,0,2,1:T(8,128)S(1)} %copy-done.1), kind=kLoop, calls=%fused_computation.8 | loop fusion | flops 11534336 | bytes 8392704 | tf_op jit(solution)/shard_map/convert_element_type | solution.py:202
  57.1 2.5 %copy.51 = bf16[32,2,16,1024]{3,2,1,0:T(8,128)(2,1)} copy(bf16[32,2,16,1024]{3,0,2,1:T(8,128)(2,1)S(1)} %get-tuple-element.10) | data formatting | bytes 4194304 | tf_op jit(solution)/shard_map/convert_element_type | solution.py:201
  59.6 1.2 %copy.52 = bf16[32,2,16,1024]{3,2,1,0:T(8,128)(2,1)S(1)} copy(bf16[32,2,16,1024]{3,0,2,1:T(8,128)(2,1)S(1)} %get-tuple-element.9) | data formatting | bytes 4194304 | tf_op jit(solution)/shard_map/convert_element_type | solution.py:202
  60.8 14.3 %all-to-all-done.1 = bf16[32,2,16,3,1,128]{5,2,4,3,1,0:T(8,128)(2,1)S(1)} async-done(((bf16[32,2,16,3,1,128]{5,2,4,3,1,0:T(8,128)(2,1)}), bf16[32,2,16,3,1,128]{5,2,4,3,1,0:T(8,128)(2,1)S(1)}, u32[]{:S(2)}, u32[]{:S(2)}) %all-to-all-start.1) | async-done | bytes 786464 | tf_op jit(solution)/shard_map/all_to_all | solution.py:191
  75.1 0.5 copy.50
  75.6 2.6 %fusion.31 = f32[384,1024]{1,0:T(8,128)S(1)} fusion(bf16[1024,1024]{1,0:T(8,128)(2,1)} %bitcast.211, bf16[128,8,3,128]{3,2,1,0:T(4,128)(2,1)S(1)} %bitcast.212), kind=kOutput, calls=%fused_computation.49 | convolution fusion | flops 805306368 | bytes 4456448 | tf_op jit(solution)/shard_map/kr,kz->rz/dot_general | solution.py:204
  78.3 1.0 %convolution_add_fusion.2 = f32[384,1024]{1,0:T(8,128)S(1)} fusion(f32[384,1024]{1,0:T(8,128)S(1)} %fusion.31, bf16[1024,1024]{1,0:T(8,128)(2,1)S(1)} %bitcast.208, bf16[128,8,3,128]{3,2,1,0:T(4,128)(2,1)S(1)} %bitcast.213), kind=kOutput, calls=%fused_computation.30 | convolution fusion | flops 805699584 | bytes 6029312 | tf_op jit(solution)/shard_map/kr,kz->rz/dot_general | solution.py:204
  79.4 1.1 %add_convert_fusion = bf16[3,1,128,1024]{3,2,1,0:T(8,128)(2,1)} fusion(f32[3,1,128,1024]{3,2,1,0:T(8,128)S(1)} %bitcast.214, bf16[3,1,128,1024]{3,2,1,0:T(8,128)(2,1)S(1)} %copy-done.3), kind=kLoop, calls=%fused_computation.27 | loop fusion | flops 1179648 | bytes 3145728 | tf_op jit(solution)/shard_map/convert_element_type | solution.py:208
  (56 shorter events, 6.0 us)
Async XLA Ops:
  5.9 2.7 %copy-start.6 = (bf16[3,1,128,1024]{3,2,1,0:T(8,128)(2,1)S(1)}, bf16[3,1,128,1024]{3,2,1,0:T(8,128)(2,1)}, u32[]{:S(2)}) copy-start(bf16[3,1,128,1024]{3,2,1,0:T(8,128)(2,1)} %param.6) | copy-start | bytes 2359300
  8.6 2.6 %copy-start = (f32[32,1,16,1024]{3,0,2,1:T(8,128)}, f32[32,1,16,1024]{3,0,2,1:T(8,128)S(1)}, u32[]{:S(2)}) copy-start(f32[32,1,16,1024]{3,0,2,1:T(8,128)S(1)} %get-tuple-element.7) | copy-start | bytes 6291460
  8.6 2.6 %copy-start.2 = (f32[32,1,16,1024]{3,0,2,1:T(8,128)}, f32[32,1,16,1024]{3,0,2,1:T(8,128)S(1)}, u32[]{:S(2)}) copy-start(f32[32,1,16,1024]{3,0,2,1:T(8,128)S(1)} %get-tuple-element.8) | copy-start | bytes 6291460
  13.7 27.9 %all-to-all-start = ((bf16[32,3,2,16,128]{4,3,2,1,0:T(8,128)(2,1)}), bf16[32,3,2,16,128]{4,3,2,1,0:T(8,128)(2,1)S(1)}, u32[]{:S(2)}, u32[]{:S(2)}) async-start(bf16[32,3,2,16,128]{4,3,2,1,0:T(8,128)(2,1)} %copy.43), calls=%async_computation | async-start | bytes 1572864 | tf_op jit(solution)/shard_map/all_to_all | solution.py:138
  43.9 0.7 copy-start.5
  49.7 5.0 %copy-start.1 = (f32[32,1,16,1024]{3,0,2,1:T(8,128)S(1)}, f32[32,1,16,1024]{3,0,2,1:T(8,128)}, u32[]{:S(2)}) copy-start(f32[32,1,16,1024]{3,0,2,1:T(8,128)} %copy-done) | copy-start | bytes 6291460
  49.7 5.0 %copy-start.4 = (f32[32,2,16]{0,2,1:T(8,128)S(1)}, f32[32,2,16]{0,2,1:T(8,128)}, u32[]{:S(2)}) copy-start(f32[32,2,16]{0,2,1:T(8,128)} %constant.134) | copy-start | bytes 12292
  50.8 24.3 %all-to-all-start.1 = ((bf16[32,2,16,3,1,128]{5,2,4,3,1,0:T(8,128)(2,1)}), bf16[32,2,16,3,1,128]{5,2,4,3,1,0:T(8,128)(2,1)S(1)}, u32[]{:S(2)}, u32[]{:S(2)}) async-start(bf16[32,2,16,3,1,128]{5,2,4,3,1,0:T(8,128)(2,1)} %bitcast.215), calls=%async_computation.1 | async-start | bytes 1572864 | tf_op jit(solution)/shard_map/all_to_all | solution.py:191
  78.2 1.1 %copy-start.3 = (bf16[3,1,128,1024]{3,2,1,0:T(8,128)(2,1)S(1)}, bf16[3,1,128,1024]{3,2,1,0:T(8,128)(2,1)}, u32[]{:S(2)}) copy-start(bf16[3,1,128,1024]{3,2,1,0:T(8,128)(2,1)} %param.7) | copy-start | bytes 2359300

commit v18 on v17

--- a/solution.py
+++ b/solution.py
@@ -166,16 +166,17 @@
         out_imag = (by_cos[:, 1] + by_sin[:, 0]) * scale
         return rounded(out_real), rounded(out_imag)
 
-    b_real, b_imag = curl_update(rounded(y_real), rounded(y_imag), wave_y, wave_z, kernel)
+    y_real, y_imag = rounded(y_real), rounded(y_imag)
+    if hermitian:
+        y_real = jnp.concatenate([y_real, rounded(by_cos[:, :, 0])], axis=1)
+        y_imag = jnp.concatenate([y_imag, rounded(-by_sin[:, :, 0])], axis=1)
+        wave_z = jnp.concatenate([wave_z, jnp.zeros((2,), F32)])
+    b_real, b_imag = curl_update(y_real, y_imag, wave_y, wave_z, kernel)
     back_real, back_imag = inverse_y(rounded(b_real), rounded(b_imag))
 
     if hermitian:
-        plane_real = by_cos[:, :, 0]
-        plane_imag = -by_sin[:, :, 0]
-        pb_real, pb_imag = curl_update(
-            rounded(plane_real), rounded(plane_imag), wave_y, jnp.zeros((2,), F32), kernel
-        )
-        pback_real, _ = inverse_y(rounded(pb_real), rounded(pb_imag))
+        pback_real = back_real[:, per_device:]
+        back_real, back_imag = back_real[:, :per_device], back_imag[:, :per_device]
         is_first = me == 0
         packed = ((lax.iota(jnp.int32, per_device) == 0) & is_first)[None, :, None, None]
         back_real = jnp.where(packed, pback_real[:, 0:1], back_real)

time: 81 us -> 80.5 us (level)
    dot_general x6 -> x4, matrix products: 4.91 us -> 4.46 us  [mat(): term = jnp.einsum(spec, part, operand, preferred_element_type=F32)]
where the time goes in v18:
time: 80.5 us; the launch traced here: 80.1 us
  waiting for transfers between devices  33.9 us (42%)
  matrix products  16 us (20%)
  other arithmetic  11.3 us (14%)
  starting transfers between devices  11.3 us (14%)
  local copies, waits for them, and re-layouts  7.05 us (9%)
    all_to_all x1, waiting for transfers between devices, on_device(): lax.all_to_all(spectrum, ('row', 'col'), split_axis=0, concat_axis=0, til...  19.6 us
    all_to_all x1, waiting for transfers between devices, on_device(): lax.all_to_all(outgoing, ('row', 'col'), split_axis=0, concat_axis=0, til...  14.3 us
    all_to_all x1, starting transfers between devices, on_device(): lax.all_to_all(spectrum, ('row', 'col'), split_axis=0, concat_axis=0, til...  7.48 us
    dot_general x4, matrix products, mat(): term = jnp.einsum(spec, part, operand, preferred_element_type=F32)  4.46 us
    all_to_all x1, starting transfers between devices, on_device(): lax.all_to_all(outgoing, ('row', 'col'), split_axis=0, concat_axis=0, til...  3.86 us
    dot_general x1, matrix products, on_device(): jnp.einsum('...k,k->...', one_hot, parts, preferred_element_type=F32)  2.98 us
    sub x2, other arithmetic, phase_table(): cosine = outer_cos * inner_cos - outer_sin * inner_sin  2.91 us
    dot_general x1, matrix products, on_device(): jnp.einsum(spec_back, returned, back_high, preferred_element_type=F32)  2.61 us
  transfers between devices with their start and end apart: 2, of which 2 were waited for; matrix products, arithmetic and copies ran while one was open for 9% of the time, Pallas kernels for 0%

profile of v18, /device:TPU:0, one launch (start us, length us, event | category | flops | bytes accessed | tf_op | source)
XLA Modules:
  0.0 80.1 jit_solution(6320427511708423415)
XLA Ops:
  1.7 0.7 reduce-precision_convert_fusion.4
  2.4 3.0 %fusion = f32[1,128,1024]{2,0,1:T(1,128)S(1)} fusion(s32[128,1024]{1,0:T(8,128)} %bitcast.179, s32[24]{0:T(128)S(1)} %and_select_fusion, bf16[8]{0:T(256)(128)(2,1)S(1)} %get-tuple-element.37, bf16[8]{0:T(256)(128)(2,1)S(1)} %get-tuple-element.36, bf16[8]{0:T(256)(128)(2,1)S(1)} %get-tuple-element.11), kind=kOutput, calls=%fused_computation | convolution fusion | flops 9437328 | bytes 1048720 | tf_op jit(solution)/shard_map/...k,k->.../dot_general | solution.py:109
  6.0 2.6 %multiply_subtract_fusion = (f32[32,1,16,1024]{3,0,2,1:T(8,128)S(1)}, f32[32,1,16,1024]{3,0,2,1:T(8,128)S(1)}) fusion(f32[32,1,16,1024]{3,2,0,1:T(8,128)S(1)} %bitcast.170, f32[32,1,16,1024]{3,2,0,1:T(8,128)S(1)} %bitcast.169, f32[32,1024]{1,0:T(8,128)S(1)} %mul.557, f32[32,1024]{1,0:T(8,128)S(1)} %mul.546, f32[1024]{0:T(1024)S(1)} %fusion.112, ...), kind=kLoop, calls=%fused_computation.23 | loop fusion | flops 4194304 | bytes 8655360 | tf_op jit(solution)/shard_map/sub | solution.py:45
  8.6 1.3 %fusion.8 = f32[3,128,32,2,16]{1,2,4,3,0:T(8,128)S(1)} fusion(bf16[3,1,128,1024]{3,2,1,0:T(8,128)(2,1)S(1)} %copy-done.6, f32[128,1024]{1,0:T(8,128)S(1)} %bitcast.176, f32[32,1,16,1024]{3,0,2,1:T(8,128)S(1)} %get-tuple-element.14, f32[32,1,16,1024]{3,0,2,1:T(8,128)S(1)} %get-tuple-element.13), kind=kOutput, calls=%fused_computation.18 | convolution fusion | flops 810418176 | bytes 7077888 | tf_op jit(solution)/shard_map/dpjz,cyz->dcpjy/dot_general | solution.py:134
  9.9 1.3 %fusion.6 = f32[3,128,32,2,16]{1,2,4,3,0:T(8,128)S(1)} fusion(bf16[3,1,128,1024]{3,2,1,0:T(8,128)(2,1)S(1)} %copy-done.6, f32[128,1024]{1,0:T(8,128)S(1)} %bitcast.177, f32[32,1,16,1024]{3,0,2,1:T(8,128)S(1)} %get-tuple-element.14, f32[32,1,16,1024]{3,0,2,1:T(8,128)S(1)} %get-tuple-element.13), kind=kOutput, calls=%fused_computation.16 | convolution fusion | flops 811073536 | bytes 7077888 | tf_op jit(solution)/shard_map/dpjz,cyz->dcpjy/dot_general | solution.py:135
  11.2 1.3 %fusion.15 = bf16[32,3,2,16,128]{4,0,3,2,1:T(8,128)(2,1)S(1)} fusion(f32[3,128,32,2,16]{1,2,4,3,0:T(8,128)S(1)} %fusion.6, f32[3,128,32,2,16]{1,2,4,3,0:T(8,128)S(1)} %fusion.8, bf16[3,1,128,1024]{3,2,1,0:T(8,128)(2,1)S(1)} %copy-done.6, f32[128,1024]{1,0:T(8,128)S(1)} %bitcast.178, f32[32,1,16,1024]{3,0,2,1:T(8,128)S(1)} %get-tuple-element.14, ...), kind=kOutput, calls=%fused_computation.32 | convolution fusion | flops 811204608 | bytes 9437184 | tf_op jit(solution)/shard_map/dpjz,cyz->dcpjy/dot_general | solution.py:133
  12.5 1.2 %copy.52 = bf16[32,3,2,16,128]{4,3,2,1,0:T(8,128)(2,1)} copy(bf16[32,3,2,16,128]{4,0,3,2,1:T(8,128)(2,1)S(1)} %fusion.15) | data formatting | bytes 1572864 | tf_op jit(solution)/shard_map/convert_element_type | solution.py:137
  13.7 7.5 %all-to-all-start = ((bf16[32,3,2,16,128]{4,3,2,1,0:T(8,128)(2,1)}), bf16[32,3,2,16,128]{4,3,2,1,0:T(8,128)(2,1)S(1)}, u32[]{:S(2)}, u32[]{:S(2)}) async-start(bf16[32,3,2,16,128]{4,3,2,1,0:T(8,128)(2,1)} %copy.52), calls=%async_computation | async-start | bytes 1572864 | tf_op jit(solution)/shard_map/all_to_all | solution.py:138
  22.0 19.6 %all-to-all-done = bf16[32,3,2,16,128]{4,3,2,1,0:T(8,128)(2,1)S(1)} async-done(((bf16[32,3,2,16,128]{4,3,2,1,0:T(8,128)(2,1)}), bf16[32,3,2,16,128]{4,3,2,1,0:T(8,128)(2,1)S(1)}, u32[]{:S(2)}, u32[]{:S(2)}) %all-to-all-start) | async-done | bytes 786464 | tf_op jit(solution)/shard_map/all_to_all | solution.py:138
  41.6 1.1 %fusion.50 = f32[3,2,16,8,1024]{4,3,2,1,0:T(8,128)S(1)} fusion(bf16[8,4,3,1,2,16,128]{6,5,4,2,1,0,3:T(8,128)(2,1)S(1)} %bitcast.166, f32[512,512]{1,0:T(8,128)S(1)} %bitcast.162, f32[512,512]{1,0:T(8,128)S(1)} %bitcast.158), kind=kOutput, calls=%fused_computation.86 | convolution fusion | flops 806879232 | bytes 6029312 | tf_op jit(solution)/shard_map/yk,cpjxy->cpjxk/dot_general | solution.py:65
  42.7 1.2 %convolution_add_fusion.1 = f32[3,2,16,8,1024]{4,3,2,1,0:T(8,128)S(1)} fusion(f32[3,2,16,8,1024]{4,3,2,1,0:T(8,128)S(1)} %fusion.50, bf16[8,4,3,1,2,16,128]{6,5,4,2,1,0,3:T(8,128)(2,1)S(1)} %bitcast.167, f32[512,512]{1,0:T(8,128)S(1)} %bitcast.163, f32[512,512]{1,0:T(8,128)S(1)} %bitcast.159), kind=kOutput, calls=%fused_computation.25 | convolution fusion | flops 808189952 | bytes 9175040 | tf_op jit(solution)/shard_map/yk,cpjxy->cpjxk/dot_general | solution.py:65
  44.9 1.1 %convolution_bitcast_fusion = f32[4,18,8,512]{3,2,1,0:T(8,128)S(1)} fusion(f32[8,8,1,1]{1,0,3,2:T(8,128)S(1)} %copy-done.5, f32[1,18,8,512]{3,2,1,0:T(8,128)S(1)} %get-tuple-element.29, f32[1,18,8,512]{3,2,1,0:T(8,128)S(1)} %get-tuple-element.10, f32[1,18,8,512]{3,2,1,0:T(8,128)S(1)} %get-tuple-element.28, f32[1,18,8,512]{3,2,1,0:T(8,128)S(1)} %get-tuple-element.9), kind=kOutput, calls=%fused_computation.31 | convolution fusion | flops 29196288 | bytes 2359552 | tf_op jit(solution)/shard_map/ab,qjbk->qjak/dot_general | solution.py:77
  46.3 1.1 %fusion.55 = f32[3,2,18,8,1024]{4,3,2,1,0:T(8,128)S(1)} fusion(bf16[3,1,18,8,512]{4,3,2,1,0:T(8,128)(2,1)S(1)} %fusion.35, bf16[3,1,18,8,512]{4,3,2,1,0:T(8,128)(2,1)S(1)} %fusion.34, f32[512,512]{1,0:T(8,128)S(1)} %bitcast.164, f32[512,512]{1,0:T(8,128)S(1)} %bitcast.160), kind=kOutput, calls=%fused_computation.91 | convolution fusion | flops 907984896 | bytes 6520832 | tf_op jit(solution)/shard_map/yk,cpjxy->cpjxk/dot_general | solution.py:65
  47.4 1.1 %convolution_add_fusion = f32[3,2,18,8,1024]{4,3,2,1,0:T(8,128)S(1)} fusion(f32[3,2,18,8,1024]{4,3,2,1,0:T(8,128)S(1)} %fusion.55, bf16[3,1,18,8,512]{4,3,2,1,0:T(8,128)(2,1)S(1)} %fusion.35, bf16[3,1,18,8,512]{4,3,2,1,0:T(8,128)(2,1)S(1)} %fusion.34, f32[512,512]{1,0:T(8,128)S(1)} %bitcast.165, f32[512,512]{1,0:T(8,128)S(1)} %bitcast.161), kind=kOutput, calls=%fused_computation.24 | convolution fusion | flops 909393920 | bytes 10059776 | tf_op jit(solution)/shard_map/yk,cpjxy->cpjxk/dot_general | solution.py:65
  49.4 0.9 %pad_maximum_fusion.3 = bf16[3,2,16,8,1,4,128]{6,2,4,0,1,5,3:T(8,128)(2,1)} fusion(bf16[3,1,16,8,1,4,128]{6,2,4,0,1,5,3:T(8,128)(2,1)S(1)} %copy.61, bf16[3,1,16,8,1,4,128]{6,2,4,0,1,5,3:T(8,128)(2,1)S(1)} %copy.60), kind=kLoop, calls=%fused_computation.84 | loop fusion | flops 393216 | bytes 1572864 | tf_op jit(solution)/shard_map/stack | solution.py:185
  50.4 3.9 %all-to-all-start.1 = ((bf16[32,2,16,3,1,128]{5,2,4,3,1,0:T(8,128)(2,1)}), bf16[32,2,16,3,1,128]{5,2,4,3,1,0:T(8,128)(2,1)S(1)}, u32[]{:S(2)}, u32[]{:S(2)}) async-start(bf16[32,2,16,3,1,128]{5,2,4,3,1,0:T(8,128)(2,1)} %bitcast.175), calls=%async_computation.1 | async-start | bytes 1572864 | tf_op jit(solution)/shard_map/all_to_all | solution.py:192
  54.3 2.4 %multiply_convert_fusion = (bf16[32,2,16,1024]{3,0,2,1:T(8,128)(2,1)S(1)}, bf16[32,2,16,1024]{3,0,2,1:T(8,128)(2,1)S(1)}) fusion(f32[32,2,16]{0,2,1:T(8,128)S(1)} %copy-done.4, f32[32,1,16,1024]{3,0,2,1:T(8,128)} %copy-done.2, f32[32,1,16,1024]{3,0,2,1:T(8,128)S(1)} %copy-done.1), kind=kLoop, calls=%fused_computation.8 | loop fusion | flops 11534336 | bytes 8392704 | tf_op jit(solution)/shard_map/convert_element_type | solution.py:203
  56.7 2.5 %copy.63 = bf16[32,2,16,1024]{3,2,1,0:T(8,128)(2,1)} copy(bf16[32,2,16,1024]{3,0,2,1:T(8,128)(2,1)S(1)} %get-tuple-element.16) | data formatting | bytes 4194304 | tf_op jit(solution)/shard_map/convert_element_type | solution.py:202
  59.2 1.2 %copy.64 = bf16[32,2,16,1024]{3,2,1,0:T(8,128)(2,1)S(1)} copy(bf16[32,2,16,1024]{3,0,2,1:T(8,128)(2,1)S(1)} %get-tuple-element.15) | data formatting | bytes 4194304 | tf_op jit(solution)/shard_map/convert_element_type | solution.py:203
  60.3 14.3 %all-to-all-done.1 = bf16[32,2,16,3,1,128]{5,2,4,3,1,0:T(8,128)(2,1)S(1)} async-done(((bf16[32,2,16,3,1,128]{5,2,4,3,1,0:T(8,128)(2,1)}), bf16[32,2,16,3,1,128]{5,2,4,3,1,0:T(8,128)(2,1)S(1)}, u32[]{:S(2)}, u32[]{:S(2)}) %all-to-all-start.1) | async-done | bytes 786464 | tf_op jit(solution)/shard_map/all_to_all | solution.py:192
  74.6 0.5 copy.62
  75.2 2.6 %fusion.40 = f32[384,1024]{1,0:T(8,128)S(1)} fusion(bf16[1024,1024]{1,0:T(8,128)(2,1)} %bitcast.171, bf16[128,8,3,128]{3,2,1,0:T(4,128)(2,1)S(1)} %bitcast.172), kind=kOutput, calls=%fused_computation.70 | convolution fusion | flops 805306368 | bytes 4456448 | tf_op jit(solution)/shard_map/kr,kz->rz/dot_general | solution.py:205
  77.8 1.0 %convolution_add_fusion.2 = f32[384,1024]{1,0:T(8,128)S(1)} fusion(f32[384,1024]{1,0:T(8,128)S(1)} %fusion.40, bf16[1024,1024]{1,0:T(8,128)(2,1)S(1)} %bitcast.168, bf16[128,8,3,128]{3,2,1,0:T(4,128)(2,1)S(1)} %bitcast.173), kind=kOutput, calls=%fused_computation.30 | convolution fusion | flops 805699584 | bytes 6029312 | tf_op jit(solution)/shard_map/kr,kz->rz/dot_general | solution.py:205
  78.9 1.1 %add_convert_fusion = bf16[3,1,128,1024]{3,2,1,0:T(8,128)(2,1)} fusion(f32[3,1,128,1024]{3,2,1,0:T(8,128)S(1)} %bitcast.174, bf16[3,1,128,1024]{3,2,1,0:T(8,128)(2,1)S(1)} %copy-done.3), kind=kLoop, calls=%fused_computation.27 | loop fusion | flops 1179648 | bytes 3145728 | tf_op jit(solution)/shard_map/convert_element_type | solution.py:209
  (50 shorter events, 5.3 us)
Async XLA Ops:
  5.9 2.7 %copy-start.6 = (bf16[3,1,128,1024]{3,2,1,0:T(8,128)(2,1)S(1)}, bf16[3,1,128,1024]{3,2,1,0:T(8,128)(2,1)}, u32[]{:S(2)}) copy-start(bf16[3,1,128,1024]{3,2,1,0:T(8,128)(2,1)} %param.6) | copy-start | bytes 2359300
  8.6 2.6 %copy-start = (f32[32,1,16,1024]{3,0,2,1:T(8,128)}, f32[32,1,16,1024]{3,0,2,1:T(8,128)S(1)}, u32[]{:S(2)}) copy-start(f32[32,1,16,1024]{3,0,2,1:T(8,128)S(1)} %get-tuple-element.13) | copy-start | bytes 6291460
  8.6 2.6 %copy-start.2 = (f32[32,1,16,1024]{3,0,2,1:T(8,128)}, f32[32,1,16,1024]{3,0,2,1:T(8,128)S(1)}, u32[]{:S(2)}) copy-start(f32[32,1,16,1024]{3,0,2,1:T(8,128)S(1)} %get-tuple-element.14) | copy-start | bytes 6291460
  13.7 27.9 %all-to-all-start = ((bf16[32,3,2,16,128]{4,3,2,1,0:T(8,128)(2,1)}), bf16[32,3,2,16,128]{4,3,2,1,0:T(8,128)(2,1)S(1)}, u32[]{:S(2)}, u32[]{:S(2)}) async-start(bf16[32,3,2,16,128]{4,3,2,1,0:T(8,128)(2,1)} %copy.52), calls=%async_computation | async-start | bytes 1572864 | tf_op jit(solution)/shard_map/all_to_all | solution.py:138
  44.2 0.7 copy-start.5
  49.2 5.0 %copy-start.1 = (f32[32,1,16,1024]{3,0,2,1:T(8,128)S(1)}, f32[32,1,16,1024]{3,0,2,1:T(8,128)}, u32[]{:S(2)}) copy-start(f32[32,1,16,1024]{3,0,2,1:T(8,128)} %copy-done) | copy-start | bytes 6291460
  49.3 5.0 %copy-start.4 = (f32[32,2,16]{0,2,1:T(8,128)S(1)}, f32[32,2,16]{0,2,1:T(8,128)}, u32[]{:S(2)}) copy-start(f32[32,2,16]{0,2,1:T(8,128)} %constant.133) | copy-start | bytes 12292
  50.4 24.3 %all-to-all-start.1 = ((bf16[32,2,16,3,1,128]{5,2,4,3,1,0:T(8,128)(2,1)}), bf16[32,2,16,3,1,128]{5,2,4,3,1,0:T(8,128)(2,1)S(1)}, u32[]{:S(2)}, u32[]{:S(2)}) async-start(bf16[32,2,16,3,1,128]{5,2,4,3,1,0:T(8,128)(2,1)} %bitcast.175), calls=%async_computation.1 | async-start | bytes 1572864 | tf_op jit(solution)/shard_map/all_to_all | solution.py:192
  77.8 1.1 %copy-start.3 = (bf16[3,1,128,1024]{3,2,1,0:T(8,128)(2,1)S(1)}, bf16[3,1,128,1024]{3,2,1,0:T(8,128)(2,1)}, u32[]{:S(2)}) copy-start(bf16[3,1,128,1024]{3,2,1,0:T(8,128)(2,1)} %param.7) | copy-start | bytes 2359300

commit v19 on v18

--- a/solution.py
+++ b/solution.py
@@ -74,12 +74,7 @@
     xi, yi, zi = y_imag[0], y_imag[1], y_imag[2]
     qy = half * wave_y
     qz = half * wave_z[:, None, None]
-    mixed = jnp.einsum(
-        "ab,qjbk->qjak",
-        kernel,
-        jnp.stack([yr, yi, zr, zi]),
-        precision=lax.Precision.HIGHEST,
-    )
+    mixed = mat(split_parts(kernel), jnp.stack([yr, yi, zr, zi]).astype(BF16), "ab,qjbk->qjak")
     gyr, gyi, gzr, gzi = mixed[0], mixed[1], mixed[2], mixed[3]
     b_real = jnp.stack([qy * zi - qz * yi, qz * xi - gzr, gyr - qy * xi])
     b_imag = jnp.stack([qz * yr - qy * zr, -qz * xr - gzi, gyi + qy * xr])

time: 80.5 us -> 80 us (level)
    dot_general x1 -> x0, matrix products: 1.12 us -> none  [curl_update(): jnp.einsum('ab,qjbk->qjak', kernel, jnp.stack([yr, yi, zr, zi]), precisio...]
    dot_general x4 -> x6, matrix products: 4.46 us -> 5.1 us  [mat(): term = jnp.einsum(spec, part, operand, preferred_element_type=F32)]
where the time goes in v19:
time: 80 us; the launch traced here: 79.5 us
  waiting for transfers between devices  33.9 us (42%)
  matrix products  15.5 us (19%)
  starting transfers between devices  11.3 us (14%)
  other arithmetic  11.2 us (14%)
  local copies, waits for them, and re-layouts  7.1 us (9%)
    all_to_all x1, waiting for transfers between devices, on_device(): lax.all_to_all(spectrum, ('row', 'col'), split_axis=0, concat_axis=0, til...  19.6 us
    all_to_all x1, waiting for transfers between devices, on_device(): lax.all_to_all(outgoing, ('row', 'col'), split_axis=0, concat_axis=0, til...  14.3 us
    all_to_all x1, starting transfers between devices, on_device(): lax.all_to_all(spectrum, ('row', 'col'), split_axis=0, concat_axis=0, til...  7.48 us
    dot_general x6, matrix products, mat(): term = jnp.einsum(spec, part, operand, preferred_element_type=F32)  5.1 us
    all_to_all x1, starting transfers between devices, on_device(): lax.all_to_all(outgoing, ('row', 'col'), split_axis=0, concat_axis=0, til...  3.85 us
    dot_general x1, matrix products, on_device(): jnp.einsum('...k,k->...', one_hot, parts, preferred_element_type=F32)  2.98 us
    sub x2, other arithmetic, phase_table(): cosine = outer_cos * inner_cos - outer_sin * inner_sin  2.91 us
    dot_general x1, matrix products, on_device(): jnp.einsum(spec_back, returned, back_high, preferred_element_type=F32)  2.61 us
  transfers between devices with their start and end apart: 2, of which 2 were waited for; matrix products, arithmetic and copies ran while one was open for 9% of the time, Pallas kernels for 0%

profile of v19, /device:TPU:0, one launch (start us, length us, event | category | flops | bytes accessed | tf_op | source)
XLA Modules:
  0.0 79.5 jit_solution(17638859695219446996)
XLA Ops:
  0.5 0.5 fusion.87
  1.0 0.7 reduce-precision_convert_fusion.4
  2.3 3.0 %fusion = f32[1,128,1024]{2,0,1:T(1,128)S(1)} fusion(s32[128,1024]{1,0:T(8,128)} %bitcast.183, s32[24]{0:T(128)S(1)} %and_select_fusion, bf16[8]{0:T(256)(128)(2,1)S(1)} %get-tuple-element.34, bf16[8]{0:T(256)(128)(2,1)S(1)} %get-tuple-element.33, bf16[8]{0:T(256)(128)(2,1)S(1)} %get-tuple-element.5), kind=kOutput, calls=%fused_computation | convolution fusion | flops 9437328 | bytes 1048720 | tf_op jit(solution)/shard_map/...k,k->.../dot_general | solution.py:104
  5.9 2.6 %multiply_subtract_fusion = (f32[32,1,16,1024]{3,0,2,1:T(8,128)S(1)}, f32[32,1,16,1024]{3,0,2,1:T(8,128)S(1)}) fusion(f32[32,1,16,1024]{3,2,0,1:T(8,128)S(1)} %bitcast.173, f32[32,1,16,1024]{3,2,0,1:T(8,128)S(1)} %bitcast.174, f32[32,1024]{1,0:T(8,128)S(1)} %mul.557, f32[32,1024]{1,0:T(8,128)S(1)} %mul.546, f32[1024]{0:T(1024)S(1)} %fusion.107, ...), kind=kLoop, calls=%fused_computation.23 | loop fusion | flops 4194304 | bytes 8655360 | tf_op jit(solution)/shard_map/sub | solution.py:45
  8.6 1.3 %fusion.8 = f32[3,128,32,2,16]{1,2,4,3,0:T(8,128)S(1)} fusion(bf16[3,1,128,1024]{3,2,1,0:T(8,128)(2,1)S(1)} %copy-done.6, f32[128,1024]{1,0:T(8,128)S(1)} %bitcast.180, f32[32,1,16,1024]{3,0,2,1:T(8,128)S(1)} %get-tuple-element.8, f32[32,1,16,1024]{3,0,2,1:T(8,128)S(1)} %get-tuple-element.7), kind=kOutput, calls=%fused_computation.18 | convolution fusion | flops 810418176 | bytes 7077888 | tf_op jit(solution)/shard_map/dpjz,cyz->dcpjy/dot_general | solution.py:129
  9.9 1.3 %fusion.6 = f32[3,128,32,2,16]{1,2,4,3,0:T(8,128)S(1)} fusion(bf16[3,1,128,1024]{3,2,1,0:T(8,128)(2,1)S(1)} %copy-done.6, f32[128,1024]{1,0:T(8,128)S(1)} %bitcast.181, f32[32,1,16,1024]{3,0,2,1:T(8,128)S(1)} %get-tuple-element.8, f32[32,1,16,1024]{3,0,2,1:T(8,128)S(1)} %get-tuple-element.7), kind=kOutput, calls=%fused_computation.16 | convolution fusion | flops 811073536 | bytes 7077888 | tf_op jit(solution)/shard_map/dpjz,cyz->dcpjy/dot_general | solution.py:130
  11.2 1.3 %fusion.16 = bf16[32,3,2,16,128]{4,0,3,2,1:T(8,128)(2,1)S(1)} fusion(f32[3,128,32,2,16]{1,2,4,3,0:T(8,128)S(1)} %fusion.6, f32[3,128,32,2,16]{1,2,4,3,0:T(8,128)S(1)} %fusion.8, bf16[3,1,128,1024]{3,2,1,0:T(8,128)(2,1)S(1)} %copy-done.6, f32[128,1024]{1,0:T(8,128)S(1)} %bitcast.182, f32[32,1,16,1024]{3,0,2,1:T(8,128)S(1)} %get-tuple-element.8, ...), kind=kOutput, calls=%fused_computation.33 | convolution fusion | flops 811204608 | bytes 9437184 | tf_op jit(solution)/shard_map/dpjz,cyz->dcpjy/dot_general | solution.py:128
  12.5 1.2 %copy.52 = bf16[32,3,2,16,128]{4,3,2,1,0:T(8,128)(2,1)} copy(bf16[32,3,2,16,128]{4,0,3,2,1:T(8,128)(2,1)S(1)} %fusion.16) | data formatting | bytes 1572864 | tf_op jit(solution)/shard_map/convert_element_type | solution.py:132
  13.7 7.5 %all-to-all-start = ((bf16[32,3,2,16,128]{4,3,2,1,0:T(8,128)(2,1)}), bf16[32,3,2,16,128]{4,3,2,1,0:T(8,128)(2,1)S(1)}, u32[]{:S(2)}, u32[]{:S(2)}) async-start(bf16[32,3,2,16,128]{4,3,2,1,0:T(8,128)(2,1)} %copy.52), calls=%async_computation | async-start | bytes 1572864 | tf_op jit(solution)/shard_map/all_to_all | solution.py:133
  22.0 19.6 %all-to-all-done = bf16[32,3,2,16,128]{4,3,2,1,0:T(8,128)(2,1)S(1)} async-done(((bf16[32,3,2,16,128]{4,3,2,1,0:T(8,128)(2,1)}), bf16[32,3,2,16,128]{4,3,2,1,0:T(8,128)(2,1)S(1)}, u32[]{:S(2)}, u32[]{:S(2)}) %all-to-all-start) | async-done | bytes 786464 | tf_op jit(solution)/shard_map/all_to_all | solution.py:133
  41.6 1.1 %fusion.44 = f32[3,2,16,8,1024]{4,3,2,1,0:T(8,128)S(1)} fusion(bf16[8,4,3,1,2,16,128]{6,5,4,2,1,0,3:T(8,128)(2,1)S(1)} %bitcast.170, f32[512,512]{1,0:T(8,128)S(1)} %bitcast.166, f32[512,512]{1,0:T(8,128)S(1)} %bitcast.162), kind=kOutput, calls=%fused_computation.80 | convolution fusion | flops 806879232 | bytes 6029312 | tf_op jit(solution)/shard_map/yk,cpjxy->cpjxk/dot_general | solution.py:65
  42.7 1.2 %convolution_add_fusion.1 = f32[3,2,16,8,1024]{4,3,2,1,0:T(8,128)S(1)} fusion(f32[3,2,16,8,1024]{4,3,2,1,0:T(8,128)S(1)} %fusion.44, bf16[8,4,3,1,2,16,128]{6,5,4,2,1,0,3:T(8,128)(2,1)S(1)} %bitcast.171, f32[512,512]{1,0:T(8,128)S(1)} %bitcast.167, f32[512,512]{1,0:T(8,128)S(1)} %bitcast.163), kind=kOutput, calls=%fused_computation.25 | convolution fusion | flops 808189952 | bytes 9175040 | tf_op jit(solution)/shard_map/yk,cpjxy->cpjxk/dot_general | solution.py:65
  45.7 1.1 %fusion.49 = f32[3,2,18,8,1024]{4,3,2,1,0:T(8,128)S(1)} fusion(bf16[3,1,18,8,512]{4,3,2,1,0:T(8,128)(2,1)S(1)} %fusion.29, bf16[3,1,18,8,512]{4,3,2,1,0:T(8,128)(2,1)S(1)} %fusion.28, f32[512,512]{1,0:T(8,128)S(1)} %bitcast.168, f32[512,512]{1,0:T(8,128)S(1)} %bitcast.164), kind=kOutput, calls=%fused_computation.86 | convolution fusion | flops 907984896 | bytes 6520832 | tf_op jit(solution)/shard_map/yk,cpjxy->cpjxk/dot_general | solution.py:65
  46.8 1.1 %convolution_add_fusion = f32[3,2,18,8,1024]{4,3,2,1,0:T(8,128)S(1)} fusion(f32[3,2,18,8,1024]{4,3,2,1,0:T(8,128)S(1)} %fusion.49, bf16[3,1,18,8,512]{4,3,2,1,0:T(8,128)(2,1)S(1)} %fusion.29, bf16[3,1,18,8,512]{4,3,2,1,0:T(8,128)(2,1)S(1)} %fusion.28, f32[512,512]{1,0:T(8,128)S(1)} %bitcast.169, f32[512,512]{1,0:T(8,128)S(1)} %bitcast.165), kind=kOutput, calls=%fused_computation.24 | convolution fusion | flops 909393920 | bytes 10059776 | tf_op jit(solution)/shard_map/yk,cpjxy->cpjxk/dot_general | solution.py:65
  48.9 0.9 %pad_maximum_fusion.3 = bf16[3,2,16,8,1,4,128]{6,2,4,0,1,5,3:T(8,128)(2,1)} fusion(bf16[3,1,16,8,1,4,128]{6,2,4,0,1,5,3:T(8,128)(2,1)S(1)} %copy.61, bf16[3,1,16,8,1,4,128]{6,2,4,0,1,5,3:T(8,128)(2,1)S(1)} %copy.60), kind=kLoop, calls=%fused_computation.78 | loop fusion | flops 393216 | bytes 1572864 | tf_op jit(solution)/shard_map/stack | solution.py:180
  49.9 3.8 %all-to-all-start.1 = ((bf16[32,2,16,3,1,128]{5,2,4,3,1,0:T(8,128)(2,1)}), bf16[32,2,16,3,1,128]{5,2,4,3,1,0:T(8,128)(2,1)S(1)}, u32[]{:S(2)}, u32[]{:S(2)}) async-start(bf16[32,2,16,3,1,128]{5,2,4,3,1,0:T(8,128)(2,1)} %bitcast.179), calls=%async_computation.1 | async-start | bytes 1572864 | tf_op jit(solution)/shard_map/all_to_all | solution.py:187
  53.7 2.4 %multiply_convert_fusion = (bf16[32,2,16,1024]{3,0,2,1:T(8,128)(2,1)S(1)}, bf16[32,2,16,1024]{3,0,2,1:T(8,128)(2,1)S(1)}) fusion(f32[32,2,16]{0,2,1:T(8,128)S(1)} %copy-done.4, f32[32,1,16,1024]{3,0,2,1:T(8,128)} %copy-done.2, f32[32,1,16,1024]{3,0,2,1:T(8,128)S(1)} %copy-done.1), kind=kLoop, calls=%fused_computation.8 | loop fusion | flops 11534336 | bytes 8392704 | tf_op jit(solution)/shard_map/convert_element_type | solution.py:198
  56.2 1.2 %copy.64 = bf16[32,2,16,1024]{3,2,1,0:T(8,128)(2,1)S(1)} copy(bf16[32,2,16,1024]{3,0,2,1:T(8,128)(2,1)S(1)} %get-tuple-element.9) | data formatting | bytes 4194304 | tf_op jit(solution)/shard_map/convert_element_type | solution.py:198
  57.3 2.5 %copy.63 = bf16[32,2,16,1024]{3,2,1,0:T(8,128)(2,1)} copy(bf16[32,2,16,1024]{3,0,2,1:T(8,128)(2,1)S(1)} %get-tuple-element.10) | data formatting | bytes 4194304 | tf_op jit(solution)/shard_map/convert_element_type | solution.py:197
  59.8 14.3 %all-to-all-done.1 = bf16[32,2,16,3,1,128]{5,2,4,3,1,0:T(8,128)(2,1)S(1)} async-done(((bf16[32,2,16,3,1,128]{5,2,4,3,1,0:T(8,128)(2,1)}), bf16[32,2,16,3,1,128]{5,2,4,3,1,0:T(8,128)(2,1)S(1)}, u32[]{:S(2)}, u32[]{:S(2)}) %all-to-all-start.1) | async-done | bytes 786464 | tf_op jit(solution)/shard_map/all_to_all | solution.py:187
  74.1 0.5 copy.62
  74.7 2.6 %fusion.34 = f32[384,1024]{1,0:T(8,128)S(1)} fusion(bf16[1024,1024]{1,0:T(8,128)(2,1)} %bitcast.175, bf16[128,8,3,128]{3,2,1,0:T(4,128)(2,1)S(1)} %bitcast.176), kind=kOutput, calls=%fused_computation.64 | convolution fusion | flops 805306368 | bytes 4456448 | tf_op jit(solution)/shard_map/kr,kz->rz/dot_general | solution.py:200
  77.3 1.0 %convolution_add_fusion.2 = f32[384,1024]{1,0:T(8,128)S(1)} fusion(f32[384,1024]{1,0:T(8,128)S(1)} %fusion.34, bf16[1024,1024]{1,0:T(8,128)(2,1)S(1)} %bitcast.172, bf16[128,8,3,128]{3,2,1,0:T(4,128)(2,1)S(1)} %bitcast.177), kind=kOutput, calls=%fused_computation.30 | convolution fusion | flops 805699584 | bytes 6029312 | tf_op jit(solution)/shard_map/kr,kz->rz/dot_general | solution.py:200
  78.4 1.1 %add_convert_fusion = bf16[3,1,128,1024]{3,2,1,0:T(8,128)(2,1)} fusion(f32[3,1,128,1024]{3,2,1,0:T(8,128)S(1)} %bitcast.178, bf16[3,1,128,1024]{3,2,1,0:T(8,128)(2,1)S(1)} %copy-done.3), kind=kLoop, calls=%fused_computation.27 | loop fusion | flops 1179648 | bytes 3145728 | tf_op jit(solution)/shard_map/convert_element_type | solution.py:204
  (54 shorter events, 5.3 us)
Async XLA Ops:
  5.9 2.7 %copy-start.6 = (bf16[3,1,128,1024]{3,2,1,0:T(8,128)(2,1)S(1)}, bf16[3,1,128,1024]{3,2,1,0:T(8,128)(2,1)}, u32[]{:S(2)}) copy-start(bf16[3,1,128,1024]{3,2,1,0:T(8,128)(2,1)} %param.6) | copy-start | bytes 2359300
  8.6 2.6 %copy-start = (f32[32,1,16,1024]{3,0,2,1:T(8,128)}, f32[32,1,16,1024]{3,0,2,1:T(8,128)S(1)}, u32[]{:S(2)}) copy-start(f32[32,1,16,1024]{3,0,2,1:T(8,128)S(1)} %get-tuple-element.7) | copy-start | bytes 6291460
  8.6 2.6 %copy-start.2 = (f32[32,1,16,1024]{3,0,2,1:T(8,128)}, f32[32,1,16,1024]{3,0,2,1:T(8,128)S(1)}, u32[]{:S(2)}) copy-start(f32[32,1,16,1024]{3,0,2,1:T(8,128)S(1)} %get-tuple-element.8) | copy-start | bytes 6291460
  13.7 27.9 %all-to-all-start = ((bf16[32,3,2,16,128]{4,3,2,1,0:T(8,128)(2,1)}), bf16[32,3,2,16,128]{4,3,2,1,0:T(8,128)(2,1)S(1)}, u32[]{:S(2)}, u32[]{:S(2)}) async-start(bf16[32,3,2,16,128]{4,3,2,1,0:T(8,128)(2,1)} %copy.52), calls=%async_computation | async-start | bytes 1572864 | tf_op jit(solution)/shard_map/all_to_all | solution.py:133
  44.0 0.7 copy-start.7
  44.2 0.8 %copy-start.5 = (bf16[8,8,1,1]{1,0,3,2:T(8,128)(2,1)S(1)}, bf16[8,8,1,1]{1,0,3,2:T(8,128)(2,1)}, u32[]{:S(2)}) copy-start(bf16[8,8,1,1]{1,0,3,2:T(8,128)(2,1)} %constant.139) | copy-start | bytes 388
  48.7 5.0 %copy-start.1 = (f32[32,1,16,1024]{3,0,2,1:T(8,128)S(1)}, f32[32,1,16,1024]{3,0,2,1:T(8,128)}, u32[]{:S(2)}) copy-start(f32[32,1,16,1024]{3,0,2,1:T(8,128)} %copy-done) | copy-start | bytes 6291460
  48.7 5.0 %copy-start.4 = (f32[32,2,16]{0,2,1:T(8,128)S(1)}, f32[32,2,16]{0,2,1:T(8,128)}, u32[]{:S(2)}) copy-start(f32[32,2,16]{0,2,1:T(8,128)} %constant.137) | copy-start | bytes 12292
  49.9 24.3 %all-to-all-start.1 = ((bf16[32,2,16,3,1,128]{5,2,4,3,1,0:T(8,128)(2,1)}), bf16[32,2,16,3,1,128]{5,2,4,3,1,0:T(8,128)(2,1)S(1)}, u32[]{:S(2)}, u32[]{:S(2)}) async-start(bf16[32,2,16,3,1,128]{5,2,4,3,1,0:T(8,128)(2,1)} %bitcast.179), calls=%async_computation.1 | async-start | bytes 1572864 | tf_op jit(solution)/shard_map/all_to_all | solution.py:187
  77.3 1.1 %copy-start.3 = (bf16[3,1,128,1024]{3,2,1,0:T(8,128)(2,1)S(1)}, bf16[3,1,128,1024]{3,2,1,0:T(8,128)(2,1)}, u32[]{:S(2)}) copy-start(bf16[3,1,128,1024]{3,2,1,0:T(8,128)(2,1)} %param.7) | copy-start | bytes 2359300

commit v20 on v19

--- a/solution.py
+++ b/solution.py
@@ -141,9 +141,10 @@
     )
 
     cos_y, sin_y = phase_table(width_y, width_y, width_y)
-    both_y_parts = split_parts(jnp.concatenate([cos_y, sin_y], axis=1))
+    both_y_parts = (jnp.concatenate(split_parts(jnp.concatenate([cos_y, sin_y], axis=1)), axis=1),)
     spec_y = "yk,cpjxy->cpjxk"
-    by_both = mat(both_y_parts, gathered, spec_y)
+    by_all = mat(both_y_parts, gathered, spec_y)
+    by_both = by_all[..., : 2 * width_y] + by_all[..., 2 * width_y :]
     by_cos, by_sin = by_both[..., :width_y], by_both[..., width_y:]
     y_real = by_cos[:, 0] + by_sin[:, 1]
     y_imag = by_cos[:, 1] - by_sin[:, 0]
@@ -154,7 +155,8 @@
 
     def inverse_y(b_real, b_imag):
         stacked = jnp.stack([b_real, b_imag], axis=1).astype(BF16)
-        by_both = mat(both_y_parts, stacked, spec_y)
+        by_all = mat(both_y_parts, stacked, spec_y)
+        by_both = by_all[..., : 2 * width_y] + by_all[..., 2 * width_y :]
         by_cos, by_sin = by_both[..., :width_y], by_both[..., width_y:]
         scale = 1.0 / width_y
         out_real = (by_cos[:, 0] - by_sin[:, 1]) * scale

time: 80 us -> 81.5 us (1.019)
  other arithmetic: 11.2 us -> 13.7 us
    add x0 -> x2, other arithmetic: none -> 2.07 us  [the longest x1 1.11 us: inverse_y(): by_both = by_all[..., :2 * width_y] + by_all[..., 2 * width_y:]]
    dot_general x6 -> x4, matrix products: 5.1 us -> 4.55 us  [mat(): term = jnp.einsum(spec, part, operand, preferred_element_type=F32)]
where the time goes in v20:
time: 81.5 us; the launch traced here: 81.1 us
  waiting for transfers between devices  33.5 us (41%)
  matrix products  15 us (18%)
  other arithmetic  13.7 us (17%)
  starting transfers between devices  11.3 us (14%)
  local copies, waits for them, and re-layouts  7.07 us (9%)
    all_to_all x1, waiting for transfers between devices, on_device(): lax.all_to_all(spectrum, ('row', 'col'), split_axis=0, concat_axis=0, til...  19.2 us
    all_to_all x1, waiting for transfers between devices, on_device(): lax.all_to_all(outgoing, ('row', 'col'), split_axis=0, concat_axis=0, til...  14.3 us
    all_to_all x1, starting transfers between devices, on_device(): lax.all_to_all(spectrum, ('row', 'col'), split_axis=0, concat_axis=0, til...  7.48 us
    dot_general x4, matrix products, mat(): term = jnp.einsum(spec, part, operand, preferred_element_type=F32)  4.55 us
    all_to_all x1, starting transfers between devices, on_device(): lax.all_to_all(outgoing, ('row', 'col'), split_axis=0, concat_axis=0, til...  3.84 us
    dot_general x1, matrix products, on_device(): jnp.einsum('...k,k->...', one_hot, parts, preferred_element_type=F32)  2.98 us
    sub x2, other arithmetic, phase_table(): cosine = outer_cos * inner_cos - outer_sin * inner_sin  2.91 us
    dot_general x1, matrix products, on_device(): jnp.einsum(spec_back, returned, back_high, preferred_element_type=F32)  2.61 us
  transfers between devices with their start and end apart: 2, of which 2 were waited for; matrix products, arithmetic and copies ran while one was open for 9% of the time, Pallas kernels for 0%

profile of v20, /device:TPU:0, one launch (start us, length us, event | category | flops | bytes accessed | tf_op | source)
XLA Modules:
  0.0 81.1 jit_solution(8714400575664360813)
XLA Ops:
  0.5 0.5 fusion.82
  1.7 0.7 reduce-precision_convert_fusion.4
  2.4 3.0 %fusion = f32[1,128,1024]{2,0,1:T(1,128)S(1)} fusion(s32[128,1024]{1,0:T(8,128)} %bitcast.168, s32[24]{0:T(128)S(1)} %and_select_fusion, bf16[8]{0:T(256)(128)(2,1)S(1)} %get-tuple-element.34, bf16[8]{0:T(256)(128)(2,1)S(1)} %get-tuple-element.33, bf16[8]{0:T(256)(128)(2,1)S(1)} %get-tuple-element.5), kind=kOutput, calls=%fused_computation | convolution fusion | flops 9437328 | bytes 1048720 | tf_op jit(solution)/shard_map/...k,k->.../dot_general | solution.py:104
  6.0 2.6 %multiply_subtract_fusion = (f32[32,1,16,1024]{3,0,2,1:T(8,128)S(1)}, f32[32,1,16,1024]{3,0,2,1:T(8,128)S(1)}) fusion(f32[32,1,16,1024]{3,2,0,1:T(8,128)S(1)} %bitcast.156, f32[32,1,16,1024]{3,2,0,1:T(8,128)S(1)} %bitcast.155, f32[32,1024]{1,0:T(8,128)S(1)} %mul.557, f32[32,1024]{1,0:T(8,128)S(1)} %mul.546, f32[1024]{0:T(1024)S(1)} %fusion.102, ...), kind=kLoop, calls=%fused_computation.26 | loop fusion | flops 4194304 | bytes 8655360 | tf_op jit(solution)/shard_map/sub | solution.py:45
  8.6 1.3 %fusion.6 = f32[3,128,32,2,16]{1,2,4,3,0:T(8,128)S(1)} fusion(bf16[3,1,128,1024]{3,2,1,0:T(8,128)(2,1)S(1)} %copy-done.6, f32[128,1024]{1,0:T(8,128)S(1)} %bitcast.165, f32[32,1,16,1024]{3,0,2,1:T(8,128)S(1)} %get-tuple-element.8, f32[32,1,16,1024]{3,0,2,1:T(8,128)S(1)} %get-tuple-element.7), kind=kOutput, calls=%fused_computation.19 | convolution fusion | flops 811073536 | bytes 7077888 | tf_op jit(solution)/shard_map/dpjz,cyz->dcpjy/dot_general | solution.py:130
  9.9 1.3 %fusion.8 = f32[3,128,32,2,16]{1,2,4,3,0:T(8,128)S(1)} fusion(bf16[3,1,128,1024]{3,2,1,0:T(8,128)(2,1)S(1)} %copy-done.6, f32[128,1024]{1,0:T(8,128)S(1)} %bitcast.166, f32[32,1,16,1024]{3,0,2,1:T(8,128)S(1)} %get-tuple-element.8, f32[32,1,16,1024]{3,0,2,1:T(8,128)S(1)} %get-tuple-element.7), kind=kOutput, calls=%fused_computation.21 | convolution fusion | flops 810418176 | bytes 7077888 | tf_op jit(solution)/shard_map/dpjz,cyz->dcpjy/dot_general | solution.py:129
  11.2 1.3 %fusion.18 = bf16[32,3,2,16,128]{4,0,3,2,1:T(8,128)(2,1)S(1)} fusion(f32[3,128,32,2,16]{1,2,4,3,0:T(8,128)S(1)} %fusion.6, f32[3,128,32,2,16]{1,2,4,3,0:T(8,128)S(1)} %fusion.8, bf16[3,1,128,1024]{3,2,1,0:T(8,128)(2,1)S(1)} %copy-done.6, f32[128,1024]{1,0:T(8,128)S(1)} %bitcast.167, f32[32,1,16,1024]{3,0,2,1:T(8,128)S(1)} %get-tuple-element.8, ...), kind=kOutput, calls=%fused_computation.36 | convolution fusion | flops 811204608 | bytes 9437184 | tf_op jit(solution)/shard_map/dpjz,cyz->dcpjy/dot_general | solution.py:128
  12.5 1.2 %copy.52 = bf16[32,3,2,16,128]{4,3,2,1,0:T(8,128)(2,1)} copy(bf16[32,3,2,16,128]{4,0,3,2,1:T(8,128)(2,1)S(1)} %fusion.18) | data formatting | bytes 1572864 | tf_op jit(solution)/shard_map/convert_element_type | solution.py:132
  13.7 7.5 %all-to-all-start = ((bf16[32,3,2,16,128]{4,3,2,1,0:T(8,128)(2,1)}), bf16[32,3,2,16,128]{4,3,2,1,0:T(8,128)(2,1)S(1)}, u32[]{:S(2)}, u32[]{:S(2)}) async-start(bf16[32,3,2,16,128]{4,3,2,1,0:T(8,128)(2,1)} %copy.52), calls=%async_computation | async-start | bytes 1572864 | tf_op jit(solution)/shard_map/all_to_all | solution.py:133
  22.4 19.2 %all-to-all-done = bf16[32,3,2,16,128]{4,3,2,1,0:T(8,128)(2,1)S(1)} async-done(((bf16[32,3,2,16,128]{4,3,2,1,0:T(8,128)(2,1)}), bf16[32,3,2,16,128]{4,3,2,1,0:T(8,128)(2,1)S(1)}, u32[]{:S(2)}, u32[]{:S(2)}) %all-to-all-start) | async-done | bytes 786464 | tf_op jit(solution)/shard_map/all_to_all | solution.py:133
  41.6 1.9 %fusion.17 = f32[3,2,16,8,2048]{4,3,2,1,0:T(8,128)S(1)} fusion(bf16[512,1024]{1,0:T(8,128)(2,1)S(1)} %get-tuple-element.12, bf16[512,1024]{1,0:T(8,128)(2,1)S(1)} %get-tuple-element.11, bf16[8,4,3,1,2,16,128]{6,5,4,2,1,0,3:T(8,128)(2,1)S(1)} %bitcast.163), kind=kOutput, calls=%fused_computation.35 | convolution fusion | flops 1614807040 | bytes 9175040 | tf_op jit(solution)/shard_map/yk,cpjxy->cpjxk/dot_general | solution.py:65
  43.5 1.0 %slice_add_fusion.1 = f32[3,2,16,8,1024]{4,3,2,1,0:T(8,128)S(1)} fusion(f32[3,2,16,8,2048]{4,3,2,1,0:T(8,128)S(1)} %fusion.17), kind=kLoop, calls=%fused_computation.11 | loop fusion | flops 786432 | bytes 9437184 | tf_op jit(solution)/shard_map/add | solution.py:147
  46.4 2.0 %fusion.16 = f32[3,2,18,8,2048]{4,3,2,1,0:T(8,128)S(1)} fusion(bf16[512,1024]{1,0:T(8,128)(2,1)S(1)} %get-tuple-element.12, bf16[512,1024]{1,0:T(8,128)(2,1)S(1)} %get-tuple-element.11, bf16[3,1,18,8,512]{4,3,2,1,0:T(8,128)(2,1)S(1)} %fusion.29, bf16[3,1,18,8,512]{4,3,2,1,0:T(8,128)(2,1)S(1)} %fusion.28), kind=kOutput, calls=%fused_computation.34 | convolution fusion | flops 1816576000 | bytes 10059776 | tf_op jit(solution)/shard_map/yk,cpjxy->cpjxk/dot_general | solution.py:65
  48.4 1.1 %slice_add_fusion = f32[3,2,18,8,1024]{4,3,2,1,0:T(8,128)S(1)} fusion(f32[3,2,18,8,2048]{4,3,2,1,0:T(8,128)S(1)} %fusion.16), kind=kLoop, calls=%fused_computation.10 | loop fusion | flops 884736 | bytes 10616832 | tf_op jit(solution)/shard_map/add | solution.py:159
  50.4 0.9 %pad_maximum_fusion.2 = bf16[3,2,16,8,1,4,128]{6,2,4,0,1,5,3:T(8,128)(2,1)} fusion(bf16[3,1,16,8,1,4,128]{6,2,4,0,1,5,3:T(8,128)(2,1)S(1)} %copy.61, bf16[3,1,16,8,1,4,128]{6,2,4,0,1,5,3:T(8,128)(2,1)S(1)} %copy.60), kind=kLoop, calls=%fused_computation.81 | loop fusion | flops 393216 | bytes 1572864 | tf_op jit(solution)/shard_map/stack | solution.py:182
  51.4 3.8 %all-to-all-start.1 = ((bf16[32,2,16,3,1,128]{5,2,4,3,1,0:T(8,128)(2,1)}), bf16[32,2,16,3,1,128]{5,2,4,3,1,0:T(8,128)(2,1)S(1)}, u32[]{:S(2)}, u32[]{:S(2)}) async-start(bf16[32,2,16,3,1,128]{5,2,4,3,1,0:T(8,128)(2,1)} %bitcast.164), calls=%async_computation.1 | async-start | bytes 1572864 | tf_op jit(solution)/shard_map/all_to_all | solution.py:189
  55.2 2.4 %multiply_convert_fusion = (bf16[32,2,16,1024]{3,0,2,1:T(8,128)(2,1)S(1)}, bf16[32,2,16,1024]{3,0,2,1:T(8,128)(2,1)S(1)}) fusion(f32[32,2,16]{0,2,1:T(8,128)S(1)} %copy-done.4, f32[32,1,16,1024]{3,0,2,1:T(8,128)} %copy-done.2, f32[32,1,16,1024]{3,0,2,1:T(8,128)S(1)} %copy-done.1), kind=kLoop, calls=%fused_computation.8 | loop fusion | flops 11534336 | bytes 8392704 | tf_op jit(solution)/shard_map/convert_element_type | solution.py:200
  57.7 2.5 %copy.63 = bf16[32,2,16,1024]{3,2,1,0:T(8,128)(2,1)} copy(bf16[32,2,16,1024]{3,0,2,1:T(8,128)(2,1)S(1)} %get-tuple-element.10) | data formatting | bytes 4194304 | tf_op jit(solution)/shard_map/convert_element_type | solution.py:199
  60.1 1.2 %copy.64 = bf16[32,2,16,1024]{3,2,1,0:T(8,128)(2,1)S(1)} copy(bf16[32,2,16,1024]{3,0,2,1:T(8,128)(2,1)S(1)} %get-tuple-element.9) | data formatting | bytes 4194304 | tf_op jit(solution)/shard_map/convert_element_type | solution.py:200
  61.3 14.3 %all-to-all-done.1 = bf16[32,2,16,3,1,128]{5,2,4,3,1,0:T(8,128)(2,1)S(1)} async-done(((bf16[32,2,16,3,1,128]{5,2,4,3,1,0:T(8,128)(2,1)}), bf16[32,2,16,3,1,128]{5,2,4,3,1,0:T(8,128)(2,1)S(1)}, u32[]{:S(2)}, u32[]{:S(2)}) %all-to-all-start.1) | async-done | bytes 786464 | tf_op jit(solution)/shard_map/all_to_all | solution.py:189
  75.6 0.5 copy.62
  76.2 2.6 %fusion.37 = f32[384,1024]{1,0:T(8,128)S(1)} fusion(bf16[1024,1024]{1,0:T(8,128)(2,1)} %bitcast.157, bf16[128,8,3,128]{3,2,1,0:T(4,128)(2,1)S(1)} %bitcast.158), kind=kOutput, calls=%fused_computation.67 | convolution fusion | flops 805306368 | bytes 4456448 | tf_op jit(solution)/shard_map/kr,kz->rz/dot_general | solution.py:202
  78.8 1.0 %convolution_add_fusion = f32[384,1024]{1,0:T(8,128)S(1)} fusion(f32[384,1024]{1,0:T(8,128)S(1)} %fusion.37, bf16[1024,1024]{1,0:T(8,128)(2,1)S(1)} %bitcast.154, bf16[128,8,3,128]{3,2,1,0:T(4,128)(2,1)S(1)} %bitcast.159), kind=kOutput, calls=%fused_computation.31 | convolution fusion | flops 805699584 | bytes 6029312 | tf_op jit(solution)/shard_map/kr,kz->rz/dot_general | solution.py:202
  79.9 1.1 %add_convert_fusion = bf16[3,1,128,1024]{3,2,1,0:T(8,128)(2,1)} fusion(f32[3,1,128,1024]{3,2,1,0:T(8,128)S(1)} %bitcast.160, bf16[3,1,128,1024]{3,2,1,0:T(8,128)(2,1)S(1)} %copy-done.3), kind=kLoop, calls=%fused_computation.28 | loop fusion | flops 1179648 | bytes 3145728 | tf_op jit(solution)/shard_map/convert_element_type | solution.py:206
  (55 shorter events, 5.7 us)
Async XLA Ops:
  5.9 2.7 %copy-start.6 = (bf16[3,1,128,1024]{3,2,1,0:T(8,128)(2,1)S(1)}, bf16[3,1,128,1024]{3,2,1,0:T(8,128)(2,1)}, u32[]{:S(2)}) copy-start(bf16[3,1,128,1024]{3,2,1,0:T(8,128)(2,1)} %param.6) | copy-start | bytes 2359300
  8.6 2.6 %copy-start = (f32[32,1,16,1024]{3,0,2,1:T(8,128)}, f32[32,1,16,1024]{3,0,2,1:T(8,128)S(1)}, u32[]{:S(2)}) copy-start(f32[32,1,16,1024]{3,0,2,1:T(8,128)S(1)} %get-tuple-element.7) | copy-start | bytes 6291460
  8.6 2.6 %copy-start.2 = (f32[32,1,16,1024]{3,0,2,1:T(8,128)}, f32[32,1,16,1024]{3,0,2,1:T(8,128)S(1)}, u32[]{:S(2)}) copy-start(f32[32,1,16,1024]{3,0,2,1:T(8,128)S(1)} %get-tuple-element.8) | copy-start | bytes 6291460
  13.7 27.9 %all-to-all-start = ((bf16[32,3,2,16,128]{4,3,2,1,0:T(8,128)(2,1)}), bf16[32,3,2,16,128]{4,3,2,1,0:T(8,128)(2,1)S(1)}, u32[]{:S(2)}, u32[]{:S(2)}) async-start(bf16[32,3,2,16,128]{4,3,2,1,0:T(8,128)(2,1)} %copy.52), calls=%async_computation | async-start | bytes 1572864 | tf_op jit(solution)/shard_map/all_to_all | solution.py:133
  44.7 0.7 copy-start.7
  44.9 0.8 %copy-start.5 = (bf16[8,8,1,1]{1,0,3,2:T(8,128)(2,1)S(1)}, bf16[8,8,1,1]{1,0,3,2:T(8,128)(2,1)}, u32[]{:S(2)}) copy-start(bf16[8,8,1,1]{1,0,3,2:T(8,128)(2,1)} %constant.139) | copy-start | bytes 388
  50.2 5.0 %copy-start.1 = (f32[32,1,16,1024]{3,0,2,1:T(8,128)S(1)}, f32[32,1,16,1024]{3,0,2,1:T(8,128)}, u32[]{:S(2)}) copy-start(f32[32,1,16,1024]{3,0,2,1:T(8,128)} %copy-done) | copy-start | bytes 6291460
  50.2 5.0 %copy-start.4 = (f32[32,2,16]{0,2,1:T(8,128)S(1)}, f32[32,2,16]{0,2,1:T(8,128)}, u32[]{:S(2)}) copy-start(f32[32,2,16]{0,2,1:T(8,128)} %constant.137) | copy-start | bytes 12292
  51.4 24.2 %all-to-all-start.1 = ((bf16[32,2,16,3,1,128]{5,2,4,3,1,0:T(8,128)(2,1)}), bf16[32,2,16,3,1,128]{5,2,4,3,1,0:T(8,128)(2,1)S(1)}, u32[]{:S(2)}, u32[]{:S(2)}) async-start(bf16[32,2,16,3,1,128]{5,2,4,3,1,0:T(8,128)(2,1)} %bitcast.164), calls=%async_computation.1 | async-start | bytes 1572864 | tf_op jit(solution)/shard_map/all_to_all | solution.py:189
  78.8 1.1 %copy-start.3 = (bf16[3,1,128,1024]{3,2,1,0:T(8,128)(2,1)S(1)}, bf16[3,1,128,1024]{3,2,1,0:T(8,128)(2,1)}, u32[]{:S(2)}) copy-start(bf16[3,1,128,1024]{3,2,1,0:T(8,128)(2,1)} %param.7) | copy-start | bytes 2359300

commit v21 on v19

--- a/solution.py
+++ b/solution.py
@@ -124,9 +124,12 @@
     lines = (members * local_x, local_y, depth)
     z_high4, z_low4 = z_high.reshape(blocks), z_low.reshape(blocks)
     e_high, e_low = e_high.reshape(lines), e_low.reshape(lines)
+    by_high = jnp.einsum(
+        spec_z, z_high4, jnp.concatenate([e_high, e_low]), preferred_element_type=F32
+    )
     spectrum = (
-        jnp.einsum(spec_z, z_high4, e_high, preferred_element_type=F32)
-        + jnp.einsum(spec_z, z_high4, e_low, preferred_element_type=F32)
+        by_high[:, : lines[0]]
+        + by_high[:, lines[0] :]
         + jnp.einsum(spec_z, z_low4, e_high, preferred_element_type=F32)
     )
     spectrum = spectrum.astype(BF16)

time: 80 us -> 79.8 us (level)
    dot_general x2 -> x1, matrix products: 2.57 us -> 1.82 us  [on_device(): jnp.einsum(spec_z, z_high4, jnp.concatenate([e_high, e_low]), preferred_e...]
where the time goes in v21:
time: 79.8 us; the launch traced here: 79.4 us
  waiting for transfers between devices  33.9 us (42%)
  matrix products  14.8 us (19%)
  other arithmetic  11.7 us (15%)
  starting transfers between devices  11.3 us (14%)
  local copies, waits for them, and re-layouts  7.22 us (9%)
    all_to_all x1, waiting for transfers between devices, on_device(): lax.all_to_all(spectrum, ('row', 'col'), split_axis=0, concat_axis=0, til...  19.6 us
    all_to_all x1, waiting for transfers between devices, on_device(): lax.all_to_all(outgoing, ('row', 'col'), split_axis=0, concat_axis=0, til...  14.3 us
    all_to_all x1, starting transfers between devices, on_device(): lax.all_to_all(spectrum, ('row', 'col'), split_axis=0, concat_axis=0, til...  7.48 us
    dot_general x6, matrix products, mat(): term = jnp.einsum(spec, part, operand, preferred_element_type=F32)  5.12 us
    all_to_all x1, starting transfers between devices, on_device(): lax.all_to_all(outgoing, ('row', 'col'), split_axis=0, concat_axis=0, til...  3.83 us
    dot_general x1, matrix products, on_device(): jnp.einsum('...k,k->...', one_hot, parts, preferred_element_type=F32)  2.98 us
    sub x2, other arithmetic, phase_table(): cosine = outer_cos * inner_cos - outer_sin * inner_sin  2.91 us
    dot_general x1, matrix products, on_device(): jnp.einsum(spec_back, returned, back_high, preferred_element_type=F32)  2.61 us
  transfers between devices with their start and end apart: 2, of which 2 were waited for; matrix products, arithmetic and copies ran while one was open for 9% of the time, Pallas kernels for 0%

profile of v21, /device:TPU:0, one launch (start us, length us, event | category | flops | bytes accessed | tf_op | source)
XLA Modules:
  0.0 79.4 jit_solution(15940000951574879996)
XLA Ops:
  0.0 0.5 fusion.85
  0.5 0.5 fusion.84
  1.7 0.7 reduce-precision_convert_fusion.5
  2.4 3.0 %fusion = f32[1,128,1024]{2,0,1:T(1,128)S(1)} fusion(s32[128,1024]{1,0:T(8,128)} %bitcast.176, s32[24]{0:T(128)S(1)} %and_select_fusion, bf16[8]{0:T(256)(128)(2,1)S(1)} %get-tuple-element.36, bf16[8]{0:T(256)(128)(2,1)S(1)} %get-tuple-element.35, bf16[8]{0:T(256)(128)(2,1)S(1)} %get-tuple-element.5), kind=kOutput, calls=%fused_computation | convolution fusion | flops 9437328 | bytes 1048720 | tf_op jit(solution)/shard_map/...k,k->.../dot_general | solution.py:104
  6.4 2.6 %multiply_subtract_fusion = (f32[32,1,16,1024]{3,0,2,1:T(8,128)S(1)}, f32[32,1,16,1024]{3,0,2,1:T(8,128)S(1)}) fusion(f32[32,1,16,1024]{3,2,0,1:T(8,128)S(1)} %bitcast.169, f32[32,1,16,1024]{3,2,0,1:T(8,128)S(1)} %bitcast.168, f32[32,1024]{1,0:T(8,128)S(1)} %mul.557, f32[32,1024]{1,0:T(8,128)S(1)} %mul.546, f32[1024]{0:T(1024)S(1)} %fusion.104, ...), kind=kLoop, calls=%fused_computation.21 | loop fusion | flops 4194304 | bytes 8655360 | tf_op jit(solution)/shard_map/sub | solution.py:45
  9.0 1.8 %fusion.10 = f32[32,6,2,16,128]{4,0,3,2,1:T(8,128)S(1)} fusion(bf16[3,128,1024]{2,1,0:T(8,128)(2,1)S(1)} %get-tuple-element.16, bf16[3,128,1024]{2,1,0:T(8,128)(2,1)S(1)} %get-tuple-element.15, f32[32,1,16,1024]{3,0,2,1:T(8,128)S(1)} %get-tuple-element.8, f32[32,1,16,1024]{3,0,2,1:T(8,128)S(1)} %get-tuple-element.7), kind=kOutput, calls=%fused_computation.23 | convolution fusion | flops 1616904192 | bytes 8912896 | tf_op jit(solution)/shard_map/dpjz,cyz->dcpjy/dot_general | solution.py:127
  11.0 1.3 %fusion.15 = bf16[32,3,2,16,128]{4,0,3,2,1:T(8,128)(2,1)S(1)} fusion(f32[32,6,2,16,128]{4,0,3,2,1:T(8,128)S(1)} %fusion.10, bf16[3,128,1024]{2,1,0:T(8,128)(2,1)S(1)} %get-tuple-element.15, f32[32,1,16,1024]{3,0,2,1:T(8,128)S(1)} %get-tuple-element.8, f32[32,1,16,1024]{3,0,2,1:T(8,128)S(1)} %get-tuple-element.7), kind=kOutput, calls=%fused_computation.28 | convolution fusion | flops 810680320 | bytes 8912896 | tf_op jit(solution)/shard_map/dpjz,cyz->dcpjy/dot_general | solution.py:133
  12.3 1.2 %copy.56 = bf16[32,3,2,16,128]{4,3,2,1,0:T(8,128)(2,1)} copy(bf16[32,3,2,16,128]{4,0,3,2,1:T(8,128)(2,1)S(1)} %fusion.15) | data formatting | bytes 1572864 | tf_op jit(solution)/shard_map/convert_element_type | solution.py:135
  13.5 7.5 %all-to-all-start = ((bf16[32,3,2,16,128]{4,3,2,1,0:T(8,128)(2,1)}), bf16[32,3,2,16,128]{4,3,2,1,0:T(8,128)(2,1)S(1)}, u32[]{:S(2)}, u32[]{:S(2)}) async-start(bf16[32,3,2,16,128]{4,3,2,1,0:T(8,128)(2,1)} %copy.56), calls=%async_computation | async-start | bytes 1572864 | tf_op jit(solution)/shard_map/all_to_all | solution.py:136
  21.8 19.6 %all-to-all-done = bf16[32,3,2,16,128]{4,3,2,1,0:T(8,128)(2,1)S(1)} async-done(((bf16[32,3,2,16,128]{4,3,2,1,0:T(8,128)(2,1)}), bf16[32,3,2,16,128]{4,3,2,1,0:T(8,128)(2,1)S(1)}, u32[]{:S(2)}, u32[]{:S(2)}) %all-to-all-start) | async-done | bytes 786464 | tf_op jit(solution)/shard_map/all_to_all | solution.py:136
  41.4 1.1 %fusion.44 = f32[3,2,16,8,1024]{4,3,2,1,0:T(8,128)S(1)} fusion(bf16[8,4,3,1,2,16,128]{6,5,4,2,1,0,3:T(8,128)(2,1)S(1)} %bitcast.165, f32[512,512]{1,0:T(8,128)S(1)} %bitcast.161, f32[512,512]{1,0:T(8,128)S(1)} %bitcast.157), kind=kOutput, calls=%fused_computation.82 | convolution fusion | flops 806879232 | bytes 6029312 | tf_op jit(solution)/shard_map/yk,cpjxy->cpjxk/dot_general | solution.py:65
  42.5 1.2 %convolution_add_fusion.1 = f32[3,2,16,8,1024]{4,3,2,1,0:T(8,128)S(1)} fusion(f32[3,2,16,8,1024]{4,3,2,1,0:T(8,128)S(1)} %fusion.44, bf16[8,4,3,1,2,16,128]{6,5,4,2,1,0,3:T(8,128)(2,1)S(1)} %bitcast.166, f32[512,512]{1,0:T(8,128)S(1)} %bitcast.162, f32[512,512]{1,0:T(8,128)S(1)} %bitcast.158), kind=kOutput, calls=%fused_computation.24 | convolution fusion | flops 808189952 | bytes 9175040 | tf_op jit(solution)/shard_map/yk,cpjxy->cpjxk/dot_general | solution.py:65
  45.6 1.1 %fusion.48 = f32[3,2,18,8,1024]{4,3,2,1,0:T(8,128)S(1)} fusion(bf16[3,1,18,8,512]{4,3,2,1,0:T(8,128)(2,1)S(1)} %fusion.31, bf16[3,1,18,8,512]{4,3,2,1,0:T(8,128)(2,1)S(1)} %fusion.30, f32[512,512]{1,0:T(8,128)S(1)} %bitcast.163, f32[512,512]{1,0:T(8,128)S(1)} %bitcast.159), kind=kOutput, calls=%fused_computation.87 | convolution fusion | flops 907984896 | bytes 6520832 | tf_op jit(solution)/shard_map/yk,cpjxy->cpjxk/dot_general | solution.py:65
  46.7 1.1 %convolution_add_fusion = f32[3,2,18,8,1024]{4,3,2,1,0:T(8,128)S(1)} fusion(f32[3,2,18,8,1024]{4,3,2,1,0:T(8,128)S(1)} %fusion.48, bf16[3,1,18,8,512]{4,3,2,1,0:T(8,128)(2,1)S(1)} %fusion.31, bf16[3,1,18,8,512]{4,3,2,1,0:T(8,128)(2,1)S(1)} %fusion.30, f32[512,512]{1,0:T(8,128)S(1)} %bitcast.164, f32[512,512]{1,0:T(8,128)S(1)} %bitcast.160), kind=kOutput, calls=%fused_computation.22 | convolution fusion | flops 909393920 | bytes 10059776 | tf_op jit(solution)/shard_map/yk,cpjxy->cpjxk/dot_general | solution.py:65
  48.7 0.9 %pad_maximum_fusion.3 = bf16[3,2,16,8,1,4,128]{6,2,4,0,1,5,3:T(8,128)(2,1)} fusion(bf16[3,1,16,8,1,4,128]{6,2,4,0,1,5,3:T(8,128)(2,1)S(1)} %copy.65, bf16[3,1,16,8,1,4,128]{6,2,4,0,1,5,3:T(8,128)(2,1)S(1)} %copy.64), kind=kLoop, calls=%fused_computation.79 | loop fusion | flops 393216 | bytes 1572864 | tf_op jit(solution)/shard_map/stack | solution.py:183
  49.7 3.8 %all-to-all-start.1 = ((bf16[32,2,16,3,1,128]{5,2,4,3,1,0:T(8,128)(2,1)}), bf16[32,2,16,3,1,128]{5,2,4,3,1,0:T(8,128)(2,1)S(1)}, u32[]{:S(2)}, u32[]{:S(2)}) async-start(bf16[32,2,16,3,1,128]{5,2,4,3,1,0:T(8,128)(2,1)} %bitcast.174), calls=%async_computation.1 | async-start | bytes 1572864 | tf_op jit(solution)/shard_map/all_to_all | solution.py:190
  53.5 2.4 %multiply_convert_fusion = (bf16[32,2,16,1024]{3,0,2,1:T(8,128)(2,1)S(1)}, bf16[32,2,16,1024]{3,0,2,1:T(8,128)(2,1)S(1)}) fusion(f32[32,2,16]{0,2,1:T(8,128)S(1)} %copy-done.5, f32[32,1,16,1024]{3,0,2,1:T(8,128)} %copy-done.2, f32[32,1,16,1024]{3,0,2,1:T(8,128)S(1)} %copy-done.1), kind=kLoop, calls=%fused_computation.8 | loop fusion | flops 11534336 | bytes 8392704 | tf_op jit(solution)/shard_map/convert_element_type | solution.py:201
  56.0 2.5 %copy.67 = bf16[32,2,16,1024]{3,2,1,0:T(8,128)(2,1)} copy(bf16[32,2,16,1024]{3,0,2,1:T(8,128)(2,1)S(1)} %get-tuple-element.10) | data formatting | bytes 4194304 | tf_op jit(solution)/shard_map/convert_element_type | solution.py:200
  58.5 1.2 %copy.68 = bf16[32,2,16,1024]{3,2,1,0:T(8,128)(2,1)S(1)} copy(bf16[32,2,16,1024]{3,0,2,1:T(8,128)(2,1)S(1)} %get-tuple-element.9) | data formatting | bytes 4194304 | tf_op jit(solution)/shard_map/convert_element_type | solution.py:201
  59.6 14.3 %all-to-all-done.1 = bf16[32,2,16,3,1,128]{5,2,4,3,1,0:T(8,128)(2,1)S(1)} async-done(((bf16[32,2,16,3,1,128]{5,2,4,3,1,0:T(8,128)(2,1)}), bf16[32,2,16,3,1,128]{5,2,4,3,1,0:T(8,128)(2,1)S(1)}, u32[]{:S(2)}, u32[]{:S(2)}) %all-to-all-start.1) | async-done | bytes 786464 | tf_op jit(solution)/shard_map/all_to_all | solution.py:190
  73.9 0.5 copy.66
  74.5 2.6 %fusion.33 = f32[384,1024]{1,0:T(8,128)S(1)} fusion(bf16[1024,1024]{1,0:T(8,128)(2,1)} %bitcast.170, bf16[128,8,3,128]{3,2,1,0:T(4,128)(2,1)S(1)} %bitcast.171), kind=kOutput, calls=%fused_computation.65 | convolution fusion | flops 805306368 | bytes 4456448 | tf_op jit(solution)/shard_map/kr,kz->rz/dot_general | solution.py:203
  77.1 1.0 %convolution_add_fusion.2 = f32[384,1024]{1,0:T(8,128)S(1)} fusion(f32[384,1024]{1,0:T(8,128)S(1)} %fusion.33, bf16[1024,1024]{1,0:T(8,128)(2,1)S(1)} %bitcast.167, bf16[128,8,3,128]{3,2,1,0:T(4,128)(2,1)S(1)} %bitcast.172), kind=kOutput, calls=%fused_computation.34 | convolution fusion | flops 805699584 | bytes 6029312 | tf_op jit(solution)/shard_map/kr,kz->rz/dot_general | solution.py:203
  78.2 1.1 %add_convert_fusion = bf16[3,1,128,1024]{3,2,1,0:T(8,128)(2,1)} fusion(f32[3,1,128,1024]{3,2,1,0:T(8,128)S(1)} %bitcast.173, bf16[3,1,128,1024]{3,2,1,0:T(8,128)(2,1)S(1)} %copy-done.4), kind=kLoop, calls=%fused_computation.32 | loop fusion | flops 1179648 | bytes 3145728 | tf_op jit(solution)/shard_map/convert_element_type | solution.py:207
  (54 shorter events, 5.3 us)
Async XLA Ops:
  1.7 3.8 %copy-start.3 = (bf16[3,1,128,1024]{3,2,1,0:T(8,128)(2,1)S(1)}, bf16[3,1,128,1024]{3,2,1,0:T(8,128)(2,1)}, u32[]{:S(2)}) copy-start(bf16[3,1,128,1024]{3,2,1,0:T(8,128)(2,1)} %param.6) | copy-start | bytes 2359300
  9.0 1.9 %copy-start = (f32[32,1,16,1024]{3,0,2,1:T(8,128)}, f32[32,1,16,1024]{3,0,2,1:T(8,128)S(1)}, u32[]{:S(2)}) copy-start(f32[32,1,16,1024]{3,0,2,1:T(8,128)S(1)} %get-tuple-element.7) | copy-start | bytes 6291460
  9.0 2.0 %copy-start.2 = (f32[32,1,16,1024]{3,0,2,1:T(8,128)}, f32[32,1,16,1024]{3,0,2,1:T(8,128)S(1)}, u32[]{:S(2)}) copy-start(f32[32,1,16,1024]{3,0,2,1:T(8,128)S(1)} %get-tuple-element.8) | copy-start | bytes 6291460
  13.5 27.9 %all-to-all-start = ((bf16[32,3,2,16,128]{4,3,2,1,0:T(8,128)(2,1)}), bf16[32,3,2,16,128]{4,3,2,1,0:T(8,128)(2,1)S(1)}, u32[]{:S(2)}, u32[]{:S(2)}) async-start(bf16[32,3,2,16,128]{4,3,2,1,0:T(8,128)(2,1)} %copy.56), calls=%async_computation | async-start | bytes 1572864 | tf_op jit(solution)/shard_map/all_to_all | solution.py:136
  43.9 0.7 copy-start.7
  44.1 0.8 %copy-start.6 = (bf16[8,8,1,1]{1,0,3,2:T(8,128)(2,1)S(1)}, bf16[8,8,1,1]{1,0,3,2:T(8,128)(2,1)}, u32[]{:S(2)}) copy-start(bf16[8,8,1,1]{1,0,3,2:T(8,128)(2,1)} %constant.139) | copy-start | bytes 388
  48.6 5.0 %copy-start.1 = (f32[32,1,16,1024]{3,0,2,1:T(8,128)S(1)}, f32[32,1,16,1024]{3,0,2,1:T(8,128)}, u32[]{:S(2)}) copy-start(f32[32,1,16,1024]{3,0,2,1:T(8,128)} %copy-done) | copy-start | bytes 6291460
  48.6 5.0 %copy-start.5 = (f32[32,2,16]{0,2,1:T(8,128)S(1)}, f32[32,2,16]{0,2,1:T(8,128)}, u32[]{:S(2)}) copy-start(f32[32,2,16]{0,2,1:T(8,128)} %constant.137) | copy-start | bytes 12292
  49.7 24.2 %all-to-all-start.1 = ((bf16[32,2,16,3,1,128]{5,2,4,3,1,0:T(8,128)(2,1)}), bf16[32,2,16,3,1,128]{5,2,4,3,1,0:T(8,128)(2,1)S(1)}, u32[]{:S(2)}, u32[]{:S(2)}) async-start(bf16[32,2,16,3,1,128]{5,2,4,3,1,0:T(8,128)(2,1)} %bitcast.174), calls=%async_computation.1 | async-start | bytes 1572864 | tf_op jit(solution)/shard_map/all_to_all | solution.py:190
  77.1 1.1 %copy-start.4 = (bf16[3,1,128,1024]{3,2,1,0:T(8,128)(2,1)S(1)}, bf16[3,1,128,1024]{3,2,1,0:T(8,128)(2,1)}, u32[]{:S(2)}) copy-start(bf16[3,1,128,1024]{3,2,1,0:T(8,128)(2,1)} %param.7) | copy-start | bytes 2359300
